TPU v7x, 32 devices: a whole 2x2x4 slice. The times are simulated.
32 devices in a mesh: section: 4 (over y, x), mp: 2 (over core), dp: 4 (over z).
Axes of the slice: x: 2, y: 2, z: 4, core: 2. Of those that a mesh axis runs over, the one named last changes fastest.
Arguments:
- target_hidden: bfloat16 [4, 256, 8192], P('dp', None, 'section'), may hold values from -43 to 43, as said below
- embeds: bfloat16 [4, 256, 8192], P('dp', None, 'section'), may hold values from -50 to 50, as said below
- token_ids: int32 [4, 256], replicated, may hold values from 0 to 8191
- lengths: int32 [4], replicated, may hold values from 1 to 32, as said below
- offsets: int32 [4], replicated, may hold values from 0 to 224, as said below
- target_gain: float32 [8192], P('section'), may hold values from 0.5 to 1.5
- draft_gain: float32 [8192], P('section'), may hold values from 0.5 to 1.5
- head: bfloat16 [8192, 8192], P(('mp', 'dp'), 'section'), may hold values from -0.1875 to 0.1875
- fc_embed: bfloat16 [8192, 8192], P('section', ('mp', 'dp')), may hold values from -0.046875 to 0.046875
- fc_feature: bfloat16 [8192, 8192], P('section', ('mp', 'dp')), may hold values from -0.046875 to 0.046875
Outputs:
- loss: float32 [], replicated
- grad_embed: float32 [8192, 8192], P('section', ('mp', 'dp'))
- grad_feature: float32 [8192, 8192], P('section', ('mp', 'dp'))
Inputs may be any that keep to these rules, and one draw needn't show every extreme that they name: `lengths`: they sum to 64, and the longest response has exactly 32 rows. offsets + lengths <= 256 in every sequence; the sequence of the longest response starts at 224. `target_hidden`: real-valued features. `embeds`: real-valued embeddings.
All inputs are finite; a program needn't handle non-finite values.
Results may differ from a plain program's by a relative error of at most 0.0035.
The roundings to bfloat16 on the way count: a program that leaves them out, or rounds other values in their place, can miss the bound.
Values may be sent and summed in bfloat16 or wider, within the bound.
No kernel may reach another device: no remote copies, remote signals or barrier semaphores. Data moves between devices by JAX's collectives and lax.ppermute only.
A program may use at most 64 MiB of HBM per device.

v0:
```python
import jax
import jax.numpy as jnp
from jax import lax
from jax.sharding import PartitionSpec as P

D = 8192
R_OWN = 8


z_weight = 0.004
label_mix = 0.1
eps_norm = 1e-05


def contract_last(operand, weights):
    return lax.dot_general(
        operand, weights, (((1,), (1,)), ((), ())), preferred_element_type=jnp.float32
    )


def contract_first(operand, weights):
    return lax.dot_general(
        operand, weights, (((0,), (0,)), ((), ())), preferred_element_type=jnp.float32
    )


def sequence_of(packed, starts):
    return jnp.sum((starts[None, :] <= packed[:, None]).astype(jnp.int32), axis=1) - 1


def tile_sums(target_logit, draft_logit, labels, column_zero):
    is_label = (
        labels[:, None] - column_zero == jnp.arange(target_logit.shape[1], dtype=jnp.int32)[None, :]
    )
    target_exp = jnp.exp(target_logit)
    return (
        jnp.sum(target_exp, axis=1),
        jnp.sum(target_exp * draft_logit, axis=1),
        jnp.sum(jnp.exp(draft_logit), axis=1),
        jnp.sum(jnp.where(is_label, draft_logit, 0.0), axis=1),
    )


def tile_grad(target_logit, draft_logit, labels, column_zero, totals):
    target_total, cross_total, draft_total, label_logit = totals
    draft_lse = jnp.log(draft_total)
    target_lse = jnp.log(target_total)
    is_label = (
        labels[:, None] - column_zero == jnp.arange(target_logit.shape[1], dtype=jnp.int32)[None, :]
    )
    logit_grad = (
        (1.0 + 2.0 * z_weight * draft_lse)[:, None] * jnp.exp(draft_logit - draft_lse[:, None])
        - (1.0 - label_mix) * jnp.exp(target_logit - target_lse[:, None])
        - label_mix * is_label.astype(jnp.float32)
    )
    return logit_grad.astype(jnp.bfloat16)


def mean_loss(totals):
    target_total, cross_total, draft_total, label_logit = totals
    draft_lse = jnp.log(draft_total)
    row_loss = (
        draft_lse
        - (1.0 - label_mix) * cross_total / target_total
        - label_mix * label_logit
        + z_weight * draft_lse * draft_lse
    )
    return jnp.mean(row_loss)


def on_device(
    target_hidden,
    embeds,
    token_ids,
    lengths,
    offsets,
    target_gain,
    draft_gain,
    head,
    fc_embed,
    fc_feature,
):
    count_dp = lax.axis_size("dp")
    count_mp = lax.axis_size("mp")
    groups = count_mp * count_dp
    my_dp = lax.axis_index("dp")
    my_mp = lax.axis_index("mp")
    owner_index = my_mp * count_dp + my_dp
    section_index = lax.axis_index("section")
    slice_width = target_hidden.shape[2]
    seq_len = target_hidden.shape[1]
    vocab_tile = head.shape[0]
    slot_count = 2 * R_OWN // count_dp
    total_rows = R_OWN * groups
    starts = jnp.cumsum(lengths) - lengths
    first_row = starts[my_dp]
    my_count = lengths[my_dp]
    my_offset = offsets[my_dp]
    residue = my_mp * count_dp + jnp.arange(count_dp, dtype=jnp.int32)
    first_slot = (first_row - residue + groups - 1) // groups
    packed = (
        groups * (first_slot[:, None] + jnp.arange(slot_count, dtype=jnp.int32)[None, :])
        + residue[:, None]
    )
    is_live = (packed < first_row + my_count).reshape(-1, 1)
    flat_position = jnp.clip(my_offset + packed - first_row, 0, seq_len - 1).reshape(-1)
    taken_embed = jnp.take(embeds[0], flat_position, axis=0)
    taken_feature = jnp.take(target_hidden[0], flat_position, axis=0)
    send_embed = jnp.where(is_live, taken_embed, jnp.zeros_like(taken_embed)).reshape(
        count_dp, slot_count, slice_width
    )
    send_feature = jnp.where(is_live, taken_feature, jnp.zeros_like(taken_feature)).reshape(
        count_dp, slot_count, slice_width
    )
    got_embed, got_feature = (
        lax.all_to_all(send_embed, "dp", split_axis=0, concat_axis=0, tiled=True),
        lax.all_to_all(send_feature, "dp", split_axis=0, concat_axis=0, tiled=True),
    )
    slot_index = jnp.arange(R_OWN, dtype=jnp.int32)
    wanted = groups * slot_index + owner_index
    source = sequence_of(wanted, starts)
    source_first = (starts[source] - owner_index + groups - 1) // groups
    pick_index = source * slot_count + slot_index - source_first
    own_embed = jnp.take(got_embed.reshape(count_dp * slot_count, slice_width), pick_index, axis=0)
    own_feature = jnp.take(
        got_feature.reshape(count_dp * slot_count, slice_width), pick_index, axis=0
    )
    embed_all, feature_all = (
        lax.all_gather(own_embed, ("mp", "dp"), axis=0, tiled=True),
        lax.all_gather(own_feature, ("mp", "dp"), axis=0, tiled=True),
    )
    row_id = jnp.arange(total_rows, dtype=jnp.int32)
    packed_all = groups * (row_id % R_OWN) + row_id // R_OWN
    seq_all = sequence_of(packed_all, starts)
    position_all = offsets[seq_all] + packed_all - starts[seq_all]
    labels = token_ids.reshape(-1)[seq_all * seq_len + position_all]
    target_square = lax.psum(
        jnp.sum(jnp.square(feature_all.astype(jnp.float32)), axis=1), "section"
    )
    target_scale = lax.rsqrt(target_square / D + eps_norm)
    target_norm = (feature_all.astype(jnp.float32) * target_scale[:, None] * target_gain).astype(
        jnp.bfloat16
    )
    partial_value = jnp.dot(embed_all, fc_embed, preferred_element_type=jnp.float32) + jnp.dot(
        feature_all, fc_feature, preferred_element_type=jnp.float32
    )
    summed = lax.psum(partial_value, "section")
    spread = lax.all_to_all(summed, ("mp", "dp"), split_axis=0, concat_axis=1, tiled=True)
    hidden = lax.dynamic_slice_in_dim(spread, section_index * slice_width, slice_width, 1)
    draft_square = lax.psum(jnp.sum(hidden * hidden, axis=1), "section")
    draft_scale = lax.rsqrt(draft_square / D + eps_norm)
    draft_norm = (hidden * draft_scale[:, None] * draft_gain).astype(jnp.bfloat16)
    target_part = contract_last(target_norm, head)
    draft_part = contract_last(lax.all_gather(draft_norm, ("mp", "dp"), axis=0, tiled=True), head)
    target_logit, draft_logit = lax.psum((target_part, draft_part), "section")
    column_zero = owner_index * vocab_tile
    totals = lax.psum(tile_sums(target_logit, draft_logit, labels, column_zero), ("mp", "dp"))
    grad_tile = tile_grad(target_logit, draft_logit, labels, column_zero, totals)
    loss = mean_loss(totals)
    draft_grad = lax.psum_scatter(
        jnp.dot(grad_tile, head, preferred_element_type=jnp.float32),
        ("mp", "dp"),
        scatter_dimension=0,
        tiled=True,
    )
    upstream = draft_grad * draft_gain
    inner_sum = lax.psum(jnp.sum(hidden * upstream, axis=1), "section")
    hidden_grad = (
        draft_scale[:, None] * upstream - hidden * (draft_scale**3 * inner_sum / D)[:, None]
    ).astype(jnp.bfloat16)
    full_grad = lax.all_gather(hidden_grad, "section", axis=1, tiled=True)
    block_grad = lax.all_to_all(full_grad, ("mp", "dp"), split_axis=1, concat_axis=0, tiled=True)
    grad_embed = contract_first(embed_all, block_grad)
    grad_feature = contract_first(feature_all, block_grad)
    return (loss, grad_embed, grad_feature)


def solution(mesh):
    return jax.shard_map(
        on_device,
        mesh=mesh,
        in_specs=(
            P("dp", None, "section"),
            P("dp", None, "section"),
            P(),
            P(),
            P(),
            P("section"),
            P("section"),
            P(("mp", "dp"), "section"),
            P("section", ("mp", "dp")),
            P("section", ("mp", "dp")),
        ),
        out_specs=(P(), P("section", ("mp", "dp")), P("section", ("mp", "dp"))),
        check_vma=False,
    )
```

profile of v0, /device:TPU:0, one launch (start us, length us, event | category | flops | bytes accessed | tf_op | source)
XLA Modules:
  0.0 335.6 jit_solution(14348024160950690089)
XLA Ops:
  7.2 1.4 dynamic_slice.13
  8.6 0.8 reduce-window.9
  9.4 0.7 bitcast_subtract_fusion
  10.1 1.5 fusion.37
  11.6 0.7 and_select_fusion.5
  12.3 1.4 subtract_clamp_fusion
  15.2 0.1 lt.69
  15.3 0.6 gather_fusion.4
  15.9 2.0 gather_fusion.2
  17.9 0.1 select_select_fusion
  18.0 0.7 reshape.273
  18.6 6.3 %all-to-all-start.1 = ((bf16[4,4,2048]{2,1,0:T(4,128)(2,1)}), bf16[4,4,2048]{2,1,0:T(4,128)(2,1)S(1)}, u32[]{:S(2)}, u32[]{:S(2)}) async-start(bf16[4,4,2048]{2,1,0:T(4,128)(2,1)} %reshape.273), calls=%async_computation.1 | async-start | bytes 131072 | tf_op jit(solution)/shard_map/all_to_all | solution.py:117
  25.1 0.6 gather_fusion
  25.8 0.7 reshape.271
  26.4 4.3 %all-to-all-done.1 = bf16[4,4,2048]{2,1,0:T(4,128)(2,1)S(1)} async-done(((bf16[4,4,2048]{2,1,0:T(4,128)(2,1)}), bf16[4,4,2048]{2,1,0:T(4,128)(2,1)S(1)}, u32[]{:S(2)}, u32[]{:S(2)}) %all-to-all-start.1) | async-done | bytes 65568 | tf_op jit(solution)/shard_map/all_to_all | solution.py:117
  30.7 3.3 all-to-all-start
  34.1 0.6 gather_fusion.5
  34.7 5.0 %all-to-all-done = bf16[4,4,2048]{2,1,0:T(4,128)(2,1)S(1)} async-done(((bf16[4,4,2048]{2,1,0:T(4,128)(2,1)}), bf16[4,4,2048]{2,1,0:T(4,128)(2,1)S(1)}, u32[]{:S(2)}, u32[]{:S(2)}) %all-to-all-start) | async-done | bytes 65568 | tf_op jit(solution)/shard_map/all_to_all | solution.py:116
  39.8 0.6 gather_fusion.3
  40.4 24.4 %all_gather.13 = bf16[64,2048]{1,0:T(8,128)(2,1)S(1)} all-gather(bf16[8,2048]{1,0:T(8,128)(2,1)S(1)} %get-tuple-element.35), channel_id=1, replica_groups=mesh['section'=4,'mp'=2,'dp'=4] {'mp','dp'}, dimensions={0}, use_global_device_ids=true | all-gather | bytes 294912 | tf_op jit(solution)/shard_map/all_gather | solution.py:130
  64.9 24.3 %all_gather.12 = bf16[64,2048]{1,0:T(8,128)(2,1)S(1)} all-gather(bf16[8,2048]{1,0:T(8,128)(2,1)S(1)} %get-tuple-element.36), channel_id=1, replica_groups=mesh['section'=4,'mp'=2,'dp'=4] {'mp','dp'}, dimensions={0}, use_global_device_ids=true | all-gather | bytes 294912 | tf_op jit(solution)/shard_map/all_gather | solution.py:129
  89.1 3.0 fusion.39
  92.2 1.6 fusion
  93.8 43.6 %all-reduce.6.cloned.1.call-done = f32[8,8,1024]{2,1,0:T(8,128)} async-done(((f32[8,8,1024]{2,1,0:T(8,128)}), f32[8,8,1024]{2,1,0:T(8,128)}) %all-reduce.6.cloned.1.call-update) | async-done | bytes 262160 | tf_op jit(solution)/shard_map/psum | solution.py:147
  137.4 4.6 %all-to-all-start.2 = ((f32[8,8,1024]{2,1,0:T(8,128)}), f32[8,8,1024]{2,1,0:T(8,128)S(1)}, u32[]{:S(2)}, u32[]{:S(2)}) async-start(f32[8,8,1024]{2,1,0:T(8,128)} %all-reduce.6.cloned.1.call-done), calls=%async_computation.2 | async-start | bytes 524288 | tf_op jit(solution)/shard_map/all_to_all | solution.py:148
  142.2 0.2 fusion.1
  142.3 9.1 %all-to-all-done.2 = f32[8,8,1024]{2,1,0:T(8,128)S(1)} async-done(((f32[8,8,1024]{2,1,0:T(8,128)}), f32[8,8,1024]{2,1,0:T(8,128)S(1)}, u32[]{:S(2)}, u32[]{:S(2)}) %all-to-all-start.2) | async-done | bytes 262176 | tf_op jit(solution)/shard_map/all_to_all | solution.py:148
  151.4 0.1 multiply_reduce_fusion.2
  151.5 8.9 %all-reduce.1 = (f32[8]{0:T(128)S(1)}, f32[64]{0:T(128)S(1)}) all-reduce(f32[8]{0:T(128)S(1)} %multiply_reduce_fusion.2, f32[64]{0:T(128)S(1)} %fusion.1), channel_id=1, replica_groups=mesh['section'=4,'mp'=2,'dp'=4] {'section'}, use_global_device_ids=true, to_apply=%region_4.7 | all-reduce | flops 72 | bytes 576 | tf_op jit(solution)/shard_map/psum | solution.py:150
  160.6 24.4 %all_gather.14 = bf16[64,2048]{1,0:T(8,128)(2,1)S(1)} all-gather(bf16[8,2048]{1,0:T(8,128)(2,1)S(1)} %multiply_convert_fusion), channel_id=1, replica_groups=mesh['section'=4,'mp'=2,'dp'=4] {'mp','dp'}, dimensions={0}, use_global_device_ids=true | all-gather | bytes 294912 | tf_op jit(solution)/shard_map/all_gather | solution.py:154
  185.0 4.3 %fusion.40 = f32[64,1024]{1,0:T(8,128)} fusion(bf16[64,2048]{1,0:T(8,128)(2,1)S(1)} %all_gather.14, bf16[1024,2048]{1,0:T(8,128)(2,1)} %param.21), kind=kOutput, calls=%fused_computation.111 | convolution fusion | flops 268435456 | bytes 4718592 | tf_op jit(solution)/shard_map/dot_general | solution.py:16
  189.3 2.1 fusion.4
  191.5 5.1 %fusion.31 = s32[64]{0:T(128)S(1)} fusion(s32[64]{0:T(128)S(1)} %convert_reduce_fusion, s32[]{:T(128)} %bitcast.19, s32[]{:T(128)} %bitcast.15, s32[]{:T(128)} %bitcast.20, s32[]{:T(128)} %bitcast.16, s32[]{:T(128)} %bitcast.22, s32[]{:T(128)} %bitcast.21, s32[]{:T(128)} %bitcast.18, s32[]{:T(128)} %bitcast.17), kind=kLoop, calls=%fused_computation.94 | loop fusion | flops 2176 | bytes 544 | tf_op jit(solution)/shard_map/select_n | solution.py:136
  196.6 0.7 gather_fusion.1
  197.3 37.7 %all-reduce.8.cloned.1.call-done = (f32[64,1024]{1,0:T(8,128)}, f32[64,1024]{1,0:T(8,128)}) async-done(((f32[64,1024]{1,0:T(8,128)}, f32[64,1024]{1,0:T(8,128)}), (f32[64,1024]{1,0:T(8,128)}, f32[64,1024]{1,0:T(8,128)})) %all-reduce.8.cloned.1.call-update) | async-done | bytes 524304 | tf_op jit(solution)/shard_map/psum | solution.py:155
  235.0 1.3 exponential_reduce_fusion
  236.3 15.9 %all-reduce = (f32[64]{0:T(128)S(1)}, f32[64]{0:T(128)S(1)}, f32[64]{0:T(128)S(1)}, f32[64]{0:T(128)S(1)}) all-reduce(f32[64]{0:T(128)S(1)} %get-tuple-element.6, f32[64]{0:T(128)S(1)} %get-tuple-element.8, f32[64]{0:T(128)S(1)} %get-tuple-element.7, f32[64]{0:T(128)S(1)} %get-tuple-element.5), channel_id=1, replica_groups=mesh['section'=4,'mp'=2,'dp'=4] {'mp','dp'}, use_global_device_ids=true, to_apply=%region_17.20 | all-reduce | flops 256 | bytes 2048 | tf_op jit(solution)/shard_map/psum | solution.py:157
  252.2 0.6 multiply_add_fusion.1
  252.8 4.1 %fusion.8 = f32[64,2048]{1,0:T(8,128)} fusion(bf16[1024,2048]{1,0:T(8,128)(2,1)} %param.21, f32[64,1024]{1,0:T(8,128)} %get-tuple-element.16, f32[64,1024]{1,0:T(8,128)} %get-tuple-element.15, f32[64]{0:T(128)S(1)} %get-tuple-element.23, f32[64]{0:T(128)S(1)} %get-tuple-element.24, f32[64]{0:T(128)S(1)} %get-tuple-element.21, s32[64]{0:T(128)S(1)} %broadcast_subtract_fusion), kind=kOutput, calls=%fused_computation.22 | convolution fusion | flops 269025280 | bytes 5243904 | tf_op jit(solution)/shard_map/dot_general | solution.py:161
  257.0 31.1 %reduce-scatter.2.cloned.1.call-done = f32[8,2048]{1,0:T(8,128)} async-done(((f32[64,2048]{1,0:T(8,128)}), f32[8,2048]{1,0:T(8,128)}) %reduce-scatter.2.cloned.1.call-update) | async-done | bytes 65552 | tf_op jit(solution)/shard_map/reduce_scatter | solution.py:160
  288.1 1.0 multiply_reduce_fusion.1
  289.1 10.0 %psum.79 = f32[8]{0:T(128)S(1)} all-reduce(f32[8]{0:T(128)S(1)} %multiply_reduce_fusion.1), channel_id=1, replica_groups=mesh['section'=4,'mp'=2,'dp'=4] {'section'}, use_global_device_ids=true, to_apply=%region_21.24 | all-reduce | flops 8 | bytes 64 | tf_op jit(solution)/shard_map/psum | solution.py:167
  299.0 0.9 subtract_convert_fusion.2
  300.0 8.3 %all_gather.15 = bf16[8,8192]{1,0:T(8,128)(2,1)} all-gather(bf16[8,2048]{1,0:T(8,128)(2,1)S(1)} %subtract_convert_fusion.2), channel_id=1, replica_groups=mesh['section'=4,'mp'=2,'dp'=4] {'section'}, dimensions={1}, use_global_device_ids=true | all-gather | bytes 163840 | tf_op jit(solution)/shard_map/all_gather | solution.py:171
  308.3 3.4 %all-to-all-start.3 = ((bf16[8,8,1024]{2,0,1:T(8,128)(2,1)}), bf16[8,8,1024]{2,0,1:T(8,128)(2,1)S(1)}, u32[]{:S(2)}, u32[]{:S(2)}) async-start(bf16[8,8,1024]{2,0,1:T(8,128)(2,1)} %bitcast.24), calls=%async_computation.4 | async-start | bytes 262144 | tf_op jit(solution)/shard_map/all_to_all | solution.py:172
  312.3 6.2 %all-to-all-done.3 = bf16[8,8,1024]{2,0,1:T(8,128)(2,1)S(1)} async-done(((bf16[8,8,1024]{2,0,1:T(8,128)(2,1)}), bf16[8,8,1024]{2,0,1:T(8,128)(2,1)S(1)}, u32[]{:S(2)}, u32[]{:S(2)}) %all-to-all-start.3) | async-done | bytes 131104 | tf_op jit(solution)/shard_map/all_to_all | solution.py:172
  318.5 4.7 %fusion.9 = f32[2048,1024]{1,0:T(8,128)} fusion(bf16[64,2048]{1,0:T(8,128)(2,1)S(1)} %all_gather.13, bf16[8,8,1024]{2,0,1:T(8,128)(2,1)S(1)} %all-to-all-done.3), kind=kOutput, calls=%fused_computation.23 | convolution fusion | flops 268435456 | bytes 8781824 | tf_op jit(solution)/shard_map/dot_general | solution.py:22
  323.2 4.7 %fusion.11 = f32[2048,1024]{1,0:T(8,128)} fusion(bf16[64,2048]{1,0:T(8,128)(2,1)S(1)} %all_gather.12, bf16[8,8,1024]{2,0,1:T(8,128)(2,1)S(1)} %all-to-all-done.3), kind=kOutput, calls=%fused_computation.25 | convolution fusion | flops 268435456 | bytes 8781824 | tf_op jit(solution)/shard_map/dot_general | solution.py:22
  (42 shorter events, 0.9 us)
Async XLA Ops:
  7.2 8.1 %copy-start = (bf16[1,256,2048]{2,1,0:T(8,128)(2,1)S(1)}, bf16[1,256,2048]{2,1,0:T(8,128)(2,1)}, u32[]{:S(2)}) copy-start(bf16[1,256,2048]{2,1,0:T(8,128)(2,1)} %param.14) | copy-start | bytes 3145732
  18.6 12.1 %all-to-all-start.1 = ((bf16[4,4,2048]{2,1,0:T(4,128)(2,1)}), bf16[4,4,2048]{2,1,0:T(4,128)(2,1)S(1)}, u32[]{:S(2)}, u32[]{:S(2)}) async-start(bf16[4,4,2048]{2,1,0:T(4,128)(2,1)} %reshape.273), calls=%async_computation.1 | async-start | bytes 131072 | tf_op jit(solution)/shard_map/all_to_all | solution.py:117
  30.7 9.0 %all-to-all-start = ((bf16[4,4,2048]{2,1,0:T(4,128)(2,1)}), bf16[4,4,2048]{2,1,0:T(4,128)(2,1)S(1)}, u32[]{:S(2)}, u32[]{:S(2)}) async-start(bf16[4,4,2048]{2,1,0:T(4,128)(2,1)} %reshape.271), calls=%async_computation | async-start | bytes 131072 | tf_op jit(solution)/shard_map/all_to_all | solution.py:116
  34.0 103.4 %all-reduce.6.cloned.1.call-start = ((), (), s32[]{:S(2)}) async-start(), calls=%async_computation.5 | async-start | bytes 524288 | tf_op jit(solution)/shard_map/psum | solution.py:147
  40.3 51.8 %copy-start.2 = (bf16[2048,1024]{1,0:T(8,128)(2,1)S(1)}, bf16[2048,1024]{1,0:T(8,128)(2,1)}, u32[]{:S(2)}) copy-start(bf16[2048,1024]{1,0:T(8,128)(2,1)} %param.23) | copy-start | bytes 12582916
  92.2 59.3 %copy-start.5 = (s32[4,256]{1,0:T(4,128)S(1)}, s32[4,256]{1,0:T(4,128)}, u32[]{:S(2)}) copy-start(s32[4,256]{1,0:T(4,128)} %param.16) | copy-start | bytes 12292
  92.2 68.3 %copy-start.3 = (f32[2048]{0:T(1024)S(1)}, f32[2048]{0:T(1024)}, u32[]{:S(2)}) copy-start(f32[2048]{0:T(1024)} %param.20) | copy-start | bytes 24580
  93.7 95.5 %copy-start.4 = (f32[2048]{0:T(1024)S(1)}, f32[2048]{0:T(1024)}, u32[]{:S(2)}) copy-start(f32[2048]{0:T(1024)} %param.19) | copy-start | bytes 24580
  137.4 14.0 %all-to-all-start.2 = ((f32[8,8,1024]{2,1,0:T(8,128)}), f32[8,8,1024]{2,1,0:T(8,128)S(1)}, u32[]{:S(2)}, u32[]{:S(2)}) async-start(f32[8,8,1024]{2,1,0:T(8,128)} %all-reduce.6.cloned.1.call-done), calls=%async_computation.2 | async-start | bytes 524288 | tf_op jit(solution)/shard_map/all_to_all | solution.py:148
  142.0 93.0 %all-reduce.8.cloned.1.call-start = ((), (), s32[]{:S(2)}) async-start(), calls=%async_computation.7 | async-start | bytes 1048576 | tf_op jit(solution)/shard_map/psum | solution.py:155
  160.5 28.8 %copy-start.1 = (bf16[1024,2048]{1,0:T(8,128)(2,1)S(1)}, bf16[1024,2048]{1,0:T(8,128)(2,1)}, u32[]{:S(2)}) copy-start(bf16[1024,2048]{1,0:T(8,128)(2,1)} %param.21) | copy-start | bytes 12582916
  191.4 96.7 %reduce-scatter.2.cloned.1.call-start = ((), (), s32[]{:S(2)}) async-start(), calls=%async_computation.6 | async-start | bytes 589824 | tf_op jit(solution)/shard_map/reduce_scatter | solution.py:160
  308.3 10.2 %all-to-all-start.3 = ((bf16[8,8,1024]{2,0,1:T(8,128)(2,1)}), bf16[8,8,1024]{2,0,1:T(8,128)(2,1)S(1)}, u32[]{:S(2)}, u32[]{:S(2)}) async-start(bf16[8,8,1024]{2,0,1:T(8,128)(2,1)} %bitcast.24), calls=%async_computation.4 | async-start | bytes 262144 | tf_op jit(solution)/shard_map/all_to_all | solution.py:172
Sparse Core Ops, SparseCore 0:
  93.9 43.4 all-reduce.5
  191.6 43.4 all-reduce.7
  257.1 30.9 reduce-scatter.1
where the time goes:
time: 337 us; the launch traced here: 336 us
  waiting for transfers between devices  137 us (41%)
  blocking collectives  116 us (34%)
  matrix products  24.4 us (7%)
  starting transfers between devices  17.7 us (5%)
  between operations  17.1 us (5%)
  other arithmetic  13.2 us (4%)
  local copies, waits for them, and re-layouts  9.64 us (3%)
    psum x1, waiting for transfers between devices, on_device(): summed = lax.psum(partial_value, 'section')  43.6 us
    psum x1, waiting for transfers between devices, on_device(): target_logit, draft_logit = lax.psum((target_part, draft_part), 'section')  37.7 us
    reduce_scatter x1, waiting for transfers between devices, on_device(): lax.psum_scatter(jnp.dot(grad_tile, head, preferred_element_type=jnp.floa...  31.1 us
    all_gather x1, blocking collectives, on_device(): lax.all_gather(own_feature, ('mp', 'dp'), axis=0, tiled=True)  24.4 us
    all_gather x1, blocking collectives, on_device(): lax.all_gather(draft_norm, ('mp', 'dp'), axis=0, tiled=True)  24.4 us
    all_gather x1, blocking collectives, on_device(): lax.all_gather(own_embed, ('mp', 'dp'), axis=0, tiled=True)  24.3 us
    psum x1, blocking collectives, on_device(): lax.psum(tile_sums(target_logit, draft_logit, labels, column_zero), ('mp'...  15.9 us
    psum x1, blocking collectives, on_device(): inner_sum = lax.psum(jnp.sum(hidden * upstream, axis=1), 'section')  9.95 us
  transfers between devices with their start and end apart: 7, of which 7 were waited for; matrix products, arithmetic and copies ran while one was open for 2% of the time, Pallas kernels for 0%

commit v1 on v0

v1 whole, which is shorter than its diff:
```python
import jax
import jax.numpy as jnp
from jax import lax
from jax.sharding import PartitionSpec as P

D = 8192
R_OWN = 8


z_weight = 0.004
label_mix = 0.1
eps_norm = 1e-05

ALL = ("section", "mp", "dp")


def contract_last(operand, weights):
    return lax.dot_general(
        operand, weights, (((1,), (1,)), ((), ())), preferred_element_type=jnp.float32
    )


def contract_first(operand, weights):
    return lax.dot_general(
        operand, weights, (((0,), (0,)), ((), ())), preferred_element_type=jnp.float32
    )


def sequence_of(packed, starts):
    return jnp.sum((starts[None, :] <= packed[:, None]).astype(jnp.int32), axis=1) - 1


def exchange(send, axes):
    return lax.all_to_all(send, axes, split_axis=0, concat_axis=0, tiled=True)


def gather_axis(x, axis):
    count = lax.axis_size(axis)
    if count == 2:
        other = lax.ppermute(x, axis, [(0, 1), (1, 0)])
        mine = lax.axis_index(axis)
        return jnp.where(mine == 0, jnp.stack([x, other]), jnp.stack([other, x]))
    return exchange(jnp.broadcast_to(x[None], (count,) + x.shape), axis)


def pad_cols(count):
    return -(-count // 128) * 128


def on_device(
    target_hidden,
    embeds,
    token_ids,
    lengths,
    offsets,
    target_gain,
    draft_gain,
    head,
    fc_embed,
    fc_feature,
):
    count_dp = lax.axis_size("dp")
    count_mp = lax.axis_size("mp")
    count_sec = lax.axis_size("section")
    groups = count_mp * count_dp
    n_dev = count_sec * groups
    my_dp = lax.axis_index("dp")
    my_mp = lax.axis_index("mp")
    my_sec = lax.axis_index("section")
    me = (my_sec * count_mp + my_mp) * count_dp + my_dp
    width = target_hidden.shape[2]
    seq_len = target_hidden.shape[1]
    vocab_tile = head.shape[0]
    block = fc_embed.shape[1]
    full_width = width * count_sec
    total_rows = R_OWN * groups
    per_dev = total_rows // n_dev
    half = 2 * R_OWN
    starts = jnp.cumsum(lengths) - lengths

    gain_full = gather_axis(draft_gain, "section").reshape(full_width)

    slot = my_mp * half + jnp.arange(half, dtype=jnp.int32)
    pos = jnp.clip(offsets[my_dp] + slot, 0, seq_len - 1)
    mine = jnp.stack([jnp.take(embeds[0], pos, axis=0), jnp.take(target_hidden[0], pos, axis=0)])
    by_dp = exchange(jnp.broadcast_to(mine[None], (count_dp,) + mine.shape), "dp")
    every = gather_axis(by_dp, "mp")
    every = every.transpose(2, 0, 1, 3, 4).reshape(2, count_mp * count_dp * half, width)
    packed = jnp.arange(total_rows, dtype=jnp.int32)
    seq_all = sequence_of(packed, starts)
    slot_all = packed - starts[seq_all]
    pick = ((slot_all // half) * count_dp + seq_all) * half + slot_all % half
    embed_all = jnp.take(every[0], pick, axis=0)
    feature_all = jnp.take(every[1], pick, axis=0)
    position_all = offsets[seq_all] + slot_all
    labels_all = token_ids.reshape(-1)[seq_all * seq_len + position_all]
    my_rows = me * per_dev + jnp.arange(per_dev, dtype=jnp.int32)
    labels = labels_all[my_rows]

    partial_value = jnp.dot(embed_all, fc_embed, preferred_element_type=jnp.float32) + jnp.dot(
        feature_all, fc_feature, preferred_element_type=jnp.float32
    )
    target_square = jnp.sum(jnp.square(feature_all.astype(jnp.float32)), axis=1)
    spare = total_rows // per_dev
    extra = jnp.pad(target_square.reshape(per_dev, spare), ((0, 0), (0, pad_cols(spare) - spare)))
    send1 = jnp.concatenate(
        [
            partial_value.reshape(n_dev, per_dev, block),
            jnp.broadcast_to(extra[None], (n_dev,) + extra.shape),
        ],
        axis=2,
    )
    got1 = exchange(send1, ALL).reshape(count_sec, groups, per_dev, -1)
    hidden = (
        jnp.sum(got1[..., :block], axis=0).transpose(1, 0, 2).reshape(per_dev, groups * block)
    )
    target_square = jnp.sum(got1[:, 0, :, block : block + spare], axis=0).reshape(total_rows)
    target_scale = lax.rsqrt(target_square / D + eps_norm)
    target_norm = (feature_all.astype(jnp.float32) * target_scale[:, None] * target_gain).astype(
        jnp.bfloat16
    )
    draft_square = jnp.sum(hidden * hidden, axis=1)
    draft_scale = lax.rsqrt(draft_square / D + eps_norm)
    draft_norm = (hidden * draft_scale[:, None] * gain_full).astype(jnp.bfloat16)

    send2 = jnp.broadcast_to(
        draft_norm.reshape(per_dev, count_sec, 1, width).transpose(1, 2, 0, 3),
        (count_sec, groups, per_dev, width),
    ).reshape(n_dev, per_dev, width)
    draft_norm_all = exchange(send2, ALL).reshape(total_rows, width)

    target_part = contract_last(target_norm, head)
    draft_part = contract_last(draft_norm_all, head)
    send3 = (
        jnp.stack([target_part, draft_part])
        .reshape(2, n_dev, per_dev, vocab_tile)
        .transpose(1, 0, 2, 3)
    )
    got3 = exchange(send3, ALL).reshape(count_sec, groups, 2, per_dev, vocab_tile)
    logits = jnp.sum(got3, axis=0).transpose(1, 2, 0, 3).reshape(2, per_dev, groups * vocab_tile)
    target_logit, draft_logit = logits[0], logits[1]
    vocab = groups * vocab_tile
    is_label = labels[:, None] == jnp.arange(vocab, dtype=jnp.int32)[None, :]
    target_exp = jnp.exp(target_logit)
    target_total = jnp.sum(target_exp, axis=1)
    cross_total = jnp.sum(target_exp * draft_logit, axis=1)
    draft_total = jnp.sum(jnp.exp(draft_logit), axis=1)
    label_logit = jnp.sum(jnp.where(is_label, draft_logit, 0.0), axis=1)
    draft_lse = jnp.log(draft_total)
    target_lse = jnp.log(target_total)
    row_loss = (
        draft_lse
        - (1.0 - label_mix) * cross_total / target_total
        - label_mix * label_logit
        + z_weight * draft_lse * draft_lse
    )
    logit_grad = (
        (
            (1.0 + 2.0 * z_weight * draft_lse)[:, None] * jnp.exp(draft_logit - draft_lse[:, None])
            - (1.0 - label_mix) * jnp.exp(target_logit - target_lse[:, None])
            - label_mix * is_label.astype(jnp.float32)
        )
    ).astype(jnp.bfloat16)

    send4 = jnp.broadcast_to(
        logit_grad.reshape(per_dev, 1, groups, vocab_tile).transpose(1, 2, 0, 3),
        (count_sec, groups, per_dev, vocab_tile),
    ).reshape(n_dev, per_dev, vocab_tile)
    grad_tile = exchange(send4, ALL).reshape(total_rows, vocab_tile)

    grad_part = jnp.dot(grad_tile, head, preferred_element_type=jnp.float32)
    loss_cols = jnp.pad(row_loss[:, None], ((0, 0), (0, 127)))
    send5 = jnp.concatenate(
        [
            grad_part.reshape(n_dev, per_dev, width),
            jnp.broadcast_to(loss_cols[None], (n_dev,) + loss_cols.shape),
        ],
        axis=2,
    )
    got5 = exchange(send5, ALL).reshape(count_sec, groups, per_dev, -1)
    draft_grad = (
        jnp.sum(got5[..., :width], axis=1).transpose(1, 0, 2).reshape(per_dev, full_width)
    )
    loss = jnp.mean(got5[..., width].reshape(total_rows))
    upstream = draft_grad * gain_full
    inner_sum = jnp.sum(hidden * upstream, axis=1)
    hidden_grad = (
        draft_scale[:, None] * upstream - hidden * (draft_scale**3 * inner_sum / D)[:, None]
    ).astype(jnp.bfloat16)

    send6 = jnp.broadcast_to(
        hidden_grad.reshape(per_dev, 1, groups, block).transpose(1, 2, 0, 3),
        (count_sec, groups, per_dev, block),
    ).reshape(n_dev, per_dev, block)
    block_grad = exchange(send6, ALL).reshape(total_rows, block)
    grad_embed = contract_first(embed_all, block_grad)
    grad_feature = contract_first(feature_all, block_grad)
    return (loss, grad_embed, grad_feature)


def solution(mesh):
    return jax.shard_map(
        on_device,
        mesh=mesh,
        in_specs=(
            P("dp", None, "section"),
            P("dp", None, "section"),
            P(),
            P(),
            P(),
            P("section"),
            P("section"),
            P(("mp", "dp"), "section"),
            P("section", ("mp", "dp")),
            P("section", ("mp", "dp")),
        ),
        out_specs=(P(), P("section", ("mp", "dp")), P("section", ("mp", "dp"))),
        check_vma=False,
    )
```

time: 337 us -> 155 us (0.46)
  blocking collectives: 116 us -> 0 us
  waiting for transfers between devices: 137 us -> 67.7 us
  between operations: 17.1 us -> 2.79 us
  starting transfers between devices: 17.7 us -> 31.1 us
  local copies, waits for them, and re-layouts: 9.64 us -> 15.6 us
    all_gather x4 -> x0, blocking collectives: 81.4 us -> none  [the longest x1 24.4 us: on_device(): lax.all_gather(own_feature, ('mp', 'dp'), axis=0, tiled=True)]
    psum x2 -> x0, waiting for transfers between devices: 81.4 us -> none  [the longest x1 43.6 us: on_device(): summed = lax.psum(partial_value, 'section')]
    all_to_all x4 -> x8, waiting for transfers between devices: 24.6 us -> 67.7 us  [exchange(): return lax.all_to_all(send, axes, split_axis=0, concat_axis=0, tiled=True)]
    psum x3 -> x0, blocking collectives: 34.8 us -> none  [the longest x1 15.9 us: on_device(): lax.psum(tile_sums(target_logit, draft_logit, labels, column_zero), ('mp'...]
    reduce_scatter x1 -> x0, waiting for transfers between devices: 31.1 us -> none  [on_device(): lax.psum_scatter(jnp.dot(grad_tile, head, preferred_element_type=jnp.floa...]
    all_to_all x4 -> x8, starting transfers between devices: 17.6 us -> 31.1 us  [exchange(): return lax.all_to_all(send, axes, split_axis=0, concat_axis=0, tiled=True)]
    broadcast_in_dim x0 -> x7, local copies, waits for them, and re-layouts: none -> 4.5 us  [the longest x1 1.33 us: gather_axis(): return exchange(jnp.broadcast_to(x[None], (count,) + x.shape), axis)]
    gather x7 -> x8, local copies, waits for them, and re-layouts: 6.66 us -> 7.6 us  [the longest x1 2.02 us: on_device(): jnp.take(embeds[0], pos, axis=0)]
  transfers between devices with their start and end apart: 7 -> 9, of which waited for: 7 -> 7; matrix products, arithmetic and copies ran while one was open for 2% -> 15% of each run, Pallas kernels for 0% -> 0%
where the time goes in v1:
time: 155 us; the launch traced here: 154 us
  waiting for transfers between devices  67.7 us (44%)
  starting transfers between devices  31.1 us (20%)
  matrix products  23.8 us (15%)
  local copies, waits for them, and re-layouts  15.6 us (10%)
  other arithmetic  13.4 us (9%)
  between operations  2.79 us (2%)
    all_to_all x8, waiting for transfers between devices, exchange(): return lax.all_to_all(send, axes, split_axis=0, concat_axis=0, tiled=True)  67.7 us
    all_to_all x8, starting transfers between devices, exchange(): return lax.all_to_all(send, axes, split_axis=0, concat_axis=0, tiled=True)  31.1 us
    dot_general x2, matrix products, contract_first(): lax.dot_general(operand, weights, (((0,), (0,)), ((), ())), preferred_ele...  9.52 us
    dot_general x2, matrix products, contract_last(): lax.dot_general(operand, weights, (((1,), (1,)), ((), ())), preferred_ele...  7.16 us
    select_n x1, other arithmetic, on_device(): labels_all = token_ids.reshape(-1)[seq_all * seq_len + position_all]  4.95 us
    dot_general x1, matrix products, on_device(): jnp.dot(embed_all, fc_embed, preferred_element_type=jnp.float32)  3.22 us
  transfers between devices with their start and end apart: 9, of which 7 were waited for; matrix products, arithmetic and copies ran while one was open for 15% of the time, Pallas kernels for 0%

profile of v1, /device:TPU:0, one launch (start us, length us, event | category | flops | bytes accessed | tf_op | source)
XLA Modules:
  0.0 154.4 jit_solution(7167872889041411199)
XLA Ops:
  0.7 1.5 fusion.47
  2.1 0.7 compare_and_fusion.1
  2.8 0.6 gather_fusion.3
  3.4 2.0 %gather_fusion.2 = bf16[16,2048]{1,0:T(8,128)(2,1)S(1)} fusion(bf16[256,2048]{1,0:T(8,128)(2,1)} %bitcast.173, s32[1024]{0:T(1024)S(1)} %pad_clamp_fusion.3), kind=kCustom, calls=%fused_computation.clone | custom fusion | bytes 131136 | tf_op jit(solution)/shard_map/jit(_take)/gather | solution.py:85
  5.5 0.8 broadcast_in_dim.42
  6.4 6.3 %all-to-all-start = ((bf16[4,2,16,2048]{3,2,1,0:T(8,128)(2,1)}), bf16[4,2,16,2048]{3,2,1,0:T(8,128)(2,1)S(1)}, u32[]{:S(2)}, u32[]{:S(2)}) async-start(bf16[4,2,16,2048]{3,2,1,0:T(8,128)(2,1)} %broadcast_in_dim.42), calls=%async_computation | async-start | bytes 1048576 | tf_op jit(solution)/shard_map/all_to_all | solution.py:34
  12.7 0.8 reduce-window.9
  13.5 0.7 bitcast_subtract_fusion.5
  14.2 13.0 %all-to-all-done = bf16[4,2,16,2048]{3,2,1,0:T(8,128)(2,1)S(1)} async-done(((bf16[4,2,16,2048]{3,2,1,0:T(8,128)(2,1)}), bf16[4,2,16,2048]{3,2,1,0:T(8,128)(2,1)S(1)}, u32[]{:S(2)}, u32[]{:S(2)}) %all-to-all-start) | async-done | bytes 524320 | tf_op jit(solution)/shard_map/all_to_all | solution.py:34
  27.2 1.3 broadcast_in_dim.44
  28.5 3.7 %all-to-all-start.2 = ((f32[4,1,2048]{2,1,0:T(1,128)}), f32[4,1,2048]{2,1,0:T(1,128)S(1)}, u32[]{:S(2)}, u32[]{:S(2)}) async-start(f32[4,1,2048]{2,1,0:T(1,128)} %broadcast_in_dim.44), calls=%async_computation.2 | async-start | bytes 65536 | tf_op jit(solution)/shard_map/all_to_all | solution.py:34
  32.3 0.7 fusion.48
  33.0 2.4 %compare_and_fusion = (pred[64]{0:T(512)(128)(4,1)S(1)}, s32[64]{0:T(128)S(1)}) fusion(s32[]{:T(128)} %bitcast.7, s32[]{:T(128)} %bitcast.6, s32[]{:T(128)} %bitcast.5, s32[]{:T(128)} %bitcast.4, s32[64]{0:T(128)S(1)} %convert_reduce_fusion), kind=kLoop, calls=%fused_computation.78 | loop fusion | flops 2560 | bytes 592 | tf_op jit(solution)/shard_map/jit(_take)/and | solution.py:94
  35.8 0.7 gather_fusion.5
  36.5 0.7 gather_fusion.4
  37.3 0.2 fusion.8
  37.6 3.2 %fusion.18 = f32[64,1024]{1,0:T(8,128)S(1)} fusion(bf16[2048,1024]{1,0:T(8,128)(2,1)} %param.22, bf16[64,2048]{1,0:T(8,128)(2,1)S(1)} %gather_fusion.5, pred[64]{0:T(512)(128)(4,1)S(1)} %get-tuple-element.9), kind=kOutput, calls=%fused_computation.35 | convolution fusion | flops 268566528 | bytes 4718656 | tf_op jit(solution)/shard_map/dot_general | solution.py:100
  40.8 0.2 copy-done.1
  41.0 0.9 convolution_add_fusion
  42.1 0.8 pad_maximum_fusion.1
  43.0 4.3 %all-to-all-start.1 = ((f32[32,2,1152]{2,1,0:T(2,128)}), f32[32,2,1152]{2,1,0:T(2,128)S(1)}, u32[]{:S(2)}, u32[]{:S(2)}) async-start(f32[32,2,1152]{2,1,0:T(2,128)} %pad_maximum_fusion.1), calls=%async_computation.1 | async-start | bytes 589824 | tf_op jit(solution)/shard_map/all_to_all | solution.py:34
  47.3 10.7 %all-to-all-done.1 = f32[32,2,1152]{2,1,0:T(2,128)S(1)} async-done(((f32[32,2,1152]{2,1,0:T(2,128)}), f32[32,2,1152]{2,1,0:T(2,128)S(1)}, u32[]{:S(2)}, u32[]{:S(2)}) %all-to-all-start.1) | async-done | bytes 294944 | tf_op jit(solution)/shard_map/all_to_all | solution.py:34
  58.4 0.9 broadcast_in_dim.46
  59.2 2.9 %all-to-all-start.3 = ((bf16[32,2,2048]{2,1,0:T(2,128)(2,1)}), bf16[32,2,2048]{2,1,0:T(2,128)(2,1)S(1)}, u32[]{:S(2)}, u32[]{:S(2)}) async-start(bf16[32,2,2048]{2,1,0:T(2,128)(2,1)} %bitcast.24), calls=%async_computation.3 | async-start | bytes 524288 | tf_op jit(solution)/shard_map/all_to_all | solution.py:34
  62.2 3.6 %fusion.11 = f32[64,1024]{1,0:T(8,128)S(1)} fusion(bf16[1024,2048]{1,0:T(8,128)(2,1)} %param.21, f32[2048]{0:T(1024)S(1)} %copy-done.2, f32[64]{0:T(128)S(1)} %rsqrt.21, bf16[64,2048]{1,0:T(8,128)(2,1)S(1)} %gather_fusion.4, pred[64]{0:T(512)(128)(4,1)S(1)} %get-tuple-element.9), kind=kOutput, calls=%fused_computation.23 | convolution fusion | flops 269090816 | bytes 4727104 | tf_op jit(solution)/shard_map/dot_general | solution.py:18
  66.1 6.3 %all-to-all-done.3 = bf16[32,2,2048]{2,1,0:T(2,128)(2,1)S(1)} async-done(((bf16[32,2,2048]{2,1,0:T(2,128)(2,1)}), bf16[32,2,2048]{2,1,0:T(2,128)(2,1)S(1)}, u32[]{:S(2)}, u32[]{:S(2)}) %all-to-all-start.3) | async-done | bytes 262176 | tf_op jit(solution)/shard_map/all_to_all | solution.py:34
  72.3 3.6 %fusion.4 = f32[1,32,2,1024]{3,1,2,0:T(8,128)S(1)} fusion(bf16[1024,2048]{1,0:T(8,128)(2,1)} %param.21, bf16[32,2,2048]{2,1,0:T(2,128)(2,1)S(1)} %all-to-all-done.3), kind=kOutput, calls=%fused_computation.10 | convolution fusion | flops 268435456 | bytes 4718592 | tf_op jit(solution)/shard_map/dot_general | solution.py:18
  76.0 1.2 copy.33
  77.2 2.7 %all-to-all-start.4 = ((f32[32,2,2,1024]{3,2,1,0:T(2,128)}), f32[32,2,2,1024]{3,2,1,0:T(2,128)S(1)}, u32[]{:S(2)}, u32[]{:S(2)}) async-start(f32[32,2,2,1024]{3,2,1,0:T(2,128)} %copy.33), calls=%async_computation.4 | async-start | bytes 1048576 | tf_op jit(solution)/shard_map/all_to_all | solution.py:34
  79.9 4.9 %fusion.40 = s32[64]{0:T(128)S(1)} fusion(s32[]{:T(128)} %bitcast.32, s32[]{:T(128)} %bitcast.33, s32[]{:T(128)} %bitcast.35, s32[]{:T(128)} %bitcast.34, s32[64]{0:T(128)S(1)} %convert_reduce_fusion, s32[]{:T(128)} %bitcast.7, s32[]{:T(128)} %bitcast.6, s32[]{:T(128)} %bitcast.5, s32[]{:T(128)} %bitcast.4), kind=kLoop, calls=%fused_computation.99 | loop fusion | flops 1280 | bytes 544 | tf_op jit(solution)/shard_map/select_n | solution.py:96
  84.8 0.7 gather_fusion
  85.6 0.6 gather_fusion.1
  86.2 7.8 %all-to-all-done.4 = f32[32,2,2,1024]{3,2,1,0:T(2,128)S(1)} async-done(((f32[32,2,2,1024]{3,2,1,0:T(2,128)}), f32[32,2,2,1024]{3,2,1,0:T(2,128)S(1)}, u32[]{:S(2)}, u32[]{:S(2)}) %all-to-all-start.4) | async-done | bytes 524320 | tf_op jit(solution)/shard_map/all_to_all | solution.py:34
  94.1 0.3 reduce_sum.122
  94.4 0.3 exponential_reduce_fusion
  94.9 0.7 broadcast_in_dim.48
  95.6 4.2 %all-to-all-start.5 = ((bf16[32,2,1024]{2,1,0:T(2,128)(2,1)}), bf16[32,2,1024]{2,1,0:T(2,128)(2,1)S(1)}, u32[]{:S(2)}, u32[]{:S(2)}) async-start(bf16[32,2,1024]{2,1,0:T(2,128)(2,1)} %bitcast.40), calls=%async_computation.5 | async-start | bytes 262144 | tf_op jit(solution)/shard_map/all_to_all | solution.py:34
  99.9 8.3 %all-to-all-done.5 = bf16[32,2,1024]{2,1,0:T(2,128)(2,1)S(1)} async-done(((bf16[32,2,1024]{2,1,0:T(2,128)(2,1)}), bf16[32,2,1024]{2,1,0:T(2,128)(2,1)S(1)}, u32[]{:S(2)}, u32[]{:S(2)}) %all-to-all-start.5) | async-done | bytes 131104 | tf_op jit(solution)/shard_map/all_to_all | solution.py:34
  108.2 3.0 %fusion = f32[32,2,2048]{2,0,1:T(8,128)S(1)} fusion(bf16[1024,2048]{1,0:T(8,128)(2,1)} %param.21, bf16[32,2,1024]{2,1,0:T(2,128)(2,1)S(1)} %all-to-all-done.5), kind=kOutput, calls=%fused_computation.6 | convolution fusion | flops 268435456 | bytes 4849664 | tf_op jit(solution)/shard_map/dot_general | solution.py:171
  111.3 1.2 copy.36
  112.5 2.6 %all-to-all-start.6 = ((f32[32,2,2176]{2,1,0:T(2,128)}), f32[32,2,2176]{2,1,0:T(2,128)S(1)}, u32[]{:S(2)}, u32[]{:S(2)}) async-start(f32[32,2,2176]{2,1,0:T(2,128)} %copy.36), calls=%async_computation.6 | async-start | bytes 1114112 | tf_op jit(solution)/shard_map/all_to_all | solution.py:34
  115.2 14.8 %all-to-all-done.6 = f32[32,2,2176]{2,1,0:T(2,128)S(1)} async-done(((f32[32,2,2176]{2,1,0:T(2,128)}), f32[32,2,2176]{2,1,0:T(2,128)S(1)}, u32[]{:S(2)}, u32[]{:S(2)}) %all-to-all-start.6) | async-done | bytes 557088 | tf_op jit(solution)/shard_map/all_to_all | solution.py:34
  130.4 0.7 broadcast_in_dim.52
  131.2 4.4 %all-to-all-start.7 = ((bf16[32,2,1024]{2,1,0:T(2,128)(2,1)}), bf16[32,2,1024]{2,1,0:T(2,128)(2,1)S(1)}, u32[]{:S(2)}, u32[]{:S(2)}) async-start(bf16[32,2,1024]{2,1,0:T(2,128)(2,1)} %bitcast.50), calls=%async_computation.7 | async-start | bytes 262144 | tf_op jit(solution)/shard_map/all_to_all | solution.py:34
  135.5 0.6 slice_reduce_fusion.2
  136.8 6.9 %all-to-all-done.7 = bf16[32,2,1024]{2,1,0:T(2,128)(2,1)S(1)} async-done(((bf16[32,2,1024]{2,1,0:T(2,128)(2,1)}), bf16[32,2,1024]{2,1,0:T(2,128)(2,1)S(1)}, u32[]{:S(2)}, u32[]{:S(2)}) %all-to-all-start.7) | async-done | bytes 131104 | tf_op jit(solution)/shard_map/all_to_all | solution.py:34
  143.8 4.8 %fusion.45 = f32[2048,1024]{1,0:T(8,128)} fusion(bf16[64,1024]{1,0:T(8,128)(2,1)S(1)} %reshape.448, bf16[64,2048]{1,0:T(8,128)(2,1)S(1)} %gather_fusion.4, pred[64]{0:T(512)(128)(4,1)S(1)} %get-tuple-element.9), kind=kOutput, calls=%fused_computation.113 | convolution fusion | flops 268566528 | bytes 8781888 | tf_op jit(solution)/shard_map/dot_general | solution.py:24
  148.6 4.8 %fusion.17 = f32[2048,1024]{1,0:T(8,128)} fusion(bf16[64,1024]{1,0:T(8,128)(2,1)S(1)} %reshape.448, bf16[64,2048]{1,0:T(8,128)(2,1)S(1)} %gather_fusion.5, pred[64]{0:T(512)(128)(4,1)S(1)} %get-tuple-element.9), kind=kOutput, calls=%fused_computation.34 | convolution fusion | flops 268566528 | bytes 8781888 | tf_op jit(solution)/shard_map/dot_general | solution.py:24
  (52 shorter events, 2.5 us)
Async XLA Ops:
  0.6 2.2 %copy-start = (bf16[1,256,2048]{2,1,0:T(8,128)(2,1)S(1)}, bf16[1,256,2048]{2,1,0:T(8,128)(2,1)}, u32[]{:S(2)}) copy-start(bf16[1,256,2048]{2,1,0:T(8,128)(2,1)} %param.14) | copy-start | bytes 3145732
  6.4 20.8 %all-to-all-start = ((bf16[4,2,16,2048]{3,2,1,0:T(8,128)(2,1)}), bf16[4,2,16,2048]{3,2,1,0:T(8,128)(2,1)S(1)}, u32[]{:S(2)}, u32[]{:S(2)}) async-start(bf16[4,2,16,2048]{3,2,1,0:T(8,128)(2,1)} %broadcast_in_dim.42), calls=%async_computation | async-start | bytes 1048576 | tf_op jit(solution)/shard_map/all_to_all | solution.py:34
  28.5 14.4 %all-to-all-start.2 = ((f32[4,1,2048]{2,1,0:T(1,128)}), f32[4,1,2048]{2,1,0:T(1,128)S(1)}, u32[]{:S(2)}, u32[]{:S(2)}) async-start(f32[4,1,2048]{2,1,0:T(1,128)} %broadcast_in_dim.44), calls=%async_computation.2 | async-start | bytes 65536 | tf_op jit(solution)/shard_map/all_to_all | solution.py:34
  32.3 3.2 %collective-permute-start = (bf16[4,2,16,2048]{3,2,1,0:T(8,128)(2,1)S(1)}, bf16[4,2,16,2048]{3,2,1,0:T(8,128)(2,1)S(1)}, u32[]{:S(2)}, u32[]{:S(2)}) collective-permute-start(bf16[4,2,16,2048]{3,2,1,0:T(8,128)(2,1)S(1)} %all-to-all-done), channel_id=1, source_target_pairs={{0,4},{4,0},{1,5},{5,1},{2,6},{6,2},{3,7},{7,3},{8,12},{12,8},{9,1... | collective-permute-start | bytes 1572872 | tf_op jit(solution)/shard_map/ppermute | solution.py:40
  37.6 3.5 %copy-start.1 = (bf16[2048,1024]{1,0:T(8,128)(2,1)S(1)}, bf16[2048,1024]{1,0:T(8,128)(2,1)}, u32[]{:S(2)}) copy-start(bf16[2048,1024]{1,0:T(8,128)(2,1)} %param.23) | copy-start | bytes 12582916
  41.0 21.2 %copy-start.2 = (f32[2048]{0:T(1024)S(1)}, f32[2048]{0:T(1024)}, u32[]{:S(2)}) copy-start(f32[2048]{0:T(1024)} %param.19) | copy-start | bytes 24580
  43.0 15.0 %all-to-all-start.1 = ((f32[32,2,1152]{2,1,0:T(2,128)}), f32[32,2,1152]{2,1,0:T(2,128)S(1)}, u32[]{:S(2)}, u32[]{:S(2)}) async-start(f32[32,2,1152]{2,1,0:T(2,128)} %pad_maximum_fusion.1), calls=%async_computation.1 | async-start | bytes 589824 | tf_op jit(solution)/shard_map/all_to_all | solution.py:34
  59.2 13.1 %all-to-all-start.3 = ((bf16[32,2,2048]{2,1,0:T(2,128)(2,1)}), bf16[32,2,2048]{2,1,0:T(2,128)(2,1)S(1)}, u32[]{:S(2)}, u32[]{:S(2)}) async-start(bf16[32,2,2048]{2,1,0:T(2,128)(2,1)} %bitcast.24), calls=%async_computation.3 | async-start | bytes 524288 | tf_op jit(solution)/shard_map/all_to_all | solution.py:34
  66.0 13.9 %copy-start.3 = (s32[4,256]{1,0:T(4,128)S(1)}, s32[4,256]{1,0:T(4,128)}, u32[]{:S(2)}) copy-start(s32[4,256]{1,0:T(4,128)} %param.16) | copy-start | bytes 12292
  77.2 16.9 %all-to-all-start.4 = ((f32[32,2,2,1024]{3,2,1,0:T(2,128)}), f32[32,2,2,1024]{3,2,1,0:T(2,128)S(1)}, u32[]{:S(2)}, u32[]{:S(2)}) async-start(f32[32,2,2,1024]{3,2,1,0:T(2,128)} %copy.33), calls=%async_computation.4 | async-start | bytes 1048576 | tf_op jit(solution)/shard_map/all_to_all | solution.py:34
  95.6 12.6 %all-to-all-start.5 = ((bf16[32,2,1024]{2,1,0:T(2,128)(2,1)}), bf16[32,2,1024]{2,1,0:T(2,128)(2,1)S(1)}, u32[]{:S(2)}, u32[]{:S(2)}) async-start(bf16[32,2,1024]{2,1,0:T(2,128)(2,1)} %bitcast.40), calls=%async_computation.5 | async-start | bytes 262144 | tf_op jit(solution)/shard_map/all_to_all | solution.py:34
  112.5 17.5 %all-to-all-start.6 = ((f32[32,2,2176]{2,1,0:T(2,128)}), f32[32,2,2176]{2,1,0:T(2,128)S(1)}, u32[]{:S(2)}, u32[]{:S(2)}) async-start(f32[32,2,2176]{2,1,0:T(2,128)} %copy.36), calls=%async_computation.6 | async-start | bytes 1114112 | tf_op jit(solution)/shard_map/all_to_all | solution.py:34
  131.2 12.6 %all-to-all-start.7 = ((bf16[32,2,1024]{2,1,0:T(2,128)(2,1)}), bf16[32,2,1024]{2,1,0:T(2,128)(2,1)S(1)}, u32[]{:S(2)}, u32[]{:S(2)}) async-start(bf16[32,2,1024]{2,1,0:T(2,128)(2,1)} %bitcast.50), calls=%async_computation.7 | async-start | bytes 262144 | tf_op jit(solution)/shard_map/all_to_all | solution.py:34

commit v2 on v1

--- a/solution.py
+++ b/solution.py
@@ -34,13 +34,13 @@
     return lax.all_to_all(send, axes, split_axis=0, concat_axis=0, tiled=True)
 
 
-def gather_axis(x, axis):
+def shifted(x, axis):
     count = lax.axis_size(axis)
-    if count == 2:
-        other = lax.ppermute(x, axis, [(0, 1), (1, 0)])
-        mine = lax.axis_index(axis)
-        return jnp.where(mine == 0, jnp.stack([x, other]), jnp.stack([other, x]))
-    return exchange(jnp.broadcast_to(x[None], (count,) + x.shape), axis)
+    parts = [x] + [
+        lax.ppermute(x, axis, [(i, (i + k) % count) for i in range(count)])
+        for k in range(1, count)
+    ]
+    return jnp.stack(parts)
 
 
 def pad_cols(count):
@@ -78,18 +78,22 @@
     half = 2 * R_OWN
     starts = jnp.cumsum(lengths) - lengths
 
-    gain_full = gather_axis(draft_gain, "section").reshape(full_width)
+    by_shift = shifted(draft_gain, "section")
+    gain_full = jnp.take(
+        by_shift, (my_sec - jnp.arange(count_sec, dtype=jnp.int32)) % count_sec, axis=0
+    ).reshape(full_width)
 
     slot = my_mp * half + jnp.arange(half, dtype=jnp.int32)
     pos = jnp.clip(offsets[my_dp] + slot, 0, seq_len - 1)
     mine = jnp.stack([jnp.take(embeds[0], pos, axis=0), jnp.take(target_hidden[0], pos, axis=0)])
-    by_dp = exchange(jnp.broadcast_to(mine[None], (count_dp,) + mine.shape), "dp")
-    every = gather_axis(by_dp, "mp")
+    every = shifted(shifted(mine, "dp"), "mp")
     every = every.transpose(2, 0, 1, 3, 4).reshape(2, count_mp * count_dp * half, width)
     packed = jnp.arange(total_rows, dtype=jnp.int32)
     seq_all = sequence_of(packed, starts)
     slot_all = packed - starts[seq_all]
-    pick = ((slot_all // half) * count_dp + seq_all) * half + slot_all % half
+    shift_mp = (my_mp - slot_all // half) % count_mp
+    shift_dp = (my_dp - seq_all) % count_dp
+    pick = (shift_mp * count_dp + shift_dp) * half + slot_all % half
     embed_all = jnp.take(every[0], pick, axis=0)
     feature_all = jnp.take(every[1], pick, axis=0)
     position_all = offsets[seq_all] + slot_all

time: 155 us -> 146 us (0.942)
  waiting for transfers between devices: 67.7 us -> 57.5 us
  starting transfers between devices: 31.1 us -> 33.4 us
    all_to_all x8 -> x6, waiting for transfers between devices: 67.7 us -> 53.8 us  [exchange(): return lax.all_to_all(send, axes, split_axis=0, concat_axis=0, tiled=True)]
    ppermute x1 -> x7, starting transfers between devices: 0.01 us -> 12.5 us  [shifted(): lax.ppermute(x, axis, [(i, (i + k) % count) for i in range(count)])]
    all_to_all x8 -> x6, starting transfers between devices: 31.1 us -> 20.9 us  [exchange(): return lax.all_to_all(send, axes, split_axis=0, concat_axis=0, tiled=True)]
    ppermute x1 -> x7, waiting for transfers between devices: 0.01 us -> 3.71 us  [shifted(): lax.ppermute(x, axis, [(i, (i + k) % count) for i in range(count)])]
    broadcast_in_dim x2, local copies, waits for them, and re-layouts: 2.17 us -> 0.16 us  [on_device(): jnp.take(by_shift, (my_sec - jnp.arange(count_sec, dtype=jnp.int32)) % co...]
  transfers between devices with their start and end apart: 9 -> 13, of which waited for: 7 -> 7; matrix products, arithmetic and copies ran while one was open for 15% -> 20% of each run, Pallas kernels for 0% -> 0%
where the time goes in v2:
time: 146 us; the launch traced here: 145 us
  waiting for transfers between devices  57.5 us (39%)
  starting transfers between devices  33.4 us (23%)
  matrix products  23.8 us (16%)
  local copies, waits for them, and re-layouts  14.2 us (10%)
  other arithmetic  13.7 us (9%)
  between operations  2.84 us (2%)
    all_to_all x6, waiting for transfers between devices, exchange(): return lax.all_to_all(send, axes, split_axis=0, concat_axis=0, tiled=True)  53.8 us
    all_to_all x6, starting transfers between devices, exchange(): return lax.all_to_all(send, axes, split_axis=0, concat_axis=0, tiled=True)  20.9 us
    ppermute x7, starting transfers between devices, shifted(): lax.ppermute(x, axis, [(i, (i + k) % count) for i in range(count)])  12.5 us
    dot_general x2, matrix products, contract_first(): lax.dot_general(operand, weights, (((0,), (0,)), ((), ())), preferred_ele...  9.52 us
    dot_general x2, matrix products, contract_last(): lax.dot_general(operand, weights, (((1,), (1,)), ((), ())), preferred_ele...  7.16 us
    select_n x1, other arithmetic, on_device(): labels_all = token_ids.reshape(-1)[seq_all * seq_len + position_all]  5.04 us
    ppermute x7, waiting for transfers between devices, shifted(): lax.ppermute(x, axis, [(i, (i + k) % count) for i in range(count)])  3.71 us
    dot_general x1, matrix products, on_device(): jnp.dot(embed_all, fc_embed, preferred_element_type=jnp.float32)  3.23 us
  transfers between devices with their start and end apart: 13, of which 7 were waited for; matrix products, arithmetic and copies ran while one was open for 20% of the time, Pallas kernels for 0%

profile of v2, /device:TPU:0, one launch (start us, length us, event | category | flops | bytes accessed | tf_op | source)
XLA Modules:
  0.0 145.5 jit_solution(2082838988990518487)
XLA Ops:
  0.6 3.0 %collective-permute-start.4 = (f32[2048]{0:T(1024)}, f32[2048]{0:T(1024)S(1)}, u32[]{:S(2)}, u32[]{:S(2)}) collective-permute-start(f32[2048]{0:T(1024)} %param.20), channel_id=1, source_target_pairs={{0,8},{8,16},{16,24},{24,0},{1,9},{9,17},{17,25},{25,1},{2,10},{10... | collective-permute-start | bytes 24584 | tf_op jit(solution)/shard_map/ppermute | solution.py:40
  3.7 1.0 collective-permute-start.6
  4.7 1.5 %fusion.55 = (s32[1]{0:T(128)}, s32[1]{0:T(128)}, s32[1]{0:T(128)}, s32[1]{0:T(128)}, s32[1]{0:T(128)}) fusion(s32[4]{0:T(128)} %param.18, s32[]{:T(128)S(6)} %select_n.116), kind=kLoop, calls=%fused_computation.143 | loop fusion | bytes 44 | tf_op jit(solution)/shard_map/gather | solution.py:99
  6.2 0.7 compare_and_fusion.1
  6.9 0.6 gather_fusion.4
  7.5 2.0 %gather_fusion.3 = bf16[16,2048]{1,0:T(8,128)(2,1)S(1)} fusion(bf16[256,2048]{1,0:T(8,128)(2,1)} %bitcast.181, s32[1024]{0:T(1024)S(1)} %pad_clamp_fusion.4), kind=kCustom, calls=%fused_computation.clone | custom fusion | bytes 131136 | tf_op jit(solution)/shard_map/jit(_take)/gather | solution.py:88
  9.6 3.1 %collective-permute-start.1 = (bf16[2,16,2048]{2,1,0:T(8,128)(2,1)S(1)}, bf16[2,16,2048]{2,1,0:T(8,128)(2,1)S(1)}, u32[]{:S(2)}, u32[]{:S(2)}) collective-permute-start(bf16[2,16,2048]{2,1,0:T(8,128)(2,1)S(1)} %get-tuple-element.18), channel_id=1, source_target_pairs={{0,2},{1,3},{2,0},{3,1},{4,6},{5,7},{6,4},{7,5},{8,10},{9,11},{10,... | collective-permute-start | bytes 393224 | tf_op jit(solution)/shard_map/ppermute | solution.py:40
  12.7 1.6 %collective-permute-start = (bf16[2,16,2048]{2,1,0:T(8,128)(2,1)S(1)}, bf16[2,16,2048]{2,1,0:T(8,128)(2,1)S(1)}, u32[]{:S(2)}, u32[]{:S(2)}) collective-permute-start(bf16[2,16,2048]{2,1,0:T(8,128)(2,1)S(1)} %get-tuple-element.18), channel_id=1, source_target_pairs={{0,1},{1,2},{2,3},{3,0},{4,5},{5,6},{6,7},{7,4},{8,9},{9,10},{10,1... | collective-permute-start | bytes 393224 | tf_op jit(solution)/shard_map/ppermute | solution.py:40
  14.3 2.2 %collective-permute-start.2 = (bf16[2,16,2048]{2,1,0:T(8,128)(2,1)S(1)}, bf16[2,16,2048]{2,1,0:T(8,128)(2,1)S(1)}, u32[]{:S(2)}, u32[]{:S(2)}) collective-permute-start(bf16[2,16,2048]{2,1,0:T(8,128)(2,1)S(1)} %get-tuple-element.18), channel_id=1, source_target_pairs={{0,3},{1,0},{2,1},{3,2},{4,7},{5,4},{6,5},{7,6},{8,11},{9,8},{10,9... | collective-permute-start | bytes 393224 | tf_op jit(solution)/shard_map/ppermute | solution.py:40
  16.5 0.8 reduce-window.9
  17.3 0.7 bitcast_subtract_fusion.5
  18.0 0.6 fusion.56
  18.8 3.7 %collective-permute-done.1 = bf16[2,16,2048]{2,1,0:T(8,128)(2,1)S(1)} collective-permute-done((bf16[2,16,2048]{2,1,0:T(8,128)(2,1)S(1)}, bf16[2,16,2048]{2,1,0:T(8,128)(2,1)S(1)}, u32[]{:S(2)}, u32[]{:S(2)}) %collective-permute-start.1) | collective-permute-done | bytes 131104 | tf_op jit(solution)/shard_map/ppermute | solution.py:40
  22.4 1.5 %collective-permute-start.5 = (f32[2048]{0:T(1024)}, f32[2048]{0:T(1024)S(1)}, u32[]{:S(2)}, u32[]{:S(2)}) collective-permute-start(f32[2048]{0:T(1024)} %param.20), channel_id=1, source_target_pairs={{0,16},{8,24},{16,0},{24,8},{1,17},{9,25},{17,1},{25,9},{2,18},{10... | collective-permute-start | bytes 24584 | tf_op jit(solution)/shard_map/ppermute | solution.py:40
  24.2 2.5 %compare_and_fusion = (pred[64]{0:T(512)(128)(4,1)S(1)}, s32[64]{0:T(128)S(1)}) fusion(s32[]{:T(128)S(6)} %axis_index.32, s32[]{:T(128)} %bitcast.7, s32[]{:T(128)} %bitcast.6, s32[]{:T(128)} %bitcast.5, s32[]{:T(128)} %bitcast.4, s32[64]{0:T(128)S(1)} %convert_reduce_fusion, s32[]{:T(128)S(6)} %axis_index.35), kind=kLoop, calls=%fused_computation.92 | loop fusion | flops 4096 | bytes 600 | tf_op jit(solution)/shard_map/jit(_take)/and | solution.py:98
  26.9 0.7 gather_fusion.6
  27.7 0.7 gather_fusion.5
  28.8 3.2 %fusion.17 = f32[64,1024]{1,0:T(8,128)S(1)} fusion(bf16[2048,1024]{1,0:T(8,128)(2,1)} %param.22, bf16[64,2048]{1,0:T(8,128)(2,1)S(1)} %gather_fusion.6, pred[64]{0:T(512)(128)(4,1)S(1)} %get-tuple-element.9), kind=kOutput, calls=%fused_computation.36 | convolution fusion | flops 268566528 | bytes 4718656 | tf_op jit(solution)/shard_map/dot_general | solution.py:104
  32.2 0.9 convolution_add_fusion
  33.3 0.8 pad_maximum_fusion.2
  34.1 4.2 %all-to-all-start = ((f32[32,2,1152]{2,1,0:T(2,128)}), f32[32,2,1152]{2,1,0:T(2,128)S(1)}, u32[]{:S(2)}, u32[]{:S(2)}) async-start(f32[32,2,1152]{2,1,0:T(2,128)} %pad_maximum_fusion.2), calls=%async_computation | async-start | bytes 589824 | tf_op jit(solution)/shard_map/all_to_all | solution.py:34
  38.4 0.6 gather_fusion
  39.0 10.0 %all-to-all-done = f32[32,2,1152]{2,1,0:T(2,128)S(1)} async-done(((f32[32,2,1152]{2,1,0:T(2,128)}), f32[32,2,1152]{2,1,0:T(2,128)S(1)}, u32[]{:S(2)}, u32[]{:S(2)}) %all-to-all-start) | async-done | bytes 294944 | tf_op jit(solution)/shard_map/all_to_all | solution.py:34
  49.4 0.9 broadcast_in_dim.94
  50.3 2.9 %all-to-all-start.1 = ((bf16[32,2,2048]{2,1,0:T(2,128)(2,1)}), bf16[32,2,2048]{2,1,0:T(2,128)(2,1)S(1)}, u32[]{:S(2)}, u32[]{:S(2)}) async-start(bf16[32,2,2048]{2,1,0:T(2,128)(2,1)} %bitcast.33), calls=%async_computation.1 | async-start | bytes 524288 | tf_op jit(solution)/shard_map/all_to_all | solution.py:34
  53.3 3.6 %fusion.10 = f32[64,1024]{1,0:T(8,128)S(1)} fusion(bf16[1024,2048]{1,0:T(8,128)(2,1)} %param.21, f32[2048]{0:T(1024)S(1)} %copy-done.3, f32[64]{0:T(128)S(1)} %rsqrt.21, bf16[64,2048]{1,0:T(8,128)(2,1)S(1)} %gather_fusion.5, pred[64]{0:T(512)(128)(4,1)S(1)} %get-tuple-element.9), kind=kOutput, calls=%fused_computation.24 | convolution fusion | flops 269090816 | bytes 4727104 | tf_op jit(solution)/shard_map/dot_general | solution.py:18
  57.1 6.3 %all-to-all-done.1 = bf16[32,2,2048]{2,1,0:T(2,128)(2,1)S(1)} async-done(((bf16[32,2,2048]{2,1,0:T(2,128)(2,1)}), bf16[32,2,2048]{2,1,0:T(2,128)(2,1)S(1)}, u32[]{:S(2)}, u32[]{:S(2)}) %all-to-all-start.1) | async-done | bytes 262176 | tf_op jit(solution)/shard_map/all_to_all | solution.py:34
  63.4 3.6 %fusion.4 = f32[1,32,2,1024]{3,1,2,0:T(8,128)S(1)} fusion(bf16[1024,2048]{1,0:T(8,128)(2,1)} %param.21, bf16[32,2,2048]{2,1,0:T(2,128)(2,1)S(1)} %all-to-all-done.1), kind=kOutput, calls=%fused_computation.11 | convolution fusion | flops 268435456 | bytes 4718592 | tf_op jit(solution)/shard_map/dot_general | solution.py:18
  67.0 1.2 copy.33
  68.2 2.7 %all-to-all-start.2 = ((f32[32,2,2,1024]{3,2,1,0:T(2,128)}), f32[32,2,2,1024]{3,2,1,0:T(2,128)S(1)}, u32[]{:S(2)}, u32[]{:S(2)}) async-start(f32[32,2,2,1024]{3,2,1,0:T(2,128)} %copy.33), calls=%async_computation.2 | async-start | bytes 1048576 | tf_op jit(solution)/shard_map/all_to_all | solution.py:34
  70.9 5.0 %fusion.46 = s32[64]{0:T(128)S(1)} fusion(s32[]{:T(128)} %bitcast.41, s32[]{:T(128)} %bitcast.42, s32[]{:T(128)} %bitcast.44, s32[]{:T(128)} %bitcast.43, s32[64]{0:T(128)S(1)} %convert_reduce_fusion, s32[]{:T(128)} %bitcast.7, s32[]{:T(128)} %bitcast.6, s32[]{:T(128)} %bitcast.5, s32[]{:T(128)} %bitcast.4), kind=kLoop, calls=%fused_computation.125 | loop fusion | flops 1280 | bytes 544 | tf_op jit(solution)/shard_map/select_n | solution.py:100
  76.0 0.7 gather_fusion.1
  76.7 0.6 gather_fusion.2
  77.4 7.8 %all-to-all-done.2 = f32[32,2,2,1024]{3,2,1,0:T(2,128)S(1)} async-done(((f32[32,2,2,1024]{3,2,1,0:T(2,128)}), f32[32,2,2,1024]{3,2,1,0:T(2,128)S(1)}, u32[]{:S(2)}, u32[]{:S(2)}) %all-to-all-start.2) | async-done | bytes 524320 | tf_op jit(solution)/shard_map/all_to_all | solution.py:34
  85.4 0.3 exponential_reduce_fusion
  85.9 0.7 broadcast_in_dim.96
  86.7 4.2 %all-to-all-start.3 = ((bf16[32,2,1024]{2,1,0:T(2,128)(2,1)}), bf16[32,2,1024]{2,1,0:T(2,128)(2,1)S(1)}, u32[]{:S(2)}, u32[]{:S(2)}) async-start(bf16[32,2,1024]{2,1,0:T(2,128)(2,1)} %bitcast.49), calls=%async_computation.3 | async-start | bytes 262144 | tf_op jit(solution)/shard_map/all_to_all | solution.py:34
  91.0 8.3 %all-to-all-done.3 = bf16[32,2,1024]{2,1,0:T(2,128)(2,1)S(1)} async-done(((bf16[32,2,1024]{2,1,0:T(2,128)(2,1)}), bf16[32,2,1024]{2,1,0:T(2,128)(2,1)S(1)}, u32[]{:S(2)}, u32[]{:S(2)}) %all-to-all-start.3) | async-done | bytes 131104 | tf_op jit(solution)/shard_map/all_to_all | solution.py:34
  99.2 3.0 %fusion = f32[32,2,2048]{2,0,1:T(8,128)S(1)} fusion(bf16[1024,2048]{1,0:T(8,128)(2,1)} %param.21, bf16[32,2,1024]{2,1,0:T(2,128)(2,1)S(1)} %all-to-all-done.3), kind=kOutput, calls=%fused_computation.7 | convolution fusion | flops 268435456 | bytes 4849664 | tf_op jit(solution)/shard_map/dot_general | solution.py:175
  102.3 1.2 copy.36
  103.5 2.6 %all-to-all-start.4 = ((f32[32,2,2176]{2,1,0:T(2,128)}), f32[32,2,2176]{2,1,0:T(2,128)S(1)}, u32[]{:S(2)}, u32[]{:S(2)}) async-start(f32[32,2,2176]{2,1,0:T(2,128)} %copy.36), calls=%async_computation.4 | async-start | bytes 1114112 | tf_op jit(solution)/shard_map/all_to_all | solution.py:34
  106.4 14.6 %all-to-all-done.4 = f32[32,2,2176]{2,1,0:T(2,128)S(1)} async-done(((f32[32,2,2176]{2,1,0:T(2,128)}), f32[32,2,2176]{2,1,0:T(2,128)S(1)}, u32[]{:S(2)}, u32[]{:S(2)}) %all-to-all-start.4) | async-done | bytes 557088 | tf_op jit(solution)/shard_map/all_to_all | solution.py:34
  121.5 0.7 broadcast_in_dim.104
  122.2 4.4 %all-to-all-start.5 = ((bf16[32,2,1024]{2,1,0:T(2,128)(2,1)}), bf16[32,2,1024]{2,1,0:T(2,128)(2,1)S(1)}, u32[]{:S(2)}, u32[]{:S(2)}) async-start(bf16[32,2,1024]{2,1,0:T(2,128)(2,1)} %bitcast.59), calls=%async_computation.5 | async-start | bytes 262144 | tf_op jit(solution)/shard_map/all_to_all | solution.py:34
  126.6 0.6 slice_reduce_fusion.2
  127.9 6.9 %all-to-all-done.5 = bf16[32,2,1024]{2,1,0:T(2,128)(2,1)S(1)} async-done(((bf16[32,2,1024]{2,1,0:T(2,128)(2,1)}), bf16[32,2,1024]{2,1,0:T(2,128)(2,1)S(1)}, u32[]{:S(2)}, u32[]{:S(2)}) %all-to-all-start.5) | async-done | bytes 131104 | tf_op jit(solution)/shard_map/all_to_all | solution.py:34
  134.8 4.8 %fusion.52 = f32[2048,1024]{1,0:T(8,128)} fusion(bf16[64,1024]{1,0:T(8,128)(2,1)S(1)} %reshape.506, bf16[64,2048]{1,0:T(8,128)(2,1)S(1)} %gather_fusion.5, pred[64]{0:T(512)(128)(4,1)S(1)} %get-tuple-element.9), kind=kOutput, calls=%fused_computation.140 | convolution fusion | flops 268566528 | bytes 8781888 | tf_op jit(solution)/shard_map/dot_general | solution.py:24
  139.6 4.8 %fusion.16 = f32[2048,1024]{1,0:T(8,128)} fusion(bf16[64,1024]{1,0:T(8,128)(2,1)S(1)} %reshape.506, bf16[64,2048]{1,0:T(8,128)(2,1)S(1)} %gather_fusion.6, pred[64]{0:T(512)(128)(4,1)S(1)} %get-tuple-element.9), kind=kOutput, calls=%fused_computation.35 | convolution fusion | flops 268566528 | bytes 8781888 | tf_op jit(solution)/shard_map/dot_general | solution.py:24
  (68 shorter events, 3.6 us)
Async XLA Ops:
  0.6 6.2 %copy-start = (bf16[1,256,2048]{2,1,0:T(8,128)(2,1)S(1)}, bf16[1,256,2048]{2,1,0:T(8,128)(2,1)}, u32[]{:S(2)}) copy-start(bf16[1,256,2048]{2,1,0:T(8,128)(2,1)} %param.14) | copy-start | bytes 3145732
  0.6 37.7 %collective-permute-start.4 = (f32[2048]{0:T(1024)}, f32[2048]{0:T(1024)S(1)}, u32[]{:S(2)}, u32[]{:S(2)}) collective-permute-start(f32[2048]{0:T(1024)} %param.20), channel_id=1, source_target_pairs={{0,8},{8,16},{16,24},{24,0},{1,9},{9,17},{17,25},{25,1},{2,10},{10... | collective-permute-start | bytes 24584 | tf_op jit(solution)/shard_map/ppermute | solution.py:40
  3.7 34.7 %collective-permute-start.6 = (f32[2048]{0:T(1024)}, f32[2048]{0:T(1024)S(1)}, u32[]{:S(2)}, u32[]{:S(2)}) collective-permute-start(f32[2048]{0:T(1024)} %param.20), channel_id=1, source_target_pairs={{0,24},{8,0},{16,8},{24,16},{1,25},{9,1},{17,9},{25,17},{2,26},{10... | collective-permute-start | bytes 24584 | tf_op jit(solution)/shard_map/ppermute | solution.py:40
  9.6 12.8 %collective-permute-start.1 = (bf16[2,16,2048]{2,1,0:T(8,128)(2,1)S(1)}, bf16[2,16,2048]{2,1,0:T(8,128)(2,1)S(1)}, u32[]{:S(2)}, u32[]{:S(2)}) collective-permute-start(bf16[2,16,2048]{2,1,0:T(8,128)(2,1)S(1)} %get-tuple-element.18), channel_id=1, source_target_pairs={{0,2},{1,3},{2,0},{3,1},{4,6},{5,7},{6,4},{7,5},{8,10},{9,11},{10,... | collective-permute-start | bytes 393224 | tf_op jit(solution)/shard_map/ppermute | solution.py:40
  12.7 11.3 %collective-permute-start = (bf16[2,16,2048]{2,1,0:T(8,128)(2,1)S(1)}, bf16[2,16,2048]{2,1,0:T(8,128)(2,1)S(1)}, u32[]{:S(2)}, u32[]{:S(2)}) collective-permute-start(bf16[2,16,2048]{2,1,0:T(8,128)(2,1)S(1)} %get-tuple-element.18), channel_id=1, source_target_pairs={{0,1},{1,2},{2,3},{3,0},{4,5},{5,6},{6,7},{7,4},{8,9},{9,10},{10,1... | collective-permute-start | bytes 393224 | tf_op jit(solution)/shard_map/ppermute | solution.py:40
  14.3 9.7 %collective-permute-start.2 = (bf16[2,16,2048]{2,1,0:T(8,128)(2,1)S(1)}, bf16[2,16,2048]{2,1,0:T(8,128)(2,1)S(1)}, u32[]{:S(2)}, u32[]{:S(2)}) collective-permute-start(bf16[2,16,2048]{2,1,0:T(8,128)(2,1)S(1)} %get-tuple-element.18), channel_id=1, source_target_pairs={{0,3},{1,0},{2,1},{3,2},{4,7},{5,4},{6,5},{7,6},{8,11},{9,8},{10,9... | collective-permute-start | bytes 393224 | tf_op jit(solution)/shard_map/ppermute | solution.py:40
  22.4 15.9 %collective-permute-start.5 = (f32[2048]{0:T(1024)}, f32[2048]{0:T(1024)S(1)}, u32[]{:S(2)}, u32[]{:S(2)}) collective-permute-start(f32[2048]{0:T(1024)} %param.20), channel_id=1, source_target_pairs={{0,16},{8,24},{16,0},{24,8},{1,17},{9,25},{17,1},{25,9},{2,18},{10... | collective-permute-start | bytes 24584 | tf_op jit(solution)/shard_map/ppermute | solution.py:40
  24.1 2.6 %collective-permute-start.3 = (bf16[4,2,16,2048]{3,2,1,0:T(8,128)(2,1)S(1)}, bf16[4,2,16,2048]{3,2,1,0:T(8,128)(2,1)S(1)}, u32[]{:S(2)}, u32[]{:S(2)}) collective-permute-start(bf16[4,2,16,2048]{3,2,1,0:T(8,128)(2,1)S(1)} %get-tuple-element.16), channel_id=1, source_target_pairs={{0,4},{4,0},{1,5},{5,1},{2,6},{6,2},{3,7},{7,3},{8,12},{12,8},{9,1... | collective-permute-start | bytes 1572872 | tf_op jit(solution)/shard_map/ppermute | solution.py:40
  28.8 3.5 %copy-start.1 = (bf16[2048,1024]{1,0:T(8,128)(2,1)S(1)}, bf16[2048,1024]{1,0:T(8,128)(2,1)}, u32[]{:S(2)}) copy-start(bf16[2048,1024]{1,0:T(8,128)(2,1)} %param.23) | copy-start | bytes 12582916
  32.2 6.1 %copy-start.2 = (f32[2048]{0:T(1024)S(1)}, f32[2048]{0:T(1024)}, u32[]{:S(2)}) copy-start(f32[2048]{0:T(1024)} %param.20) | copy-start | bytes 24580
  32.2 21.0 %copy-start.3 = (f32[2048]{0:T(1024)S(1)}, f32[2048]{0:T(1024)}, u32[]{:S(2)}) copy-start(f32[2048]{0:T(1024)} %param.19) | copy-start | bytes 24580
  34.1 14.9 %all-to-all-start = ((f32[32,2,1152]{2,1,0:T(2,128)}), f32[32,2,1152]{2,1,0:T(2,128)S(1)}, u32[]{:S(2)}, u32[]{:S(2)}) async-start(f32[32,2,1152]{2,1,0:T(2,128)} %pad_maximum_fusion.2), calls=%async_computation | async-start | bytes 589824 | tf_op jit(solution)/shard_map/all_to_all | solution.py:34
  50.3 13.1 %all-to-all-start.1 = ((bf16[32,2,2048]{2,1,0:T(2,128)(2,1)}), bf16[32,2,2048]{2,1,0:T(2,128)(2,1)S(1)}, u32[]{:S(2)}, u32[]{:S(2)}) async-start(bf16[32,2,2048]{2,1,0:T(2,128)(2,1)} %bitcast.33), calls=%async_computation.1 | async-start | bytes 524288 | tf_op jit(solution)/shard_map/all_to_all | solution.py:34
  57.0 13.9 %copy-start.4 = (s32[4,256]{1,0:T(4,128)S(1)}, s32[4,256]{1,0:T(4,128)}, u32[]{:S(2)}) copy-start(s32[4,256]{1,0:T(4,128)} %param.16) | copy-start | bytes 12292
  68.2 16.9 %all-to-all-start.2 = ((f32[32,2,2,1024]{3,2,1,0:T(2,128)}), f32[32,2,2,1024]{3,2,1,0:T(2,128)S(1)}, u32[]{:S(2)}, u32[]{:S(2)}) async-start(f32[32,2,2,1024]{3,2,1,0:T(2,128)} %copy.33), calls=%async_computation.2 | async-start | bytes 1048576 | tf_op jit(solution)/shard_map/all_to_all | solution.py:34
  86.7 12.6 %all-to-all-start.3 = ((bf16[32,2,1024]{2,1,0:T(2,128)(2,1)}), bf16[32,2,1024]{2,1,0:T(2,128)(2,1)S(1)}, u32[]{:S(2)}, u32[]{:S(2)}) async-start(bf16[32,2,1024]{2,1,0:T(2,128)(2,1)} %bitcast.49), calls=%async_computation.3 | async-start | bytes 262144 | tf_op jit(solution)/shard_map/all_to_all | solution.py:34
  103.5 17.5 %all-to-all-start.4 = ((f32[32,2,2176]{2,1,0:T(2,128)}), f32[32,2,2176]{2,1,0:T(2,128)S(1)}, u32[]{:S(2)}, u32[]{:S(2)}) async-start(f32[32,2,2176]{2,1,0:T(2,128)} %copy.36), calls=%async_computation.4 | async-start | bytes 1114112 | tf_op jit(solution)/shard_map/all_to_all | solution.py:34
  122.2 12.6 %all-to-all-start.5 = ((bf16[32,2,1024]{2,1,0:T(2,128)(2,1)}), bf16[32,2,1024]{2,1,0:T(2,128)(2,1)S(1)}, u32[]{:S(2)}, u32[]{:S(2)}) async-start(bf16[32,2,1024]{2,1,0:T(2,128)(2,1)} %bitcast.59), calls=%async_computation.5 | async-start | bytes 262144 | tf_op jit(solution)/shard_map/all_to_all | solution.py:34

commit v3 on v2

--- a/solution.py
+++ b/solution.py
@@ -78,14 +78,13 @@
     half = 2 * R_OWN
     starts = jnp.cumsum(lengths) - lengths
 
-    by_shift = shifted(draft_gain, "section")
-    gain_full = jnp.take(
-        by_shift, (my_sec - jnp.arange(count_sec, dtype=jnp.int32)) % count_sec, axis=0
-    ).reshape(full_width)
-
-    slot = my_mp * half + jnp.arange(half, dtype=jnp.int32)
-    pos = jnp.clip(offsets[my_dp] + slot, 0, seq_len - 1)
-    mine = jnp.stack([jnp.take(embeds[0], pos, axis=0), jnp.take(target_hidden[0], pos, axis=0)])
+    first = jnp.minimum(offsets[my_dp] + my_mp * half, seq_len - half)
+    mine = jnp.stack(
+        [
+            lax.dynamic_slice_in_dim(embeds[0], first, half, axis=0),
+            lax.dynamic_slice_in_dim(target_hidden[0], first, half, axis=0),
+        ]
+    )
     every = shifted(shifted(mine, "dp"), "mp")
     every = every.transpose(2, 0, 1, 3, 4).reshape(2, count_mp * count_dp * half, width)
     packed = jnp.arange(total_rows, dtype=jnp.int32)
@@ -93,7 +92,10 @@
     slot_all = packed - starts[seq_all]
     shift_mp = (my_mp - slot_all // half) % count_mp
     shift_dp = (my_dp - seq_all) % count_dp
-    pick = (shift_mp * count_dp + shift_dp) * half + slot_all % half
+    base = offsets[seq_all] + (slot_all // half) * half
+    lag = base - jnp.minimum(base, seq_len - half)
+    within = jnp.minimum(slot_all % half + lag, half - 1)
+    pick = (shift_mp * count_dp + shift_dp) * half + within
     embed_all = jnp.take(every[0], pick, axis=0)
     feature_all = jnp.take(every[1], pick, axis=0)
     position_all = offsets[seq_all] + slot_all
@@ -105,8 +107,13 @@
         feature_all, fc_feature, preferred_element_type=jnp.float32
     )
     target_square = jnp.sum(jnp.square(feature_all.astype(jnp.float32)), axis=1)
-    spare = total_rows // per_dev
-    extra = jnp.pad(target_square.reshape(per_dev, spare), ((0, 0), (0, pad_cols(spare) - spare)))
+    piece = width // groups
+    spare = pad_cols(-(-(total_rows + piece) // per_dev))
+    gain_piece = lax.dynamic_slice_in_dim(draft_gain, (my_mp * count_dp + my_dp) * piece, piece)
+    extra = jnp.pad(
+        jnp.concatenate([target_square, gain_piece]),
+        (0, per_dev * spare - total_rows - piece),
+    ).reshape(per_dev, spare)
     send1 = jnp.concatenate(
         [
             partial_value.reshape(n_dev, per_dev, block),
@@ -118,7 +125,9 @@
     hidden = (
         jnp.sum(got1[..., :block], axis=0).transpose(1, 0, 2).reshape(per_dev, groups * block)
     )
-    target_square = jnp.sum(got1[:, 0, :, block : block + spare], axis=0).reshape(total_rows)
+    extra_got = got1[..., block:].reshape(count_sec, groups, per_dev * spare)
+    target_square = jnp.sum(extra_got[:, 0, :total_rows], axis=0)
+    gain_full = extra_got[:, :, total_rows : total_rows + piece].reshape(full_width)
     target_scale = lax.rsqrt(target_square / D + eps_norm)
     target_norm = (feature_all.astype(jnp.float32) * target_scale[:, None] * target_gain).astype(
         jnp.bfloat16
@@ -135,13 +144,10 @@
 
     target_part = contract_last(target_norm, head)
     draft_part = contract_last(draft_norm_all, head)
-    send3 = (
-        jnp.stack([target_part, draft_part])
-        .reshape(2, n_dev, per_dev, vocab_tile)
-        .transpose(1, 0, 2, 3)
-    )
-    got3 = exchange(send3, ALL).reshape(count_sec, groups, 2, per_dev, vocab_tile)
-    logits = jnp.sum(got3, axis=0).transpose(1, 2, 0, 3).reshape(2, per_dev, groups * vocab_tile)
+    send3 = jnp.stack([target_part, draft_part]).reshape(2, n_dev, per_dev, vocab_tile)
+    got3 = lax.all_to_all(send3, ALL, split_axis=1, concat_axis=1, tiled=True)
+    got3 = got3.reshape(2, count_sec, groups, per_dev, vocab_tile)
+    logits = jnp.sum(got3, axis=1).transpose(0, 2, 1, 3).reshape(2, per_dev, groups * vocab_tile)
     target_logit, draft_logit = logits[0], logits[1]
     vocab = groups * vocab_tile
     is_label = labels[:, None] == jnp.arange(vocab, dtype=jnp.int32)[None, :]

time: 146 us -> 146 us (level)
  blocking collectives: 0 us -> 17.1 us
  waiting for transfers between devices: 57.5 us -> 48.7 us
  starting transfers between devices: 33.4 us -> 25.1 us
  local copies, waits for them, and re-layouts: 14.2 us -> 12.6 us
    all_to_all x6 -> x4, waiting for transfers between devices: 53.8 us -> 36.4 us  [exchange(): return lax.all_to_all(send, axes, split_axis=0, concat_axis=0, tiled=True)]
    all_to_all x0 -> x1, blocking collectives: none -> 17.1 us  [exchange(): return lax.all_to_all(send, axes, split_axis=0, concat_axis=0, tiled=True)]
    all_to_all x0 -> x1, waiting for transfers between devices: none -> 7.75 us  [on_device(): got3 = lax.all_to_all(send3, ALL, split_axis=1, concat_axis=1, tiled=True)]
    all_to_all x6 -> x4, starting transfers between devices: 20.9 us -> 14.4 us  [exchange(): return lax.all_to_all(send, axes, split_axis=0, concat_axis=0, tiled=True)]
    ppermute x7 -> x4, starting transfers between devices: 12.5 us -> 8.02 us  [shifted(): lax.ppermute(x, axis, [(i, (i + k) % count) for i in range(count)])]
    gather x5 -> x1, local copies, waits for them, and re-layouts: 4.71 us -> 1.52 us  [on_device(): base = offsets[seq_all] + slot_all // half * half]
    all_to_all x0 -> x1, starting transfers between devices: none -> 2.66 us  [on_device(): got3 = lax.all_to_all(send3, ALL, split_axis=1, concat_axis=1, tiled=True)]
    and x1, other arithmetic: 2.52 us -> 5.06 us  [on_device(): feature_all = jnp.take(every[1], pick, axis=0)]
  transfers between devices with their start and end apart: 13 -> 9, of which waited for: 7 -> 7; matrix products, arithmetic and copies ran while one was open for 20% -> 13% of each run, Pallas kernels for 0% -> 0%
where the time goes in v3:
time: 146 us; the launch traced here: 145 us
  waiting for transfers between devices  48.7 us (33%)
  starting transfers between devices  25.1 us (17%)
  matrix products  23.8 us (16%)
  blocking collectives  17.1 us (12%)
  other arithmetic  14.7 us (10%)
  local copies, waits for them, and re-layouts  12.6 us (9%)
  between operations  3.43 us (2%)
    all_to_all x4, waiting for transfers between devices, exchange(): return lax.all_to_all(send, axes, split_axis=0, concat_axis=0, tiled=True)  36.4 us
    all_to_all x1, blocking collectives, exchange(): return lax.all_to_all(send, axes, split_axis=0, concat_axis=0, tiled=True)  17.1 us
    all_to_all x4, starting transfers between devices, exchange(): return lax.all_to_all(send, axes, split_axis=0, concat_axis=0, tiled=True)  14.4 us
    dot_general x2, matrix products, contract_first(): lax.dot_general(operand, weights, (((0,), (0,)), ((), ())), preferred_ele...  9.52 us
    ppermute x4, starting transfers between devices, shifted(): lax.ppermute(x, axis, [(i, (i + k) % count) for i in range(count)])  8.02 us
    all_to_all x1, waiting for transfers between devices, on_device(): got3 = lax.all_to_all(send3, ALL, split_axis=1, concat_axis=1, tiled=True)  7.75 us
    dot_general x2, matrix products, contract_last(): lax.dot_general(operand, weights, (((1,), (1,)), ((), ())), preferred_ele...  7.17 us
    and x1, other arithmetic, on_device(): feature_all = jnp.take(every[1], pick, axis=0)  5.06 us
  transfers between devices with their start and end apart: 9, of which 7 were waited for; matrix products, arithmetic and copies ran while one was open for 13% of the time, Pallas kernels for 0%

profile of v3, /device:TPU:0, one launch (start us, length us, event | category | flops | bytes accessed | tf_op | source)
XLA Modules:
  0.0 145.4 jit_solution(976434471907004777)
XLA Ops:
  0.6 1.5 %fusion.53 = (s32[1]{0:T(128)}, s32[1]{0:T(128)}, s32[1]{0:T(128)}, s32[1]{0:T(128)}, s32[1]{0:T(128)}) fusion(s32[4]{0:T(128)} %param.16, s32[]{:T(128)S(6)} %select_n.74), kind=kLoop, calls=%fused_computation.127 | loop fusion | bytes 44 | tf_op jit(solution)/shard_map/gather | solution.py:95
  2.8 1.0 constant_dynamic-slice_fusion
  3.8 4.1 %collective-permute-start.1 = (bf16[2,16,2048]{2,1,0:T(8,128)(2,1)S(1)}, bf16[2,16,2048]{2,1,0:T(8,128)(2,1)S(1)}, u32[]{:S(2)}, u32[]{:S(2)}) collective-permute-start(bf16[2,16,2048]{2,1,0:T(8,128)(2,1)S(1)} %get-tuple-element.15), channel_id=1, source_target_pairs={{0,2},{1,3},{2,0},{3,1},{4,6},{5,7},{6,4},{7,5},{8,10},{9,11},{10,... | collective-permute-start | bytes 393224 | tf_op jit(solution)/shard_map/ppermute | solution.py:40
  8.0 1.6 %collective-permute-start = (bf16[2,16,2048]{2,1,0:T(8,128)(2,1)S(1)}, bf16[2,16,2048]{2,1,0:T(8,128)(2,1)S(1)}, u32[]{:S(2)}, u32[]{:S(2)}) collective-permute-start(bf16[2,16,2048]{2,1,0:T(8,128)(2,1)S(1)} %get-tuple-element.15), channel_id=1, source_target_pairs={{0,1},{1,2},{2,3},{3,0},{4,5},{5,6},{6,7},{7,4},{8,9},{9,10},{10,1... | collective-permute-start | bytes 393224 | tf_op jit(solution)/shard_map/ppermute | solution.py:40
  9.5 2.2 %collective-permute-start.2 = (bf16[2,16,2048]{2,1,0:T(8,128)(2,1)S(1)}, bf16[2,16,2048]{2,1,0:T(8,128)(2,1)S(1)}, u32[]{:S(2)}, u32[]{:S(2)}) collective-permute-start(bf16[2,16,2048]{2,1,0:T(8,128)(2,1)S(1)} %get-tuple-element.15), channel_id=1, source_target_pairs={{0,3},{1,0},{2,1},{3,2},{4,7},{5,4},{6,5},{7,6},{8,11},{9,8},{10,9... | collective-permute-start | bytes 393224 | tf_op jit(solution)/shard_map/ppermute | solution.py:40
  11.8 0.8 reduce-window.9
  12.6 0.8 dynamic_slice.15
  13.4 0.7 bitcast_subtract_fusion.5
  14.0 3.9 %collective-permute-done.1 = bf16[2,16,2048]{2,1,0:T(8,128)(2,1)S(1)} collective-permute-done((bf16[2,16,2048]{2,1,0:T(8,128)(2,1)S(1)}, bf16[2,16,2048]{2,1,0:T(8,128)(2,1)S(1)}, u32[]{:S(2)}, u32[]{:S(2)}) %collective-permute-start.1) | collective-permute-done | bytes 131104 | tf_op jit(solution)/shard_map/ppermute | solution.py:40
  18.0 0.6 collective-permute-done.2
  18.8 0.6 fusion.52
  19.5 5.1 %compare_and_fusion = (pred[64]{0:T(512)(128)(4,1)S(1)}, s32[64]{0:T(128)S(1)}) fusion(s32[]{:T(128)} %bitcast.12, s32[]{:T(128)} %bitcast.11, s32[]{:T(128)} %bitcast.10, s32[]{:T(128)} %bitcast.9, s32[]{:T(128)S(6)} %axis_index.32, s32[]{:T(128)} %bitcast.7, s32[]{:T(128)} %bitcast.6, s32[]{:T(128)} %bitcast.5, s32[]{:T(128)} %bitcast.4, ...), kind=kLoop, calls=%fused_computation.77 | loop fusion | flops 4672 | bytes 616 | tf_op jit(solution)/shard_map/jit(_take)/and | solution.py:100
  24.8 0.7 gather_fusion.3
  25.6 0.7 gather_fusion.2
  26.3 0.2 fusion.7
  26.6 3.2 %fusion.17 = f32[64,1024]{1,0:T(8,128)S(1)} fusion(bf16[2048,1024]{1,0:T(8,128)(2,1)} %param.20, bf16[64,2048]{1,0:T(8,128)(2,1)S(1)} %gather_fusion.3, pred[64]{0:T(512)(128)(4,1)S(1)} %get-tuple-element.8), kind=kOutput, calls=%fused_computation.33 | convolution fusion | flops 268566528 | bytes 4718656 | tf_op jit(solution)/shard_map/dot_general | solution.py:106
  29.9 0.2 copy-done
  30.1 0.9 convolution_add_fusion
  31.3 17.1 %all_to_all.30 = f32[32,2,1280]{2,1,0:T(2,128)S(1)} all-to-all(f32[32,2,1280]{2,1,0:T(2,128)S(1)} %pad_maximum_fusion.3), channel_id=1, replica_groups=mesh['section'=4,'mp'=2,'dp'=4] {'section','mp','dp'}, dimensions={0} | all-to-all | bytes 655360 | tf_op jit(solution)/shard_map/all_to_all | solution.py:34
  48.6 0.2 fusion.28
  49.0 0.9 broadcast_in_dim.34
  49.8 3.2 %all-to-all-start.1 = ((bf16[32,2,2048]{2,1,0:T(2,128)(2,1)}), bf16[32,2,2048]{2,1,0:T(2,128)(2,1)S(1)}, u32[]{:S(2)}, u32[]{:S(2)}) async-start(bf16[32,2,2048]{2,1,0:T(2,128)(2,1)} %bitcast.29), calls=%async_computation.1 | async-start | bytes 524288 | tf_op jit(solution)/shard_map/all_to_all | solution.py:34
  53.1 3.6 %fusion.10 = f32[64,1024]{1,0:T(8,128)S(1)} fusion(bf16[1024,2048]{1,0:T(8,128)(2,1)} %param.19, f32[2048]{0:T(1024)S(1)} %copy-done.1, f32[64]{0:T(128)S(1)} %add_rsqrt_fusion.1, bf16[64,2048]{1,0:T(8,128)(2,1)S(1)} %gather_fusion.2, pred[64]{0:T(512)(128)(4,1)S(1)} %get-tuple-element.8), kind=kOutput, calls=%fused_computation.21 | convolution fusion | flops 269090816 | bytes 4727104 | tf_op jit(solution)/shard_map/dot_general | solution.py:18
  56.9 6.3 %all-to-all-done.1 = bf16[32,2,2048]{2,1,0:T(2,128)(2,1)S(1)} async-done(((bf16[32,2,2048]{2,1,0:T(2,128)(2,1)}), bf16[32,2,2048]{2,1,0:T(2,128)(2,1)S(1)}, u32[]{:S(2)}, u32[]{:S(2)}) %all-to-all-start.1) | async-done | bytes 262176 | tf_op jit(solution)/shard_map/all_to_all | solution.py:34
  63.3 3.6 %fusion.4 = f32[1,32,2,1024]{3,1,2,0:T(8,128)S(1)} fusion(bf16[1024,2048]{1,0:T(8,128)(2,1)} %param.19, bf16[32,2,2048]{2,1,0:T(2,128)(2,1)S(1)} %all-to-all-done.1), kind=kOutput, calls=%fused_computation.8 | convolution fusion | flops 268435456 | bytes 4718592 | tf_op jit(solution)/shard_map/dot_general | solution.py:18
  66.9 1.2 copy.33
  68.1 2.7 %all-to-all-start.2 = ((f32[2,32,2,1024]{3,2,0,1:T(2,128)}), f32[2,32,2,1024]{3,2,0,1:T(2,128)S(1)}, u32[]{:S(2)}, u32[]{:S(2)}) async-start(f32[2,32,2,1024]{3,2,0,1:T(2,128)} %copy.33), calls=%async_computation.2 | async-start | bytes 1048576 | tf_op jit(solution)/shard_map/all_to_all | solution.py:148
  70.8 5.0 %fusion.41 = s32[64]{0:T(128)S(1)} fusion(s32[64]{0:T(128)S(1)} %convert_reduce_fusion, s32[]{:T(128)} %bitcast.12, s32[]{:T(128)} %bitcast.11, s32[]{:T(128)} %bitcast.10, s32[]{:T(128)} %bitcast.9, s32[]{:T(128)} %bitcast.7, s32[]{:T(128)} %bitcast.6, s32[]{:T(128)} %bitcast.5, s32[]{:T(128)} %bitcast.4), kind=kLoop, calls=%fused_computation.101 | loop fusion | flops 1280 | bytes 544 | tf_op jit(solution)/shard_map/select_n | solution.py:102
  75.9 0.7 gather_fusion
  76.6 0.6 gather_fusion.1
  77.3 7.8 %all-to-all-done.2 = f32[2,32,2,1024]{3,2,0,1:T(2,128)S(1)} async-done(((f32[2,32,2,1024]{3,2,0,1:T(2,128)}), f32[2,32,2,1024]{3,2,0,1:T(2,128)S(1)}, u32[]{:S(2)}, u32[]{:S(2)}) %all-to-all-start.2) | async-done | bytes 524320 | tf_op jit(solution)/shard_map/all_to_all | solution.py:148
  85.0 0.3 reduce_sum.122
  85.3 0.3 exponential_reduce_fusion
  85.6 0.2 fusion.33
  85.8 0.7 broadcast_in_dim.36
  86.6 4.2 %all-to-all-start.3 = ((bf16[32,2,1024]{2,1,0:T(2,128)(2,1)}), bf16[32,2,1024]{2,1,0:T(2,128)(2,1)S(1)}, u32[]{:S(2)}, u32[]{:S(2)}) async-start(bf16[32,2,1024]{2,1,0:T(2,128)(2,1)} %bitcast.40), calls=%async_computation.3 | async-start | bytes 262144 | tf_op jit(solution)/shard_map/all_to_all | solution.py:34
  90.9 8.3 %all-to-all-done.3 = bf16[32,2,1024]{2,1,0:T(2,128)(2,1)S(1)} async-done(((bf16[32,2,1024]{2,1,0:T(2,128)(2,1)}), bf16[32,2,1024]{2,1,0:T(2,128)(2,1)S(1)}, u32[]{:S(2)}, u32[]{:S(2)}) %all-to-all-start.3) | async-done | bytes 131104 | tf_op jit(solution)/shard_map/all_to_all | solution.py:34
  99.1 3.0 %fusion = f32[32,2,2048]{2,0,1:T(8,128)S(1)} fusion(bf16[1024,2048]{1,0:T(8,128)(2,1)} %param.19, bf16[32,2,1024]{2,1,0:T(2,128)(2,1)S(1)} %all-to-all-done.3), kind=kOutput, calls=%fused_computation.4 | convolution fusion | flops 268435456 | bytes 4849664 | tf_op jit(solution)/shard_map/dot_general | solution.py:181
  102.2 1.2 copy.36
  103.4 2.6 %all-to-all-start.4 = ((f32[32,2,2176]{2,1,0:T(2,128)}), f32[32,2,2176]{2,1,0:T(2,128)S(1)}, u32[]{:S(2)}, u32[]{:S(2)}) async-start(f32[32,2,2176]{2,1,0:T(2,128)} %copy.36), calls=%async_computation.4 | async-start | bytes 1114112 | tf_op jit(solution)/shard_map/all_to_all | solution.py:34
  106.1 14.9 %all-to-all-done.4 = f32[32,2,2176]{2,1,0:T(2,128)S(1)} async-done(((f32[32,2,2176]{2,1,0:T(2,128)}), f32[32,2,2176]{2,1,0:T(2,128)S(1)}, u32[]{:S(2)}, u32[]{:S(2)}) %all-to-all-start.4) | async-done | bytes 557088 | tf_op jit(solution)/shard_map/all_to_all | solution.py:34
  121.1 0.2 fusion.29
  121.4 0.7 broadcast_in_dim.40
  122.1 4.4 %all-to-all-start.5 = ((bf16[32,2,1024]{2,1,0:T(2,128)(2,1)}), bf16[32,2,1024]{2,1,0:T(2,128)(2,1)S(1)}, u32[]{:S(2)}, u32[]{:S(2)}) async-start(bf16[32,2,1024]{2,1,0:T(2,128)(2,1)} %bitcast.50), calls=%async_computation.5 | async-start | bytes 262144 | tf_op jit(solution)/shard_map/all_to_all | solution.py:34
  126.5 0.6 slice_reduce_fusion.2
  127.8 6.9 %all-to-all-done.5 = bf16[32,2,1024]{2,1,0:T(2,128)(2,1)S(1)} async-done(((bf16[32,2,1024]{2,1,0:T(2,128)(2,1)}), bf16[32,2,1024]{2,1,0:T(2,128)(2,1)S(1)}, u32[]{:S(2)}, u32[]{:S(2)}) %all-to-all-start.5) | async-done | bytes 131104 | tf_op jit(solution)/shard_map/all_to_all | solution.py:34
  134.7 4.8 %fusion.48 = f32[2048,1024]{1,0:T(8,128)} fusion(bf16[64,1024]{1,0:T(8,128)(2,1)S(1)} %reshape.432, bf16[64,2048]{1,0:T(8,128)(2,1)S(1)} %gather_fusion.2, pred[64]{0:T(512)(128)(4,1)S(1)} %get-tuple-element.8), kind=kOutput, calls=%fused_computation.122 | convolution fusion | flops 268566528 | bytes 8781888 | tf_op jit(solution)/shard_map/dot_general | solution.py:24
  139.5 4.8 %fusion.16 = f32[2048,1024]{1,0:T(8,128)} fusion(bf16[64,1024]{1,0:T(8,128)(2,1)S(1)} %reshape.432, bf16[64,2048]{1,0:T(8,128)(2,1)S(1)} %gather_fusion.3, pred[64]{0:T(512)(128)(4,1)S(1)} %get-tuple-element.8), kind=kOutput, calls=%fused_computation.32 | convolution fusion | flops 268566528 | bytes 8781888 | tf_op jit(solution)/shard_map/dot_general | solution.py:24
  (48 shorter events, 2.1 us)
Async XLA Ops:
  3.8 14.1 %collective-permute-start.1 = (bf16[2,16,2048]{2,1,0:T(8,128)(2,1)S(1)}, bf16[2,16,2048]{2,1,0:T(8,128)(2,1)S(1)}, u32[]{:S(2)}, u32[]{:S(2)}) collective-permute-start(bf16[2,16,2048]{2,1,0:T(8,128)(2,1)S(1)} %get-tuple-element.15), channel_id=1, source_target_pairs={{0,2},{1,3},{2,0},{3,1},{4,6},{5,7},{6,4},{7,5},{8,10},{9,11},{10,... | collective-permute-start | bytes 393224 | tf_op jit(solution)/shard_map/ppermute | solution.py:40
  8.0 10.0 %collective-permute-start = (bf16[2,16,2048]{2,1,0:T(8,128)(2,1)S(1)}, bf16[2,16,2048]{2,1,0:T(8,128)(2,1)S(1)}, u32[]{:S(2)}, u32[]{:S(2)}) collective-permute-start(bf16[2,16,2048]{2,1,0:T(8,128)(2,1)S(1)} %get-tuple-element.15), channel_id=1, source_target_pairs={{0,1},{1,2},{2,3},{3,0},{4,5},{5,6},{6,7},{7,4},{8,9},{9,10},{10,1... | collective-permute-start | bytes 393224 | tf_op jit(solution)/shard_map/ppermute | solution.py:40
  9.5 9.1 %collective-permute-start.2 = (bf16[2,16,2048]{2,1,0:T(8,128)(2,1)S(1)}, bf16[2,16,2048]{2,1,0:T(8,128)(2,1)S(1)}, u32[]{:S(2)}, u32[]{:S(2)}) collective-permute-start(bf16[2,16,2048]{2,1,0:T(8,128)(2,1)S(1)} %get-tuple-element.15), channel_id=1, source_target_pairs={{0,3},{1,0},{2,1},{3,2},{4,7},{5,4},{6,5},{7,6},{8,11},{9,8},{10,9... | collective-permute-start | bytes 393224 | tf_op jit(solution)/shard_map/ppermute | solution.py:40
  18.7 5.9 %collective-permute-start.3 = (bf16[4,2,16,2048]{3,2,1,0:T(8,128)(2,1)S(1)}, bf16[4,2,16,2048]{3,2,1,0:T(8,128)(2,1)S(1)}, u32[]{:S(2)}, u32[]{:S(2)}) collective-permute-start(bf16[4,2,16,2048]{3,2,1,0:T(8,128)(2,1)S(1)} %get-tuple-element.13), channel_id=1, source_target_pairs={{0,4},{4,0},{1,5},{5,1},{2,6},{6,2},{3,7},{7,3},{8,12},{12,8},{9,1... | collective-permute-start | bytes 1572872 | tf_op jit(solution)/shard_map/ppermute | solution.py:40
  26.6 3.5 %copy-start = (bf16[2048,1024]{1,0:T(8,128)(2,1)S(1)}, bf16[2048,1024]{1,0:T(8,128)(2,1)}, u32[]{:S(2)}) copy-start(bf16[2048,1024]{1,0:T(8,128)(2,1)} %param.21) | copy-start | bytes 12582916
  30.1 23.0 %copy-start.1 = (f32[2048]{0:T(1024)S(1)}, f32[2048]{0:T(1024)}, u32[]{:S(2)}) copy-start(f32[2048]{0:T(1024)} %param.17) | copy-start | bytes 24580
  49.8 13.4 %all-to-all-start.1 = ((bf16[32,2,2048]{2,1,0:T(2,128)(2,1)}), bf16[32,2,2048]{2,1,0:T(2,128)(2,1)S(1)}, u32[]{:S(2)}, u32[]{:S(2)}) async-start(bf16[32,2,2048]{2,1,0:T(2,128)(2,1)} %bitcast.29), calls=%async_computation.1 | async-start | bytes 524288 | tf_op jit(solution)/shard_map/all_to_all | solution.py:34
  56.8 14.0 %copy-start.2 = (s32[4,256]{1,0:T(4,128)S(1)}, s32[4,256]{1,0:T(4,128)}, u32[]{:S(2)}) copy-start(s32[4,256]{1,0:T(4,128)} %param.14) | copy-start | bytes 12292
  68.1 16.9 %all-to-all-start.2 = ((f32[2,32,2,1024]{3,2,0,1:T(2,128)}), f32[2,32,2,1024]{3,2,0,1:T(2,128)S(1)}, u32[]{:S(2)}, u32[]{:S(2)}) async-start(f32[2,32,2,1024]{3,2,0,1:T(2,128)} %copy.33), calls=%async_computation.2 | async-start | bytes 1048576 | tf_op jit(solution)/shard_map/all_to_all | solution.py:148
  86.6 12.6 %all-to-all-start.3 = ((bf16[32,2,1024]{2,1,0:T(2,128)(2,1)}), bf16[32,2,1024]{2,1,0:T(2,128)(2,1)S(1)}, u32[]{:S(2)}, u32[]{:S(2)}) async-start(bf16[32,2,1024]{2,1,0:T(2,128)(2,1)} %bitcast.40), calls=%async_computation.3 | async-start | bytes 262144 | tf_op jit(solution)/shard_map/all_to_all | solution.py:34
  103.4 17.5 %all-to-all-start.4 = ((f32[32,2,2176]{2,1,0:T(2,128)}), f32[32,2,2176]{2,1,0:T(2,128)S(1)}, u32[]{:S(2)}, u32[]{:S(2)}) async-start(f32[32,2,2176]{2,1,0:T(2,128)} %copy.36), calls=%async_computation.4 | async-start | bytes 1114112 | tf_op jit(solution)/shard_map/all_to_all | solution.py:34
  122.1 12.6 %all-to-all-start.5 = ((bf16[32,2,1024]{2,1,0:T(2,128)(2,1)}), bf16[32,2,1024]{2,1,0:T(2,128)(2,1)S(1)}, u32[]{:S(2)}, u32[]{:S(2)}) async-start(bf16[32,2,1024]{2,1,0:T(2,128)(2,1)} %bitcast.50), calls=%async_computation.5 | async-start | bytes 262144 | tf_op jit(solution)/shard_map/all_to_all | solution.py:34

commit v4 on v3

--- a/solution.py
+++ b/solution.py
@@ -26,8 +26,13 @@
     )
 
 
-def sequence_of(packed, starts):
-    return jnp.sum((starts[None, :] <= packed[:, None]).astype(jnp.int32), axis=1) - 1
+def locate(packed, starts, lengths, offsets):
+    rel = packed[:, None] - starts[None, :]
+    inside = (rel >= 0) & (rel < lengths[None, :])
+    seq = jnp.sum(jnp.where(inside, jnp.arange(starts.shape[0], dtype=jnp.int32)[None, :], 0), axis=1)
+    slot = jnp.sum(jnp.where(inside, rel, 0), axis=1)
+    offset = jnp.sum(jnp.where(inside, offsets[None, :], 0), axis=1)
+    return seq, slot, offset
 
 
 def exchange(send, axes):
@@ -76,7 +81,9 @@
     total_rows = R_OWN * groups
     per_dev = total_rows // n_dev
     half = 2 * R_OWN
-    starts = jnp.cumsum(lengths) - lengths
+    count_seq = lengths.shape[0]
+    earlier = jnp.arange(count_seq)[None, :] < jnp.arange(count_seq)[:, None]
+    starts = jnp.sum(jnp.where(earlier, lengths[None, :], 0), axis=1)
 
     first = jnp.minimum(offsets[my_dp] + my_mp * half, seq_len - half)
     mine = jnp.stack(
@@ -88,20 +95,23 @@
     every = shifted(shifted(mine, "dp"), "mp")
     every = every.transpose(2, 0, 1, 3, 4).reshape(2, count_mp * count_dp * half, width)
     packed = jnp.arange(total_rows, dtype=jnp.int32)
-    seq_all = sequence_of(packed, starts)
-    slot_all = packed - starts[seq_all]
+    seq_all, slot_all, offset_all = locate(packed, starts, lengths, offsets)
     shift_mp = (my_mp - slot_all // half) % count_mp
     shift_dp = (my_dp - seq_all) % count_dp
-    base = offsets[seq_all] + (slot_all // half) * half
+    base = offset_all + (slot_all // half) * half
     lag = base - jnp.minimum(base, seq_len - half)
     within = jnp.minimum(slot_all % half + lag, half - 1)
     pick = (shift_mp * count_dp + shift_dp) * half + within
     embed_all = jnp.take(every[0], pick, axis=0)
     feature_all = jnp.take(every[1], pick, axis=0)
-    position_all = offsets[seq_all] + slot_all
-    labels_all = token_ids.reshape(-1)[seq_all * seq_len + position_all]
     my_rows = me * per_dev + jnp.arange(per_dev, dtype=jnp.int32)
-    labels = labels_all[my_rows]
+    my_seq, my_slot, my_offset = locate(my_rows, starts, lengths, offsets)
+    flat = my_seq * seq_len + my_offset + my_slot
+    ids = token_ids.reshape(-1)
+    labels = jnp.sum(
+        jnp.where(jnp.arange(ids.shape[0], dtype=jnp.int32)[None, :] == flat[:, None], ids, 0),
+        axis=1,
+    )
 
     partial_value = jnp.dot(embed_all, fc_embed, preferred_element_type=jnp.float32) + jnp.dot(
         feature_all, fc_feature, preferred_element_type=jnp.float32

time: 146 us -> 142 us (0.973)
  other arithmetic: 14.7 us -> 4.98 us
  waiting for transfers between devices: 48.7 us -> 56.5 us
  local copies, waits for them, and re-layouts: 12.6 us -> 10.3 us
    all_to_all x1, waiting for transfers between devices: 7.75 us -> 13.7 us  [on_device(): got3 = lax.all_to_all(send3, ALL, split_axis=1, concat_axis=1, tiled=True)]
    select_n x2 -> x0, other arithmetic: 5.04 us -> none  [the longest x1 5.04 us: on_device(): labels_all = token_ids.reshape(-1)[seq_all * seq_len + position_all]]
    and x1, other arithmetic: 5.06 us -> 0.03 us  [on_device(): feature_all = jnp.take(every[1], pick, axis=0)]
    gather x4 -> x0, local copies, waits for them, and re-layouts: 3.53 us -> none  [the longest x1 1.52 us: on_device(): base = offsets[seq_all] + slot_all // half * half]
    reduce_sum x1 -> x4, other arithmetic: 0.08 us -> 1.94 us  [the longest x1 0.77 us: on_device(): starts = jnp.sum(jnp.where(earlier, lengths[None, :], 0), axis=1)]
    ppermute x4, waiting for transfers between devices: 4.57 us -> 6.37 us  [shifted(): lax.ppermute(x, axis, [(i, (i + k) % count) for i in range(count)])]
  transfers between devices with their start and end apart: 9 -> 9, of which waited for: 7 -> 8; matrix products, arithmetic and copies ran while one was open for 13% -> 5% of each run, Pallas kernels for 0% -> 0%
where the time goes in v4:
time: 142 us; the launch traced here: 141 us
  waiting for transfers between devices  56.5 us (40%)
  starting transfers between devices  25.1 us (18%)
  matrix products  23.8 us (17%)
  blocking collectives  17 us (12%)
  local copies, waits for them, and re-layouts  10.3 us (7%)
  other arithmetic  4.98 us (4%)
  between operations  3.44 us (2%)
    all_to_all x4, waiting for transfers between devices, exchange(): return lax.all_to_all(send, axes, split_axis=0, concat_axis=0, tiled=True)  36.4 us
    all_to_all x1, blocking collectives, exchange(): return lax.all_to_all(send, axes, split_axis=0, concat_axis=0, tiled=True)  17 us
    all_to_all x4, starting transfers between devices, exchange(): return lax.all_to_all(send, axes, split_axis=0, concat_axis=0, tiled=True)  14.4 us
    all_to_all x1, waiting for transfers between devices, on_device(): got3 = lax.all_to_all(send3, ALL, split_axis=1, concat_axis=1, tiled=True)  13.7 us
    dot_general x2, matrix products, contract_first(): lax.dot_general(operand, weights, (((0,), (0,)), ((), ())), preferred_ele...  9.52 us
    ppermute x4, starting transfers between devices, shifted(): lax.ppermute(x, axis, [(i, (i + k) % count) for i in range(count)])  8.02 us
    dot_general x2, matrix products, contract_last(): lax.dot_general(operand, weights, (((1,), (1,)), ((), ())), preferred_ele...  7.17 us
    ppermute x4, waiting for transfers between devices, shifted(): lax.ppermute(x, axis, [(i, (i + k) % count) for i in range(count)])  6.37 us
  transfers between devices with their start and end apart: 9, of which 8 were waited for; matrix products, arithmetic and copies ran while one was open for 5% of the time, Pallas kernels for 0%

profile of v4, /device:TPU:0, one launch (start us, length us, event | category | flops | bytes accessed | tf_op | source)
XLA Modules:
  0.0 141.1 jit_solution(4551913530544988409)
XLA Ops:
  0.6 1.2 dynamic_slice.12
  2.5 1.0 constant_dynamic-slice_fusion
  3.6 4.1 %collective-permute-start.1 = (bf16[2,16,2048]{2,1,0:T(8,128)(2,1)S(1)}, bf16[2,16,2048]{2,1,0:T(8,128)(2,1)S(1)}, u32[]{:S(2)}, u32[]{:S(2)}) collective-permute-start(bf16[2,16,2048]{2,1,0:T(8,128)(2,1)S(1)} %get-tuple-element.21), channel_id=1, source_target_pairs={{0,2},{1,3},{2,0},{3,1},{4,6},{5,7},{6,4},{7,5},{8,10},{9,11},{10,... | collective-permute-start | bytes 393224 | tf_op jit(solution)/shard_map/ppermute | solution.py:45
  7.7 1.6 %collective-permute-start = (bf16[2,16,2048]{2,1,0:T(8,128)(2,1)S(1)}, bf16[2,16,2048]{2,1,0:T(8,128)(2,1)S(1)}, u32[]{:S(2)}, u32[]{:S(2)}) collective-permute-start(bf16[2,16,2048]{2,1,0:T(8,128)(2,1)S(1)} %get-tuple-element.21), channel_id=1, source_target_pairs={{0,1},{1,2},{2,3},{3,0},{4,5},{5,6},{6,7},{7,4},{8,9},{9,10},{10,1... | collective-permute-start | bytes 393224 | tf_op jit(solution)/shard_map/ppermute | solution.py:45
  9.3 2.2 %collective-permute-start.2 = (bf16[2,16,2048]{2,1,0:T(8,128)(2,1)S(1)}, bf16[2,16,2048]{2,1,0:T(8,128)(2,1)S(1)}, u32[]{:S(2)}, u32[]{:S(2)}) collective-permute-start(bf16[2,16,2048]{2,1,0:T(8,128)(2,1)S(1)} %get-tuple-element.21), channel_id=1, source_target_pairs={{0,3},{1,0},{2,1},{3,2},{4,7},{5,4},{6,5},{7,6},{8,11},{9,8},{10,9... | collective-permute-start | bytes 393224 | tf_op jit(solution)/shard_map/ppermute | solution.py:45
  11.5 0.8 dynamic_slice.15
  12.3 5.4 %collective-permute-done.1 = bf16[2,16,2048]{2,1,0:T(8,128)(2,1)S(1)} collective-permute-done((bf16[2,16,2048]{2,1,0:T(8,128)(2,1)S(1)}, bf16[2,16,2048]{2,1,0:T(8,128)(2,1)S(1)}, u32[]{:S(2)}, u32[]{:S(2)}) %collective-permute-start.1) | collective-permute-done | bytes 131104 | tf_op jit(solution)/shard_map/ppermute | solution.py:45
  17.7 0.6 collective-permute-done.2
  18.5 0.8 select_reduce_fusion.3
  19.3 0.8 select_reduce_fusion.2
  20.1 0.3 collective-permute-done.3
  20.6 0.7 gather_fusion.1
  21.3 0.7 gather_fusion
  22.1 0.2 fusion.7
  22.4 3.2 %fusion.17 = f32[64,1024]{1,0:T(8,128)S(1)} fusion(bf16[2048,1024]{1,0:T(8,128)(2,1)} %param.20, bf16[64,2048]{1,0:T(8,128)(2,1)S(1)} %gather_fusion.1, pred[64]{0:T(512)(128)(4,1)S(1)} %get-tuple-element.14), kind=kOutput, calls=%fused_computation.31 | convolution fusion | flops 268566528 | bytes 4718656 | tf_op jit(solution)/shard_map/dot_general | solution.py:116
  25.7 0.2 copy-done
  25.9 0.9 convolution_add_fusion
  26.8 0.1 reshape.335
  27.1 17.0 %all_to_all.30 = f32[32,2,1280]{2,1,0:T(2,128)S(1)} all-to-all(f32[32,2,1280]{2,1,0:T(2,128)S(1)} %pad_maximum_fusion.3), channel_id=1, replica_groups=mesh['section'=4,'mp'=2,'dp'=4] {'section','mp','dp'}, dimensions={0} | all-to-all | bytes 655360 | tf_op jit(solution)/shard_map/all_to_all | solution.py:39
  44.3 0.2 fusion.28
  44.7 0.9 broadcast_in_dim.136
  45.5 3.2 %all-to-all-start.1 = ((bf16[32,2,2048]{2,1,0:T(2,128)(2,1)}), bf16[32,2,2048]{2,1,0:T(2,128)(2,1)S(1)}, u32[]{:S(2)}, u32[]{:S(2)}) async-start(bf16[32,2,2048]{2,1,0:T(2,128)(2,1)} %bitcast.15), calls=%async_computation.1 | async-start | bytes 524288 | tf_op jit(solution)/shard_map/all_to_all | solution.py:39
  48.8 3.6 %fusion.10 = f32[64,1024]{1,0:T(8,128)S(1)} fusion(bf16[1024,2048]{1,0:T(8,128)(2,1)} %param.19, f32[2048]{0:T(1024)S(1)} %copy-done.1, f32[64]{0:T(128)S(1)} %add_rsqrt_fusion.1, bf16[64,2048]{1,0:T(8,128)(2,1)S(1)} %gather_fusion, pred[64]{0:T(512)(128)(4,1)S(1)} %get-tuple-element.14), kind=kOutput, calls=%fused_computation.19 | convolution fusion | flops 269090816 | bytes 4727104 | tf_op jit(solution)/shard_map/dot_general | solution.py:18
  52.4 0.2 stack.45
  52.7 6.3 %all-to-all-done.1 = bf16[32,2,2048]{2,1,0:T(2,128)(2,1)S(1)} async-done(((bf16[32,2,2048]{2,1,0:T(2,128)(2,1)}), bf16[32,2,2048]{2,1,0:T(2,128)(2,1)S(1)}, u32[]{:S(2)}, u32[]{:S(2)}) %all-to-all-start.1) | async-done | bytes 262176 | tf_op jit(solution)/shard_map/all_to_all | solution.py:39
  59.0 3.6 %fusion.4 = f32[1,32,2,1024]{3,1,2,0:T(8,128)S(1)} fusion(bf16[1024,2048]{1,0:T(8,128)(2,1)} %param.19, bf16[32,2,2048]{2,1,0:T(2,128)(2,1)S(1)} %all-to-all-done.1), kind=kOutput, calls=%fused_computation.6 | convolution fusion | flops 268435456 | bytes 4718592 | tf_op jit(solution)/shard_map/dot_general | solution.py:18
  62.6 1.2 copy.30
  63.8 2.7 %all-to-all-start.2 = ((f32[2,32,2,1024]{3,2,0,1:T(2,128)}), f32[2,32,2,1024]{3,2,0,1:T(2,128)S(1)}, u32[]{:S(2)}, u32[]{:S(2)}) async-start(f32[2,32,2,1024]{3,2,0,1:T(2,128)} %copy.30), calls=%async_computation.2 | async-start | bytes 1048576 | tf_op jit(solution)/shard_map/all_to_all | solution.py:158
  66.6 0.2 select_reduce_fusion.5
  66.8 0.2 fusion.34
  67.0 13.7 %all-to-all-done.2 = f32[2,32,2,1024]{3,2,0,1:T(2,128)S(1)} async-done(((f32[2,32,2,1024]{3,2,0,1:T(2,128)}), f32[2,32,2,1024]{3,2,0,1:T(2,128)S(1)}, u32[]{:S(2)}, u32[]{:S(2)}) %all-to-all-start.2) | async-done | bytes 524320 | tf_op jit(solution)/shard_map/all_to_all | solution.py:158
  80.7 0.3 reduce_sum.188
  81.0 0.3 exponential_reduce_fusion
  81.3 0.2 fusion.33
  81.5 0.7 broadcast_in_dim.142
  82.2 4.2 %all-to-all-start.3 = ((bf16[32,2,1024]{2,1,0:T(2,128)(2,1)}), bf16[32,2,1024]{2,1,0:T(2,128)(2,1)S(1)}, u32[]{:S(2)}, u32[]{:S(2)}) async-start(bf16[32,2,1024]{2,1,0:T(2,128)(2,1)} %bitcast.24), calls=%async_computation.3 | async-start | bytes 262144 | tf_op jit(solution)/shard_map/all_to_all | solution.py:39
  86.5 8.3 %all-to-all-done.3 = bf16[32,2,1024]{2,1,0:T(2,128)(2,1)S(1)} async-done(((bf16[32,2,1024]{2,1,0:T(2,128)(2,1)}), bf16[32,2,1024]{2,1,0:T(2,128)(2,1)S(1)}, u32[]{:S(2)}, u32[]{:S(2)}) %all-to-all-start.3) | async-done | bytes 131104 | tf_op jit(solution)/shard_map/all_to_all | solution.py:39
  94.8 3.0 %fusion = f32[32,2,2048]{2,0,1:T(8,128)S(1)} fusion(bf16[1024,2048]{1,0:T(8,128)(2,1)} %param.19, bf16[32,2,1024]{2,1,0:T(2,128)(2,1)S(1)} %all-to-all-done.3), kind=kOutput, calls=%fused_computation.2 | convolution fusion | flops 268435456 | bytes 4849664 | tf_op jit(solution)/shard_map/dot_general | solution.py:191
  97.9 1.2 copy.33
  99.1 2.6 %all-to-all-start.4 = ((f32[32,2,2176]{2,1,0:T(2,128)}), f32[32,2,2176]{2,1,0:T(2,128)S(1)}, u32[]{:S(2)}, u32[]{:S(2)}) async-start(f32[32,2,2176]{2,1,0:T(2,128)} %copy.33), calls=%async_computation.4 | async-start | bytes 1114112 | tf_op jit(solution)/shard_map/all_to_all | solution.py:39
  101.8 14.9 %all-to-all-done.4 = f32[32,2,2176]{2,1,0:T(2,128)S(1)} async-done(((f32[32,2,2176]{2,1,0:T(2,128)}), f32[32,2,2176]{2,1,0:T(2,128)S(1)}, u32[]{:S(2)}, u32[]{:S(2)}) %all-to-all-start.4) | async-done | bytes 557088 | tf_op jit(solution)/shard_map/all_to_all | solution.py:39
  116.7 0.2 fusion.29
  117.1 0.7 broadcast_in_dim.146
  117.8 4.4 %all-to-all-start.5 = ((bf16[32,2,1024]{2,1,0:T(2,128)(2,1)}), bf16[32,2,1024]{2,1,0:T(2,128)(2,1)S(1)}, u32[]{:S(2)}, u32[]{:S(2)}) async-start(bf16[32,2,1024]{2,1,0:T(2,128)(2,1)} %bitcast.34), calls=%async_computation.5 | async-start | bytes 262144 | tf_op jit(solution)/shard_map/all_to_all | solution.py:39
  122.2 0.6 slice_reduce_fusion.2
  123.5 6.9 %all-to-all-done.5 = bf16[32,2,1024]{2,1,0:T(2,128)(2,1)S(1)} async-done(((bf16[32,2,1024]{2,1,0:T(2,128)(2,1)}), bf16[32,2,1024]{2,1,0:T(2,128)(2,1)S(1)}, u32[]{:S(2)}, u32[]{:S(2)}) %all-to-all-start.5) | async-done | bytes 131104 | tf_op jit(solution)/shard_map/all_to_all | solution.py:39
  130.4 4.8 %fusion.50 = f32[2048,1024]{1,0:T(8,128)} fusion(bf16[64,1024]{1,0:T(8,128)(2,1)S(1)} %reshape.346, bf16[64,2048]{1,0:T(8,128)(2,1)S(1)} %gather_fusion, pred[64]{0:T(512)(128)(4,1)S(1)} %get-tuple-element.14), kind=kOutput, calls=%fused_computation.117 | convolution fusion | flops 268566528 | bytes 8781888 | tf_op jit(solution)/shard_map/dot_general | solution.py:24
  135.2 4.8 %fusion.16 = f32[2048,1024]{1,0:T(8,128)} fusion(bf16[64,1024]{1,0:T(8,128)(2,1)S(1)} %reshape.346, bf16[64,2048]{1,0:T(8,128)(2,1)S(1)} %gather_fusion.1, pred[64]{0:T(512)(128)(4,1)S(1)} %get-tuple-element.14), kind=kOutput, calls=%fused_computation.30 | convolution fusion | flops 268566528 | bytes 8781888 | tf_op jit(solution)/shard_map/dot_general | solution.py:24
  (48 shorter events, 1.7 us)
Async XLA Ops:
  3.6 14.1 %collective-permute-start.1 = (bf16[2,16,2048]{2,1,0:T(8,128)(2,1)S(1)}, bf16[2,16,2048]{2,1,0:T(8,128)(2,1)S(1)}, u32[]{:S(2)}, u32[]{:S(2)}) collective-permute-start(bf16[2,16,2048]{2,1,0:T(8,128)(2,1)S(1)} %get-tuple-element.21), channel_id=1, source_target_pairs={{0,2},{1,3},{2,0},{3,1},{4,6},{5,7},{6,4},{7,5},{8,10},{9,11},{10,... | collective-permute-start | bytes 393224 | tf_op jit(solution)/shard_map/ppermute | solution.py:45
  7.7 10.0 %collective-permute-start = (bf16[2,16,2048]{2,1,0:T(8,128)(2,1)S(1)}, bf16[2,16,2048]{2,1,0:T(8,128)(2,1)S(1)}, u32[]{:S(2)}, u32[]{:S(2)}) collective-permute-start(bf16[2,16,2048]{2,1,0:T(8,128)(2,1)S(1)} %get-tuple-element.21), channel_id=1, source_target_pairs={{0,1},{1,2},{2,3},{3,0},{4,5},{5,6},{6,7},{7,4},{8,9},{9,10},{10,1... | collective-permute-start | bytes 393224 | tf_op jit(solution)/shard_map/ppermute | solution.py:45
  9.3 9.1 %collective-permute-start.2 = (bf16[2,16,2048]{2,1,0:T(8,128)(2,1)S(1)}, bf16[2,16,2048]{2,1,0:T(8,128)(2,1)S(1)}, u32[]{:S(2)}, u32[]{:S(2)}) collective-permute-start(bf16[2,16,2048]{2,1,0:T(8,128)(2,1)S(1)} %get-tuple-element.21), channel_id=1, source_target_pairs={{0,3},{1,0},{2,1},{3,2},{4,7},{5,4},{6,5},{7,6},{8,11},{9,8},{10,9... | collective-permute-start | bytes 393224 | tf_op jit(solution)/shard_map/ppermute | solution.py:45
  18.4 2.0 %collective-permute-start.3 = (bf16[4,2,16,2048]{3,2,1,0:T(8,128)(2,1)S(1)}, bf16[4,2,16,2048]{3,2,1,0:T(8,128)(2,1)S(1)}, u32[]{:S(2)}, u32[]{:S(2)}) collective-permute-start(bf16[4,2,16,2048]{3,2,1,0:T(8,128)(2,1)S(1)} %get-tuple-element.19), channel_id=1, source_target_pairs={{0,4},{4,0},{1,5},{5,1},{2,6},{6,2},{3,7},{7,3},{8,12},{12,8},{9,1... | collective-permute-start | bytes 1572872 | tf_op jit(solution)/shard_map/ppermute | solution.py:45
  22.4 3.5 %copy-start = (bf16[2048,1024]{1,0:T(8,128)(2,1)S(1)}, bf16[2048,1024]{1,0:T(8,128)(2,1)}, u32[]{:S(2)}) copy-start(bf16[2048,1024]{1,0:T(8,128)(2,1)} %param.21) | copy-start | bytes 12582916
  25.9 22.9 %copy-start.1 = (f32[2048]{0:T(1024)S(1)}, f32[2048]{0:T(1024)}, u32[]{:S(2)}) copy-start(f32[2048]{0:T(1024)} %param.17) | copy-start | bytes 24580
  45.5 13.4 %all-to-all-start.1 = ((bf16[32,2,2048]{2,1,0:T(2,128)(2,1)}), bf16[32,2,2048]{2,1,0:T(2,128)(2,1)S(1)}, u32[]{:S(2)}, u32[]{:S(2)}) async-start(bf16[32,2,2048]{2,1,0:T(2,128)(2,1)} %bitcast.15), calls=%async_computation.1 | async-start | bytes 524288 | tf_op jit(solution)/shard_map/all_to_all | solution.py:39
  52.5 14.0 %copy-start.2 = (s32[4,256]{1,0:T(4,128)S(1)}, s32[4,256]{1,0:T(4,128)}, u32[]{:S(2)}) copy-start(s32[4,256]{1,0:T(4,128)} %param.14) | copy-start | bytes 12292
  52.5 14.0 %copy-start.3 = (s32[4]{0:T(128)S(1)}, s32[4]{0:T(128)}, u32[]{:S(2)}) copy-start(s32[4]{0:T(128)} %param.16) | copy-start | bytes 52
  52.5 14.0 %copy-start.4 = (s32[4]{0:T(128)S(1)}, s32[4]{0:T(128)}, u32[]{:S(2)}) copy-start(s32[4]{0:T(128)} %param.15) | copy-start | bytes 52
  63.8 16.9 %all-to-all-start.2 = ((f32[2,32,2,1024]{3,2,0,1:T(2,128)}), f32[2,32,2,1024]{3,2,0,1:T(2,128)S(1)}, u32[]{:S(2)}, u32[]{:S(2)}) async-start(f32[2,32,2,1024]{3,2,0,1:T(2,128)} %copy.30), calls=%async_computation.2 | async-start | bytes 1048576 | tf_op jit(solution)/shard_map/all_to_all | solution.py:158
  82.2 12.6 %all-to-all-start.3 = ((bf16[32,2,1024]{2,1,0:T(2,128)(2,1)}), bf16[32,2,1024]{2,1,0:T(2,128)(2,1)S(1)}, u32[]{:S(2)}, u32[]{:S(2)}) async-start(bf16[32,2,1024]{2,1,0:T(2,128)(2,1)} %bitcast.24), calls=%async_computation.3 | async-start | bytes 262144 | tf_op jit(solution)/shard_map/all_to_all | solution.py:39
  99.1 17.5 %all-to-all-start.4 = ((f32[32,2,2176]{2,1,0:T(2,128)}), f32[32,2,2176]{2,1,0:T(2,128)S(1)}, u32[]{:S(2)}, u32[]{:S(2)}) async-start(f32[32,2,2176]{2,1,0:T(2,128)} %copy.33), calls=%async_computation.4 | async-start | bytes 1114112 | tf_op jit(solution)/shard_map/all_to_all | solution.py:39
  117.8 12.6 %all-to-all-start.5 = ((bf16[32,2,1024]{2,1,0:T(2,128)(2,1)}), bf16[32,2,1024]{2,1,0:T(2,128)(2,1)S(1)}, u32[]{:S(2)}, u32[]{:S(2)}) async-start(bf16[32,2,1024]{2,1,0:T(2,128)(2,1)} %bitcast.34), calls=%async_computation.5 | async-start | bytes 262144 | tf_op jit(solution)/shard_map/all_to_all | solution.py:39

commit v5 on v4

--- a/solution.py
+++ b/solution.py
@@ -189,19 +189,35 @@
     grad_tile = exchange(send4, ALL).reshape(total_rows, vocab_tile)
 
     grad_part = jnp.dot(grad_tile, head, preferred_element_type=jnp.float32)
-    loss_cols = jnp.pad(row_loss[:, None], ((0, 0), (0, 127)))
-    send5 = jnp.concatenate(
-        [
-            grad_part.reshape(n_dev, per_dev, width),
-            jnp.broadcast_to(loss_cols[None], (n_dev,) + loss_cols.shape),
-        ],
-        axis=2,
-    )
-    got5 = exchange(send5, ALL).reshape(count_sec, groups, per_dev, -1)
+    by_mp = grad_part.reshape(count_sec, count_mp, count_dp, per_dev, width).transpose(1, 0, 2, 3, 4)
+    loss_cols = jnp.broadcast_to(
+        jnp.pad(row_loss[:, None], ((0, 0), (0, 127))), (count_sec, count_dp, per_dev, 128)
+    )
+    got_mp = []
+    for k in range(count_mp):
+        payload = jnp.concatenate(
+            [lax.dynamic_index_in_dim(by_mp, (my_mp + k) % count_mp, 0, keepdims=False), loss_cols],
+            axis=3,
+        )
+        if k:
+            payload = lax.ppermute(payload, "mp", [(i, (i + k) % count_mp) for i in range(count_mp)])
+        got_mp.append(payload)
+    got_mp = jnp.stack(got_mp)
+    reduced = jnp.sum(got_mp[..., :width], axis=0)
+    pair = jnp.take(
+        got_mp[:, 0, 0, :, width], (my_mp - jnp.arange(count_mp, dtype=jnp.int32)) % count_mp, axis=0
+    )
+    pair_cols = jnp.broadcast_to(
+        jnp.pad(pair.T, ((0, 0), (0, 128 - count_mp))), (count_sec, count_dp, per_dev, 128)
+    )
+    send5 = jnp.concatenate([reduced, pair_cols], axis=3).reshape(
+        count_sec * count_dp, per_dev, width + 128
+    )
+    got5 = exchange(send5, ("section", "dp")).reshape(count_sec, count_dp, per_dev, width + 128)
     draft_grad = (
         jnp.sum(got5[..., :width], axis=1).transpose(1, 0, 2).reshape(per_dev, full_width)
     )
-    loss = jnp.mean(got5[..., width].reshape(total_rows))
+    loss = jnp.mean(got5[..., width : width + count_mp])
     upstream = draft_grad * gain_full
     inner_sum = jnp.sum(hidden * upstream, axis=1)
     hidden_grad = (

time: 142 us -> 141 us (level)
  waiting for transfers between devices: 56.5 us -> 54.5 us
    all_to_all x4, waiting for transfers between devices: 36.4 us -> 32.9 us  [exchange(): return lax.all_to_all(send, axes, split_axis=0, concat_axis=0, tiled=True)]
    ppermute x0 -> x1, waiting for transfers between devices: none -> 1.5 us  [on_device(): lax.ppermute(payload, 'mp', [(i, (i + k) % count_mp) for i in range(count...]
  transfers between devices with their start and end apart: 9 -> 10, of which waited for: 8 -> 9; matrix products, arithmetic and copies ran while one was open for 5% -> 5% of each run, Pallas kernels for 0% -> 0%
where the time goes in v5:
time: 141 us; the launch traced here: 140 us
  waiting for transfers between devices  54.5 us (39%)
  starting transfers between devices  24.4 us (17%)
  matrix products  24 us (17%)
  blocking collectives  17 us (12%)
  local copies, waits for them, and re-layouts  10.3 us (7%)
  other arithmetic  6.33 us (4%)
  between operations  3.53 us (3%)
    all_to_all x4, waiting for transfers between devices, exchange(): return lax.all_to_all(send, axes, split_axis=0, concat_axis=0, tiled=True)  32.9 us
    all_to_all x1, blocking collectives, exchange(): return lax.all_to_all(send, axes, split_axis=0, concat_axis=0, tiled=True)  17 us
    all_to_all x1, waiting for transfers between devices, on_device(): got3 = lax.all_to_all(send3, ALL, split_axis=1, concat_axis=1, tiled=True)  13.7 us
    all_to_all x4, starting transfers between devices, exchange(): return lax.all_to_all(send, axes, split_axis=0, concat_axis=0, tiled=True)  13.7 us
    dot_general x2, matrix products, contract_first(): lax.dot_general(operand, weights, (((0,), (0,)), ((), ())), preferred_ele...  9.51 us
    ppermute x4, starting transfers between devices, shifted(): lax.ppermute(x, axis, [(i, (i + k) % count) for i in range(count)])  8.02 us
    dot_general x2, matrix products, contract_last(): lax.dot_general(operand, weights, (((1,), (1,)), ((), ())), preferred_ele...  7.17 us
    ppermute x4, waiting for transfers between devices, shifted(): lax.ppermute(x, axis, [(i, (i + k) % count) for i in range(count)])  6.38 us
  transfers between devices with their start and end apart: 10, of which 9 were waited for; matrix products, arithmetic and copies ran while one was open for 5% of the time, Pallas kernels for 0%

profile of v5, /device:TPU:0, one launch (start us, length us, event | category | flops | bytes accessed | tf_op | source)
XLA Modules:
  0.0 140.2 jit_solution(5808627347125864719)
XLA Ops:
  0.6 1.2 dynamic_slice.15
  2.5 1.0 constant_dynamic-slice_fusion.2
  3.6 4.1 %collective-permute-start.1 = (bf16[2,16,2048]{2,1,0:T(8,128)(2,1)S(1)}, bf16[2,16,2048]{2,1,0:T(8,128)(2,1)S(1)}, u32[]{:S(2)}, u32[]{:S(2)}) collective-permute-start(bf16[2,16,2048]{2,1,0:T(8,128)(2,1)S(1)} %get-tuple-element.23), channel_id=1, source_target_pairs={{0,2},{1,3},{2,0},{3,1},{4,6},{5,7},{6,4},{7,5},{8,10},{9,11},{10,... | collective-permute-start | bytes 393224 | tf_op jit(solution)/shard_map/ppermute | solution.py:45
  7.7 1.6 %collective-permute-start = (bf16[2,16,2048]{2,1,0:T(8,128)(2,1)S(1)}, bf16[2,16,2048]{2,1,0:T(8,128)(2,1)S(1)}, u32[]{:S(2)}, u32[]{:S(2)}) collective-permute-start(bf16[2,16,2048]{2,1,0:T(8,128)(2,1)S(1)} %get-tuple-element.23), channel_id=1, source_target_pairs={{0,1},{1,2},{2,3},{3,0},{4,5},{5,6},{6,7},{7,4},{8,9},{9,10},{10,1... | collective-permute-start | bytes 393224 | tf_op jit(solution)/shard_map/ppermute | solution.py:45
  9.3 2.2 %collective-permute-start.2 = (bf16[2,16,2048]{2,1,0:T(8,128)(2,1)S(1)}, bf16[2,16,2048]{2,1,0:T(8,128)(2,1)S(1)}, u32[]{:S(2)}, u32[]{:S(2)}) collective-permute-start(bf16[2,16,2048]{2,1,0:T(8,128)(2,1)S(1)} %get-tuple-element.23), channel_id=1, source_target_pairs={{0,3},{1,0},{2,1},{3,2},{4,7},{5,4},{6,5},{7,6},{8,11},{9,8},{10,9... | collective-permute-start | bytes 393224 | tf_op jit(solution)/shard_map/ppermute | solution.py:45
  11.5 0.8 dynamic_slice.18
  12.3 5.4 %collective-permute-done.1 = bf16[2,16,2048]{2,1,0:T(8,128)(2,1)S(1)} collective-permute-done((bf16[2,16,2048]{2,1,0:T(8,128)(2,1)S(1)}, bf16[2,16,2048]{2,1,0:T(8,128)(2,1)S(1)}, u32[]{:S(2)}, u32[]{:S(2)}) %collective-permute-start.1) | collective-permute-done | bytes 131104 | tf_op jit(solution)/shard_map/ppermute | solution.py:45
  17.7 0.6 collective-permute-done.2
  18.5 0.8 select_reduce_fusion.4
  19.3 0.8 select_reduce_fusion.3
  20.1 0.3 collective-permute-done.3
  20.6 0.7 gather_fusion.2
  21.4 0.7 gather_fusion.1
  22.1 0.2 fusion.9
  22.4 3.2 %fusion.20 = f32[64,1024]{1,0:T(8,128)S(1)} fusion(bf16[2048,1024]{1,0:T(8,128)(2,1)} %param.20, bf16[64,2048]{1,0:T(8,128)(2,1)S(1)} %gather_fusion.2, pred[64]{0:T(512)(128)(4,1)S(1)} %get-tuple-element.14), kind=kOutput, calls=%fused_computation.40 | convolution fusion | flops 268566528 | bytes 4718656 | tf_op jit(solution)/shard_map/dot_general | solution.py:116
  25.7 0.2 copy-done
  25.9 0.9 convolution_add_fusion
  27.1 17.0 %all_to_all.30 = f32[32,2,1280]{2,1,0:T(2,128)S(1)} all-to-all(f32[32,2,1280]{2,1,0:T(2,128)S(1)} %pad_maximum_fusion.4), channel_id=1, replica_groups=mesh['section'=4,'mp'=2,'dp'=4] {'section','mp','dp'}, dimensions={0} | all-to-all | bytes 655360 | tf_op jit(solution)/shard_map/all_to_all | solution.py:39
  44.7 0.9 broadcast_in_dim.142
  45.6 3.2 %all-to-all-start.1 = ((bf16[32,2,2048]{2,1,0:T(2,128)(2,1)}), bf16[32,2,2048]{2,1,0:T(2,128)(2,1)S(1)}, u32[]{:S(2)}, u32[]{:S(2)}) async-start(bf16[32,2,2048]{2,1,0:T(2,128)(2,1)} %bitcast.15), calls=%async_computation.1 | async-start | bytes 524288 | tf_op jit(solution)/shard_map/all_to_all | solution.py:39
  48.8 3.6 %fusion.13 = f32[64,1024]{1,0:T(8,128)S(1)} fusion(bf16[1024,2048]{1,0:T(8,128)(2,1)} %param.19, f32[2048]{0:T(1024)S(1)} %copy-done.1, f32[64]{0:T(128)S(1)} %add_rsqrt_fusion.1, bf16[64,2048]{1,0:T(8,128)(2,1)S(1)} %gather_fusion.1, pred[64]{0:T(512)(128)(4,1)S(1)} %get-tuple-element.14), kind=kOutput, calls=%fused_computation.26 | convolution fusion | flops 269090816 | bytes 4727104 | tf_op jit(solution)/shard_map/dot_general | solution.py:18
  52.7 6.3 %all-to-all-done.1 = bf16[32,2,2048]{2,1,0:T(2,128)(2,1)S(1)} async-done(((bf16[32,2,2048]{2,1,0:T(2,128)(2,1)}), bf16[32,2,2048]{2,1,0:T(2,128)(2,1)S(1)}, u32[]{:S(2)}, u32[]{:S(2)}) %all-to-all-start.1) | async-done | bytes 262176 | tf_op jit(solution)/shard_map/all_to_all | solution.py:39
  59.0 3.6 %fusion.4 = f32[1,32,2,1024]{3,1,2,0:T(8,128)S(1)} fusion(bf16[1024,2048]{1,0:T(8,128)(2,1)} %param.19, bf16[32,2,2048]{2,1,0:T(2,128)(2,1)S(1)} %all-to-all-done.1), kind=kOutput, calls=%fused_computation.7 | convolution fusion | flops 268435456 | bytes 4718592 | tf_op jit(solution)/shard_map/dot_general | solution.py:18
  62.7 1.2 copy.53
  63.9 2.7 %all-to-all-start.2 = ((f32[2,32,2,1024]{3,2,0,1:T(2,128)}), f32[2,32,2,1024]{3,2,0,1:T(2,128)S(1)}, u32[]{:S(2)}, u32[]{:S(2)}) async-start(f32[2,32,2,1024]{3,2,0,1:T(2,128)} %copy.53), calls=%async_computation.2 | async-start | bytes 1048576 | tf_op jit(solution)/shard_map/all_to_all | solution.py:158
  66.6 0.2 select_reduce_fusion.6
  66.9 0.2 fusion.36
  67.0 13.7 %all-to-all-done.2 = f32[2,32,2,1024]{3,2,0,1:T(2,128)S(1)} async-done(((f32[2,32,2,1024]{3,2,0,1:T(2,128)}), f32[2,32,2,1024]{3,2,0,1:T(2,128)S(1)}, u32[]{:S(2)}, u32[]{:S(2)}) %all-to-all-start.2) | async-done | bytes 524320 | tf_op jit(solution)/shard_map/all_to_all | solution.py:158
  80.8 0.3 reduce_sum.197
  81.5 0.7 broadcast_in_dim.148
  82.2 4.2 %all-to-all-start.3 = ((bf16[32,2,1024]{2,1,0:T(2,128)(2,1)}), bf16[32,2,1024]{2,1,0:T(2,128)(2,1)S(1)}, u32[]{:S(2)}, u32[]{:S(2)}) async-start(bf16[32,2,1024]{2,1,0:T(2,128)(2,1)} %bitcast.24), calls=%async_computation.3 | async-start | bytes 262144 | tf_op jit(solution)/shard_map/all_to_all | solution.py:39
  86.6 8.2 %all-to-all-done.3 = bf16[32,2,1024]{2,1,0:T(2,128)(2,1)S(1)} async-done(((bf16[32,2,1024]{2,1,0:T(2,128)(2,1)}), bf16[32,2,1024]{2,1,0:T(2,128)(2,1)S(1)}, u32[]{:S(2)}, u32[]{:S(2)}) %all-to-all-start.3) | async-done | bytes 131104 | tf_op jit(solution)/shard_map/all_to_all | solution.py:39
  94.8 3.2 %fusion = f32[4,2,4,2,2048]{4,2,3,1,0:T(4,128)S(1)} fusion(bf16[1024,2048]{1,0:T(8,128)(2,1)} %param.19, bf16[4,2,4,2,1024]{4,3,2,1,0:T(2,128)(2,1)S(1)} %bitcast.140), kind=kOutput, calls=%fused_computation.3 | convolution fusion | flops 268435456 | bytes 4849664 | tf_op jit(solution)/shard_map/dot_general | solution.py:191
  98.0 0.2 copy.79
  98.2 0.2 copy.78
  98.4 0.3 fusion.12
  98.9 1.5 %collective-permute-done.4 = f32[4,4,2,2176]{3,2,1,0:T(2,128)S(1)} collective-permute-done((f32[4,4,2,2176]{3,2,1,0:T(2,128)S(1)}, f32[4,4,2,2176]{3,2,1,0:T(2,128)S(1)}, u32[]{:S(2)}, u32[]{:S(2)}) %collective-permute-start.4) | collective-permute-done | bytes 278560 | tf_op jit(solution)/shard_map/ppermute | solution.py:203
  100.4 0.4 fusion.8
  100.8 0.6 gather_fusion
  101.5 0.8 pad_maximum_fusion.5
  102.4 3.5 %all-to-all-start.4 = ((f32[16,2,2176]{2,1,0:T(2,128)}), f32[16,2,2176]{2,1,0:T(2,128)S(1)}, u32[]{:S(2)}, u32[]{:S(2)}) async-start(f32[16,2,2176]{2,1,0:T(2,128)} %bitcast.37), calls=%async_computation.4 | async-start | bytes 557056 | tf_op jit(solution)/shard_map/all_to_all | solution.py:39
  105.9 11.4 %all-to-all-done.4 = f32[16,2,2176]{2,1,0:T(2,128)S(1)} async-done(((f32[16,2,2176]{2,1,0:T(2,128)}), f32[16,2,2176]{2,1,0:T(2,128)S(1)}, u32[]{:S(2)}, u32[]{:S(2)}) %all-to-all-start.4) | async-done | bytes 278560 | tf_op jit(solution)/shard_map/all_to_all | solution.py:39
  117.8 0.7 broadcast_in_dim.154
  118.5 2.8 %all-to-all-start.5 = ((bf16[32,2,1024]{2,1,0:T(2,128)(2,1)}), bf16[32,2,1024]{2,1,0:T(2,128)(2,1)S(1)}, u32[]{:S(2)}, u32[]{:S(2)}) async-start(bf16[32,2,1024]{2,1,0:T(2,128)(2,1)} %bitcast.44), calls=%async_computation.5 | async-start | bytes 262144 | tf_op jit(solution)/shard_map/all_to_all | solution.py:39
  121.3 0.6 slice_reduce_fusion.2
  122.5 6.9 %all-to-all-done.5 = bf16[32,2,1024]{2,1,0:T(2,128)(2,1)S(1)} async-done(((bf16[32,2,1024]{2,1,0:T(2,128)(2,1)}), bf16[32,2,1024]{2,1,0:T(2,128)(2,1)S(1)}, u32[]{:S(2)}, u32[]{:S(2)}) %all-to-all-start.5) | async-done | bytes 131104 | tf_op jit(solution)/shard_map/all_to_all | solution.py:39
  129.5 4.8 %fusion.56 = f32[2048,1024]{1,0:T(8,128)} fusion(bf16[64,1024]{1,0:T(8,128)(2,1)S(1)} %reshape.407, bf16[64,2048]{1,0:T(8,128)(2,1)S(1)} %gather_fusion.1, pred[64]{0:T(512)(128)(4,1)S(1)} %get-tuple-element.14), kind=kOutput, calls=%fused_computation.144 | convolution fusion | flops 268566528 | bytes 8781888 | tf_op jit(solution)/shard_map/dot_general | solution.py:24
  134.3 4.8 %fusion.19 = f32[2048,1024]{1,0:T(8,128)} fusion(bf16[64,1024]{1,0:T(8,128)(2,1)S(1)} %reshape.407, bf16[64,2048]{1,0:T(8,128)(2,1)S(1)} %gather_fusion.2, pred[64]{0:T(512)(128)(4,1)S(1)} %get-tuple-element.14), kind=kOutput, calls=%fused_computation.39 | convolution fusion | flops 268566528 | bytes 8781888 | tf_op jit(solution)/shard_map/dot_general | solution.py:24
  (65 shorter events, 3.1 us)
Async XLA Ops:
  3.6 14.1 %collective-permute-start.1 = (bf16[2,16,2048]{2,1,0:T(8,128)(2,1)S(1)}, bf16[2,16,2048]{2,1,0:T(8,128)(2,1)S(1)}, u32[]{:S(2)}, u32[]{:S(2)}) collective-permute-start(bf16[2,16,2048]{2,1,0:T(8,128)(2,1)S(1)} %get-tuple-element.23), channel_id=1, source_target_pairs={{0,2},{1,3},{2,0},{3,1},{4,6},{5,7},{6,4},{7,5},{8,10},{9,11},{10,... | collective-permute-start | bytes 393224 | tf_op jit(solution)/shard_map/ppermute | solution.py:45
  7.7 10.0 %collective-permute-start = (bf16[2,16,2048]{2,1,0:T(8,128)(2,1)S(1)}, bf16[2,16,2048]{2,1,0:T(8,128)(2,1)S(1)}, u32[]{:S(2)}, u32[]{:S(2)}) collective-permute-start(bf16[2,16,2048]{2,1,0:T(8,128)(2,1)S(1)} %get-tuple-element.23), channel_id=1, source_target_pairs={{0,1},{1,2},{2,3},{3,0},{4,5},{5,6},{6,7},{7,4},{8,9},{9,10},{10,1... | collective-permute-start | bytes 393224 | tf_op jit(solution)/shard_map/ppermute | solution.py:45
  9.3 9.1 %collective-permute-start.2 = (bf16[2,16,2048]{2,1,0:T(8,128)(2,1)S(1)}, bf16[2,16,2048]{2,1,0:T(8,128)(2,1)S(1)}, u32[]{:S(2)}, u32[]{:S(2)}) collective-permute-start(bf16[2,16,2048]{2,1,0:T(8,128)(2,1)S(1)} %get-tuple-element.23), channel_id=1, source_target_pairs={{0,3},{1,0},{2,1},{3,2},{4,7},{5,4},{6,5},{7,6},{8,11},{9,8},{10,9... | collective-permute-start | bytes 393224 | tf_op jit(solution)/shard_map/ppermute | solution.py:45
  18.4 2.0 %collective-permute-start.3 = (bf16[4,2,16,2048]{3,2,1,0:T(8,128)(2,1)S(1)}, bf16[4,2,16,2048]{3,2,1,0:T(8,128)(2,1)S(1)}, u32[]{:S(2)}, u32[]{:S(2)}) collective-permute-start(bf16[4,2,16,2048]{3,2,1,0:T(8,128)(2,1)S(1)} %get-tuple-element.21), channel_id=1, source_target_pairs={{0,4},{4,0},{1,5},{5,1},{2,6},{6,2},{3,7},{7,3},{8,12},{12,8},{9,1... | collective-permute-start | bytes 1572872 | tf_op jit(solution)/shard_map/ppermute | solution.py:45
  22.4 3.5 %copy-start = (bf16[2048,1024]{1,0:T(8,128)(2,1)S(1)}, bf16[2048,1024]{1,0:T(8,128)(2,1)}, u32[]{:S(2)}) copy-start(bf16[2048,1024]{1,0:T(8,128)(2,1)} %param.21) | copy-start | bytes 12582916
  25.9 22.9 %copy-start.1 = (f32[2048]{0:T(1024)S(1)}, f32[2048]{0:T(1024)}, u32[]{:S(2)}) copy-start(f32[2048]{0:T(1024)} %param.17) | copy-start | bytes 24580
  45.6 13.4 %all-to-all-start.1 = ((bf16[32,2,2048]{2,1,0:T(2,128)(2,1)}), bf16[32,2,2048]{2,1,0:T(2,128)(2,1)S(1)}, u32[]{:S(2)}, u32[]{:S(2)}) async-start(bf16[32,2,2048]{2,1,0:T(2,128)(2,1)} %bitcast.15), calls=%async_computation.1 | async-start | bytes 524288 | tf_op jit(solution)/shard_map/all_to_all | solution.py:39
  52.6 14.0 %copy-start.2 = (s32[4,256]{1,0:T(4,128)S(1)}, s32[4,256]{1,0:T(4,128)}, u32[]{:S(2)}) copy-start(s32[4,256]{1,0:T(4,128)} %param.14) | copy-start | bytes 12292
  52.6 14.0 %copy-start.3 = (s32[4]{0:T(128)S(1)}, s32[4]{0:T(128)}, u32[]{:S(2)}) copy-start(s32[4]{0:T(128)} %param.16) | copy-start | bytes 52
  52.6 14.0 %copy-start.4 = (s32[4]{0:T(128)S(1)}, s32[4]{0:T(128)}, u32[]{:S(2)}) copy-start(s32[4]{0:T(128)} %param.15) | copy-start | bytes 52
  63.9 16.9 %all-to-all-start.2 = ((f32[2,32,2,1024]{3,2,0,1:T(2,128)}), f32[2,32,2,1024]{3,2,0,1:T(2,128)S(1)}, u32[]{:S(2)}, u32[]{:S(2)}) async-start(f32[2,32,2,1024]{3,2,0,1:T(2,128)} %copy.53), calls=%async_computation.2 | async-start | bytes 1048576 | tf_op jit(solution)/shard_map/all_to_all | solution.py:158
  82.2 12.6 %all-to-all-start.3 = ((bf16[32,2,1024]{2,1,0:T(2,128)(2,1)}), bf16[32,2,1024]{2,1,0:T(2,128)(2,1)S(1)}, u32[]{:S(2)}, u32[]{:S(2)}) async-start(bf16[32,2,1024]{2,1,0:T(2,128)(2,1)} %bitcast.24), calls=%async_computation.3 | async-start | bytes 262144 | tf_op jit(solution)/shard_map/all_to_all | solution.py:39
  98.7 1.6 %collective-permute-start.4 = (f32[4,4,2,2176]{3,2,1,0:T(2,128)S(1)}, f32[4,4,2,2176]{3,2,1,0:T(2,128)S(1)}, u32[]{:S(2)}, u32[]{:S(2)}) collective-permute-start(f32[4,4,2,2176]{3,2,1,0:T(2,128)S(1)} %get-tuple-element.27), channel_id=1, source_target_pairs={{0,4},{4,0},{1,5},{5,1},{2,6},{6,2},{3,7},{7,3},{8,12},{12,8},{9,1... | collective-permute-start | bytes 835592 | tf_op jit(solution)/shard_map/ppermute | solution.py:203
  102.4 15.0 %all-to-all-start.4 = ((f32[16,2,2176]{2,1,0:T(2,128)}), f32[16,2,2176]{2,1,0:T(2,128)S(1)}, u32[]{:S(2)}, u32[]{:S(2)}) async-start(f32[16,2,2176]{2,1,0:T(2,128)} %bitcast.37), calls=%async_computation.4 | async-start | bytes 557056 | tf_op jit(solution)/shard_map/all_to_all | solution.py:39
  118.5 11.0 %all-to-all-start.5 = ((bf16[32,2,1024]{2,1,0:T(2,128)(2,1)}), bf16[32,2,1024]{2,1,0:T(2,128)(2,1)S(1)}, u32[]{:S(2)}, u32[]{:S(2)}) async-start(bf16[32,2,1024]{2,1,0:T(2,128)(2,1)} %bitcast.44), calls=%async_computation.5 | async-start | bytes 262144 | tf_op jit(solution)/shard_map/all_to_all | solution.py:39

commit v6 on v5

--- a/solution.py
+++ b/solution.py
@@ -85,23 +85,22 @@
     earlier = jnp.arange(count_seq)[None, :] < jnp.arange(count_seq)[:, None]
     starts = jnp.sum(jnp.where(earlier, lengths[None, :], 0), axis=1)
 
-    first = jnp.minimum(offsets[my_dp] + my_mp * half, seq_len - half)
+    cap = half * count_mp
+    first = jnp.minimum(offsets[my_dp], seq_len - cap)
     mine = jnp.stack(
         [
-            lax.dynamic_slice_in_dim(embeds[0], first, half, axis=0),
-            lax.dynamic_slice_in_dim(target_hidden[0], first, half, axis=0),
+            lax.dynamic_slice_in_dim(embeds[0], first, cap, axis=0),
+            lax.dynamic_slice_in_dim(target_hidden[0], first, cap, axis=0),
         ]
     )
-    every = shifted(shifted(mine, "dp"), "mp")
-    every = every.transpose(2, 0, 1, 3, 4).reshape(2, count_mp * count_dp * half, width)
+    every = shifted(mine, "dp")
+    every = every.transpose(1, 0, 2, 3).reshape(2, count_dp * cap, width)
     packed = jnp.arange(total_rows, dtype=jnp.int32)
     seq_all, slot_all, offset_all = locate(packed, starts, lengths, offsets)
-    shift_mp = (my_mp - slot_all // half) % count_mp
     shift_dp = (my_dp - seq_all) % count_dp
-    base = offset_all + (slot_all // half) * half
-    lag = base - jnp.minimum(base, seq_len - half)
-    within = jnp.minimum(slot_all % half + lag, half - 1)
-    pick = (shift_mp * count_dp + shift_dp) * half + within
+    lag = offset_all - jnp.minimum(offset_all, seq_len - cap)
+    within = jnp.minimum(slot_all + lag, cap - 1)
+    pick = shift_dp * cap + within
     embed_all = jnp.take(every[0], pick, axis=0)
     feature_all = jnp.take(every[1], pick, axis=0)
     my_rows = me * per_dev + jnp.arange(per_dev, dtype=jnp.int32)

time: 141 us -> 150 us (1.064)
  waiting for transfers between devices: 54.5 us -> 61.1 us
  blocking collectives: 17 us -> 19.8 us
    ppermute x4 -> x3, waiting for transfers between devices: 6.38 us -> 13 us  [shifted(): lax.ppermute(x, axis, [(i, (i + k) % count) for i in range(count)])]
    all_to_all x1, blocking collectives: 17 us -> 19.8 us  [exchange(): return lax.all_to_all(send, axes, split_axis=0, concat_axis=0, tiled=True)]
    ppermute x4 -> x3, starting transfers between devices: 8.02 us -> 7.95 us  [shifted(): lax.ppermute(x, axis, [(i, (i + k) % count) for i in range(count)])]
  transfers between devices with their start and end apart: 10 -> 9, of which waited for: 9 -> 8; matrix products, arithmetic and copies ran while one was open for 5% -> 5% of each run, Pallas kernels for 0% -> 0%
where the time goes in v6:
time: 150 us; the launch traced here: 149 us
  waiting for transfers between devices  61.1 us (41%)
  starting transfers between devices  24.4 us (16%)
  matrix products  24 us (16%)
  blocking collectives  19.8 us (13%)
  local copies, waits for them, and re-layouts  10.4 us (7%)
  other arithmetic  6.28 us (4%)
  between operations  3.52 us (2%)
    all_to_all x4, waiting for transfers between devices, exchange(): return lax.all_to_all(send, axes, split_axis=0, concat_axis=0, tiled=True)  32.9 us
    all_to_all x1, blocking collectives, exchange(): return lax.all_to_all(send, axes, split_axis=0, concat_axis=0, tiled=True)  19.8 us
    all_to_all x1, waiting for transfers between devices, on_device(): got3 = lax.all_to_all(send3, ALL, split_axis=1, concat_axis=1, tiled=True)  13.7 us
    all_to_all x4, starting transfers between devices, exchange(): return lax.all_to_all(send, axes, split_axis=0, concat_axis=0, tiled=True)  13.7 us
    ppermute x3, waiting for transfers between devices, shifted(): lax.ppermute(x, axis, [(i, (i + k) % count) for i in range(count)])  13 us
    dot_general x2, matrix products, contract_first(): lax.dot_general(operand, weights, (((0,), (0,)), ((), ())), preferred_ele...  9.52 us
    ppermute x3, starting transfers between devices, shifted(): lax.ppermute(x, axis, [(i, (i + k) % count) for i in range(count)])  7.95 us
    dot_general x2, matrix products, contract_last(): lax.dot_general(operand, weights, (((1,), (1,)), ((), ())), preferred_ele...  7.17 us
  transfers between devices with their start and end apart: 9, of which 8 were waited for; matrix products, arithmetic and copies ran while one was open for 5% of the time, Pallas kernels for 0%

profile of v6, /device:TPU:0, one launch (start us, length us, event | category | flops | bytes accessed | tf_op | source)
XLA Modules:
  0.0 149.5 jit_solution(11413508618568650195)
XLA Ops:
  0.6 1.2 dynamic_slice.15
  2.5 1.1 constant_dynamic-slice_fusion.2
  3.7 4.1 %collective-permute-start.1 = (bf16[2,32,2048]{2,1,0:T(8,128)(2,1)S(1)}, bf16[2,32,2048]{2,1,0:T(8,128)(2,1)S(1)}, u32[]{:S(2)}, u32[]{:S(2)}) collective-permute-start(bf16[2,32,2048]{2,1,0:T(8,128)(2,1)S(1)} %get-tuple-element.21), channel_id=1, source_target_pairs={{0,2},{1,3},{2,0},{3,1},{4,6},{5,7},{6,4},{7,5},{8,10},{9,11},{10,... | collective-permute-start | bytes 786440 | tf_op jit(solution)/shard_map/ppermute | solution.py:45
  7.8 1.5 %collective-permute-start = (bf16[2,32,2048]{2,1,0:T(8,128)(2,1)S(1)}, bf16[2,32,2048]{2,1,0:T(8,128)(2,1)S(1)}, u32[]{:S(2)}, u32[]{:S(2)}) collective-permute-start(bf16[2,32,2048]{2,1,0:T(8,128)(2,1)S(1)} %get-tuple-element.21), channel_id=1, source_target_pairs={{0,1},{1,2},{2,3},{3,0},{4,5},{5,6},{6,7},{7,4},{8,9},{9,10},{10,1... | collective-permute-start | bytes 786440 | tf_op jit(solution)/shard_map/ppermute | solution.py:45
  9.3 2.3 %collective-permute-start.2 = (bf16[2,32,2048]{2,1,0:T(8,128)(2,1)S(1)}, bf16[2,32,2048]{2,1,0:T(8,128)(2,1)S(1)}, u32[]{:S(2)}, u32[]{:S(2)}) collective-permute-start(bf16[2,32,2048]{2,1,0:T(8,128)(2,1)S(1)} %get-tuple-element.21), channel_id=1, source_target_pairs={{0,3},{1,0},{2,1},{3,2},{4,7},{5,4},{6,5},{7,6},{8,11},{9,8},{10,9... | collective-permute-start | bytes 786440 | tf_op jit(solution)/shard_map/ppermute | solution.py:45
  11.6 0.8 select_reduce_fusion.4
  12.4 0.8 select_reduce_fusion.1
  13.1 0.8 dynamic_slice.18
  13.9 12.3 %collective-permute-done.1 = bf16[2,32,2048]{2,1,0:T(8,128)(2,1)S(1)} collective-permute-done((bf16[2,32,2048]{2,1,0:T(8,128)(2,1)S(1)}, bf16[2,32,2048]{2,1,0:T(8,128)(2,1)S(1)}, u32[]{:S(2)}, u32[]{:S(2)}) %collective-permute-start.1) | collective-permute-done | bytes 262176 | tf_op jit(solution)/shard_map/ppermute | solution.py:45
  26.2 0.7 collective-permute-done.2
  27.1 0.7 gather_fusion.2
  27.9 0.7 gather_fusion.1
  28.6 0.2 fusion.9
  29.0 3.2 %fusion.20 = f32[64,1024]{1,0:T(8,128)S(1)} fusion(bf16[2048,1024]{1,0:T(8,128)(2,1)} %param.20, bf16[64,2048]{1,0:T(8,128)(2,1)S(1)} %gather_fusion.2, pred[64]{0:T(512)(128)(4,1)S(1)} %get-tuple-element.14), kind=kOutput, calls=%fused_computation.39 | convolution fusion | flops 268566528 | bytes 4718656 | tf_op jit(solution)/shard_map/dot_general | solution.py:115
  32.2 0.2 copy-done
  32.4 0.9 convolution_add_fusion
  33.7 19.8 %all_to_all.30 = f32[32,2,1280]{2,1,0:T(2,128)S(1)} all-to-all(f32[32,2,1280]{2,1,0:T(2,128)S(1)} %pad_maximum_fusion.3), channel_id=1, replica_groups=mesh['section'=4,'mp'=2,'dp'=4] {'section','mp','dp'}, dimensions={0} | all-to-all | bytes 655360 | tf_op jit(solution)/shard_map/all_to_all | solution.py:39
  54.0 0.9 broadcast_in_dim.142
  54.9 3.2 %all-to-all-start.1 = ((bf16[32,2,2048]{2,1,0:T(2,128)(2,1)}), bf16[32,2,2048]{2,1,0:T(2,128)(2,1)S(1)}, u32[]{:S(2)}, u32[]{:S(2)}) async-start(bf16[32,2,2048]{2,1,0:T(2,128)(2,1)} %bitcast.13), calls=%async_computation.1 | async-start | bytes 524288 | tf_op jit(solution)/shard_map/all_to_all | solution.py:39
  58.1 3.6 %fusion.13 = f32[64,1024]{1,0:T(8,128)S(1)} fusion(bf16[1024,2048]{1,0:T(8,128)(2,1)} %param.19, f32[2048]{0:T(1024)S(1)} %copy-done.1, f32[64]{0:T(128)S(1)} %add_rsqrt_fusion.1, bf16[64,2048]{1,0:T(8,128)(2,1)S(1)} %gather_fusion.1, pred[64]{0:T(512)(128)(4,1)S(1)} %get-tuple-element.14), kind=kOutput, calls=%fused_computation.25 | convolution fusion | flops 269090816 | bytes 4727104 | tf_op jit(solution)/shard_map/dot_general | solution.py:18
  62.0 6.3 %all-to-all-done.1 = bf16[32,2,2048]{2,1,0:T(2,128)(2,1)S(1)} async-done(((bf16[32,2,2048]{2,1,0:T(2,128)(2,1)}), bf16[32,2,2048]{2,1,0:T(2,128)(2,1)S(1)}, u32[]{:S(2)}, u32[]{:S(2)}) %all-to-all-start.1) | async-done | bytes 262176 | tf_op jit(solution)/shard_map/all_to_all | solution.py:39
  68.4 3.6 %fusion.4 = f32[1,32,2,1024]{3,1,2,0:T(8,128)S(1)} fusion(bf16[1024,2048]{1,0:T(8,128)(2,1)} %param.19, bf16[32,2,2048]{2,1,0:T(2,128)(2,1)S(1)} %all-to-all-done.1), kind=kOutput, calls=%fused_computation.7 | convolution fusion | flops 268435456 | bytes 4718592 | tf_op jit(solution)/shard_map/dot_general | solution.py:18
  72.0 1.2 copy.53
  73.2 2.7 %all-to-all-start.2 = ((f32[2,32,2,1024]{3,2,0,1:T(2,128)}), f32[2,32,2,1024]{3,2,0,1:T(2,128)S(1)}, u32[]{:S(2)}, u32[]{:S(2)}) async-start(f32[2,32,2,1024]{3,2,0,1:T(2,128)} %copy.53), calls=%async_computation.2 | async-start | bytes 1048576 | tf_op jit(solution)/shard_map/all_to_all | solution.py:157
  75.9 0.2 select_reduce_fusion.6
  76.2 0.2 fusion.36
  76.3 13.7 %all-to-all-done.2 = f32[2,32,2,1024]{3,2,0,1:T(2,128)S(1)} async-done(((f32[2,32,2,1024]{3,2,0,1:T(2,128)}), f32[2,32,2,1024]{3,2,0,1:T(2,128)S(1)}, u32[]{:S(2)}, u32[]{:S(2)}) %all-to-all-start.2) | async-done | bytes 524320 | tf_op jit(solution)/shard_map/all_to_all | solution.py:157
  90.1 0.3 reduce_sum.197
  90.8 0.7 broadcast_in_dim.148
  91.5 4.2 %all-to-all-start.3 = ((bf16[32,2,1024]{2,1,0:T(2,128)(2,1)}), bf16[32,2,1024]{2,1,0:T(2,128)(2,1)S(1)}, u32[]{:S(2)}, u32[]{:S(2)}) async-start(bf16[32,2,1024]{2,1,0:T(2,128)(2,1)} %bitcast.22), calls=%async_computation.3 | async-start | bytes 262144 | tf_op jit(solution)/shard_map/all_to_all | solution.py:39
  95.9 8.2 %all-to-all-done.3 = bf16[32,2,1024]{2,1,0:T(2,128)(2,1)S(1)} async-done(((bf16[32,2,1024]{2,1,0:T(2,128)(2,1)}), bf16[32,2,1024]{2,1,0:T(2,128)(2,1)S(1)}, u32[]{:S(2)}, u32[]{:S(2)}) %all-to-all-start.3) | async-done | bytes 131104 | tf_op jit(solution)/shard_map/all_to_all | solution.py:39
  104.1 3.2 %fusion = f32[4,2,4,2,2048]{4,2,3,1,0:T(4,128)S(1)} fusion(bf16[1024,2048]{1,0:T(8,128)(2,1)} %param.19, bf16[4,2,4,2,1024]{4,3,2,1,0:T(2,128)(2,1)S(1)} %bitcast.137), kind=kOutput, calls=%fused_computation.3 | convolution fusion | flops 268435456 | bytes 4849664 | tf_op jit(solution)/shard_map/dot_general | solution.py:190
  107.3 0.2 copy.79
  107.5 0.2 copy.78
  107.8 0.3 fusion.12
  108.2 1.5 %collective-permute-done.3 = f32[4,4,2,2176]{3,2,1,0:T(2,128)S(1)} collective-permute-done((f32[4,4,2,2176]{3,2,1,0:T(2,128)S(1)}, f32[4,4,2,2176]{3,2,1,0:T(2,128)S(1)}, u32[]{:S(2)}, u32[]{:S(2)}) %collective-permute-start.3) | collective-permute-done | bytes 278560 | tf_op jit(solution)/shard_map/ppermute | solution.py:202
  109.7 0.4 fusion.8
  110.1 0.6 gather_fusion
  110.9 0.8 pad_maximum_fusion.4
  111.7 3.5 %all-to-all-start.4 = ((f32[16,2,2176]{2,1,0:T(2,128)}), f32[16,2,2176]{2,1,0:T(2,128)S(1)}, u32[]{:S(2)}, u32[]{:S(2)}) async-start(f32[16,2,2176]{2,1,0:T(2,128)} %bitcast.35), calls=%async_computation.4 | async-start | bytes 557056 | tf_op jit(solution)/shard_map/all_to_all | solution.py:39
  115.3 11.4 %all-to-all-done.4 = f32[16,2,2176]{2,1,0:T(2,128)S(1)} async-done(((f32[16,2,2176]{2,1,0:T(2,128)}), f32[16,2,2176]{2,1,0:T(2,128)S(1)}, u32[]{:S(2)}, u32[]{:S(2)}) %all-to-all-start.4) | async-done | bytes 278560 | tf_op jit(solution)/shard_map/all_to_all | solution.py:39
  126.8 0.2 fusion.31
  127.1 0.7 broadcast_in_dim.154
  127.8 2.8 %all-to-all-start.5 = ((bf16[32,2,1024]{2,1,0:T(2,128)(2,1)}), bf16[32,2,1024]{2,1,0:T(2,128)(2,1)S(1)}, u32[]{:S(2)}, u32[]{:S(2)}) async-start(bf16[32,2,1024]{2,1,0:T(2,128)(2,1)} %bitcast.42), calls=%async_computation.5 | async-start | bytes 262144 | tf_op jit(solution)/shard_map/all_to_all | solution.py:39
  130.6 0.6 slice_reduce_fusion.2
  131.9 6.9 %all-to-all-done.5 = bf16[32,2,1024]{2,1,0:T(2,128)(2,1)S(1)} async-done(((bf16[32,2,1024]{2,1,0:T(2,128)(2,1)}), bf16[32,2,1024]{2,1,0:T(2,128)(2,1)S(1)}, u32[]{:S(2)}, u32[]{:S(2)}) %all-to-all-start.5) | async-done | bytes 131104 | tf_op jit(solution)/shard_map/all_to_all | solution.py:39
  138.8 4.8 %fusion.55 = f32[2048,1024]{1,0:T(8,128)} fusion(bf16[64,1024]{1,0:T(8,128)(2,1)S(1)} %reshape.409, bf16[64,2048]{1,0:T(8,128)(2,1)S(1)} %gather_fusion.1, pred[64]{0:T(512)(128)(4,1)S(1)} %get-tuple-element.14), kind=kOutput, calls=%fused_computation.134 | convolution fusion | flops 268566528 | bytes 8781888 | tf_op jit(solution)/shard_map/dot_general | solution.py:24
  143.6 4.8 %fusion.19 = f32[2048,1024]{1,0:T(8,128)} fusion(bf16[64,1024]{1,0:T(8,128)(2,1)S(1)} %reshape.409, bf16[64,2048]{1,0:T(8,128)(2,1)S(1)} %gather_fusion.2, pred[64]{0:T(512)(128)(4,1)S(1)} %get-tuple-element.14), kind=kOutput, calls=%fused_computation.38 | convolution fusion | flops 268566528 | bytes 8781888 | tf_op jit(solution)/shard_map/dot_general | solution.py:24
  (62 shorter events, 2.8 us)
Async XLA Ops:
  3.7 22.6 %collective-permute-start.1 = (bf16[2,32,2048]{2,1,0:T(8,128)(2,1)S(1)}, bf16[2,32,2048]{2,1,0:T(8,128)(2,1)S(1)}, u32[]{:S(2)}, u32[]{:S(2)}) collective-permute-start(bf16[2,32,2048]{2,1,0:T(8,128)(2,1)S(1)} %get-tuple-element.21), channel_id=1, source_target_pairs={{0,2},{1,3},{2,0},{3,1},{4,6},{5,7},{6,4},{7,5},{8,10},{9,11},{10,... | collective-permute-start | bytes 786440 | tf_op jit(solution)/shard_map/ppermute | solution.py:45
  7.8 18.4 %collective-permute-start = (bf16[2,32,2048]{2,1,0:T(8,128)(2,1)S(1)}, bf16[2,32,2048]{2,1,0:T(8,128)(2,1)S(1)}, u32[]{:S(2)}, u32[]{:S(2)}) collective-permute-start(bf16[2,32,2048]{2,1,0:T(8,128)(2,1)S(1)} %get-tuple-element.21), channel_id=1, source_target_pairs={{0,1},{1,2},{2,3},{3,0},{4,5},{5,6},{6,7},{7,4},{8,9},{9,10},{10,1... | collective-permute-start | bytes 786440 | tf_op jit(solution)/shard_map/ppermute | solution.py:45
  9.3 17.6 %collective-permute-start.2 = (bf16[2,32,2048]{2,1,0:T(8,128)(2,1)S(1)}, bf16[2,32,2048]{2,1,0:T(8,128)(2,1)S(1)}, u32[]{:S(2)}, u32[]{:S(2)}) collective-permute-start(bf16[2,32,2048]{2,1,0:T(8,128)(2,1)S(1)} %get-tuple-element.21), channel_id=1, source_target_pairs={{0,3},{1,0},{2,1},{3,2},{4,7},{5,4},{6,5},{7,6},{8,11},{9,8},{10,9... | collective-permute-start | bytes 786440 | tf_op jit(solution)/shard_map/ppermute | solution.py:45
  29.0 3.5 %copy-start = (bf16[2048,1024]{1,0:T(8,128)(2,1)S(1)}, bf16[2048,1024]{1,0:T(8,128)(2,1)}, u32[]{:S(2)}) copy-start(bf16[2048,1024]{1,0:T(8,128)(2,1)} %param.21) | copy-start | bytes 12582916
  32.4 25.7 %copy-start.1 = (f32[2048]{0:T(1024)S(1)}, f32[2048]{0:T(1024)}, u32[]{:S(2)}) copy-start(f32[2048]{0:T(1024)} %param.17) | copy-start | bytes 24580
  54.9 13.4 %all-to-all-start.1 = ((bf16[32,2,2048]{2,1,0:T(2,128)(2,1)}), bf16[32,2,2048]{2,1,0:T(2,128)(2,1)S(1)}, u32[]{:S(2)}, u32[]{:S(2)}) async-start(bf16[32,2,2048]{2,1,0:T(2,128)(2,1)} %bitcast.13), calls=%async_computation.1 | async-start | bytes 524288 | tf_op jit(solution)/shard_map/all_to_all | solution.py:39
  61.9 14.0 %copy-start.2 = (s32[4,256]{1,0:T(4,128)S(1)}, s32[4,256]{1,0:T(4,128)}, u32[]{:S(2)}) copy-start(s32[4,256]{1,0:T(4,128)} %param.14) | copy-start | bytes 12292
  61.9 14.0 %copy-start.3 = (s32[4]{0:T(128)S(1)}, s32[4]{0:T(128)}, u32[]{:S(2)}) copy-start(s32[4]{0:T(128)} %param.16) | copy-start | bytes 52
  61.9 14.0 %copy-start.4 = (s32[4]{0:T(128)S(1)}, s32[4]{0:T(128)}, u32[]{:S(2)}) copy-start(s32[4]{0:T(128)} %param.15) | copy-start | bytes 52
  73.2 16.9 %all-to-all-start.2 = ((f32[2,32,2,1024]{3,2,0,1:T(2,128)}), f32[2,32,2,1024]{3,2,0,1:T(2,128)S(1)}, u32[]{:S(2)}, u32[]{:S(2)}) async-start(f32[2,32,2,1024]{3,2,0,1:T(2,128)} %copy.53), calls=%async_computation.2 | async-start | bytes 1048576 | tf_op jit(solution)/shard_map/all_to_all | solution.py:157
  91.5 12.6 %all-to-all-start.3 = ((bf16[32,2,1024]{2,1,0:T(2,128)(2,1)}), bf16[32,2,1024]{2,1,0:T(2,128)(2,1)S(1)}, u32[]{:S(2)}, u32[]{:S(2)}) async-start(bf16[32,2,1024]{2,1,0:T(2,128)(2,1)} %bitcast.22), calls=%async_computation.3 | async-start | bytes 262144 | tf_op jit(solution)/shard_map/all_to_all | solution.py:39
  108.0 1.6 %collective-permute-start.3 = (f32[4,4,2,2176]{3,2,1,0:T(2,128)S(1)}, f32[4,4,2,2176]{3,2,1,0:T(2,128)S(1)}, u32[]{:S(2)}, u32[]{:S(2)}) collective-permute-start(f32[4,4,2,2176]{3,2,1,0:T(2,128)S(1)} %get-tuple-element.25), channel_id=1, source_target_pairs={{0,4},{4,0},{1,5},{5,1},{2,6},{6,2},{3,7},{7,3},{8,12},{12,8},{9,1... | collective-permute-start | bytes 835592 | tf_op jit(solution)/shard_map/ppermute | solution.py:202
  111.7 15.0 %all-to-all-start.4 = ((f32[16,2,2176]{2,1,0:T(2,128)}), f32[16,2,2176]{2,1,0:T(2,128)S(1)}, u32[]{:S(2)}, u32[]{:S(2)}) async-start(f32[16,2,2176]{2,1,0:T(2,128)} %bitcast.35), calls=%async_computation.4 | async-start | bytes 557056 | tf_op jit(solution)/shard_map/all_to_all | solution.py:39
  127.8 11.0 %all-to-all-start.5 = ((bf16[32,2,1024]{2,1,0:T(2,128)(2,1)}), bf16[32,2,1024]{2,1,0:T(2,128)(2,1)S(1)}, u32[]{:S(2)}, u32[]{:S(2)}) async-start(bf16[32,2,1024]{2,1,0:T(2,128)(2,1)} %bitcast.42), calls=%async_computation.5 | async-start | bytes 262144 | tf_op jit(solution)/shard_map/all_to_all | solution.py:39

commit v7 on v4

--- a/solution.py
+++ b/solution.py
@@ -46,6 +46,26 @@
         for k in range(1, count)
     ]
     return jnp.stack(parts)
+
+
+def section_sum(x):
+    count = lax.axis_size("section")
+    if count & (count - 1):
+        mine = lax.axis_index("section")
+        parts = jnp.stack(
+            [x]
+            + [
+                lax.ppermute(x, "section", [(i, (i + k) % count) for i in range(count)])
+                for k in range(1, count)
+            ]
+        )
+        return jnp.sum(jnp.take(parts, (mine - jnp.arange(count)) % count, axis=0), axis=0)
+    parts = [x] + [
+        lax.ppermute(x, "section", [(i, i ^ k) for i in range(count)]) for k in range(1, count)
+    ]
+    while len(parts) > 1:
+        parts = [parts[i] + parts[i + 1] for i in range(0, len(parts), 2)]
+    return parts[0]
 
 
 def pad_cols(count):
@@ -104,11 +124,9 @@
     pick = (shift_mp * count_dp + shift_dp) * half + within
     embed_all = jnp.take(every[0], pick, axis=0)
     feature_all = jnp.take(every[1], pick, axis=0)
-    my_rows = me * per_dev + jnp.arange(per_dev, dtype=jnp.int32)
-    my_seq, my_slot, my_offset = locate(my_rows, starts, lengths, offsets)
-    flat = my_seq * seq_len + my_offset + my_slot
+    flat = seq_all * seq_len + offset_all + slot_all
     ids = token_ids.reshape(-1)
-    labels = jnp.sum(
+    labels_all = jnp.sum(
         jnp.where(jnp.arange(ids.shape[0], dtype=jnp.int32)[None, :] == flat[:, None], ids, 0),
         axis=1,
     )
@@ -152,20 +170,25 @@
     ).reshape(n_dev, per_dev, width)
     draft_norm_all = exchange(send2, ALL).reshape(total_rows, width)
 
-    target_part = contract_last(target_norm, head)
-    draft_part = contract_last(draft_norm_all, head)
-    send3 = jnp.stack([target_part, draft_part]).reshape(2, n_dev, per_dev, vocab_tile)
-    got3 = lax.all_to_all(send3, ALL, split_axis=1, concat_axis=1, tiled=True)
-    got3 = got3.reshape(2, count_sec, groups, per_dev, vocab_tile)
-    logits = jnp.sum(got3, axis=1).transpose(0, 2, 1, 3).reshape(2, per_dev, groups * vocab_tile)
-    target_logit, draft_logit = logits[0], logits[1]
-    vocab = groups * vocab_tile
-    is_label = labels[:, None] == jnp.arange(vocab, dtype=jnp.int32)[None, :]
+    target_logit = section_sum(contract_last(target_norm, head))
+    draft_logit = section_sum(contract_last(draft_norm_all, head))
+    column_zero = (my_mp * count_dp + my_dp) * vocab_tile
+    is_label = (
+        labels_all[:, None] - column_zero == jnp.arange(vocab_tile, dtype=jnp.int32)[None, :]
+    )
     target_exp = jnp.exp(target_logit)
-    target_total = jnp.sum(target_exp, axis=1)
-    cross_total = jnp.sum(target_exp * draft_logit, axis=1)
-    draft_total = jnp.sum(jnp.exp(draft_logit), axis=1)
-    label_logit = jnp.sum(jnp.where(is_label, draft_logit, 0.0), axis=1)
+    sums = jnp.stack(
+        [
+            jnp.sum(target_exp, axis=1),
+            jnp.sum(target_exp * draft_logit, axis=1),
+            jnp.sum(jnp.exp(draft_logit), axis=1),
+            jnp.sum(jnp.where(is_label, draft_logit, 0.0), axis=1),
+        ]
+    )
+    sums = jnp.sum(
+        exchange(jnp.broadcast_to(sums[None], (groups,) + sums.shape), ("mp", "dp")), axis=0
+    )
+    target_total, cross_total, draft_total, label_logit = sums[0], sums[1], sums[2], sums[3]
     draft_lse = jnp.log(draft_total)
     target_lse = jnp.log(target_total)
     row_loss = (
@@ -174,7 +197,8 @@
         - label_mix * label_logit
         + z_weight * draft_lse * draft_lse
     )
-    logit_grad = (
+    loss = jnp.mean(row_loss)
+    grad_tile = (
         (
             (1.0 + 2.0 * z_weight * draft_lse)[:, None] * jnp.exp(draft_logit - draft_lse[:, None])
             - (1.0 - label_mix) * jnp.exp(target_logit - target_lse[:, None])
@@ -182,26 +206,18 @@
         )
     ).astype(jnp.bfloat16)
 
-    send4 = jnp.broadcast_to(
-        logit_grad.reshape(per_dev, 1, groups, vocab_tile).transpose(1, 2, 0, 3),
-        (count_sec, groups, per_dev, vocab_tile),
-    ).reshape(n_dev, per_dev, vocab_tile)
-    grad_tile = exchange(send4, ALL).reshape(total_rows, vocab_tile)
-
     grad_part = jnp.dot(grad_tile, head, preferred_element_type=jnp.float32)
-    loss_cols = jnp.pad(row_loss[:, None], ((0, 0), (0, 127)))
-    send5 = jnp.concatenate(
-        [
-            grad_part.reshape(n_dev, per_dev, width),
-            jnp.broadcast_to(loss_cols[None], (n_dev,) + loss_cols.shape),
-        ],
-        axis=2,
-    )
-    got5 = exchange(send5, ALL).reshape(count_sec, groups, per_dev, -1)
-    draft_grad = (
-        jnp.sum(got5[..., :width], axis=1).transpose(1, 0, 2).reshape(per_dev, full_width)
-    )
-    loss = jnp.mean(got5[..., width].reshape(total_rows))
+    by_mp = grad_part.reshape(count_sec, count_mp, count_dp, per_dev, width).transpose(1, 0, 2, 3, 4)
+    reduced = lax.dynamic_index_in_dim(by_mp, my_mp, 0, keepdims=False)
+    for k in range(1, count_mp):
+        reduced = reduced + lax.ppermute(
+            lax.dynamic_index_in_dim(by_mp, (my_mp + k) % count_mp, 0, keepdims=False),
+            "mp",
+            [(i, (i + k) % count_mp) for i in range(count_mp)],
+        )
+    send5 = reduced.reshape(count_sec * count_dp, per_dev, width)
+    got5 = exchange(send5, ("section", "dp")).reshape(count_sec, count_dp, per_dev, width)
+    draft_grad = jnp.sum(got5, axis=1).transpose(1, 0, 2).reshape(per_dev, full_width)
     upstream = draft_grad * gain_full
     inner_sum = jnp.sum(hidden * upstream, axis=1)
     hidden_grad = (

time: 142 us -> 137 us (0.965)
  blocking collectives: 17 us -> 0 us
  starting transfers between devices: 25.1 us -> 34.9 us
  waiting for transfers between devices: 56.5 us -> 59.5 us
  local copies, waits for them, and re-layouts: 10.3 us -> 8.62 us
    all_to_all x1 -> x0, blocking collectives: 17 us -> none  [exchange(): return lax.all_to_all(send, axes, split_axis=0, concat_axis=0, tiled=True)]
    ppermute x0 -> x7, waiting for transfers between devices: none -> 14.3 us  [the longest x6 12.8 us: section_sum(): lax.ppermute(x, 'section', [(i, i ^ k) for i in range(count)])]
    all_to_all x1 -> x0, waiting for transfers between devices: 13.7 us -> none  [on_device(): got3 = lax.all_to_all(send3, ALL, split_axis=1, concat_axis=1, tiled=True)]
    ppermute x0 -> x7, starting transfers between devices: none -> 7.29 us  [the longest x6 7.11 us: section_sum(): lax.ppermute(x, 'section', [(i, i ^ k) for i in range(count)])]
    all_to_all x4 -> x5, starting transfers between devices: 14.4 us -> 19.6 us  [exchange(): return lax.all_to_all(send, axes, split_axis=0, concat_axis=0, tiled=True)]
    all_to_all x1 -> x0, starting transfers between devices: 2.66 us -> none  [on_device(): got3 = lax.all_to_all(send3, ALL, split_axis=1, concat_axis=1, tiled=True)]
    all_to_all x4 -> x5, waiting for transfers between devices: 36.4 us -> 38.8 us  [exchange(): return lax.all_to_all(send, axes, split_axis=0, concat_axis=0, tiled=True)]
    another operation x3 -> x0, local copies, waits for them, and re-layouts: 1.44 us -> none  [on_device(): jnp.stack([target_part, draft_part]).reshape(2, n_dev, per_dev, vocab_tile)]
  transfers between devices with their start and end apart: 9 -> 16, of which waited for: 8 -> 12; matrix products, arithmetic and copies ran while one was open for 5% -> 7% of each run, Pallas kernels for 0% -> 0%
where the time goes in v7:
time: 137 us
  waiting for transfers between devices  59.5 us (43%)
  starting transfers between devices  34.9 us (25%)
  matrix products  23.9 us (17%)
  local copies, waits for them, and re-layouts  8.62 us (6%)
  other arithmetic  6.33 us (5%)
  between operations  3.37 us (2%)
    all_to_all x5, waiting for transfers between devices, exchange(): return lax.all_to_all(send, axes, split_axis=0, concat_axis=0, tiled=True)  38.8 us
    all_to_all x5, starting transfers between devices, exchange(): return lax.all_to_all(send, axes, split_axis=0, concat_axis=0, tiled=True)  19.6 us
    ppermute x6, waiting for transfers between devices, section_sum(): lax.ppermute(x, 'section', [(i, i ^ k) for i in range(count)])  12.8 us
    dot_general x2, matrix products, contract_first(): lax.dot_general(operand, weights, (((0,), (0,)), ((), ())), preferred_ele...  9.52 us
    ppermute x4, starting transfers between devices, shifted(): lax.ppermute(x, axis, [(i, (i + k) % count) for i in range(count)])  8.02 us
    dot_general x2, matrix products, contract_last(): lax.dot_general(operand, weights, (((1,), (1,)), ((), ())), preferred_ele...  7.17 us
    ppermute x6, starting transfers between devices, section_sum(): lax.ppermute(x, 'section', [(i, i ^ k) for i in range(count)])  7.11 us
    ppermute x4, waiting for transfers between devices, shifted(): lax.ppermute(x, axis, [(i, (i + k) % count) for i in range(count)])  6.49 us
  transfers between devices with their start and end apart: 16, of which 12 were waited for; matrix products, arithmetic and copies ran while one was open for 7% of the time, Pallas kernels for 0%

profile of v7, /device:TPU:0, one launch (start us, length us, event | category | flops | bytes accessed | tf_op | source)
XLA Modules:
  0.0 136.7 jit_solution(858279729016016023)
XLA Ops:
  0.6 1.2 dynamic_slice.15
  2.5 1.0 constant_dynamic-slice_fusion
  3.6 4.1 %collective-permute-start.1 = (bf16[2,16,2048]{2,1,0:T(8,128)(2,1)S(1)}, bf16[2,16,2048]{2,1,0:T(8,128)(2,1)S(1)}, u32[]{:S(2)}, u32[]{:S(2)}) collective-permute-start(bf16[2,16,2048]{2,1,0:T(8,128)(2,1)S(1)} %get-tuple-element.20), channel_id=1, source_target_pairs={{0,2},{1,3},{2,0},{3,1},{4,6},{5,7},{6,4},{7,5},{8,10},{9,11},{10,... | collective-permute-start | bytes 393224 | tf_op jit(solution)/shard_map/ppermute | solution.py:45
  7.7 1.6 %collective-permute-start = (bf16[2,16,2048]{2,1,0:T(8,128)(2,1)S(1)}, bf16[2,16,2048]{2,1,0:T(8,128)(2,1)S(1)}, u32[]{:S(2)}, u32[]{:S(2)}) collective-permute-start(bf16[2,16,2048]{2,1,0:T(8,128)(2,1)S(1)} %get-tuple-element.20), channel_id=1, source_target_pairs={{0,1},{1,2},{2,3},{3,0},{4,5},{5,6},{6,7},{7,4},{8,9},{9,10},{10,1... | collective-permute-start | bytes 393224 | tf_op jit(solution)/shard_map/ppermute | solution.py:45
  9.3 2.2 %collective-permute-start.2 = (bf16[2,16,2048]{2,1,0:T(8,128)(2,1)S(1)}, bf16[2,16,2048]{2,1,0:T(8,128)(2,1)S(1)}, u32[]{:S(2)}, u32[]{:S(2)}) collective-permute-start(bf16[2,16,2048]{2,1,0:T(8,128)(2,1)S(1)} %get-tuple-element.20), channel_id=1, source_target_pairs={{0,3},{1,0},{2,1},{3,2},{4,7},{5,4},{6,5},{7,6},{8,11},{9,8},{10,9... | collective-permute-start | bytes 393224 | tf_op jit(solution)/shard_map/ppermute | solution.py:45
  11.5 0.8 dynamic_slice.18
  12.3 5.4 %collective-permute-done.1 = bf16[2,16,2048]{2,1,0:T(8,128)(2,1)S(1)} collective-permute-done((bf16[2,16,2048]{2,1,0:T(8,128)(2,1)S(1)}, bf16[2,16,2048]{2,1,0:T(8,128)(2,1)S(1)}, u32[]{:S(2)}, u32[]{:S(2)}) %collective-permute-start.1) | collective-permute-done | bytes 131104 | tf_op jit(solution)/shard_map/ppermute | solution.py:45
  17.7 0.7 collective-permute-done.2
  18.6 0.8 select_reduce_fusion.5
  19.4 0.8 select_reduce_fusion.4
  20.2 0.3 collective-permute-done.3
  20.7 0.7 gather_fusion.1
  21.5 0.7 gather_fusion
  22.6 3.2 %fusion.16 = f32[64,1024]{1,0:T(8,128)S(1)} fusion(bf16[2048,1024]{1,0:T(8,128)(2,1)} %param.20, bf16[64,2048]{1,0:T(8,128)(2,1)S(1)} %gather_fusion.1, pred[64]{0:T(512)(128)(4,1)S(1)} %get-tuple-element.13), kind=kOutput, calls=%fused_computation.40 | convolution fusion | flops 268566528 | bytes 4718656 | tf_op jit(solution)/shard_map/dot_general | solution.py:134
  26.0 0.9 convolution_add_fusion
  27.1 0.9 pad_maximum_fusion.1
  28.0 6.1 %all-to-all-start = ((f32[32,2,1280]{2,1,0:T(2,128)}), f32[32,2,1280]{2,1,0:T(2,128)S(1)}, u32[]{:S(2)}, u32[]{:S(2)}) async-start(f32[32,2,1280]{2,1,0:T(2,128)} %pad_maximum_fusion.1), calls=%async_computation | async-start | bytes 655360 | tf_op jit(solution)/shard_map/all_to_all | solution.py:39
  34.1 11.0 %all-to-all-done = f32[32,2,1280]{2,1,0:T(2,128)S(1)} async-done(((f32[32,2,1280]{2,1,0:T(2,128)}), f32[32,2,1280]{2,1,0:T(2,128)S(1)}, u32[]{:S(2)}, u32[]{:S(2)}) %all-to-all-start) | async-done | bytes 327712 | tf_op jit(solution)/shard_map/all_to_all | solution.py:39
  45.8 0.9 broadcast_in_dim.105
  46.6 3.2 %all-to-all-start.1 = ((bf16[32,2,2048]{2,1,0:T(2,128)(2,1)}), bf16[32,2,2048]{2,1,0:T(2,128)(2,1)S(1)}, u32[]{:S(2)}, u32[]{:S(2)}) async-start(bf16[32,2,2048]{2,1,0:T(2,128)(2,1)} %bitcast.15), calls=%async_computation.1 | async-start | bytes 524288 | tf_op jit(solution)/shard_map/all_to_all | solution.py:39
  49.9 3.6 %fusion.3 = f32[64,1024]{1,0:T(8,128)S(1)} fusion(bf16[1024,2048]{1,0:T(8,128)(2,1)} %param.19, f32[2048]{0:T(1024)S(1)} %copy-done.1, f32[64]{0:T(128)S(1)} %add_rsqrt_fusion.1, bf16[64,2048]{1,0:T(8,128)(2,1)S(1)} %gather_fusion, pred[64]{0:T(512)(128)(4,1)S(1)} %get-tuple-element.13), kind=kOutput, calls=%fused_computation.11 | convolution fusion | flops 269090816 | bytes 4727104 | tf_op jit(solution)/shard_map/dot_general | solution.py:18
  53.5 2.7 %collective-permute-start.6 = (f32[64,1024]{1,0:T(8,128)S(1)}, f32[64,1024]{1,0:T(8,128)S(1)}, u32[]{:S(2)}, u32[]{:S(2)}) collective-permute-start(f32[64,1024]{1,0:T(8,128)S(1)} %fusion.3), channel_id=1, source_target_pairs={{0,24},{8,16},{16,8},{24,0},{1,25},{9,17},{17,9},{25,1},{2,26},{10... | collective-permute-start | bytes 786440 | tf_op jit(solution)/shard_map/ppermute | solution.py:64
  56.2 0.6 collective-permute-start.5
  57.0 3.3 %all-to-all-done.1 = bf16[32,2,2048]{2,1,0:T(2,128)(2,1)S(1)} async-done(((bf16[32,2,2048]{2,1,0:T(2,128)(2,1)}), bf16[32,2,2048]{2,1,0:T(2,128)(2,1)S(1)}, u32[]{:S(2)}, u32[]{:S(2)}) %all-to-all-start.1) | async-done | bytes 262176 | tf_op jit(solution)/shard_map/all_to_all | solution.py:39
  60.4 3.6 %fusion.41 = f32[64,1024]{1,0:T(8,128)S(1)} fusion(bf16[64,2048]{1,0:T(8,128)(2,1)S(1)} %reshape.191, bf16[1024,2048]{1,0:T(8,128)(2,1)} %param.19), kind=kOutput, calls=%fused_computation.110 | convolution fusion | flops 268435456 | bytes 4718592 | tf_op jit(solution)/shard_map/dot_general | solution.py:18
  64.0 0.8 collective-permute-start.9
  64.9 1.6 %collective-permute-start.8 = (f32[64,1024]{1,0:T(8,128)S(1)}, f32[64,1024]{1,0:T(8,128)S(1)}, u32[]{:S(2)}, u32[]{:S(2)}) collective-permute-start(f32[64,1024]{1,0:T(8,128)S(1)} %fusion.41), channel_id=1, source_target_pairs={{0,16},{8,24},{16,0},{24,8},{1,17},{9,25},{17,1},{25,9},{2,18},{10... | collective-permute-start | bytes 786440 | tf_op jit(solution)/shard_map/ppermute | solution.py:64
  66.4 1.1 collective-permute-start.7
  67.8 2.3 %collective-permute-done.5 = f32[64,1024]{1,0:T(8,128)S(1)} collective-permute-done((f32[64,1024]{1,0:T(8,128)S(1)}, f32[64,1024]{1,0:T(8,128)S(1)}, u32[]{:S(2)}, u32[]{:S(2)}) %collective-permute-start.5) | collective-permute-done | bytes 262176 | tf_op jit(solution)/shard_map/ppermute | solution.py:64
  70.0 5.7 %collective-permute-done.9 = f32[64,1024]{1,0:T(8,128)S(1)} collective-permute-done((f32[64,1024]{1,0:T(8,128)S(1)}, f32[64,1024]{1,0:T(8,128)S(1)}, u32[]{:S(2)}, u32[]{:S(2)}) %collective-permute-start.9) | collective-permute-done | bytes 262176 | tf_op jit(solution)/shard_map/ppermute | solution.py:64
  75.8 4.8 %collective-permute-done.8 = f32[64,1024]{1,0:T(8,128)S(1)} collective-permute-done((f32[64,1024]{1,0:T(8,128)S(1)}, f32[64,1024]{1,0:T(8,128)S(1)}, u32[]{:S(2)}, u32[]{:S(2)}) %collective-permute-start.8) | collective-permute-done | bytes 262176 | tf_op jit(solution)/shard_map/ppermute | solution.py:64
  80.9 0.7 reshape.221
  81.6 4.2 %all-to-all-start.2 = ((f32[8,1,256]{2,1,0:T(1,128)}), f32[8,1,256]{2,1,0:T(1,128)S(1)}, u32[]{:S(2)}, u32[]{:S(2)}) async-start(f32[8,1,256]{2,1,0:T(1,128)} %reshape.221), calls=%async_computation.2 | async-start | bytes 16384 | tf_op jit(solution)/shard_map/all_to_all | solution.py:39
  85.8 5.6 %all-to-all-done.2 = f32[8,1,256]{2,1,0:T(1,128)S(1)} async-done(((f32[8,1,256]{2,1,0:T(1,128)}), f32[8,1,256]{2,1,0:T(1,128)S(1)}, u32[]{:S(2)}, u32[]{:S(2)}) %all-to-all-start.2) | async-done | bytes 8224 | tf_op jit(solution)/shard_map/all_to_all | solution.py:39
  91.4 0.5 broadcast.155
  91.9 0.7 reduce.3
  92.7 0.6 multiply_add_fusion
  93.3 3.1 %fusion.7 = f32[64,2048]{1,0:T(8,128)S(1)} fusion(bf16[1024,2048]{1,0:T(8,128)(2,1)} %param.19, f32[64,1024]{1,0:T(8,128)S(1)} %get-tuple-element.12, f32[64,1024]{1,0:T(8,128)S(1)} %get-tuple-element.11, f32[64]{0:T(128)S(1)} %get-tuple-element.26, f32[64]{0:T(128)S(1)} %get-tuple-element.25, f32[64]{0:T(128)S(1)} %get-tuple-element.23, ...), kind=kOutput, calls=%fused_computation.30 | convolution fusion | flops 269025280 | bytes 5243904 | tf_op jit(solution)/shard_map/dot_general | solution.py:209
  96.5 0.3 reshape.193
  97.0 1.4 %collective-permute-done.10 = f32[4,4,2,2048]{3,2,1,0:T(2,128)S(1)} collective-permute-done((f32[4,4,2,2048]{3,2,1,0:T(2,128)S(1)}, f32[4,4,2,2048]{3,2,1,0:T(2,128)S(1)}, u32[]{:S(2)}, u32[]{:S(2)}) %collective-permute-start.10) | collective-permute-done | bytes 262176 | tf_op jit(solution)/shard_map/ppermute | solution.py:213
  98.4 0.8 bitcast_add_fusion
  99.3 3.5 %all-to-all-start.3 = ((f32[16,2,2048]{2,1,0:T(2,128)}), f32[16,2,2048]{2,1,0:T(2,128)S(1)}, u32[]{:S(2)}, u32[]{:S(2)}) async-start(f32[16,2,2048]{2,1,0:T(2,128)} %bitcast.25), calls=%async_computation.3 | async-start | bytes 524288 | tf_op jit(solution)/shard_map/all_to_all | solution.py:39
  102.8 11.1 %all-to-all-done.3 = f32[16,2,2048]{2,1,0:T(2,128)S(1)} async-done(((f32[16,2,2048]{2,1,0:T(2,128)}), f32[16,2,2048]{2,1,0:T(2,128)S(1)}, u32[]{:S(2)}, u32[]{:S(2)}) %all-to-all-start.3) | async-done | bytes 262176 | tf_op jit(solution)/shard_map/all_to_all | solution.py:39
  114.3 0.7 broadcast_in_dim.111
  115.0 2.6 %all-to-all-start.4 = ((bf16[32,2,1024]{2,1,0:T(2,128)(2,1)}), bf16[32,2,1024]{2,1,0:T(2,128)(2,1)S(1)}, u32[]{:S(2)}, u32[]{:S(2)}) async-start(bf16[32,2,1024]{2,1,0:T(2,128)(2,1)} %bitcast.32), calls=%async_computation.4 | async-start | bytes 262144 | tf_op jit(solution)/shard_map/all_to_all | solution.py:39
  118.3 7.7 %all-to-all-done.4 = bf16[32,2,1024]{2,1,0:T(2,128)(2,1)S(1)} async-done(((bf16[32,2,1024]{2,1,0:T(2,128)(2,1)}), bf16[32,2,1024]{2,1,0:T(2,128)(2,1)S(1)}, u32[]{:S(2)}, u32[]{:S(2)}) %all-to-all-start.4) | async-done | bytes 131104 | tf_op jit(solution)/shard_map/all_to_all | solution.py:39
  126.1 4.8 %fusion.37 = f32[2048,1024]{1,0:T(8,128)} fusion(bf16[64,1024]{1,0:T(8,128)(2,1)S(1)} %reshape.198, bf16[64,2048]{1,0:T(8,128)(2,1)S(1)} %gather_fusion, pred[64]{0:T(512)(128)(4,1)S(1)} %get-tuple-element.13), kind=kOutput, calls=%fused_computation.106 | convolution fusion | flops 268566528 | bytes 8781888 | tf_op jit(solution)/shard_map/dot_general | solution.py:24
  130.8 4.8 %fusion.15 = f32[2048,1024]{1,0:T(8,128)} fusion(bf16[64,1024]{1,0:T(8,128)(2,1)S(1)} %reshape.198, bf16[64,2048]{1,0:T(8,128)(2,1)S(1)} %gather_fusion.1, pred[64]{0:T(512)(128)(4,1)S(1)} %get-tuple-element.13), kind=kOutput, calls=%fused_computation.39 | convolution fusion | flops 268566528 | bytes 8781888 | tf_op jit(solution)/shard_map/dot_general | solution.py:24
  (55 shorter events, 3.4 us)
Async XLA Ops:
  3.6 14.1 %collective-permute-start.1 = (bf16[2,16,2048]{2,1,0:T(8,128)(2,1)S(1)}, bf16[2,16,2048]{2,1,0:T(8,128)(2,1)S(1)}, u32[]{:S(2)}, u32[]{:S(2)}) collective-permute-start(bf16[2,16,2048]{2,1,0:T(8,128)(2,1)S(1)} %get-tuple-element.20), channel_id=1, source_target_pairs={{0,2},{1,3},{2,0},{3,1},{4,6},{5,7},{6,4},{7,5},{8,10},{9,11},{10,... | collective-permute-start | bytes 393224 | tf_op jit(solution)/shard_map/ppermute | solution.py:45
  7.7 10.0 %collective-permute-start = (bf16[2,16,2048]{2,1,0:T(8,128)(2,1)S(1)}, bf16[2,16,2048]{2,1,0:T(8,128)(2,1)S(1)}, u32[]{:S(2)}, u32[]{:S(2)}) collective-permute-start(bf16[2,16,2048]{2,1,0:T(8,128)(2,1)S(1)} %get-tuple-element.20), channel_id=1, source_target_pairs={{0,1},{1,2},{2,3},{3,0},{4,5},{5,6},{6,7},{7,4},{8,9},{9,10},{10,1... | collective-permute-start | bytes 393224 | tf_op jit(solution)/shard_map/ppermute | solution.py:45
  9.3 9.2 %collective-permute-start.2 = (bf16[2,16,2048]{2,1,0:T(8,128)(2,1)S(1)}, bf16[2,16,2048]{2,1,0:T(8,128)(2,1)S(1)}, u32[]{:S(2)}, u32[]{:S(2)}) collective-permute-start(bf16[2,16,2048]{2,1,0:T(8,128)(2,1)S(1)} %get-tuple-element.20), channel_id=1, source_target_pairs={{0,3},{1,0},{2,1},{3,2},{4,7},{5,4},{6,5},{7,6},{8,11},{9,8},{10,9... | collective-permute-start | bytes 393224 | tf_op jit(solution)/shard_map/ppermute | solution.py:45
  18.5 2.0 %collective-permute-start.3 = (bf16[4,2,16,2048]{3,2,1,0:T(8,128)(2,1)S(1)}, bf16[4,2,16,2048]{3,2,1,0:T(8,128)(2,1)S(1)}, u32[]{:S(2)}, u32[]{:S(2)}) collective-permute-start(bf16[4,2,16,2048]{3,2,1,0:T(8,128)(2,1)S(1)} %get-tuple-element.18), channel_id=1, source_target_pairs={{0,4},{4,0},{1,5},{5,1},{2,6},{6,2},{3,7},{7,3},{8,12},{12,8},{9,1... | collective-permute-start | bytes 1572872 | tf_op jit(solution)/shard_map/ppermute | solution.py:45
  22.6 3.5 %copy-start = (bf16[2048,1024]{1,0:T(8,128)(2,1)S(1)}, bf16[2048,1024]{1,0:T(8,128)(2,1)}, u32[]{:S(2)}) copy-start(bf16[2048,1024]{1,0:T(8,128)(2,1)} %param.21) | copy-start | bytes 12582916
  26.0 8.0 %copy-start.2 = (s32[4,256]{1,0:T(4,128)S(1)}, s32[4,256]{1,0:T(4,128)}, u32[]{:S(2)}) copy-start(s32[4,256]{1,0:T(4,128)} %param.14) | copy-start | bytes 12292
  26.0 23.8 %copy-start.1 = (f32[2048]{0:T(1024)S(1)}, f32[2048]{0:T(1024)}, u32[]{:S(2)}) copy-start(f32[2048]{0:T(1024)} %param.17) | copy-start | bytes 24580
  28.0 17.1 %all-to-all-start = ((f32[32,2,1280]{2,1,0:T(2,128)}), f32[32,2,1280]{2,1,0:T(2,128)S(1)}, u32[]{:S(2)}, u32[]{:S(2)}) async-start(f32[32,2,1280]{2,1,0:T(2,128)} %pad_maximum_fusion.1), calls=%async_computation | async-start | bytes 655360 | tf_op jit(solution)/shard_map/all_to_all | solution.py:39
  46.6 13.7 %all-to-all-start.1 = ((bf16[32,2,2048]{2,1,0:T(2,128)(2,1)}), bf16[32,2,2048]{2,1,0:T(2,128)(2,1)S(1)}, u32[]{:S(2)}, u32[]{:S(2)}) async-start(bf16[32,2,2048]{2,1,0:T(2,128)(2,1)} %bitcast.15), calls=%async_computation.1 | async-start | bytes 524288 | tf_op jit(solution)/shard_map/all_to_all | solution.py:39
  53.5 13.0 %collective-permute-start.6 = (f32[64,1024]{1,0:T(8,128)S(1)}, f32[64,1024]{1,0:T(8,128)S(1)}, u32[]{:S(2)}, u32[]{:S(2)}) collective-permute-start(f32[64,1024]{1,0:T(8,128)S(1)} %fusion.3), channel_id=1, source_target_pairs={{0,24},{8,16},{16,8},{24,0},{1,25},{9,17},{17,9},{25,1},{2,26},{10... | collective-permute-start | bytes 786440 | tf_op jit(solution)/shard_map/ppermute | solution.py:64
  56.2 13.9 %collective-permute-start.5 = (f32[64,1024]{1,0:T(8,128)S(1)}, f32[64,1024]{1,0:T(8,128)S(1)}, u32[]{:S(2)}, u32[]{:S(2)}) collective-permute-start(f32[64,1024]{1,0:T(8,128)S(1)} %fusion.3), channel_id=1, source_target_pairs={{0,16},{8,24},{16,0},{24,8},{1,17},{9,25},{17,1},{25,9},{2,18},{10... | collective-permute-start | bytes 786440 | tf_op jit(solution)/shard_map/ppermute | solution.py:64
  56.7 13.3 %collective-permute-start.4 = (f32[64,1024]{1,0:T(8,128)S(1)}, f32[64,1024]{1,0:T(8,128)S(1)}, u32[]{:S(2)}, u32[]{:S(2)}) collective-permute-start(f32[64,1024]{1,0:T(8,128)S(1)} %fusion.3), channel_id=1, source_target_pairs={{0,8},{8,0},{16,24},{24,16},{1,9},{9,1},{17,25},{25,17},{2,10},{10... | collective-permute-start | bytes 786440 | tf_op jit(solution)/shard_map/ppermute | solution.py:64
  64.0 11.7 %collective-permute-start.9 = (f32[64,1024]{1,0:T(8,128)S(1)}, f32[64,1024]{1,0:T(8,128)S(1)}, u32[]{:S(2)}, u32[]{:S(2)}) collective-permute-start(f32[64,1024]{1,0:T(8,128)S(1)} %fusion.41), channel_id=1, source_target_pairs={{0,24},{8,16},{16,8},{24,0},{1,25},{9,17},{17,9},{25,1},{2,26},{10... | collective-permute-start | bytes 786440 | tf_op jit(solution)/shard_map/ppermute | solution.py:64
  64.9 15.7 %collective-permute-start.8 = (f32[64,1024]{1,0:T(8,128)S(1)}, f32[64,1024]{1,0:T(8,128)S(1)}, u32[]{:S(2)}, u32[]{:S(2)}) collective-permute-start(f32[64,1024]{1,0:T(8,128)S(1)} %fusion.41), channel_id=1, source_target_pairs={{0,16},{8,24},{16,0},{24,8},{1,17},{9,25},{17,1},{25,9},{2,18},{10... | collective-permute-start | bytes 786440 | tf_op jit(solution)/shard_map/ppermute | solution.py:64
  66.4 14.2 %collective-permute-start.7 = (f32[64,1024]{1,0:T(8,128)S(1)}, f32[64,1024]{1,0:T(8,128)S(1)}, u32[]{:S(2)}, u32[]{:S(2)}) collective-permute-start(f32[64,1024]{1,0:T(8,128)S(1)} %fusion.41), channel_id=1, source_target_pairs={{0,8},{8,0},{16,24},{24,16},{1,9},{9,1},{17,25},{25,17},{2,10},{10... | collective-permute-start | bytes 786440 | tf_op jit(solution)/shard_map/ppermute | solution.py:64
  81.6 9.8 %all-to-all-start.2 = ((f32[8,1,256]{2,1,0:T(1,128)}), f32[8,1,256]{2,1,0:T(1,128)S(1)}, u32[]{:S(2)}, u32[]{:S(2)}) async-start(f32[8,1,256]{2,1,0:T(1,128)} %reshape.221), calls=%async_computation.2 | async-start | bytes 16384 | tf_op jit(solution)/shard_map/all_to_all | solution.py:39
  96.8 1.6 %collective-permute-start.10 = (f32[4,4,2,2048]{3,2,1,0:T(2,128)S(1)}, f32[4,4,2,2048]{3,2,1,0:T(2,128)S(1)}, u32[]{:S(2)}, u32[]{:S(2)}) collective-permute-start(f32[4,4,2,2048]{3,2,1,0:T(2,128)S(1)} %dynamic-slice_bitcast_fusion), channel_id=1, source_target_pairs={{0,4},{4,0},{1,5},{5,1},{2,6},{6,2},{3,7},{7,3},{8,12},{12,8},{9,1... | collective-permute-start | bytes 786440 | tf_op jit(solution)/shard_map/ppermute | solution.py:213
  99.3 14.7 %all-to-all-start.3 = ((f32[16,2,2048]{2,1,0:T(2,128)}), f32[16,2,2048]{2,1,0:T(2,128)S(1)}, u32[]{:S(2)}, u32[]{:S(2)}) async-start(f32[16,2,2048]{2,1,0:T(2,128)} %bitcast.25), calls=%async_computation.3 | async-start | bytes 524288 | tf_op jit(solution)/shard_map/all_to_all | solution.py:39
  115.0 11.0 %all-to-all-start.4 = ((bf16[32,2,1024]{2,1,0:T(2,128)(2,1)}), bf16[32,2,1024]{2,1,0:T(2,128)(2,1)S(1)}, u32[]{:S(2)}, u32[]{:S(2)}) async-start(bf16[32,2,1024]{2,1,0:T(2,128)(2,1)} %bitcast.32), calls=%async_computation.4 | async-start | bytes 262144 | tf_op jit(solution)/shard_map/all_to_all | solution.py:39

commit v8 on v7

--- a/solution.py
+++ b/solution.py
@@ -60,12 +60,11 @@
             ]
         )
         return jnp.sum(jnp.take(parts, (mine - jnp.arange(count)) % count, axis=0), axis=0)
-    parts = [x] + [
-        lax.ppermute(x, "section", [(i, i ^ k) for i in range(count)]) for k in range(1, count)
-    ]
-    while len(parts) > 1:
-        parts = [parts[i] + parts[i + 1] for i in range(0, len(parts), 2)]
-    return parts[0]
+    step = 1
+    while step < count:
+        x = x + lax.ppermute(x, "section", [(i, i ^ step) for i in range(count)])
+        step *= 2
+    return x
 
 
 def pad_cols(count):

time: 137 us -> 135 us (0.985)
  blocking collectives: 0 us -> 16.9 us
  starting transfers between devices: 34.9 us -> 25.2 us
  waiting for transfers between devices: 59.5 us -> 50.5 us
    all_to_all x0 -> x1, blocking collectives: none -> 16.9 us  [exchange(): return lax.all_to_all(send, axes, split_axis=0, concat_axis=0, tiled=True)]
    all_to_all x5 -> x4, waiting for transfers between devices: 38.8 us -> 29.2 us  [exchange(): return lax.all_to_all(send, axes, split_axis=0, concat_axis=0, tiled=True)]
    all_to_all x5 -> x4, starting transfers between devices: 19.6 us -> 12.7 us  [exchange(): return lax.all_to_all(send, axes, split_axis=0, concat_axis=0, tiled=True)]
    ppermute x6 -> x4, starting transfers between devices: 7.11 us -> 4.35 us  [section_sum(): x = x + lax.ppermute(x, 'section', [(i, i ^ step) for i in range(count)])]
    ppermute x6 -> x4, waiting for transfers between devices: 12.8 us -> 13.4 us  [section_sum(): x = x + lax.ppermute(x, 'section', [(i, i ^ step) for i in range(count)])]
  transfers between devices with their start and end apart: 16 -> 13, of which waited for: 12 -> 10; matrix products, arithmetic and copies ran while one was open for 7% -> 7% of each run, Pallas kernels for 0% -> 0%
where the time goes in v8:
time: 135 us; the launch traced here: 134 us
  waiting for transfers between devices  50.5 us (37%)
  starting transfers between devices  25.2 us (19%)
  matrix products  23.9 us (18%)
  blocking collectives  16.9 us (13%)
  local copies, waits for them, and re-layouts  8.62 us (6%)
  other arithmetic  5.63 us (4%)
  between operations  3.41 us (3%)
    all_to_all x4, waiting for transfers between devices, exchange(): return lax.all_to_all(send, axes, split_axis=0, concat_axis=0, tiled=True)  29.2 us
    all_to_all x1, blocking collectives, exchange(): return lax.all_to_all(send, axes, split_axis=0, concat_axis=0, tiled=True)  16.9 us
    ppermute x4, waiting for transfers between devices, section_sum(): x = x + lax.ppermute(x, 'section', [(i, i ^ step) for i in range(count)])  13.4 us
    all_to_all x4, starting transfers between devices, exchange(): return lax.all_to_all(send, axes, split_axis=0, concat_axis=0, tiled=True)  12.7 us
    dot_general x2, matrix products, contract_first(): lax.dot_general(operand, weights, (((0,), (0,)), ((), ())), preferred_ele...  9.52 us
    ppermute x4, starting transfers between devices, shifted(): lax.ppermute(x, axis, [(i, (i + k) % count) for i in range(count)])  8.02 us
    dot_general x2, matrix products, contract_last(): lax.dot_general(operand, weights, (((1,), (1,)), ((), ())), preferred_ele...  7.17 us
    ppermute x4, waiting for transfers between devices, shifted(): lax.ppermute(x, axis, [(i, (i + k) % count) for i in range(count)])  6.49 us
  transfers between devices with their start and end apart: 13, of which 10 were waited for; matrix products, arithmetic and copies ran while one was open for 7% of the time, Pallas kernels for 0%

profile of v8, /device:TPU:0, one launch (start us, length us, event | category | flops | bytes accessed | tf_op | source)
XLA Modules:
  0.0 134.3 jit_solution(13567697618038984678)
XLA Ops:
  0.6 1.2 dynamic_slice.15
  2.5 1.0 constant_dynamic-slice_fusion
  3.6 4.1 %collective-permute-start.1 = (bf16[2,16,2048]{2,1,0:T(8,128)(2,1)S(1)}, bf16[2,16,2048]{2,1,0:T(8,128)(2,1)S(1)}, u32[]{:S(2)}, u32[]{:S(2)}) collective-permute-start(bf16[2,16,2048]{2,1,0:T(8,128)(2,1)S(1)} %get-tuple-element.20), channel_id=1, source_target_pairs={{0,2},{1,3},{2,0},{3,1},{4,6},{5,7},{6,4},{7,5},{8,10},{9,11},{10,... | collective-permute-start | bytes 393224 | tf_op jit(solution)/shard_map/ppermute | solution.py:45
  7.7 1.6 %collective-permute-start = (bf16[2,16,2048]{2,1,0:T(8,128)(2,1)S(1)}, bf16[2,16,2048]{2,1,0:T(8,128)(2,1)S(1)}, u32[]{:S(2)}, u32[]{:S(2)}) collective-permute-start(bf16[2,16,2048]{2,1,0:T(8,128)(2,1)S(1)} %get-tuple-element.20), channel_id=1, source_target_pairs={{0,1},{1,2},{2,3},{3,0},{4,5},{5,6},{6,7},{7,4},{8,9},{9,10},{10,1... | collective-permute-start | bytes 393224 | tf_op jit(solution)/shard_map/ppermute | solution.py:45
  9.3 2.2 %collective-permute-start.2 = (bf16[2,16,2048]{2,1,0:T(8,128)(2,1)S(1)}, bf16[2,16,2048]{2,1,0:T(8,128)(2,1)S(1)}, u32[]{:S(2)}, u32[]{:S(2)}) collective-permute-start(bf16[2,16,2048]{2,1,0:T(8,128)(2,1)S(1)} %get-tuple-element.20), channel_id=1, source_target_pairs={{0,3},{1,0},{2,1},{3,2},{4,7},{5,4},{6,5},{7,6},{8,11},{9,8},{10,9... | collective-permute-start | bytes 393224 | tf_op jit(solution)/shard_map/ppermute | solution.py:45
  11.5 0.8 dynamic_slice.18
  12.3 5.4 %collective-permute-done.1 = bf16[2,16,2048]{2,1,0:T(8,128)(2,1)S(1)} collective-permute-done((bf16[2,16,2048]{2,1,0:T(8,128)(2,1)S(1)}, bf16[2,16,2048]{2,1,0:T(8,128)(2,1)S(1)}, u32[]{:S(2)}, u32[]{:S(2)}) %collective-permute-start.1) | collective-permute-done | bytes 131104 | tf_op jit(solution)/shard_map/ppermute | solution.py:45
  17.7 0.7 collective-permute-done.2
  18.6 0.8 select_reduce_fusion.5
  19.4 0.8 select_reduce_fusion.4
  20.2 0.3 collective-permute-done.3
  20.7 0.7 gather_fusion.1
  21.5 0.7 gather_fusion
  22.2 0.2 fusion
  22.6 3.2 %fusion.16 = f32[64,1024]{1,0:T(8,128)S(1)} fusion(bf16[2048,1024]{1,0:T(8,128)(2,1)} %param.20, bf16[64,2048]{1,0:T(8,128)(2,1)S(1)} %gather_fusion.1, pred[64]{0:T(512)(128)(4,1)S(1)} %get-tuple-element.13), kind=kOutput, calls=%fused_computation.38 | convolution fusion | flops 268566528 | bytes 4718656 | tf_op jit(solution)/shard_map/dot_general | solution.py:133
  25.8 0.2 copy-done
  26.0 0.9 convolution_add_fusion
  27.2 16.9 %all_to_all.25 = f32[32,2,1280]{2,1,0:T(2,128)S(1)} all-to-all(f32[32,2,1280]{2,1,0:T(2,128)S(1)} %pad_maximum_fusion.1), channel_id=1, replica_groups=mesh['section'=4,'mp'=2,'dp'=4] {'section','mp','dp'}, dimensions={0} | all-to-all | bytes 655360 | tf_op jit(solution)/shard_map/all_to_all | solution.py:39
  44.8 0.9 broadcast_in_dim.105
  45.7 3.2 %all-to-all-start.1 = ((bf16[32,2,2048]{2,1,0:T(2,128)(2,1)}), bf16[32,2,2048]{2,1,0:T(2,128)(2,1)S(1)}, u32[]{:S(2)}, u32[]{:S(2)}) async-start(bf16[32,2,2048]{2,1,0:T(2,128)(2,1)} %bitcast.15), calls=%async_computation.1 | async-start | bytes 524288 | tf_op jit(solution)/shard_map/all_to_all | solution.py:39
  49.0 3.6 %fusion.3 = f32[64,1024]{1,0:T(8,128)S(1)} fusion(bf16[1024,2048]{1,0:T(8,128)(2,1)} %param.19, f32[2048]{0:T(1024)S(1)} %copy-done.1, f32[64]{0:T(128)S(1)} %add_rsqrt_fusion.1, bf16[64,2048]{1,0:T(8,128)(2,1)S(1)} %gather_fusion, pred[64]{0:T(512)(128)(4,1)S(1)} %get-tuple-element.13), kind=kOutput, calls=%fused_computation.11 | convolution fusion | flops 269090816 | bytes 4727104 | tf_op jit(solution)/shard_map/dot_general | solution.py:18
  52.5 1.8 %collective-permute-start.4 = (f32[64,1024]{1,0:T(8,128)S(1)}, f32[64,1024]{1,0:T(8,128)S(1)}, u32[]{:S(2)}, u32[]{:S(2)}) collective-permute-start(f32[64,1024]{1,0:T(8,128)S(1)} %fusion.3), channel_id=1, source_target_pairs={{0,8},{8,0},{16,24},{24,16},{1,9},{9,1},{17,25},{25,17},{2,10},{10... | collective-permute-start | bytes 786440 | tf_op jit(solution)/shard_map/ppermute | solution.py:65
  54.4 4.9 %all-to-all-done.1 = bf16[32,2,2048]{2,1,0:T(2,128)(2,1)S(1)} async-done(((bf16[32,2,2048]{2,1,0:T(2,128)(2,1)}), bf16[32,2,2048]{2,1,0:T(2,128)(2,1)S(1)}, u32[]{:S(2)}, u32[]{:S(2)}) %all-to-all-start.1) | async-done | bytes 262176 | tf_op jit(solution)/shard_map/all_to_all | solution.py:39
  59.4 3.6 %fusion.41 = f32[64,1024]{1,0:T(8,128)S(1)} fusion(bf16[64,2048]{1,0:T(8,128)(2,1)S(1)} %reshape.191, bf16[1024,2048]{1,0:T(8,128)(2,1)} %param.19), kind=kOutput, calls=%fused_computation.108 | convolution fusion | flops 268435456 | bytes 4718592 | tf_op jit(solution)/shard_map/dot_general | solution.py:18
  62.9 0.9 collective-permute-start.6
  63.9 0.6 collective-permute-start.5
  64.5 6.9 %collective-permute-done.6 = f32[64,1024]{1,0:T(8,128)S(1)} collective-permute-done((f32[64,1024]{1,0:T(8,128)S(1)}, f32[64,1024]{1,0:T(8,128)S(1)}, u32[]{:S(2)}, u32[]{:S(2)}) %collective-permute-start.6) | collective-permute-done | bytes 262176 | tf_op jit(solution)/shard_map/ppermute | solution.py:65
  71.5 1.0 collective-permute-start.7
  72.5 0.2 select_reduce_fusion.1
  72.7 6.5 %collective-permute-done.7 = f32[64,1024]{1,0:T(8,128)S(1)} collective-permute-done((f32[64,1024]{1,0:T(8,128)S(1)}, f32[64,1024]{1,0:T(8,128)S(1)}, u32[]{:S(2)}, u32[]{:S(2)}) %collective-permute-start.7) | collective-permute-done | bytes 262176 | tf_op jit(solution)/shard_map/ppermute | solution.py:65
  79.1 0.2 exponential_reduce_fusion.1
  79.4 0.7 reshape.221
  80.1 3.3 %all-to-all-start.2 = ((f32[8,1,256]{2,1,0:T(1,128)}), f32[8,1,256]{2,1,0:T(1,128)S(1)}, u32[]{:S(2)}, u32[]{:S(2)}) async-start(f32[8,1,256]{2,1,0:T(1,128)} %reshape.221), calls=%async_computation.2 | async-start | bytes 16384 | tf_op jit(solution)/shard_map/all_to_all | solution.py:39
  83.4 5.5 %all-to-all-done.2 = f32[8,1,256]{2,1,0:T(1,128)S(1)} async-done(((f32[8,1,256]{2,1,0:T(1,128)}), f32[8,1,256]{2,1,0:T(1,128)S(1)}, u32[]{:S(2)}, u32[]{:S(2)}) %all-to-all-start.2) | async-done | bytes 8224 | tf_op jit(solution)/shard_map/all_to_all | solution.py:39
  89.0 0.5 broadcast.155
  89.5 0.7 reduce.3
  90.2 0.6 multiply_add_fusion
  90.9 3.1 %fusion.7 = f32[64,2048]{1,0:T(8,128)S(1)} fusion(bf16[1024,2048]{1,0:T(8,128)(2,1)} %param.19, f32[64,1024]{1,0:T(8,128)S(1)} %get-tuple-element.12, f32[64,1024]{1,0:T(8,128)S(1)} %get-tuple-element.11, f32[64]{0:T(128)S(1)} %get-tuple-element.26, f32[64]{0:T(128)S(1)} %get-tuple-element.25, f32[64]{0:T(128)S(1)} %get-tuple-element.23, ...), kind=kOutput, calls=%fused_computation.28 | convolution fusion | flops 269025280 | bytes 5243904 | tf_op jit(solution)/shard_map/dot_general | solution.py:208
  94.0 0.3 reshape.193
  94.5 1.4 %collective-permute-done.8 = f32[4,4,2,2048]{3,2,1,0:T(2,128)S(1)} collective-permute-done((f32[4,4,2,2048]{3,2,1,0:T(2,128)S(1)}, f32[4,4,2,2048]{3,2,1,0:T(2,128)S(1)}, u32[]{:S(2)}, u32[]{:S(2)}) %collective-permute-start.8) | collective-permute-done | bytes 262176 | tf_op jit(solution)/shard_map/ppermute | solution.py:212
  96.0 0.8 bitcast_add_fusion
  96.8 3.5 %all-to-all-start.3 = ((f32[16,2,2048]{2,1,0:T(2,128)}), f32[16,2,2048]{2,1,0:T(2,128)S(1)}, u32[]{:S(2)}, u32[]{:S(2)}) async-start(f32[16,2,2048]{2,1,0:T(2,128)} %bitcast.25), calls=%async_computation.3 | async-start | bytes 524288 | tf_op jit(solution)/shard_map/all_to_all | solution.py:39
  100.4 11.1 %all-to-all-done.3 = f32[16,2,2048]{2,1,0:T(2,128)S(1)} async-done(((f32[16,2,2048]{2,1,0:T(2,128)}), f32[16,2,2048]{2,1,0:T(2,128)S(1)}, u32[]{:S(2)}, u32[]{:S(2)}) %all-to-all-start.3) | async-done | bytes 262176 | tf_op jit(solution)/shard_map/all_to_all | solution.py:39
  111.9 0.7 broadcast_in_dim.111
  112.6 2.6 %all-to-all-start.4 = ((bf16[32,2,1024]{2,1,0:T(2,128)(2,1)}), bf16[32,2,1024]{2,1,0:T(2,128)(2,1)S(1)}, u32[]{:S(2)}, u32[]{:S(2)}) async-start(bf16[32,2,1024]{2,1,0:T(2,128)(2,1)} %bitcast.32), calls=%async_computation.4 | async-start | bytes 262144 | tf_op jit(solution)/shard_map/all_to_all | solution.py:39
  115.8 7.7 %all-to-all-done.4 = bf16[32,2,1024]{2,1,0:T(2,128)(2,1)S(1)} async-done(((bf16[32,2,1024]{2,1,0:T(2,128)(2,1)}), bf16[32,2,1024]{2,1,0:T(2,128)(2,1)S(1)}, u32[]{:S(2)}, u32[]{:S(2)}) %all-to-all-start.4) | async-done | bytes 131104 | tf_op jit(solution)/shard_map/all_to_all | solution.py:39
  123.6 4.8 %fusion.37 = f32[2048,1024]{1,0:T(8,128)} fusion(bf16[64,1024]{1,0:T(8,128)(2,1)S(1)} %reshape.198, bf16[64,2048]{1,0:T(8,128)(2,1)S(1)} %gather_fusion, pred[64]{0:T(512)(128)(4,1)S(1)} %get-tuple-element.13), kind=kOutput, calls=%fused_computation.104 | convolution fusion | flops 268566528 | bytes 8781888 | tf_op jit(solution)/shard_map/dot_general | solution.py:24
  128.4 4.8 %fusion.15 = f32[2048,1024]{1,0:T(8,128)} fusion(bf16[64,1024]{1,0:T(8,128)(2,1)S(1)} %reshape.198, bf16[64,2048]{1,0:T(8,128)(2,1)S(1)} %gather_fusion.1, pred[64]{0:T(512)(128)(4,1)S(1)} %get-tuple-element.13), kind=kOutput, calls=%fused_computation.37 | convolution fusion | flops 268566528 | bytes 8781888 | tf_op jit(solution)/shard_map/dot_general | solution.py:24
  (52 shorter events, 2.4 us)
Async XLA Ops:
  3.6 14.1 %collective-permute-start.1 = (bf16[2,16,2048]{2,1,0:T(8,128)(2,1)S(1)}, bf16[2,16,2048]{2,1,0:T(8,128)(2,1)S(1)}, u32[]{:S(2)}, u32[]{:S(2)}) collective-permute-start(bf16[2,16,2048]{2,1,0:T(8,128)(2,1)S(1)} %get-tuple-element.20), channel_id=1, source_target_pairs={{0,2},{1,3},{2,0},{3,1},{4,6},{5,7},{6,4},{7,5},{8,10},{9,11},{10,... | collective-permute-start | bytes 393224 | tf_op jit(solution)/shard_map/ppermute | solution.py:45
  7.7 10.0 %collective-permute-start = (bf16[2,16,2048]{2,1,0:T(8,128)(2,1)S(1)}, bf16[2,16,2048]{2,1,0:T(8,128)(2,1)S(1)}, u32[]{:S(2)}, u32[]{:S(2)}) collective-permute-start(bf16[2,16,2048]{2,1,0:T(8,128)(2,1)S(1)} %get-tuple-element.20), channel_id=1, source_target_pairs={{0,1},{1,2},{2,3},{3,0},{4,5},{5,6},{6,7},{7,4},{8,9},{9,10},{10,1... | collective-permute-start | bytes 393224 | tf_op jit(solution)/shard_map/ppermute | solution.py:45
  9.3 9.2 %collective-permute-start.2 = (bf16[2,16,2048]{2,1,0:T(8,128)(2,1)S(1)}, bf16[2,16,2048]{2,1,0:T(8,128)(2,1)S(1)}, u32[]{:S(2)}, u32[]{:S(2)}) collective-permute-start(bf16[2,16,2048]{2,1,0:T(8,128)(2,1)S(1)} %get-tuple-element.20), channel_id=1, source_target_pairs={{0,3},{1,0},{2,1},{3,2},{4,7},{5,4},{6,5},{7,6},{8,11},{9,8},{10,9... | collective-permute-start | bytes 393224 | tf_op jit(solution)/shard_map/ppermute | solution.py:45
  18.5 2.0 %collective-permute-start.3 = (bf16[4,2,16,2048]{3,2,1,0:T(8,128)(2,1)S(1)}, bf16[4,2,16,2048]{3,2,1,0:T(8,128)(2,1)S(1)}, u32[]{:S(2)}, u32[]{:S(2)}) collective-permute-start(bf16[4,2,16,2048]{3,2,1,0:T(8,128)(2,1)S(1)} %get-tuple-element.18), channel_id=1, source_target_pairs={{0,4},{4,0},{1,5},{5,1},{2,6},{6,2},{3,7},{7,3},{8,12},{12,8},{9,1... | collective-permute-start | bytes 1572872 | tf_op jit(solution)/shard_map/ppermute | solution.py:45
  22.6 3.5 %copy-start = (bf16[2048,1024]{1,0:T(8,128)(2,1)S(1)}, bf16[2048,1024]{1,0:T(8,128)(2,1)}, u32[]{:S(2)}) copy-start(bf16[2048,1024]{1,0:T(8,128)(2,1)} %param.21) | copy-start | bytes 12582916
  26.0 22.9 %copy-start.1 = (f32[2048]{0:T(1024)S(1)}, f32[2048]{0:T(1024)}, u32[]{:S(2)}) copy-start(f32[2048]{0:T(1024)} %param.17) | copy-start | bytes 24580
  45.7 13.5 %all-to-all-start.1 = ((bf16[32,2,2048]{2,1,0:T(2,128)(2,1)}), bf16[32,2,2048]{2,1,0:T(2,128)(2,1)S(1)}, u32[]{:S(2)}, u32[]{:S(2)}) async-start(bf16[32,2,2048]{2,1,0:T(2,128)(2,1)} %bitcast.15), calls=%async_computation.1 | async-start | bytes 524288 | tf_op jit(solution)/shard_map/all_to_all | solution.py:39
  48.9 14.9 %copy-start.2 = (s32[4,256]{1,0:T(4,128)S(1)}, s32[4,256]{1,0:T(4,128)}, u32[]{:S(2)}) copy-start(s32[4,256]{1,0:T(4,128)} %param.14) | copy-start | bytes 12292
  52.5 11.3 %collective-permute-start.4 = (f32[64,1024]{1,0:T(8,128)S(1)}, f32[64,1024]{1,0:T(8,128)S(1)}, u32[]{:S(2)}, u32[]{:S(2)}) collective-permute-start(f32[64,1024]{1,0:T(8,128)S(1)} %fusion.3), channel_id=1, source_target_pairs={{0,8},{8,0},{16,24},{24,16},{1,9},{9,1},{17,25},{25,17},{2,10},{10... | collective-permute-start | bytes 786440 | tf_op jit(solution)/shard_map/ppermute | solution.py:65
  62.9 8.5 %collective-permute-start.6 = (f32[64,1024]{1,0:T(8,128)S(1)}, f32[64,1024]{1,0:T(8,128)S(1)}, u32[]{:S(2)}, u32[]{:S(2)}) collective-permute-start(f32[64,1024]{1,0:T(8,128)S(1)} %fusion.41), channel_id=1, source_target_pairs={{0,8},{8,0},{16,24},{24,16},{1,9},{9,1},{17,25},{25,17},{2,10},{10... | collective-permute-start | bytes 786440 | tf_op jit(solution)/shard_map/ppermute | solution.py:65
  63.9 8.7 %collective-permute-start.5 = (f32[64,1024]{1,0:T(8,128)S(1)}, f32[64,1024]{1,0:T(8,128)S(1)}, u32[]{:S(2)}, u32[]{:S(2)}) collective-permute-start(f32[64,1024]{1,0:T(8,128)S(1)} %add.146), channel_id=1, source_target_pairs={{0,16},{8,24},{16,0},{24,8},{1,17},{9,25},{17,1},{25,9},{2,18},{10... | collective-permute-start | bytes 786440 | tf_op jit(solution)/shard_map/ppermute | solution.py:65
  71.5 7.7 %collective-permute-start.7 = (f32[64,1024]{1,0:T(8,128)S(1)}, f32[64,1024]{1,0:T(8,128)S(1)}, u32[]{:S(2)}, u32[]{:S(2)}) collective-permute-start(f32[64,1024]{1,0:T(8,128)S(1)} %add.149), channel_id=1, source_target_pairs={{0,16},{8,24},{16,0},{24,8},{1,17},{9,25},{17,1},{25,9},{2,18},{10... | collective-permute-start | bytes 786440 | tf_op jit(solution)/shard_map/ppermute | solution.py:65
  80.1 8.9 %all-to-all-start.2 = ((f32[8,1,256]{2,1,0:T(1,128)}), f32[8,1,256]{2,1,0:T(1,128)S(1)}, u32[]{:S(2)}, u32[]{:S(2)}) async-start(f32[8,1,256]{2,1,0:T(1,128)} %reshape.221), calls=%async_computation.2 | async-start | bytes 16384 | tf_op jit(solution)/shard_map/all_to_all | solution.py:39
  94.4 1.6 %collective-permute-start.8 = (f32[4,4,2,2048]{3,2,1,0:T(2,128)S(1)}, f32[4,4,2,2048]{3,2,1,0:T(2,128)S(1)}, u32[]{:S(2)}, u32[]{:S(2)}) collective-permute-start(f32[4,4,2,2048]{3,2,1,0:T(2,128)S(1)} %dynamic-slice_bitcast_fusion), channel_id=1, source_target_pairs={{0,4},{4,0},{1,5},{5,1},{2,6},{6,2},{3,7},{7,3},{8,12},{12,8},{9,1... | collective-permute-start | bytes 786440 | tf_op jit(solution)/shard_map/ppermute | solution.py:212
  96.8 14.7 %all-to-all-start.3 = ((f32[16,2,2048]{2,1,0:T(2,128)}), f32[16,2,2048]{2,1,0:T(2,128)S(1)}, u32[]{:S(2)}, u32[]{:S(2)}) async-start(f32[16,2,2048]{2,1,0:T(2,128)} %bitcast.25), calls=%async_computation.3 | async-start | bytes 524288 | tf_op jit(solution)/shard_map/all_to_all | solution.py:39
  112.6 11.0 %all-to-all-start.4 = ((bf16[32,2,1024]{2,1,0:T(2,128)(2,1)}), bf16[32,2,1024]{2,1,0:T(2,128)(2,1)S(1)}, u32[]{:S(2)}, u32[]{:S(2)}) async-start(bf16[32,2,1024]{2,1,0:T(2,128)(2,1)} %bitcast.32), calls=%async_computation.4 | async-start | bytes 262144 | tf_op jit(solution)/shard_map/all_to_all | solution.py:39

commit v9 on v8

--- a/solution.py
+++ b/solution.py
@@ -133,14 +133,16 @@
     partial_value = jnp.dot(embed_all, fc_embed, preferred_element_type=jnp.float32) + jnp.dot(
         feature_all, fc_feature, preferred_element_type=jnp.float32
     )
-    target_square = jnp.sum(jnp.square(feature_all.astype(jnp.float32)), axis=1)
+    target_square = section_sum(jnp.sum(jnp.square(feature_all.astype(jnp.float32)), axis=1))
+    target_scale = lax.rsqrt(target_square / D + eps_norm)
+    target_norm = (feature_all.astype(jnp.float32) * target_scale[:, None] * target_gain).astype(
+        jnp.bfloat16
+    )
+    target_logit = section_sum(contract_last(target_norm, head))
     piece = width // groups
-    spare = pad_cols(-(-(total_rows + piece) // per_dev))
+    spare = pad_cols(-(-piece // per_dev))
     gain_piece = lax.dynamic_slice_in_dim(draft_gain, (my_mp * count_dp + my_dp) * piece, piece)
-    extra = jnp.pad(
-        jnp.concatenate([target_square, gain_piece]),
-        (0, per_dev * spare - total_rows - piece),
-    ).reshape(per_dev, spare)
+    extra = jnp.pad(gain_piece, (0, per_dev * spare - piece)).reshape(per_dev, spare)
     send1 = jnp.concatenate(
         [
             partial_value.reshape(n_dev, per_dev, block),
@@ -153,12 +155,7 @@
         jnp.sum(got1[..., :block], axis=0).transpose(1, 0, 2).reshape(per_dev, groups * block)
     )
     extra_got = got1[..., block:].reshape(count_sec, groups, per_dev * spare)
-    target_square = jnp.sum(extra_got[:, 0, :total_rows], axis=0)
-    gain_full = extra_got[:, :, total_rows : total_rows + piece].reshape(full_width)
-    target_scale = lax.rsqrt(target_square / D + eps_norm)
-    target_norm = (feature_all.astype(jnp.float32) * target_scale[:, None] * target_gain).astype(
-        jnp.bfloat16
-    )
+    gain_full = extra_got[:, :, :piece].reshape(full_width)
     draft_square = jnp.sum(hidden * hidden, axis=1)
     draft_scale = lax.rsqrt(draft_square / D + eps_norm)
     draft_norm = (hidden * draft_scale[:, None] * gain_full).astype(jnp.bfloat16)
@@ -169,7 +166,6 @@
     ).reshape(n_dev, per_dev, width)
     draft_norm_all = exchange(send2, ALL).reshape(total_rows, width)
 
-    target_logit = section_sum(contract_last(target_norm, head))
     draft_logit = section_sum(contract_last(draft_norm_all, head))
     column_zero = (my_mp * count_dp + my_dp) * vocab_tile
     is_label = (

time: 135 us -> 135 us (level)
  blocking collectives: 16.9 us -> 0 us
  starting transfers between devices: 25.2 us -> 34.5 us
  waiting for transfers between devices: 50.5 us -> 58.1 us
    all_to_all x1 -> x0, blocking collectives: 16.9 us -> none  [exchange(): return lax.all_to_all(send, axes, split_axis=0, concat_axis=0, tiled=True)]
    all_to_all x4 -> x5, starting transfers between devices: 12.7 us -> 18.4 us  [exchange(): return lax.all_to_all(send, axes, split_axis=0, concat_axis=0, tiled=True)]
    all_to_all x4 -> x5, waiting for transfers between devices: 29.2 us -> 34.2 us  [exchange(): return lax.all_to_all(send, axes, split_axis=0, concat_axis=0, tiled=True)]
    ppermute x4 -> x6, starting transfers between devices: 4.35 us -> 7.89 us  [section_sum(): x = x + lax.ppermute(x, 'section', [(i, i ^ step) for i in range(count)])]
    ppermute x4 -> x6, waiting for transfers between devices: 13.4 us -> 15.2 us  [section_sum(): x = x + lax.ppermute(x, 'section', [(i, i ^ step) for i in range(count)])]
  transfers between devices with their start and end apart: 13 -> 16, of which waited for: 10 -> 12; matrix products, arithmetic and copies ran while one was open for 7% -> 8% of each run, Pallas kernels for 0% -> 0%
where the time goes in v9:
time: 135 us; the launch traced here: 134 us
  waiting for transfers between devices  58.1 us (43%)
  starting transfers between devices  34.5 us (26%)
  matrix products  24 us (18%)
  local copies, waits for them, and re-layouts  7.82 us (6%)
  other arithmetic  6.25 us (5%)
  between operations  3.43 us (3%)
    all_to_all x5, waiting for transfers between devices, exchange(): return lax.all_to_all(send, axes, split_axis=0, concat_axis=0, tiled=True)  34.2 us
    all_to_all x5, starting transfers between devices, exchange(): return lax.all_to_all(send, axes, split_axis=0, concat_axis=0, tiled=True)  18.4 us
    ppermute x6, waiting for transfers between devices, section_sum(): x = x + lax.ppermute(x, 'section', [(i, i ^ step) for i in range(count)])  15.2 us
    dot_general x2, matrix products, contract_first(): lax.dot_general(operand, weights, (((0,), (0,)), ((), ())), preferred_ele...  9.52 us
    ppermute x4, starting transfers between devices, shifted(): lax.ppermute(x, axis, [(i, (i + k) % count) for i in range(count)])  8.02 us
    ppermute x6, starting transfers between devices, section_sum(): x = x + lax.ppermute(x, 'section', [(i, i ^ step) for i in range(count)])  7.89 us
    dot_general x2, matrix products, contract_last(): lax.dot_general(operand, weights, (((1,), (1,)), ((), ())), preferred_ele...  7.18 us
    ppermute x4, waiting for transfers between devices, shifted(): lax.ppermute(x, axis, [(i, (i + k) % count) for i in range(count)])  7.17 us
  transfers between devices with their start and end apart: 16, of which 12 were waited for; matrix products, arithmetic and copies ran while one was open for 8% of the time, Pallas kernels for 0%

profile of v9, /device:TPU:0, one launch (start us, length us, event | category | flops | bytes accessed | tf_op | source)
XLA Modules:
  0.0 134.0 jit_solution(957698968720860978)
XLA Ops:
  0.7 1.2 dynamic_slice.15
  2.6 1.0 constant_dynamic-slice_fusion
  3.6 4.1 %collective-permute-start.1 = (bf16[2,16,2048]{2,1,0:T(8,128)(2,1)S(1)}, bf16[2,16,2048]{2,1,0:T(8,128)(2,1)S(1)}, u32[]{:S(2)}, u32[]{:S(2)}) collective-permute-start(bf16[2,16,2048]{2,1,0:T(8,128)(2,1)S(1)} %get-tuple-element.20), channel_id=1, source_target_pairs={{0,2},{1,3},{2,0},{3,1},{4,6},{5,7},{6,4},{7,5},{8,10},{9,11},{10,... | collective-permute-start | bytes 393224 | tf_op jit(solution)/shard_map/ppermute | solution.py:45
  7.7 1.6 %collective-permute-start = (bf16[2,16,2048]{2,1,0:T(8,128)(2,1)S(1)}, bf16[2,16,2048]{2,1,0:T(8,128)(2,1)S(1)}, u32[]{:S(2)}, u32[]{:S(2)}) collective-permute-start(bf16[2,16,2048]{2,1,0:T(8,128)(2,1)S(1)} %get-tuple-element.20), channel_id=1, source_target_pairs={{0,1},{1,2},{2,3},{3,0},{4,5},{5,6},{6,7},{7,4},{8,9},{9,10},{10,1... | collective-permute-start | bytes 393224 | tf_op jit(solution)/shard_map/ppermute | solution.py:45
  9.3 2.2 %collective-permute-start.2 = (bf16[2,16,2048]{2,1,0:T(8,128)(2,1)S(1)}, bf16[2,16,2048]{2,1,0:T(8,128)(2,1)S(1)}, u32[]{:S(2)}, u32[]{:S(2)}) collective-permute-start(bf16[2,16,2048]{2,1,0:T(8,128)(2,1)S(1)} %get-tuple-element.20), channel_id=1, source_target_pairs={{0,3},{1,0},{2,1},{3,2},{4,7},{5,4},{6,5},{7,6},{8,11},{9,8},{10,9... | collective-permute-start | bytes 393224 | tf_op jit(solution)/shard_map/ppermute | solution.py:45
  11.5 0.8 select_reduce_fusion.5
  12.3 5.4 %collective-permute-done.1 = bf16[2,16,2048]{2,1,0:T(8,128)(2,1)S(1)} collective-permute-done((bf16[2,16,2048]{2,1,0:T(8,128)(2,1)S(1)}, bf16[2,16,2048]{2,1,0:T(8,128)(2,1)S(1)}, u32[]{:S(2)}, u32[]{:S(2)}) %collective-permute-start.1) | collective-permute-done | bytes 131104 | tf_op jit(solution)/shard_map/ppermute | solution.py:45
  17.7 0.7 collective-permute-done.2
  18.7 0.8 select_reduce_fusion.4
  19.5 1.0 collective-permute-done.3
  20.7 0.7 gather_fusion
  21.5 0.7 gather_fusion.1
  22.2 3.2 %fusion.16 = f32[64,1024]{1,0:T(8,128)S(1)} fusion(bf16[2048,1024]{1,0:T(8,128)(2,1)} %param.20, bf16[64,2048]{1,0:T(8,128)(2,1)S(1)} %gather_fusion.1, pred[64]{0:T(512)(128)(4,1)S(1)} %get-tuple-element.13), kind=kOutput, calls=%fused_computation.38 | convolution fusion | flops 268566528 | bytes 4718656 | tf_op jit(solution)/shard_map/dot_general | solution.py:133
  25.7 0.9 convolution_add_fusion
  26.8 0.8 pad_maximum_fusion.1
  27.6 6.1 %all-to-all-start = ((f32[32,2,1152]{2,1,0:T(2,128)}), f32[32,2,1152]{2,1,0:T(2,128)S(1)}, u32[]{:S(2)}, u32[]{:S(2)}) async-start(f32[32,2,1152]{2,1,0:T(2,128)} %pad_maximum_fusion.1), calls=%async_computation | async-start | bytes 589824 | tf_op jit(solution)/shard_map/all_to_all | solution.py:39
  33.9 1.8 %collective-permute-start.4 = (f32[64]{0:T(128)S(1)}, f32[64]{0:T(128)S(1)}, u32[]{:S(2)}, u32[]{:S(2)}) collective-permute-start(f32[64]{0:T(128)S(1)} %fusion), channel_id=1, source_target_pairs={{0,8},{8,0},{16,24},{24,16},{1,9},{9,1},{17,25},{25,17},{2,10},{10... | collective-permute-start | bytes 776 | tf_op jit(solution)/shard_map/ppermute | solution.py:65
  35.7 1.9 %collective-permute-done.4 = f32[64]{0:T(128)S(1)} collective-permute-done((f32[64]{0:T(128)S(1)}, f32[64]{0:T(128)S(1)}, u32[]{:S(2)}, u32[]{:S(2)}) %collective-permute-start.4) | collective-permute-done | bytes 288 | tf_op jit(solution)/shard_map/ppermute | solution.py:65
  37.6 1.7 %collective-permute-start.5 = (f32[64]{0:T(128)S(1)}, f32[64]{0:T(128)S(1)}, u32[]{:S(2)}, u32[]{:S(2)}) collective-permute-start(f32[64]{0:T(128)S(1)} %add.141), channel_id=1, source_target_pairs={{0,16},{8,24},{16,0},{24,8},{1,17},{9,25},{17,1},{25,9},{2,18},{10... | collective-permute-start | bytes 776 | tf_op jit(solution)/shard_map/ppermute | solution.py:65
  39.3 5.1 %all-to-all-done = f32[32,2,1152]{2,1,0:T(2,128)S(1)} async-done(((f32[32,2,1152]{2,1,0:T(2,128)}), f32[32,2,1152]{2,1,0:T(2,128)S(1)}, u32[]{:S(2)}, u32[]{:S(2)}) %all-to-all-start) | async-done | bytes 294944 | tf_op jit(solution)/shard_map/all_to_all | solution.py:39
  44.9 0.9 broadcast_in_dim.105
  45.8 2.9 %all-to-all-start.1 = ((bf16[32,2,2048]{2,1,0:T(2,128)(2,1)}), bf16[32,2,2048]{2,1,0:T(2,128)(2,1)S(1)}, u32[]{:S(2)}, u32[]{:S(2)}) async-start(bf16[32,2,2048]{2,1,0:T(2,128)(2,1)} %bitcast.16), calls=%async_computation.1 | async-start | bytes 524288 | tf_op jit(solution)/shard_map/all_to_all | solution.py:39
  48.7 3.6 %fusion.3 = f32[64,1024]{1,0:T(8,128)S(1)} fusion(bf16[1024,2048]{1,0:T(8,128)(2,1)} %param.19, f32[2048]{0:T(1024)S(1)} %copy-done.2, f32[64]{0:T(128)S(1)} %add_rsqrt_fusion.1, bf16[64,2048]{1,0:T(8,128)(2,1)S(1)} %gather_fusion, pred[64]{0:T(512)(128)(4,1)S(1)} %get-tuple-element.13), kind=kOutput, calls=%fused_computation.11 | convolution fusion | flops 269090816 | bytes 4727104 | tf_op jit(solution)/shard_map/dot_general | solution.py:18
  52.3 1.8 %collective-permute-start.6 = (f32[64,1024]{1,0:T(8,128)S(1)}, f32[64,1024]{1,0:T(8,128)S(1)}, u32[]{:S(2)}, u32[]{:S(2)}) collective-permute-start(f32[64,1024]{1,0:T(8,128)S(1)} %fusion.3), channel_id=1, source_target_pairs={{0,8},{8,0},{16,24},{24,16},{1,9},{9,1},{17,25},{25,17},{2,10},{10... | collective-permute-start | bytes 786440 | tf_op jit(solution)/shard_map/ppermute | solution.py:65
  54.1 4.8 %all-to-all-done.1 = bf16[32,2,2048]{2,1,0:T(2,128)(2,1)S(1)} async-done(((bf16[32,2,2048]{2,1,0:T(2,128)(2,1)}), bf16[32,2,2048]{2,1,0:T(2,128)(2,1)S(1)}, u32[]{:S(2)}, u32[]{:S(2)}) %all-to-all-start.1) | async-done | bytes 262176 | tf_op jit(solution)/shard_map/all_to_all | solution.py:39
  59.1 3.6 %fusion.40 = f32[64,1024]{1,0:T(8,128)S(1)} fusion(bf16[64,2048]{1,0:T(8,128)(2,1)S(1)} %reshape.183, bf16[1024,2048]{1,0:T(8,128)(2,1)} %param.19), kind=kOutput, calls=%fused_computation.104 | convolution fusion | flops 268435456 | bytes 4718592 | tf_op jit(solution)/shard_map/dot_general | solution.py:18
  62.7 1.0 collective-permute-start.8
  63.7 0.6 collective-permute-start.7
  64.3 6.9 %collective-permute-done.8 = f32[64,1024]{1,0:T(8,128)S(1)} collective-permute-done((f32[64,1024]{1,0:T(8,128)S(1)}, f32[64,1024]{1,0:T(8,128)S(1)}, u32[]{:S(2)}, u32[]{:S(2)}) %collective-permute-start.8) | collective-permute-done | bytes 262176 | tf_op jit(solution)/shard_map/ppermute | solution.py:65
  71.2 1.0 collective-permute-start.9
  72.4 6.5 %collective-permute-done.9 = f32[64,1024]{1,0:T(8,128)S(1)} collective-permute-done((f32[64,1024]{1,0:T(8,128)S(1)}, f32[64,1024]{1,0:T(8,128)S(1)}, u32[]{:S(2)}, u32[]{:S(2)}) %collective-permute-start.9) | collective-permute-done | bytes 262176 | tf_op jit(solution)/shard_map/ppermute | solution.py:65
  79.1 0.7 reshape.213
  79.8 3.3 %all-to-all-start.2 = ((f32[8,1,256]{2,1,0:T(1,128)}), f32[8,1,256]{2,1,0:T(1,128)S(1)}, u32[]{:S(2)}, u32[]{:S(2)}) async-start(f32[8,1,256]{2,1,0:T(1,128)} %reshape.213), calls=%async_computation.2 | async-start | bytes 16384 | tf_op jit(solution)/shard_map/all_to_all | solution.py:39
  83.2 5.5 %all-to-all-done.2 = f32[8,1,256]{2,1,0:T(1,128)S(1)} async-done(((f32[8,1,256]{2,1,0:T(1,128)}), f32[8,1,256]{2,1,0:T(1,128)S(1)}, u32[]{:S(2)}, u32[]{:S(2)}) %all-to-all-start.2) | async-done | bytes 8224 | tf_op jit(solution)/shard_map/all_to_all | solution.py:39
  88.7 0.5 broadcast.140
  89.2 0.7 reduce.2
  90.0 0.6 multiply_add_fusion
  90.6 3.1 %fusion.7 = f32[64,2048]{1,0:T(8,128)S(1)} fusion(bf16[1024,2048]{1,0:T(8,128)(2,1)} %param.19, f32[64,1024]{1,0:T(8,128)S(1)} %get-tuple-element.12, f32[64,1024]{1,0:T(8,128)S(1)} %get-tuple-element.11, f32[64]{0:T(128)S(1)} %get-tuple-element.24, f32[64]{0:T(128)S(1)} %get-tuple-element.23, f32[64]{0:T(128)S(1)} %get-tuple-element.21, ...), kind=kOutput, calls=%fused_computation.28 | convolution fusion | flops 269025280 | bytes 5243904 | tf_op jit(solution)/shard_map/dot_general | solution.py:204
  93.8 0.3 reshape.185
  94.3 1.4 %collective-permute-done.10 = f32[4,4,2,2048]{3,2,1,0:T(2,128)S(1)} collective-permute-done((f32[4,4,2,2048]{3,2,1,0:T(2,128)S(1)}, f32[4,4,2,2048]{3,2,1,0:T(2,128)S(1)}, u32[]{:S(2)}, u32[]{:S(2)}) %collective-permute-start.10) | collective-permute-done | bytes 262176 | tf_op jit(solution)/shard_map/ppermute | solution.py:208
  95.7 0.8 bitcast_add_fusion
  96.5 3.5 %all-to-all-start.3 = ((f32[16,2,2048]{2,1,0:T(2,128)}), f32[16,2,2048]{2,1,0:T(2,128)S(1)}, u32[]{:S(2)}, u32[]{:S(2)}) async-start(f32[16,2,2048]{2,1,0:T(2,128)} %bitcast.26), calls=%async_computation.3 | async-start | bytes 524288 | tf_op jit(solution)/shard_map/all_to_all | solution.py:39
  100.1 11.1 %all-to-all-done.3 = f32[16,2,2048]{2,1,0:T(2,128)S(1)} async-done(((f32[16,2,2048]{2,1,0:T(2,128)}), f32[16,2,2048]{2,1,0:T(2,128)S(1)}, u32[]{:S(2)}, u32[]{:S(2)}) %all-to-all-start.3) | async-done | bytes 262176 | tf_op jit(solution)/shard_map/all_to_all | solution.py:39
  111.6 0.7 broadcast_in_dim.111
  112.3 2.6 %all-to-all-start.4 = ((bf16[32,2,1024]{2,1,0:T(2,128)(2,1)}), bf16[32,2,1024]{2,1,0:T(2,128)(2,1)S(1)}, u32[]{:S(2)}, u32[]{:S(2)}) async-start(bf16[32,2,1024]{2,1,0:T(2,128)(2,1)} %bitcast.33), calls=%async_computation.4 | async-start | bytes 262144 | tf_op jit(solution)/shard_map/all_to_all | solution.py:39
  115.6 7.7 %all-to-all-done.4 = bf16[32,2,1024]{2,1,0:T(2,128)(2,1)S(1)} async-done(((bf16[32,2,1024]{2,1,0:T(2,128)(2,1)}), bf16[32,2,1024]{2,1,0:T(2,128)(2,1)S(1)}, u32[]{:S(2)}, u32[]{:S(2)}) %all-to-all-start.4) | async-done | bytes 131104 | tf_op jit(solution)/shard_map/all_to_all | solution.py:39
  123.3 4.8 %fusion.37 = f32[2048,1024]{1,0:T(8,128)} fusion(bf16[64,1024]{1,0:T(8,128)(2,1)S(1)} %reshape.190, bf16[64,2048]{1,0:T(8,128)(2,1)S(1)} %gather_fusion, pred[64]{0:T(512)(128)(4,1)S(1)} %get-tuple-element.13), kind=kOutput, calls=%fused_computation.101 | convolution fusion | flops 268566528 | bytes 8781888 | tf_op jit(solution)/shard_map/dot_general | solution.py:24
  128.1 4.8 %fusion.15 = f32[2048,1024]{1,0:T(8,128)} fusion(bf16[64,1024]{1,0:T(8,128)(2,1)S(1)} %reshape.190, bf16[64,2048]{1,0:T(8,128)(2,1)S(1)} %gather_fusion.1, pred[64]{0:T(512)(128)(4,1)S(1)} %get-tuple-element.13), kind=kOutput, calls=%fused_computation.37 | convolution fusion | flops 268566528 | bytes 8781888 | tf_op jit(solution)/shard_map/dot_general | solution.py:24
  (55 shorter events, 3.0 us)
Async XLA Ops:
  0.6 18.0 %copy-start = (f32[2048]{0:T(1024)S(1)}, f32[2048]{0:T(1024)}, u32[]{:S(2)}) copy-start(f32[2048]{0:T(1024)} %param.18) | copy-start | bytes 24580
  3.6 14.1 %collective-permute-start.1 = (bf16[2,16,2048]{2,1,0:T(8,128)(2,1)S(1)}, bf16[2,16,2048]{2,1,0:T(8,128)(2,1)S(1)}, u32[]{:S(2)}, u32[]{:S(2)}) collective-permute-start(bf16[2,16,2048]{2,1,0:T(8,128)(2,1)S(1)} %get-tuple-element.20), channel_id=1, source_target_pairs={{0,2},{1,3},{2,0},{3,1},{4,6},{5,7},{6,4},{7,5},{8,10},{9,11},{10,... | collective-permute-start | bytes 393224 | tf_op jit(solution)/shard_map/ppermute | solution.py:45
  7.7 10.0 %collective-permute-start = (bf16[2,16,2048]{2,1,0:T(8,128)(2,1)S(1)}, bf16[2,16,2048]{2,1,0:T(8,128)(2,1)S(1)}, u32[]{:S(2)}, u32[]{:S(2)}) collective-permute-start(bf16[2,16,2048]{2,1,0:T(8,128)(2,1)S(1)} %get-tuple-element.20), channel_id=1, source_target_pairs={{0,1},{1,2},{2,3},{3,0},{4,5},{5,6},{6,7},{7,4},{8,9},{9,10},{10,1... | collective-permute-start | bytes 393224 | tf_op jit(solution)/shard_map/ppermute | solution.py:45
  9.3 9.2 %collective-permute-start.2 = (bf16[2,16,2048]{2,1,0:T(8,128)(2,1)S(1)}, bf16[2,16,2048]{2,1,0:T(8,128)(2,1)S(1)}, u32[]{:S(2)}, u32[]{:S(2)}) collective-permute-start(bf16[2,16,2048]{2,1,0:T(8,128)(2,1)S(1)} %get-tuple-element.20), channel_id=1, source_target_pairs={{0,3},{1,0},{2,1},{3,2},{4,7},{5,4},{6,5},{7,6},{8,11},{9,8},{10,9... | collective-permute-start | bytes 393224 | tf_op jit(solution)/shard_map/ppermute | solution.py:45
  18.5 2.0 %collective-permute-start.3 = (bf16[4,2,16,2048]{3,2,1,0:T(8,128)(2,1)S(1)}, bf16[4,2,16,2048]{3,2,1,0:T(8,128)(2,1)S(1)}, u32[]{:S(2)}, u32[]{:S(2)}) collective-permute-start(bf16[4,2,16,2048]{3,2,1,0:T(8,128)(2,1)S(1)} %get-tuple-element.18), channel_id=1, source_target_pairs={{0,4},{4,0},{1,5},{5,1},{2,6},{6,2},{3,7},{7,3},{8,12},{12,8},{9,1... | collective-permute-start | bytes 1572872 | tf_op jit(solution)/shard_map/ppermute | solution.py:45
  22.2 3.5 %copy-start.1 = (bf16[2048,1024]{1,0:T(8,128)(2,1)S(1)}, bf16[2048,1024]{1,0:T(8,128)(2,1)}, u32[]{:S(2)}) copy-start(bf16[2048,1024]{1,0:T(8,128)(2,1)} %param.21) | copy-start | bytes 12582916
  25.7 23.0 %copy-start.2 = (f32[2048]{0:T(1024)S(1)}, f32[2048]{0:T(1024)}, u32[]{:S(2)}) copy-start(f32[2048]{0:T(1024)} %param.17) | copy-start | bytes 24580
  27.6 16.8 %all-to-all-start = ((f32[32,2,1152]{2,1,0:T(2,128)}), f32[32,2,1152]{2,1,0:T(2,128)S(1)}, u32[]{:S(2)}, u32[]{:S(2)}) async-start(f32[32,2,1152]{2,1,0:T(2,128)} %pad_maximum_fusion.1), calls=%async_computation | async-start | bytes 589824 | tf_op jit(solution)/shard_map/all_to_all | solution.py:39
  33.9 3.7 %collective-permute-start.4 = (f32[64]{0:T(128)S(1)}, f32[64]{0:T(128)S(1)}, u32[]{:S(2)}, u32[]{:S(2)}) collective-permute-start(f32[64]{0:T(128)S(1)} %fusion), channel_id=1, source_target_pairs={{0,8},{8,0},{16,24},{24,16},{1,9},{9,1},{17,25},{25,17},{2,10},{10... | collective-permute-start | bytes 776 | tf_op jit(solution)/shard_map/ppermute | solution.py:65
  37.6 11.1 %collective-permute-start.5 = (f32[64]{0:T(128)S(1)}, f32[64]{0:T(128)S(1)}, u32[]{:S(2)}, u32[]{:S(2)}) collective-permute-start(f32[64]{0:T(128)S(1)} %add.141), channel_id=1, source_target_pairs={{0,16},{8,24},{16,0},{24,8},{1,17},{9,25},{17,1},{25,9},{2,18},{10... | collective-permute-start | bytes 776 | tf_op jit(solution)/shard_map/ppermute | solution.py:65
  45.8 13.2 %all-to-all-start.1 = ((bf16[32,2,2048]{2,1,0:T(2,128)(2,1)}), bf16[32,2,2048]{2,1,0:T(2,128)(2,1)S(1)}, u32[]{:S(2)}, u32[]{:S(2)}) async-start(bf16[32,2,2048]{2,1,0:T(2,128)(2,1)} %bitcast.16), calls=%async_computation.1 | async-start | bytes 524288 | tf_op jit(solution)/shard_map/all_to_all | solution.py:39
  48.7 14.9 %copy-start.3 = (s32[4,256]{1,0:T(4,128)S(1)}, s32[4,256]{1,0:T(4,128)}, u32[]{:S(2)}) copy-start(s32[4,256]{1,0:T(4,128)} %param.14) | copy-start | bytes 12292
  52.3 11.3 %collective-permute-start.6 = (f32[64,1024]{1,0:T(8,128)S(1)}, f32[64,1024]{1,0:T(8,128)S(1)}, u32[]{:S(2)}, u32[]{:S(2)}) collective-permute-start(f32[64,1024]{1,0:T(8,128)S(1)} %fusion.3), channel_id=1, source_target_pairs={{0,8},{8,0},{16,24},{24,16},{1,9},{9,1},{17,25},{25,17},{2,10},{10... | collective-permute-start | bytes 786440 | tf_op jit(solution)/shard_map/ppermute | solution.py:65
  62.7 8.5 %collective-permute-start.8 = (f32[64,1024]{1,0:T(8,128)S(1)}, f32[64,1024]{1,0:T(8,128)S(1)}, u32[]{:S(2)}, u32[]{:S(2)}) collective-permute-start(f32[64,1024]{1,0:T(8,128)S(1)} %fusion.40), channel_id=1, source_target_pairs={{0,8},{8,0},{16,24},{24,16},{1,9},{9,1},{17,25},{25,17},{2,10},{10... | collective-permute-start | bytes 786440 | tf_op jit(solution)/shard_map/ppermute | solution.py:65
  63.7 8.7 %collective-permute-start.7 = (f32[64,1024]{1,0:T(8,128)S(1)}, f32[64,1024]{1,0:T(8,128)S(1)}, u32[]{:S(2)}, u32[]{:S(2)}) collective-permute-start(f32[64,1024]{1,0:T(8,128)S(1)} %add.145), channel_id=1, source_target_pairs={{0,16},{8,24},{16,0},{24,8},{1,17},{9,25},{17,1},{25,9},{2,18},{10... | collective-permute-start | bytes 786440 | tf_op jit(solution)/shard_map/ppermute | solution.py:65
  71.2 7.7 %collective-permute-start.9 = (f32[64,1024]{1,0:T(8,128)S(1)}, f32[64,1024]{1,0:T(8,128)S(1)}, u32[]{:S(2)}, u32[]{:S(2)}) collective-permute-start(f32[64,1024]{1,0:T(8,128)S(1)} %add.151), channel_id=1, source_target_pairs={{0,16},{8,24},{16,0},{24,8},{1,17},{9,25},{17,1},{25,9},{2,18},{10... | collective-permute-start | bytes 786440 | tf_op jit(solution)/shard_map/ppermute | solution.py:65
  79.8 8.9 %all-to-all-start.2 = ((f32[8,1,256]{2,1,0:T(1,128)}), f32[8,1,256]{2,1,0:T(1,128)S(1)}, u32[]{:S(2)}, u32[]{:S(2)}) async-start(f32[8,1,256]{2,1,0:T(1,128)} %reshape.213), calls=%async_computation.2 | async-start | bytes 16384 | tf_op jit(solution)/shard_map/all_to_all | solution.py:39
  94.1 1.6 %collective-permute-start.10 = (f32[4,4,2,2048]{3,2,1,0:T(2,128)S(1)}, f32[4,4,2,2048]{3,2,1,0:T(2,128)S(1)}, u32[]{:S(2)}, u32[]{:S(2)}) collective-permute-start(f32[4,4,2,2048]{3,2,1,0:T(2,128)S(1)} %dynamic-slice_bitcast_fusion), channel_id=1, source_target_pairs={{0,4},{4,0},{1,5},{5,1},{2,6},{6,2},{3,7},{7,3},{8,12},{12,8},{9,1... | collective-permute-start | bytes 786440 | tf_op jit(solution)/shard_map/ppermute | solution.py:208
  96.5 14.7 %all-to-all-start.3 = ((f32[16,2,2048]{2,1,0:T(2,128)}), f32[16,2,2048]{2,1,0:T(2,128)S(1)}, u32[]{:S(2)}, u32[]{:S(2)}) async-start(f32[16,2,2048]{2,1,0:T(2,128)} %bitcast.26), calls=%async_computation.3 | async-start | bytes 524288 | tf_op jit(solution)/shard_map/all_to_all | solution.py:39
  112.3 11.0 %all-to-all-start.4 = ((bf16[32,2,1024]{2,1,0:T(2,128)(2,1)}), bf16[32,2,1024]{2,1,0:T(2,128)(2,1)S(1)}, u32[]{:S(2)}, u32[]{:S(2)}) async-start(bf16[32,2,1024]{2,1,0:T(2,128)(2,1)} %bitcast.33), calls=%async_computation.4 | async-start | bytes 262144 | tf_op jit(solution)/shard_map/all_to_all | solution.py:39

commit v10 on v9

--- a/solution.py
+++ b/solution.py
@@ -138,7 +138,7 @@
     target_norm = (feature_all.astype(jnp.float32) * target_scale[:, None] * target_gain).astype(
         jnp.bfloat16
     )
-    target_logit = section_sum(contract_last(target_norm, head))
+    target_part = contract_last(target_norm, head)
     piece = width // groups
     spare = pad_cols(-(-piece // per_dev))
     gain_piece = lax.dynamic_slice_in_dim(draft_gain, (my_mp * count_dp + my_dp) * piece, piece)
@@ -150,7 +150,8 @@
         ],
         axis=2,
     )
-    got1 = exchange(send1, ALL).reshape(count_sec, groups, per_dev, -1)
+    got1, target_logit = lax.optimization_barrier((exchange(send1, ALL), section_sum(target_part)))
+    got1 = got1.reshape(count_sec, groups, per_dev, -1)
     hidden = (
         jnp.sum(got1[..., :block], axis=0).transpose(1, 0, 2).reshape(per_dev, groups * block)
     )

time: 135 us -> 148 us (1.096)
  blocking collectives: 0 us -> 15.1 us
  starting transfers between devices: 34.5 us -> 30.9 us
  waiting for transfers between devices: 58.1 us -> 60.8 us
    all_to_all x0 -> x1, blocking collectives: none -> 15.1 us  [exchange(): return lax.all_to_all(send, axes, split_axis=0, concat_axis=0, tiled=True)]
    ppermute x6, waiting for transfers between devices: 15.2 us -> 28 us  [section_sum(): x = x + lax.ppermute(x, 'section', [(i, i ^ step) for i in range(count)])]
    all_to_all x5 -> x4, waiting for transfers between devices: 34.2 us -> 24.3 us  [exchange(): return lax.all_to_all(send, axes, split_axis=0, concat_axis=0, tiled=True)]
    all_to_all x5 -> x4, starting transfers between devices: 18.4 us -> 13.9 us  [exchange(): return lax.all_to_all(send, axes, split_axis=0, concat_axis=0, tiled=True)]
  transfers between devices with their start and end apart: 16 -> 15, of which waited for: 12 -> 11; matrix products, arithmetic and copies ran while one was open for 8% -> 7% of each run, Pallas kernels for 0% -> 0%
where the time goes in v10:
time: 148 us; the launch traced here: 147 us
  waiting for transfers between devices  60.8 us (41%)
  starting transfers between devices  30.9 us (21%)
  matrix products  23.8 us (16%)
  blocking collectives  15.1 us (10%)
  local copies, waits for them, and re-layouts  6.91 us (5%)
  other arithmetic  6.27 us (4%)
  between operations  3.44 us (2%)
    ppermute x6, waiting for transfers between devices, section_sum(): x = x + lax.ppermute(x, 'section', [(i, i ^ step) for i in range(count)])  28 us
    all_to_all x4, waiting for transfers between devices, exchange(): return lax.all_to_all(send, axes, split_axis=0, concat_axis=0, tiled=True)  24.3 us
    all_to_all x1, blocking collectives, exchange(): return lax.all_to_all(send, axes, split_axis=0, concat_axis=0, tiled=True)  15.1 us
    all_to_all x4, starting transfers between devices, exchange(): return lax.all_to_all(send, axes, split_axis=0, concat_axis=0, tiled=True)  13.9 us
    dot_general x2, matrix products, contract_first(): lax.dot_general(operand, weights, (((0,), (0,)), ((), ())), preferred_ele...  9.52 us
    ppermute x6, starting transfers between devices, section_sum(): x = x + lax.ppermute(x, 'section', [(i, i ^ step) for i in range(count)])  8.81 us
    ppermute x4, starting transfers between devices, shifted(): lax.ppermute(x, axis, [(i, (i + k) % count) for i in range(count)])  8.02 us
    dot_general x2, matrix products, contract_last(): lax.dot_general(operand, weights, (((1,), (1,)), ((), ())), preferred_ele...  7.18 us
  transfers between devices with their start and end apart: 15, of which 11 were waited for; matrix products, arithmetic and copies ran while one was open for 7% of the time, Pallas kernels for 0%

profile of v10, /device:TPU:0, one launch (start us, length us, event | category | flops | bytes accessed | tf_op | source)
XLA Modules:
  0.0 147.2 jit_solution(4891847961806030911)
XLA Ops:
  0.7 1.2 dynamic_slice.15
  2.6 1.0 constant_dynamic-slice_fusion
  3.6 4.1 %collective-permute-start.1 = (bf16[2,16,2048]{2,1,0:T(8,128)(2,1)S(1)}, bf16[2,16,2048]{2,1,0:T(8,128)(2,1)S(1)}, u32[]{:S(2)}, u32[]{:S(2)}) collective-permute-start(bf16[2,16,2048]{2,1,0:T(8,128)(2,1)S(1)} %get-tuple-element.23), channel_id=1, source_target_pairs={{0,2},{1,3},{2,0},{3,1},{4,6},{5,7},{6,4},{7,5},{8,10},{9,11},{10,... | collective-permute-start | bytes 393224 | tf_op jit(solution)/shard_map/ppermute | solution.py:45
  7.7 1.6 %collective-permute-start = (bf16[2,16,2048]{2,1,0:T(8,128)(2,1)S(1)}, bf16[2,16,2048]{2,1,0:T(8,128)(2,1)S(1)}, u32[]{:S(2)}, u32[]{:S(2)}) collective-permute-start(bf16[2,16,2048]{2,1,0:T(8,128)(2,1)S(1)} %get-tuple-element.23), channel_id=1, source_target_pairs={{0,1},{1,2},{2,3},{3,0},{4,5},{5,6},{6,7},{7,4},{8,9},{9,10},{10,1... | collective-permute-start | bytes 393224 | tf_op jit(solution)/shard_map/ppermute | solution.py:45
  9.3 2.2 %collective-permute-start.2 = (bf16[2,16,2048]{2,1,0:T(8,128)(2,1)S(1)}, bf16[2,16,2048]{2,1,0:T(8,128)(2,1)S(1)}, u32[]{:S(2)}, u32[]{:S(2)}) collective-permute-start(bf16[2,16,2048]{2,1,0:T(8,128)(2,1)S(1)} %get-tuple-element.23), channel_id=1, source_target_pairs={{0,3},{1,0},{2,1},{3,2},{4,7},{5,4},{6,5},{7,6},{8,11},{9,8},{10,9... | collective-permute-start | bytes 393224 | tf_op jit(solution)/shard_map/ppermute | solution.py:45
  11.5 0.8 select_reduce_fusion.5
  12.3 5.4 %collective-permute-done.1 = bf16[2,16,2048]{2,1,0:T(8,128)(2,1)S(1)} collective-permute-done((bf16[2,16,2048]{2,1,0:T(8,128)(2,1)S(1)}, bf16[2,16,2048]{2,1,0:T(8,128)(2,1)S(1)}, u32[]{:S(2)}, u32[]{:S(2)}) %collective-permute-start.1) | collective-permute-done | bytes 131104 | tf_op jit(solution)/shard_map/ppermute | solution.py:45
  17.7 0.6 collective-permute-done.2
  18.6 0.8 select_reduce_fusion.4
  19.4 1.0 collective-permute-done.3
  20.6 0.7 gather_fusion.1
  21.4 0.7 gather_fusion
  22.1 0.2 fusion
  22.4 1.7 %collective-permute-start.4 = (f32[64]{0:T(128)S(1)}, f32[64]{0:T(128)S(1)}, u32[]{:S(2)}, u32[]{:S(2)}) collective-permute-start(f32[64]{0:T(128)S(1)} %fusion), channel_id=1, source_target_pairs={{0,8},{8,0},{16,24},{24,16},{1,9},{9,1},{17,25},{25,17},{2,10},{10... | collective-permute-start | bytes 776 | tf_op jit(solution)/shard_map/ppermute | solution.py:65
  24.0 3.1 %fusion.16 = f32[64,1024]{1,0:T(8,128)S(1)} fusion(bf16[2048,1024]{1,0:T(8,128)(2,1)} %param.20, bf16[64,2048]{1,0:T(8,128)(2,1)S(1)} %gather_fusion, pred[64]{0:T(512)(128)(4,1)S(1)} %get-tuple-element.16), kind=kOutput, calls=%fused_computation.38 | convolution fusion | flops 268566528 | bytes 4718656 | tf_op jit(solution)/shard_map/dot_general | solution.py:133
  27.1 0.9 convolution_add_fusion
  28.2 1.6 %collective-permute-start.5 = (f32[64]{0:T(128)S(1)}, f32[64]{0:T(128)S(1)}, u32[]{:S(2)}, u32[]{:S(2)}) collective-permute-start(f32[64]{0:T(128)S(1)} %add.144), channel_id=1, source_target_pairs={{0,16},{8,24},{16,0},{24,8},{1,17},{9,25},{17,1},{25,9},{2,18},{10... | collective-permute-start | bytes 776 | tf_op jit(solution)/shard_map/ppermute | solution.py:65
  29.8 0.8 pad_maximum_fusion.1
  30.7 4.5 %all-to-all-start = ((f32[32,2,1152]{2,1,0:T(2,128)}), f32[32,2,1152]{2,1,0:T(2,128)S(1)}, u32[]{:S(2)}, u32[]{:S(2)}) async-start(f32[32,2,1152]{2,1,0:T(2,128)} %pad_maximum_fusion.1), calls=%async_computation | async-start | bytes 589824 | tf_op jit(solution)/shard_map/all_to_all | solution.py:39
  35.2 3.6 %fusion.3 = f32[64,1024]{1,0:T(8,128)S(1)} fusion(bf16[1024,2048]{1,0:T(8,128)(2,1)} %param.19, f32[2048]{0:T(1024)S(1)} %copy-done.2, f32[64]{0:T(128)S(1)} %add_rsqrt_fusion.1, bf16[64,2048]{1,0:T(8,128)(2,1)S(1)} %gather_fusion.1, pred[64]{0:T(512)(128)(4,1)S(1)} %get-tuple-element.16), kind=kOutput, calls=%fused_computation.11 | convolution fusion | flops 269090816 | bytes 4727104 | tf_op jit(solution)/shard_map/dot_general | solution.py:18
  38.8 1.8 %collective-permute-start.6 = (f32[64,1024]{1,0:T(8,128)S(1)}, f32[64,1024]{1,0:T(8,128)S(1)}, u32[]{:S(2)}, u32[]{:S(2)}) collective-permute-start(f32[64,1024]{1,0:T(8,128)S(1)} %fusion.3), channel_id=1, source_target_pairs={{0,8},{8,0},{16,24},{24,16},{1,9},{9,1},{17,25},{25,17},{2,10},{10... | collective-permute-start | bytes 786440 | tf_op jit(solution)/shard_map/ppermute | solution.py:65
  40.6 7.8 %collective-permute-done.6 = f32[64,1024]{1,0:T(8,128)S(1)} collective-permute-done((f32[64,1024]{1,0:T(8,128)S(1)}, f32[64,1024]{1,0:T(8,128)S(1)}, u32[]{:S(2)}, u32[]{:S(2)}) %collective-permute-start.6) | collective-permute-done | bytes 262176 | tf_op jit(solution)/shard_map/ppermute | solution.py:65
  48.5 1.7 %collective-permute-start.7 = (f32[64,1024]{1,0:T(8,128)S(1)}, f32[64,1024]{1,0:T(8,128)S(1)}, u32[]{:S(2)}, u32[]{:S(2)}) collective-permute-start(f32[64,1024]{1,0:T(8,128)S(1)} %add.148), channel_id=1, source_target_pairs={{0,16},{8,24},{16,0},{24,8},{1,17},{9,25},{17,1},{25,9},{2,18},{10... | collective-permute-start | bytes 786440 | tf_op jit(solution)/shard_map/ppermute | solution.py:65
  50.1 6.1 %collective-permute-done.7 = f32[64,1024]{1,0:T(8,128)S(1)} collective-permute-done((f32[64,1024]{1,0:T(8,128)S(1)}, f32[64,1024]{1,0:T(8,128)S(1)}, u32[]{:S(2)}, u32[]{:S(2)}) %collective-permute-start.7) | collective-permute-done | bytes 262176 | tf_op jit(solution)/shard_map/ppermute | solution.py:65
  57.0 15.1 %all_to_all.25 = bf16[32,2,2048]{2,1,0:T(2,128)(2,1)S(1)} all-to-all(bf16[32,2,2048]{2,1,0:T(2,128)(2,1)S(1)} %bitcast.82), channel_id=1, replica_groups=mesh['section'=4,'mp'=2,'dp'=4] {'section','mp','dp'}, dimensions={0} | all-to-all | bytes 524288 | tf_op jit(solution)/shard_map/all_to_all | solution.py:39
  72.1 3.6 %fusion.40 = f32[64,1024]{1,0:T(8,128)S(1)} fusion(bf16[64,2048]{1,0:T(8,128)(2,1)S(1)} %reshape.183, bf16[1024,2048]{1,0:T(8,128)(2,1)} %param.19), kind=kOutput, calls=%fused_computation.104 | convolution fusion | flops 268435456 | bytes 4718592 | tf_op jit(solution)/shard_map/dot_general | solution.py:18
  75.7 1.0 collective-permute-start.8
  76.8 7.6 %collective-permute-done.8 = f32[64,1024]{1,0:T(8,128)S(1)} collective-permute-done((f32[64,1024]{1,0:T(8,128)S(1)}, f32[64,1024]{1,0:T(8,128)S(1)}, u32[]{:S(2)}, u32[]{:S(2)}) %collective-permute-start.8) | collective-permute-done | bytes 262176 | tf_op jit(solution)/shard_map/ppermute | solution.py:65
  84.4 1.0 collective-permute-start.9
  85.6 6.6 %collective-permute-done.9 = f32[64,1024]{1,0:T(8,128)S(1)} collective-permute-done((f32[64,1024]{1,0:T(8,128)S(1)}, f32[64,1024]{1,0:T(8,128)S(1)}, u32[]{:S(2)}, u32[]{:S(2)}) %collective-permute-start.9) | collective-permute-done | bytes 262176 | tf_op jit(solution)/shard_map/ppermute | solution.py:65
  92.1 0.2 exponential_reduce_fusion.1
  92.4 0.7 reshape.213
  93.1 3.3 %all-to-all-start.2 = ((f32[8,1,256]{2,1,0:T(1,128)}), f32[8,1,256]{2,1,0:T(1,128)S(1)}, u32[]{:S(2)}, u32[]{:S(2)}) async-start(f32[8,1,256]{2,1,0:T(1,128)} %reshape.213), calls=%async_computation.2 | async-start | bytes 16384 | tf_op jit(solution)/shard_map/all_to_all | solution.py:39
  96.4 5.5 %all-to-all-done.2 = f32[8,1,256]{2,1,0:T(1,128)S(1)} async-done(((f32[8,1,256]{2,1,0:T(1,128)}), f32[8,1,256]{2,1,0:T(1,128)S(1)}, u32[]{:S(2)}, u32[]{:S(2)}) %all-to-all-start.2) | async-done | bytes 8224 | tf_op jit(solution)/shard_map/all_to_all | solution.py:39
  101.9 0.5 broadcast.140
  102.4 0.7 reduce.2
  103.2 0.6 multiply_add_fusion
  103.8 3.1 %fusion.7 = f32[64,2048]{1,0:T(8,128)S(1)} fusion(bf16[1024,2048]{1,0:T(8,128)(2,1)} %param.19, f32[64,1024]{1,0:T(8,128)S(1)} %add.149, f32[64,1024]{1,0:T(8,128)S(1)} %get-tuple-element.15, f32[64]{0:T(128)S(1)} %get-tuple-element.27, f32[64]{0:T(128)S(1)} %get-tuple-element.26, f32[64]{0:T(128)S(1)} %get-tuple-element.24, s32[64]{0:T(128)S(1)} %broadcast_subtract_fusion), kind=kOutput, calls=%fused_computation.28 | convolution fusion | flops 269025280 | bytes 5243904 | tf_op jit(solution)/shard_map/dot_general | solution.py:205
  107.0 0.3 reshape.185
  107.5 1.4 collective-permute-done.10
  108.9 0.8 bitcast_add_fusion
  109.8 3.5 %all-to-all-start.3 = ((f32[16,2,2048]{2,1,0:T(2,128)}), f32[16,2,2048]{2,1,0:T(2,128)S(1)}, u32[]{:S(2)}, u32[]{:S(2)}) async-start(f32[16,2,2048]{2,1,0:T(2,128)} %bitcast.26), calls=%async_computation.3 | async-start | bytes 524288 | tf_op jit(solution)/shard_map/all_to_all | solution.py:39
  113.4 11.1 %all-to-all-done.3 = f32[16,2,2048]{2,1,0:T(2,128)S(1)} async-done(((f32[16,2,2048]{2,1,0:T(2,128)}), f32[16,2,2048]{2,1,0:T(2,128)S(1)}, u32[]{:S(2)}, u32[]{:S(2)}) %all-to-all-start.3) | async-done | bytes 262176 | tf_op jit(solution)/shard_map/all_to_all | solution.py:39
  124.8 0.7 broadcast_in_dim.111
  125.6 2.6 %all-to-all-start.4 = ((bf16[32,2,1024]{2,1,0:T(2,128)(2,1)}), bf16[32,2,1024]{2,1,0:T(2,128)(2,1)S(1)}, u32[]{:S(2)}, u32[]{:S(2)}) async-start(bf16[32,2,1024]{2,1,0:T(2,128)(2,1)} %bitcast.33), calls=%async_computation.4 | async-start | bytes 262144 | tf_op jit(solution)/shard_map/all_to_all | solution.py:39
  128.8 7.7 %all-to-all-done.4 = bf16[32,2,1024]{2,1,0:T(2,128)(2,1)S(1)} async-done(((bf16[32,2,1024]{2,1,0:T(2,128)(2,1)}), bf16[32,2,1024]{2,1,0:T(2,128)(2,1)S(1)}, u32[]{:S(2)}, u32[]{:S(2)}) %all-to-all-start.4) | async-done | bytes 131104 | tf_op jit(solution)/shard_map/all_to_all | solution.py:39
  136.6 4.8 %fusion.37 = f32[2048,1024]{1,0:T(8,128)} fusion(bf16[64,1024]{1,0:T(8,128)(2,1)S(1)} %reshape.190, bf16[64,2048]{1,0:T(8,128)(2,1)S(1)} %gather_fusion.1, pred[64]{0:T(512)(128)(4,1)S(1)} %get-tuple-element.16), kind=kOutput, calls=%fused_computation.101 | convolution fusion | flops 268566528 | bytes 8781888 | tf_op jit(solution)/shard_map/dot_general | solution.py:24
  141.4 4.8 %fusion.15 = f32[2048,1024]{1,0:T(8,128)} fusion(bf16[64,1024]{1,0:T(8,128)(2,1)S(1)} %reshape.190, bf16[64,2048]{1,0:T(8,128)(2,1)S(1)} %gather_fusion, pred[64]{0:T(512)(128)(4,1)S(1)} %get-tuple-element.16), kind=kOutput, calls=%fused_computation.37 | convolution fusion | flops 268566528 | bytes 8781888 | tf_op jit(solution)/shard_map/dot_general | solution.py:24
  (55 shorter events, 2.5 us)
Async XLA Ops:
  0.6 17.9 %copy-start = (f32[2048]{0:T(1024)S(1)}, f32[2048]{0:T(1024)}, u32[]{:S(2)}) copy-start(f32[2048]{0:T(1024)} %param.18) | copy-start | bytes 24580
  3.6 14.1 %collective-permute-start.1 = (bf16[2,16,2048]{2,1,0:T(8,128)(2,1)S(1)}, bf16[2,16,2048]{2,1,0:T(8,128)(2,1)S(1)}, u32[]{:S(2)}, u32[]{:S(2)}) collective-permute-start(bf16[2,16,2048]{2,1,0:T(8,128)(2,1)S(1)} %get-tuple-element.23), channel_id=1, source_target_pairs={{0,2},{1,3},{2,0},{3,1},{4,6},{5,7},{6,4},{7,5},{8,10},{9,11},{10,... | collective-permute-start | bytes 393224 | tf_op jit(solution)/shard_map/ppermute | solution.py:45
  7.7 10.0 %collective-permute-start = (bf16[2,16,2048]{2,1,0:T(8,128)(2,1)S(1)}, bf16[2,16,2048]{2,1,0:T(8,128)(2,1)S(1)}, u32[]{:S(2)}, u32[]{:S(2)}) collective-permute-start(bf16[2,16,2048]{2,1,0:T(8,128)(2,1)S(1)} %get-tuple-element.23), channel_id=1, source_target_pairs={{0,1},{1,2},{2,3},{3,0},{4,5},{5,6},{6,7},{7,4},{8,9},{9,10},{10,1... | collective-permute-start | bytes 393224 | tf_op jit(solution)/shard_map/ppermute | solution.py:45
  9.3 9.1 %collective-permute-start.2 = (bf16[2,16,2048]{2,1,0:T(8,128)(2,1)S(1)}, bf16[2,16,2048]{2,1,0:T(8,128)(2,1)S(1)}, u32[]{:S(2)}, u32[]{:S(2)}) collective-permute-start(bf16[2,16,2048]{2,1,0:T(8,128)(2,1)S(1)} %get-tuple-element.23), channel_id=1, source_target_pairs={{0,3},{1,0},{2,1},{3,2},{4,7},{5,4},{6,5},{7,6},{8,11},{9,8},{10,9... | collective-permute-start | bytes 393224 | tf_op jit(solution)/shard_map/ppermute | solution.py:45
  18.4 2.0 %collective-permute-start.3 = (bf16[4,2,16,2048]{3,2,1,0:T(8,128)(2,1)S(1)}, bf16[4,2,16,2048]{3,2,1,0:T(8,128)(2,1)S(1)}, u32[]{:S(2)}, u32[]{:S(2)}) collective-permute-start(bf16[4,2,16,2048]{3,2,1,0:T(8,128)(2,1)S(1)} %get-tuple-element.21), channel_id=1, source_target_pairs={{0,4},{4,0},{1,5},{5,1},{2,6},{6,2},{3,7},{7,3},{8,12},{12,8},{9,1... | collective-permute-start | bytes 1572872 | tf_op jit(solution)/shard_map/ppermute | solution.py:45
  22.1 5.0 %copy-start.1 = (bf16[2048,1024]{1,0:T(8,128)(2,1)S(1)}, bf16[2048,1024]{1,0:T(8,128)(2,1)}, u32[]{:S(2)}) copy-start(bf16[2048,1024]{1,0:T(8,128)(2,1)} %param.21) | copy-start | bytes 12582916
  22.4 5.8 %collective-permute-start.4 = (f32[64]{0:T(128)S(1)}, f32[64]{0:T(128)S(1)}, u32[]{:S(2)}, u32[]{:S(2)}) collective-permute-start(f32[64]{0:T(128)S(1)} %fusion), channel_id=1, source_target_pairs={{0,8},{8,0},{16,24},{24,16},{1,9},{9,1},{17,25},{25,17},{2,10},{10... | collective-permute-start | bytes 776 | tf_op jit(solution)/shard_map/ppermute | solution.py:65
  27.1 8.1 %copy-start.2 = (f32[2048]{0:T(1024)S(1)}, f32[2048]{0:T(1024)}, u32[]{:S(2)}) copy-start(f32[2048]{0:T(1024)} %param.17) | copy-start | bytes 24580
  28.2 6.9 %collective-permute-start.5 = (f32[64]{0:T(128)S(1)}, f32[64]{0:T(128)S(1)}, u32[]{:S(2)}, u32[]{:S(2)}) collective-permute-start(f32[64]{0:T(128)S(1)} %add.144), channel_id=1, source_target_pairs={{0,16},{8,24},{16,0},{24,8},{1,17},{9,25},{17,1},{25,9},{2,18},{10... | collective-permute-start | bytes 776 | tf_op jit(solution)/shard_map/ppermute | solution.py:65
  30.7 25.6 %all-to-all-start = ((f32[32,2,1152]{2,1,0:T(2,128)}), f32[32,2,1152]{2,1,0:T(2,128)S(1)}, u32[]{:S(2)}, u32[]{:S(2)}) async-start(f32[32,2,1152]{2,1,0:T(2,128)} %pad_maximum_fusion.1), calls=%async_computation | async-start | bytes 589824 | tf_op jit(solution)/shard_map/all_to_all | solution.py:39
  38.8 38.0 %copy-start.3 = (s32[4,256]{1,0:T(4,128)S(1)}, s32[4,256]{1,0:T(4,128)}, u32[]{:S(2)}) copy-start(s32[4,256]{1,0:T(4,128)} %param.14) | copy-start | bytes 12292
  38.8 9.6 %collective-permute-start.6 = (f32[64,1024]{1,0:T(8,128)S(1)}, f32[64,1024]{1,0:T(8,128)S(1)}, u32[]{:S(2)}, u32[]{:S(2)}) collective-permute-start(f32[64,1024]{1,0:T(8,128)S(1)} %fusion.3), channel_id=1, source_target_pairs={{0,8},{8,0},{16,24},{24,16},{1,9},{9,1},{17,25},{25,17},{2,10},{10... | collective-permute-start | bytes 786440 | tf_op jit(solution)/shard_map/ppermute | solution.py:65
  48.5 7.8 %collective-permute-start.7 = (f32[64,1024]{1,0:T(8,128)S(1)}, f32[64,1024]{1,0:T(8,128)S(1)}, u32[]{:S(2)}, u32[]{:S(2)}) collective-permute-start(f32[64,1024]{1,0:T(8,128)S(1)} %add.148), channel_id=1, source_target_pairs={{0,16},{8,24},{16,0},{24,8},{1,17},{9,25},{17,1},{25,9},{2,18},{10... | collective-permute-start | bytes 786440 | tf_op jit(solution)/shard_map/ppermute | solution.py:65
  75.7 8.6 %collective-permute-start.8 = (f32[64,1024]{1,0:T(8,128)S(1)}, f32[64,1024]{1,0:T(8,128)S(1)}, u32[]{:S(2)}, u32[]{:S(2)}) collective-permute-start(f32[64,1024]{1,0:T(8,128)S(1)} %fusion.40), channel_id=1, source_target_pairs={{0,8},{8,0},{16,24},{24,16},{1,9},{9,1},{17,25},{25,17},{2,10},{10... | collective-permute-start | bytes 786440 | tf_op jit(solution)/shard_map/ppermute | solution.py:65
  84.4 7.8 %collective-permute-start.9 = (f32[64,1024]{1,0:T(8,128)S(1)}, f32[64,1024]{1,0:T(8,128)S(1)}, u32[]{:S(2)}, u32[]{:S(2)}) collective-permute-start(f32[64,1024]{1,0:T(8,128)S(1)} %add.151), channel_id=1, source_target_pairs={{0,16},{8,24},{16,0},{24,8},{1,17},{9,25},{17,1},{25,9},{2,18},{10... | collective-permute-start | bytes 786440 | tf_op jit(solution)/shard_map/ppermute | solution.py:65
  93.1 8.9 %all-to-all-start.2 = ((f32[8,1,256]{2,1,0:T(1,128)}), f32[8,1,256]{2,1,0:T(1,128)S(1)}, u32[]{:S(2)}, u32[]{:S(2)}) async-start(f32[8,1,256]{2,1,0:T(1,128)} %reshape.213), calls=%async_computation.2 | async-start | bytes 16384 | tf_op jit(solution)/shard_map/all_to_all | solution.py:39
  107.3 1.6 %collective-permute-start.10 = (f32[4,4,2,2048]{3,2,1,0:T(2,128)S(1)}, f32[4,4,2,2048]{3,2,1,0:T(2,128)S(1)}, u32[]{:S(2)}, u32[]{:S(2)}) collective-permute-start(f32[4,4,2,2048]{3,2,1,0:T(2,128)S(1)} %dynamic-slice_bitcast_fusion), channel_id=1, source_target_pairs={{0,4},{4,0},{1,5},{5,1},{2,6},{6,2},{3,7},{7,3},{8,12},{12,8},{9,1... | collective-permute-start | bytes 786440 | tf_op jit(solution)/shard_map/ppermute | solution.py:209
  109.8 14.7 %all-to-all-start.3 = ((f32[16,2,2048]{2,1,0:T(2,128)}), f32[16,2,2048]{2,1,0:T(2,128)S(1)}, u32[]{:S(2)}, u32[]{:S(2)}) async-start(f32[16,2,2048]{2,1,0:T(2,128)} %bitcast.26), calls=%async_computation.3 | async-start | bytes 524288 | tf_op jit(solution)/shard_map/all_to_all | solution.py:39
  125.6 11.0 %all-to-all-start.4 = ((bf16[32,2,1024]{2,1,0:T(2,128)(2,1)}), bf16[32,2,1024]{2,1,0:T(2,128)(2,1)S(1)}, u32[]{:S(2)}, u32[]{:S(2)}) async-start(bf16[32,2,1024]{2,1,0:T(2,128)(2,1)} %bitcast.33), calls=%async_computation.4 | async-start | bytes 262144 | tf_op jit(solution)/shard_map/all_to_all | solution.py:39

commit v11 on v9

--- a/solution.py
+++ b/solution.py
@@ -60,10 +60,15 @@
             ]
         )
         return jnp.sum(jnp.take(parts, (mine - jnp.arange(count)) % count, axis=0), axis=0)
-    step = 1
-    while step < count:
-        x = x + lax.ppermute(x, "section", [(i, i ^ step) for i in range(count)])
-        step *= 2
+    count_mp = lax.axis_size("mp")
+    steps = [1 << b for b in range(count.bit_length() - 1)]
+    for level in range(len(steps)):
+        pairs = []
+        for i in range(count):
+            for m in range(count_mp):
+                step = steps[level] if m % 2 == 0 else steps[len(steps) - 1 - level]
+                pairs.append((i * count_mp + m, (i ^ step) * count_mp + m))
+        x = x + lax.ppermute(x, ("section", "mp"), pairs)
     return x
 
 

time: 135 us -> 134 us (level)
  no operation moved by 1% of the time
where the time goes in v11:
time: 134 us; the launch traced here: 133 us
  waiting for transfers between devices  57.7 us (43%)
  starting transfers between devices  34.3 us (26%)
  matrix products  24 us (18%)
  local copies, waits for them, and re-layouts  7.82 us (6%)
  other arithmetic  6.25 us (5%)
  between operations  3.43 us (3%)
    all_to_all x5, waiting for transfers between devices, exchange(): return lax.all_to_all(send, axes, split_axis=0, concat_axis=0, tiled=True)  34.2 us
    all_to_all x5, starting transfers between devices, exchange(): return lax.all_to_all(send, axes, split_axis=0, concat_axis=0, tiled=True)  18.4 us
    ppermute x6, waiting for transfers between devices, section_sum(): x = x + lax.ppermute(x, ('section', 'mp'), pairs)  14.9 us
    dot_general x2, matrix products, contract_first(): lax.dot_general(operand, weights, (((0,), (0,)), ((), ())), preferred_ele...  9.52 us
    ppermute x4, starting transfers between devices, shifted(): lax.ppermute(x, axis, [(i, (i + k) % count) for i in range(count)])  8.02 us
    ppermute x6, starting transfers between devices, section_sum(): x = x + lax.ppermute(x, ('section', 'mp'), pairs)  7.67 us
    dot_general x2, matrix products, contract_last(): lax.dot_general(operand, weights, (((1,), (1,)), ((), ())), preferred_ele...  7.18 us
    ppermute x4, waiting for transfers between devices, shifted(): lax.ppermute(x, axis, [(i, (i + k) % count) for i in range(count)])  7.17 us
  transfers between devices with their start and end apart: 16, of which 12 were waited for; matrix products, arithmetic and copies ran while one was open for 8% of the time, Pallas kernels for 0%

profile of v11, /device:TPU:0, one launch (start us, length us, event | category | flops | bytes accessed | tf_op | source)
XLA Modules:
  0.0 133.5 jit_solution(7286857497769566441)
XLA Ops:
  0.7 1.2 dynamic_slice.15
  2.6 1.0 constant_dynamic-slice_fusion
  3.6 4.1 %collective-permute-start.1 = (bf16[2,16,2048]{2,1,0:T(8,128)(2,1)S(1)}, bf16[2,16,2048]{2,1,0:T(8,128)(2,1)S(1)}, u32[]{:S(2)}, u32[]{:S(2)}) collective-permute-start(bf16[2,16,2048]{2,1,0:T(8,128)(2,1)S(1)} %get-tuple-element.20), channel_id=1, source_target_pairs={{0,2},{1,3},{2,0},{3,1},{4,6},{5,7},{6,4},{7,5},{8,10},{9,11},{10,... | collective-permute-start | bytes 393224 | tf_op jit(solution)/shard_map/ppermute | solution.py:45
  7.7 1.6 %collective-permute-start = (bf16[2,16,2048]{2,1,0:T(8,128)(2,1)S(1)}, bf16[2,16,2048]{2,1,0:T(8,128)(2,1)S(1)}, u32[]{:S(2)}, u32[]{:S(2)}) collective-permute-start(bf16[2,16,2048]{2,1,0:T(8,128)(2,1)S(1)} %get-tuple-element.20), channel_id=1, source_target_pairs={{0,1},{1,2},{2,3},{3,0},{4,5},{5,6},{6,7},{7,4},{8,9},{9,10},{10,1... | collective-permute-start | bytes 393224 | tf_op jit(solution)/shard_map/ppermute | solution.py:45
  9.3 2.2 %collective-permute-start.2 = (bf16[2,16,2048]{2,1,0:T(8,128)(2,1)S(1)}, bf16[2,16,2048]{2,1,0:T(8,128)(2,1)S(1)}, u32[]{:S(2)}, u32[]{:S(2)}) collective-permute-start(bf16[2,16,2048]{2,1,0:T(8,128)(2,1)S(1)} %get-tuple-element.20), channel_id=1, source_target_pairs={{0,3},{1,0},{2,1},{3,2},{4,7},{5,4},{6,5},{7,6},{8,11},{9,8},{10,9... | collective-permute-start | bytes 393224 | tf_op jit(solution)/shard_map/ppermute | solution.py:45
  11.5 0.8 select_reduce_fusion.5
  12.3 5.4 %collective-permute-done.1 = bf16[2,16,2048]{2,1,0:T(8,128)(2,1)S(1)} collective-permute-done((bf16[2,16,2048]{2,1,0:T(8,128)(2,1)S(1)}, bf16[2,16,2048]{2,1,0:T(8,128)(2,1)S(1)}, u32[]{:S(2)}, u32[]{:S(2)}) %collective-permute-start.1) | collective-permute-done | bytes 131104 | tf_op jit(solution)/shard_map/ppermute | solution.py:45
  17.7 0.7 collective-permute-done.2
  18.7 0.8 select_reduce_fusion.4
  19.5 1.0 collective-permute-done.3
  20.7 0.7 gather_fusion
  21.5 0.7 gather_fusion.1
  22.2 3.2 %fusion.16 = f32[64,1024]{1,0:T(8,128)S(1)} fusion(bf16[2048,1024]{1,0:T(8,128)(2,1)} %param.20, bf16[64,2048]{1,0:T(8,128)(2,1)S(1)} %gather_fusion.1, pred[64]{0:T(512)(128)(4,1)S(1)} %get-tuple-element.13), kind=kOutput, calls=%fused_computation.38 | convolution fusion | flops 268566528 | bytes 4718656 | tf_op jit(solution)/shard_map/dot_general | solution.py:138
  25.7 0.9 convolution_add_fusion
  26.8 0.8 pad_maximum_fusion.1
  27.6 6.1 %all-to-all-start = ((f32[32,2,1152]{2,1,0:T(2,128)}), f32[32,2,1152]{2,1,0:T(2,128)S(1)}, u32[]{:S(2)}, u32[]{:S(2)}) async-start(f32[32,2,1152]{2,1,0:T(2,128)} %pad_maximum_fusion.1), calls=%async_computation | async-start | bytes 589824 | tf_op jit(solution)/shard_map/all_to_all | solution.py:39
  33.9 1.8 %collective-permute-start.4 = (f32[64]{0:T(128)S(1)}, f32[64]{0:T(128)S(1)}, u32[]{:S(2)}, u32[]{:S(2)}) collective-permute-start(f32[64]{0:T(128)S(1)} %fusion), channel_id=1, source_target_pairs={{0,8},{4,20},{8,0},{12,28},{16,24},{20,4},{24,16},{28,12},{1,9},{5... | collective-permute-start | bytes 776 | tf_op jit(solution)/shard_map/ppermute | solution.py:71
  35.7 1.9 %collective-permute-done.4 = f32[64]{0:T(128)S(1)} collective-permute-done((f32[64]{0:T(128)S(1)}, f32[64]{0:T(128)S(1)}, u32[]{:S(2)}, u32[]{:S(2)}) %collective-permute-start.4) | collective-permute-done | bytes 288 | tf_op jit(solution)/shard_map/ppermute | solution.py:71
  37.6 1.7 %collective-permute-start.5 = (f32[64]{0:T(128)S(1)}, f32[64]{0:T(128)S(1)}, u32[]{:S(2)}, u32[]{:S(2)}) collective-permute-start(f32[64]{0:T(128)S(1)} %add.141), channel_id=1, source_target_pairs={{0,16},{4,12},{8,24},{12,4},{16,0},{20,28},{24,8},{28,20},{1,17},{... | collective-permute-start | bytes 776 | tf_op jit(solution)/shard_map/ppermute | solution.py:71
  39.3 5.1 %all-to-all-done = f32[32,2,1152]{2,1,0:T(2,128)S(1)} async-done(((f32[32,2,1152]{2,1,0:T(2,128)}), f32[32,2,1152]{2,1,0:T(2,128)S(1)}, u32[]{:S(2)}, u32[]{:S(2)}) %all-to-all-start) | async-done | bytes 294944 | tf_op jit(solution)/shard_map/all_to_all | solution.py:39
  44.9 0.9 broadcast_in_dim.105
  45.8 2.9 %all-to-all-start.1 = ((bf16[32,2,2048]{2,1,0:T(2,128)(2,1)}), bf16[32,2,2048]{2,1,0:T(2,128)(2,1)S(1)}, u32[]{:S(2)}, u32[]{:S(2)}) async-start(bf16[32,2,2048]{2,1,0:T(2,128)(2,1)} %bitcast.16), calls=%async_computation.1 | async-start | bytes 524288 | tf_op jit(solution)/shard_map/all_to_all | solution.py:39
  48.7 3.6 %fusion.3 = f32[64,1024]{1,0:T(8,128)S(1)} fusion(bf16[1024,2048]{1,0:T(8,128)(2,1)} %param.19, f32[2048]{0:T(1024)S(1)} %copy-done.2, f32[64]{0:T(128)S(1)} %add_rsqrt_fusion.1, bf16[64,2048]{1,0:T(8,128)(2,1)S(1)} %gather_fusion, pred[64]{0:T(512)(128)(4,1)S(1)} %get-tuple-element.13), kind=kOutput, calls=%fused_computation.11 | convolution fusion | flops 269090816 | bytes 4727104 | tf_op jit(solution)/shard_map/dot_general | solution.py:18
  52.3 1.8 %collective-permute-start.6 = (f32[64,1024]{1,0:T(8,128)S(1)}, f32[64,1024]{1,0:T(8,128)S(1)}, u32[]{:S(2)}, u32[]{:S(2)}) collective-permute-start(f32[64,1024]{1,0:T(8,128)S(1)} %fusion.3), channel_id=1, source_target_pairs={{0,8},{4,20},{8,0},{12,28},{16,24},{20,4},{24,16},{28,12},{1,9},{5... | collective-permute-start | bytes 786440 | tf_op jit(solution)/shard_map/ppermute | solution.py:71
  54.1 4.8 %all-to-all-done.1 = bf16[32,2,2048]{2,1,0:T(2,128)(2,1)S(1)} async-done(((bf16[32,2,2048]{2,1,0:T(2,128)(2,1)}), bf16[32,2,2048]{2,1,0:T(2,128)(2,1)S(1)}, u32[]{:S(2)}, u32[]{:S(2)}) %all-to-all-start.1) | async-done | bytes 262176 | tf_op jit(solution)/shard_map/all_to_all | solution.py:39
  59.1 3.6 %fusion.40 = f32[64,1024]{1,0:T(8,128)S(1)} fusion(bf16[64,2048]{1,0:T(8,128)(2,1)S(1)} %reshape.183, bf16[1024,2048]{1,0:T(8,128)(2,1)} %param.19), kind=kOutput, calls=%fused_computation.104 | convolution fusion | flops 268435456 | bytes 4718592 | tf_op jit(solution)/shard_map/dot_general | solution.py:18
  62.7 1.0 collective-permute-start.8
  63.7 0.6 collective-permute-start.7
  64.3 7.6 %collective-permute-done.8 = f32[64,1024]{1,0:T(8,128)S(1)} collective-permute-done((f32[64,1024]{1,0:T(8,128)S(1)}, f32[64,1024]{1,0:T(8,128)S(1)}, u32[]{:S(2)}, u32[]{:S(2)}) %collective-permute-start.8) | collective-permute-done | bytes 262176 | tf_op jit(solution)/shard_map/ppermute | solution.py:71
  71.9 0.8 collective-permute-start.9
  72.9 5.5 %collective-permute-done.9 = f32[64,1024]{1,0:T(8,128)S(1)} collective-permute-done((f32[64,1024]{1,0:T(8,128)S(1)}, f32[64,1024]{1,0:T(8,128)S(1)}, u32[]{:S(2)}, u32[]{:S(2)}) %collective-permute-start.9) | collective-permute-done | bytes 262176 | tf_op jit(solution)/shard_map/ppermute | solution.py:71
  78.6 0.7 reshape.213
  79.3 3.3 %all-to-all-start.2 = ((f32[8,1,256]{2,1,0:T(1,128)}), f32[8,1,256]{2,1,0:T(1,128)S(1)}, u32[]{:S(2)}, u32[]{:S(2)}) async-start(f32[8,1,256]{2,1,0:T(1,128)} %reshape.213), calls=%async_computation.2 | async-start | bytes 16384 | tf_op jit(solution)/shard_map/all_to_all | solution.py:39
  82.6 5.5 %all-to-all-done.2 = f32[8,1,256]{2,1,0:T(1,128)S(1)} async-done(((f32[8,1,256]{2,1,0:T(1,128)}), f32[8,1,256]{2,1,0:T(1,128)S(1)}, u32[]{:S(2)}, u32[]{:S(2)}) %all-to-all-start.2) | async-done | bytes 8224 | tf_op jit(solution)/shard_map/all_to_all | solution.py:39
  88.2 0.5 broadcast.140
  88.7 0.7 reduce.2
  89.5 0.6 multiply_add_fusion
  90.1 3.1 %fusion.7 = f32[64,2048]{1,0:T(8,128)S(1)} fusion(bf16[1024,2048]{1,0:T(8,128)(2,1)} %param.19, f32[64,1024]{1,0:T(8,128)S(1)} %get-tuple-element.12, f32[64,1024]{1,0:T(8,128)S(1)} %get-tuple-element.11, f32[64]{0:T(128)S(1)} %get-tuple-element.24, f32[64]{0:T(128)S(1)} %get-tuple-element.23, f32[64]{0:T(128)S(1)} %get-tuple-element.21, ...), kind=kOutput, calls=%fused_computation.28 | convolution fusion | flops 269025280 | bytes 5243904 | tf_op jit(solution)/shard_map/dot_general | solution.py:209
  93.2 0.3 reshape.185
  93.8 1.4 %collective-permute-done.10 = f32[4,4,2,2048]{3,2,1,0:T(2,128)S(1)} collective-permute-done((f32[4,4,2,2048]{3,2,1,0:T(2,128)S(1)}, f32[4,4,2,2048]{3,2,1,0:T(2,128)S(1)}, u32[]{:S(2)}, u32[]{:S(2)}) %collective-permute-start.10) | collective-permute-done | bytes 262176 | tf_op jit(solution)/shard_map/ppermute | solution.py:213
  95.2 0.8 bitcast_add_fusion
  96.0 3.5 %all-to-all-start.3 = ((f32[16,2,2048]{2,1,0:T(2,128)}), f32[16,2,2048]{2,1,0:T(2,128)S(1)}, u32[]{:S(2)}, u32[]{:S(2)}) async-start(f32[16,2,2048]{2,1,0:T(2,128)} %bitcast.26), calls=%async_computation.3 | async-start | bytes 524288 | tf_op jit(solution)/shard_map/all_to_all | solution.py:39
  99.6 11.1 %all-to-all-done.3 = f32[16,2,2048]{2,1,0:T(2,128)S(1)} async-done(((f32[16,2,2048]{2,1,0:T(2,128)}), f32[16,2,2048]{2,1,0:T(2,128)S(1)}, u32[]{:S(2)}, u32[]{:S(2)}) %all-to-all-start.3) | async-done | bytes 262176 | tf_op jit(solution)/shard_map/all_to_all | solution.py:39
  111.1 0.7 broadcast_in_dim.111
  111.8 2.6 %all-to-all-start.4 = ((bf16[32,2,1024]{2,1,0:T(2,128)(2,1)}), bf16[32,2,1024]{2,1,0:T(2,128)(2,1)S(1)}, u32[]{:S(2)}, u32[]{:S(2)}) async-start(bf16[32,2,1024]{2,1,0:T(2,128)(2,1)} %bitcast.33), calls=%async_computation.4 | async-start | bytes 262144 | tf_op jit(solution)/shard_map/all_to_all | solution.py:39
  115.0 7.7 %all-to-all-done.4 = bf16[32,2,1024]{2,1,0:T(2,128)(2,1)S(1)} async-done(((bf16[32,2,1024]{2,1,0:T(2,128)(2,1)}), bf16[32,2,1024]{2,1,0:T(2,128)(2,1)S(1)}, u32[]{:S(2)}, u32[]{:S(2)}) %all-to-all-start.4) | async-done | bytes 131104 | tf_op jit(solution)/shard_map/all_to_all | solution.py:39
  122.8 4.8 %fusion.37 = f32[2048,1024]{1,0:T(8,128)} fusion(bf16[64,1024]{1,0:T(8,128)(2,1)S(1)} %reshape.190, bf16[64,2048]{1,0:T(8,128)(2,1)S(1)} %gather_fusion, pred[64]{0:T(512)(128)(4,1)S(1)} %get-tuple-element.13), kind=kOutput, calls=%fused_computation.101 | convolution fusion | flops 268566528 | bytes 8781888 | tf_op jit(solution)/shard_map/dot_general | solution.py:24
  127.6 4.8 %fusion.15 = f32[2048,1024]{1,0:T(8,128)} fusion(bf16[64,1024]{1,0:T(8,128)(2,1)S(1)} %reshape.190, bf16[64,2048]{1,0:T(8,128)(2,1)S(1)} %gather_fusion.1, pred[64]{0:T(512)(128)(4,1)S(1)} %get-tuple-element.13), kind=kOutput, calls=%fused_computation.37 | convolution fusion | flops 268566528 | bytes 8781888 | tf_op jit(solution)/shard_map/dot_general | solution.py:24
  (55 shorter events, 3.0 us)
Async XLA Ops:
  0.6 18.0 %copy-start = (f32[2048]{0:T(1024)S(1)}, f32[2048]{0:T(1024)}, u32[]{:S(2)}) copy-start(f32[2048]{0:T(1024)} %param.18) | copy-start | bytes 24580
  3.6 14.1 %collective-permute-start.1 = (bf16[2,16,2048]{2,1,0:T(8,128)(2,1)S(1)}, bf16[2,16,2048]{2,1,0:T(8,128)(2,1)S(1)}, u32[]{:S(2)}, u32[]{:S(2)}) collective-permute-start(bf16[2,16,2048]{2,1,0:T(8,128)(2,1)S(1)} %get-tuple-element.20), channel_id=1, source_target_pairs={{0,2},{1,3},{2,0},{3,1},{4,6},{5,7},{6,4},{7,5},{8,10},{9,11},{10,... | collective-permute-start | bytes 393224 | tf_op jit(solution)/shard_map/ppermute | solution.py:45
  7.7 10.0 %collective-permute-start = (bf16[2,16,2048]{2,1,0:T(8,128)(2,1)S(1)}, bf16[2,16,2048]{2,1,0:T(8,128)(2,1)S(1)}, u32[]{:S(2)}, u32[]{:S(2)}) collective-permute-start(bf16[2,16,2048]{2,1,0:T(8,128)(2,1)S(1)} %get-tuple-element.20), channel_id=1, source_target_pairs={{0,1},{1,2},{2,3},{3,0},{4,5},{5,6},{6,7},{7,4},{8,9},{9,10},{10,1... | collective-permute-start | bytes 393224 | tf_op jit(solution)/shard_map/ppermute | solution.py:45
  9.3 9.2 %collective-permute-start.2 = (bf16[2,16,2048]{2,1,0:T(8,128)(2,1)S(1)}, bf16[2,16,2048]{2,1,0:T(8,128)(2,1)S(1)}, u32[]{:S(2)}, u32[]{:S(2)}) collective-permute-start(bf16[2,16,2048]{2,1,0:T(8,128)(2,1)S(1)} %get-tuple-element.20), channel_id=1, source_target_pairs={{0,3},{1,0},{2,1},{3,2},{4,7},{5,4},{6,5},{7,6},{8,11},{9,8},{10,9... | collective-permute-start | bytes 393224 | tf_op jit(solution)/shard_map/ppermute | solution.py:45
  18.5 2.0 %collective-permute-start.3 = (bf16[4,2,16,2048]{3,2,1,0:T(8,128)(2,1)S(1)}, bf16[4,2,16,2048]{3,2,1,0:T(8,128)(2,1)S(1)}, u32[]{:S(2)}, u32[]{:S(2)}) collective-permute-start(bf16[4,2,16,2048]{3,2,1,0:T(8,128)(2,1)S(1)} %get-tuple-element.18), channel_id=1, source_target_pairs={{0,4},{4,0},{1,5},{5,1},{2,6},{6,2},{3,7},{7,3},{8,12},{12,8},{9,1... | collective-permute-start | bytes 1572872 | tf_op jit(solution)/shard_map/ppermute | solution.py:45
  22.2 3.5 %copy-start.1 = (bf16[2048,1024]{1,0:T(8,128)(2,1)S(1)}, bf16[2048,1024]{1,0:T(8,128)(2,1)}, u32[]{:S(2)}) copy-start(bf16[2048,1024]{1,0:T(8,128)(2,1)} %param.21) | copy-start | bytes 12582916
  25.7 23.0 %copy-start.2 = (f32[2048]{0:T(1024)S(1)}, f32[2048]{0:T(1024)}, u32[]{:S(2)}) copy-start(f32[2048]{0:T(1024)} %param.17) | copy-start | bytes 24580
  27.6 16.8 %all-to-all-start = ((f32[32,2,1152]{2,1,0:T(2,128)}), f32[32,2,1152]{2,1,0:T(2,128)S(1)}, u32[]{:S(2)}, u32[]{:S(2)}) async-start(f32[32,2,1152]{2,1,0:T(2,128)} %pad_maximum_fusion.1), calls=%async_computation | async-start | bytes 589824 | tf_op jit(solution)/shard_map/all_to_all | solution.py:39
  33.9 3.7 %collective-permute-start.4 = (f32[64]{0:T(128)S(1)}, f32[64]{0:T(128)S(1)}, u32[]{:S(2)}, u32[]{:S(2)}) collective-permute-start(f32[64]{0:T(128)S(1)} %fusion), channel_id=1, source_target_pairs={{0,8},{4,20},{8,0},{12,28},{16,24},{20,4},{24,16},{28,12},{1,9},{5... | collective-permute-start | bytes 776 | tf_op jit(solution)/shard_map/ppermute | solution.py:71
  37.6 11.1 %collective-permute-start.5 = (f32[64]{0:T(128)S(1)}, f32[64]{0:T(128)S(1)}, u32[]{:S(2)}, u32[]{:S(2)}) collective-permute-start(f32[64]{0:T(128)S(1)} %add.141), channel_id=1, source_target_pairs={{0,16},{4,12},{8,24},{12,4},{16,0},{20,28},{24,8},{28,20},{1,17},{... | collective-permute-start | bytes 776 | tf_op jit(solution)/shard_map/ppermute | solution.py:71
  45.8 13.2 %all-to-all-start.1 = ((bf16[32,2,2048]{2,1,0:T(2,128)(2,1)}), bf16[32,2,2048]{2,1,0:T(2,128)(2,1)S(1)}, u32[]{:S(2)}, u32[]{:S(2)}) async-start(bf16[32,2,2048]{2,1,0:T(2,128)(2,1)} %bitcast.16), calls=%async_computation.1 | async-start | bytes 524288 | tf_op jit(solution)/shard_map/all_to_all | solution.py:39
  48.7 14.9 %copy-start.3 = (s32[4,256]{1,0:T(4,128)S(1)}, s32[4,256]{1,0:T(4,128)}, u32[]{:S(2)}) copy-start(s32[4,256]{1,0:T(4,128)} %param.14) | copy-start | bytes 12292
  52.3 11.3 %collective-permute-start.6 = (f32[64,1024]{1,0:T(8,128)S(1)}, f32[64,1024]{1,0:T(8,128)S(1)}, u32[]{:S(2)}, u32[]{:S(2)}) collective-permute-start(f32[64,1024]{1,0:T(8,128)S(1)} %fusion.3), channel_id=1, source_target_pairs={{0,8},{4,20},{8,0},{12,28},{16,24},{20,4},{24,16},{28,12},{1,9},{5... | collective-permute-start | bytes 786440 | tf_op jit(solution)/shard_map/ppermute | solution.py:71
  62.7 9.2 %collective-permute-start.8 = (f32[64,1024]{1,0:T(8,128)S(1)}, f32[64,1024]{1,0:T(8,128)S(1)}, u32[]{:S(2)}, u32[]{:S(2)}) collective-permute-start(f32[64,1024]{1,0:T(8,128)S(1)} %fusion.40), channel_id=1, source_target_pairs={{0,8},{4,20},{8,0},{12,28},{16,24},{20,4},{24,16},{28,12},{1,9},{5... | collective-permute-start | bytes 786440 | tf_op jit(solution)/shard_map/ppermute | solution.py:71
  63.7 9.2 %collective-permute-start.7 = (f32[64,1024]{1,0:T(8,128)S(1)}, f32[64,1024]{1,0:T(8,128)S(1)}, u32[]{:S(2)}, u32[]{:S(2)}) collective-permute-start(f32[64,1024]{1,0:T(8,128)S(1)} %add.145), channel_id=1, source_target_pairs={{0,16},{4,12},{8,24},{12,4},{16,0},{20,28},{24,8},{28,20},{1,17},{... | collective-permute-start | bytes 786440 | tf_op jit(solution)/shard_map/ppermute | solution.py:71
  71.9 6.4 %collective-permute-start.9 = (f32[64,1024]{1,0:T(8,128)S(1)}, f32[64,1024]{1,0:T(8,128)S(1)}, u32[]{:S(2)}, u32[]{:S(2)}) collective-permute-start(f32[64,1024]{1,0:T(8,128)S(1)} %add.151), channel_id=1, source_target_pairs={{0,16},{4,12},{8,24},{12,4},{16,0},{20,28},{24,8},{28,20},{1,17},{... | collective-permute-start | bytes 786440 | tf_op jit(solution)/shard_map/ppermute | solution.py:71
  79.3 8.9 %all-to-all-start.2 = ((f32[8,1,256]{2,1,0:T(1,128)}), f32[8,1,256]{2,1,0:T(1,128)S(1)}, u32[]{:S(2)}, u32[]{:S(2)}) async-start(f32[8,1,256]{2,1,0:T(1,128)} %reshape.213), calls=%async_computation.2 | async-start | bytes 16384 | tf_op jit(solution)/shard_map/all_to_all | solution.py:39
  93.6 1.6 %collective-permute-start.10 = (f32[4,4,2,2048]{3,2,1,0:T(2,128)S(1)}, f32[4,4,2,2048]{3,2,1,0:T(2,128)S(1)}, u32[]{:S(2)}, u32[]{:S(2)}) collective-permute-start(f32[4,4,2,2048]{3,2,1,0:T(2,128)S(1)} %dynamic-slice_bitcast_fusion), channel_id=1, source_target_pairs={{0,4},{4,0},{1,5},{5,1},{2,6},{6,2},{3,7},{7,3},{8,12},{12,8},{9,1... | collective-permute-start | bytes 786440 | tf_op jit(solution)/shard_map/ppermute | solution.py:213
  96.0 14.7 %all-to-all-start.3 = ((f32[16,2,2048]{2,1,0:T(2,128)}), f32[16,2,2048]{2,1,0:T(2,128)S(1)}, u32[]{:S(2)}, u32[]{:S(2)}) async-start(f32[16,2,2048]{2,1,0:T(2,128)} %bitcast.26), calls=%async_computation.3 | async-start | bytes 524288 | tf_op jit(solution)/shard_map/all_to_all | solution.py:39
  111.8 11.0 %all-to-all-start.4 = ((bf16[32,2,1024]{2,1,0:T(2,128)(2,1)}), bf16[32,2,1024]{2,1,0:T(2,128)(2,1)S(1)}, u32[]{:S(2)}, u32[]{:S(2)}) async-start(bf16[32,2,1024]{2,1,0:T(2,128)(2,1)} %bitcast.33), calls=%async_computation.4 | async-start | bytes 262144 | tf_op jit(solution)/shard_map/all_to_all | solution.py:39

commit v12 on v11

--- a/solution.py
+++ b/solution.py
@@ -143,7 +143,7 @@
     target_norm = (feature_all.astype(jnp.float32) * target_scale[:, None] * target_gain).astype(
         jnp.bfloat16
     )
-    target_logit = section_sum(contract_last(target_norm, head))
+    target_part = contract_last(target_norm, head)
     piece = width // groups
     spare = pad_cols(-(-piece // per_dev))
     gain_piece = lax.dynamic_slice_in_dim(draft_gain, (my_mp * count_dp + my_dp) * piece, piece)
@@ -155,7 +155,9 @@
         ],
         axis=2,
     )
-    got1 = exchange(send1, ALL).reshape(count_sec, groups, per_dev, -1)
+    got1, target_part = lax.optimization_barrier((exchange(send1, ALL), target_part))
+    target_logit = section_sum(target_part)
+    got1 = got1.reshape(count_sec, groups, per_dev, -1)
     hidden = (
         jnp.sum(got1[..., :block], axis=0).transpose(1, 0, 2).reshape(per_dev, groups * block)
     )

time: 134 us -> 137 us (1.022)
  starting transfers between devices: 34.3 us -> 37.4 us
    all_to_all x5, starting transfers between devices: 18.4 us -> 21.3 us  [exchange(): return lax.all_to_all(send, axes, split_axis=0, concat_axis=0, tiled=True)]
    all_to_all x5, waiting for transfers between devices: 34.2 us -> 32.7 us  [exchange(): return lax.all_to_all(send, axes, split_axis=0, concat_axis=0, tiled=True)]
    ppermute x6, waiting for transfers between devices: 14.9 us -> 16.4 us  [section_sum(): x = x + lax.ppermute(x, ('section', 'mp'), pairs)]
  transfers between devices with their start and end apart: 16 -> 16, of which waited for: 12 -> 12; matrix products, arithmetic and copies ran while one was open for 8% -> 7% of each run, Pallas kernels for 0% -> 0%
where the time goes in v12:
time: 137 us
  waiting for transfers between devices  57.7 us (42%)
  starting transfers between devices  37.4 us (27%)
  matrix products  24 us (18%)
  local copies, waits for them, and re-layouts  7.82 us (6%)
  other arithmetic  6.24 us (5%)
  between operations  3.42 us (2%)
    all_to_all x5, waiting for transfers between devices, exchange(): return lax.all_to_all(send, axes, split_axis=0, concat_axis=0, tiled=True)  32.7 us
    all_to_all x5, starting transfers between devices, exchange(): return lax.all_to_all(send, axes, split_axis=0, concat_axis=0, tiled=True)  21.3 us
    ppermute x6, waiting for transfers between devices, section_sum(): x = x + lax.ppermute(x, ('section', 'mp'), pairs)  16.4 us
    dot_general x2, matrix products, contract_first(): lax.dot_general(operand, weights, (((0,), (0,)), ((), ())), preferred_ele...  9.52 us
    ppermute x4, starting transfers between devices, shifted(): lax.ppermute(x, axis, [(i, (i + k) % count) for i in range(count)])  8.02 us
    ppermute x6, starting transfers between devices, section_sum(): x = x + lax.ppermute(x, ('section', 'mp'), pairs)  7.96 us
    dot_general x2, matrix products, contract_last(): lax.dot_general(operand, weights, (((1,), (1,)), ((), ())), preferred_ele...  7.18 us
    ppermute x4, waiting for transfers between devices, shifted(): lax.ppermute(x, axis, [(i, (i + k) % count) for i in range(count)])  7.17 us
  transfers between devices with their start and end apart: 16, of which 12 were waited for; matrix products, arithmetic and copies ran while one was open for 7% of the time, Pallas kernels for 0%

profile of v12, /device:TPU:0, one launch (start us, length us, event | category | flops | bytes accessed | tf_op | source)
XLA Modules:
  0.0 136.6 jit_solution(14791995861321168297)
XLA Ops:
  0.7 1.2 dynamic_slice.15
  2.6 1.0 constant_dynamic-slice_fusion
  3.6 4.1 %collective-permute-start.1 = (bf16[2,16,2048]{2,1,0:T(8,128)(2,1)S(1)}, bf16[2,16,2048]{2,1,0:T(8,128)(2,1)S(1)}, u32[]{:S(2)}, u32[]{:S(2)}) collective-permute-start(bf16[2,16,2048]{2,1,0:T(8,128)(2,1)S(1)} %get-tuple-element.24), channel_id=1, source_target_pairs={{0,2},{1,3},{2,0},{3,1},{4,6},{5,7},{6,4},{7,5},{8,10},{9,11},{10,... | collective-permute-start | bytes 393224 | tf_op jit(solution)/shard_map/ppermute | solution.py:45
  7.7 1.6 %collective-permute-start = (bf16[2,16,2048]{2,1,0:T(8,128)(2,1)S(1)}, bf16[2,16,2048]{2,1,0:T(8,128)(2,1)S(1)}, u32[]{:S(2)}, u32[]{:S(2)}) collective-permute-start(bf16[2,16,2048]{2,1,0:T(8,128)(2,1)S(1)} %get-tuple-element.24), channel_id=1, source_target_pairs={{0,1},{1,2},{2,3},{3,0},{4,5},{5,6},{6,7},{7,4},{8,9},{9,10},{10,1... | collective-permute-start | bytes 393224 | tf_op jit(solution)/shard_map/ppermute | solution.py:45
  9.3 2.2 %collective-permute-start.2 = (bf16[2,16,2048]{2,1,0:T(8,128)(2,1)S(1)}, bf16[2,16,2048]{2,1,0:T(8,128)(2,1)S(1)}, u32[]{:S(2)}, u32[]{:S(2)}) collective-permute-start(bf16[2,16,2048]{2,1,0:T(8,128)(2,1)S(1)} %get-tuple-element.24), channel_id=1, source_target_pairs={{0,3},{1,0},{2,1},{3,2},{4,7},{5,4},{6,5},{7,6},{8,11},{9,8},{10,9... | collective-permute-start | bytes 393224 | tf_op jit(solution)/shard_map/ppermute | solution.py:45
  11.5 0.8 select_reduce_fusion.5
  12.3 5.4 %collective-permute-done.1 = bf16[2,16,2048]{2,1,0:T(8,128)(2,1)S(1)} collective-permute-done((bf16[2,16,2048]{2,1,0:T(8,128)(2,1)S(1)}, bf16[2,16,2048]{2,1,0:T(8,128)(2,1)S(1)}, u32[]{:S(2)}, u32[]{:S(2)}) %collective-permute-start.1) | collective-permute-done | bytes 131104 | tf_op jit(solution)/shard_map/ppermute | solution.py:45
  17.7 0.7 collective-permute-done.2
  18.7 0.8 select_reduce_fusion.4
  19.5 1.0 collective-permute-done.3
  20.7 0.7 gather_fusion.1
  21.5 0.7 gather_fusion
  22.2 3.2 %fusion.16 = f32[64,1024]{1,0:T(8,128)S(1)} fusion(bf16[2048,1024]{1,0:T(8,128)(2,1)} %param.20, bf16[64,2048]{1,0:T(8,128)(2,1)S(1)} %gather_fusion, pred[64]{0:T(512)(128)(4,1)S(1)} %get-tuple-element.17), kind=kOutput, calls=%fused_computation.38 | convolution fusion | flops 268566528 | bytes 4718656 | tf_op jit(solution)/shard_map/dot_general | solution.py:138
  25.7 0.9 convolution_add_fusion
  26.8 0.8 pad_maximum_fusion.1
  27.6 6.1 %all-to-all-start = ((f32[32,2,1152]{2,1,0:T(2,128)}), f32[32,2,1152]{2,1,0:T(2,128)S(1)}, u32[]{:S(2)}, u32[]{:S(2)}) async-start(f32[32,2,1152]{2,1,0:T(2,128)} %pad_maximum_fusion.1), calls=%async_computation | async-start | bytes 589824 | tf_op jit(solution)/shard_map/all_to_all | solution.py:39
  33.9 1.8 %collective-permute-start.4 = (f32[64]{0:T(128)S(1)}, f32[64]{0:T(128)S(1)}, u32[]{:S(2)}, u32[]{:S(2)}) collective-permute-start(f32[64]{0:T(128)S(1)} %fusion), channel_id=1, source_target_pairs={{0,8},{4,20},{8,0},{12,28},{16,24},{20,4},{24,16},{28,12},{1,9},{5... | collective-permute-start | bytes 776 | tf_op jit(solution)/shard_map/ppermute | solution.py:71
  35.7 1.9 %collective-permute-done.4 = f32[64]{0:T(128)S(1)} collective-permute-done((f32[64]{0:T(128)S(1)}, f32[64]{0:T(128)S(1)}, u32[]{:S(2)}, u32[]{:S(2)}) %collective-permute-start.4) | collective-permute-done | bytes 288 | tf_op jit(solution)/shard_map/ppermute | solution.py:71
  37.6 1.7 %collective-permute-start.5 = (f32[64]{0:T(128)S(1)}, f32[64]{0:T(128)S(1)}, u32[]{:S(2)}, u32[]{:S(2)}) collective-permute-start(f32[64]{0:T(128)S(1)} %add.144), channel_id=1, source_target_pairs={{0,16},{4,12},{8,24},{12,4},{16,0},{20,28},{24,8},{28,20},{1,17},{... | collective-permute-start | bytes 776 | tf_op jit(solution)/shard_map/ppermute | solution.py:71
  39.3 1.9 %collective-permute-done.5 = f32[64]{0:T(128)S(1)} collective-permute-done((f32[64]{0:T(128)S(1)}, f32[64]{0:T(128)S(1)}, u32[]{:S(2)}, u32[]{:S(2)}) %collective-permute-start.5) | collective-permute-done | bytes 288 | tf_op jit(solution)/shard_map/ppermute | solution.py:71
  41.2 3.6 %fusion.3 = f32[64,1024]{1,0:T(8,128)S(1)} fusion(bf16[1024,2048]{1,0:T(8,128)(2,1)} %param.19, f32[2048]{0:T(1024)S(1)} %copy-done.2, f32[64]{0:T(128)S(1)} %add_rsqrt_fusion.1, bf16[64,2048]{1,0:T(8,128)(2,1)S(1)} %gather_fusion.1, pred[64]{0:T(512)(128)(4,1)S(1)} %get-tuple-element.17), kind=kOutput, calls=%fused_computation.11 | convolution fusion | flops 269090816 | bytes 4727104 | tf_op jit(solution)/shard_map/dot_general | solution.py:18
  45.3 0.9 broadcast_in_dim.105
  46.2 5.8 %all-to-all-start.1 = ((bf16[32,2,2048]{2,1,0:T(2,128)(2,1)}), bf16[32,2,2048]{2,1,0:T(2,128)(2,1)S(1)}, u32[]{:S(2)}, u32[]{:S(2)}) async-start(bf16[32,2,2048]{2,1,0:T(2,128)(2,1)} %bitcast.16), calls=%async_computation.1 | async-start | bytes 524288 | tf_op jit(solution)/shard_map/all_to_all | solution.py:39
  52.0 1.8 %collective-permute-start.6 = (f32[64,1024]{1,0:T(8,128)S(1)}, f32[64,1024]{1,0:T(8,128)S(1)}, u32[]{:S(2)}, u32[]{:S(2)}) collective-permute-start(f32[64,1024]{1,0:T(8,128)S(1)} %fusion.3), channel_id=1, source_target_pairs={{0,8},{4,20},{8,0},{12,28},{16,24},{20,4},{24,16},{28,12},{1,9},{5... | collective-permute-start | bytes 786440 | tf_op jit(solution)/shard_map/ppermute | solution.py:71
  53.8 8.4 %all-to-all-done.1 = bf16[32,2,2048]{2,1,0:T(2,128)(2,1)S(1)} async-done(((bf16[32,2,2048]{2,1,0:T(2,128)(2,1)}), bf16[32,2,2048]{2,1,0:T(2,128)(2,1)S(1)}, u32[]{:S(2)}, u32[]{:S(2)}) %all-to-all-start.1) | async-done | bytes 262176 | tf_op jit(solution)/shard_map/all_to_all | solution.py:39
  62.3 3.6 %fusion.40 = f32[64,1024]{1,0:T(8,128)S(1)} fusion(bf16[64,2048]{1,0:T(8,128)(2,1)S(1)} %reshape.183, bf16[1024,2048]{1,0:T(8,128)(2,1)} %param.19), kind=kOutput, calls=%fused_computation.104 | convolution fusion | flops 268435456 | bytes 4718592 | tf_op jit(solution)/shard_map/dot_general | solution.py:18
  65.9 1.0 collective-permute-start.8
  67.0 0.6 collective-permute-start.7
  67.6 7.4 %collective-permute-done.8 = f32[64,1024]{1,0:T(8,128)S(1)} collective-permute-done((f32[64,1024]{1,0:T(8,128)S(1)}, f32[64,1024]{1,0:T(8,128)S(1)}, u32[]{:S(2)}, u32[]{:S(2)}) %collective-permute-start.8) | collective-permute-done | bytes 262176 | tf_op jit(solution)/shard_map/ppermute | solution.py:71
  75.0 1.0 collective-permute-start.9
  76.2 5.3 %collective-permute-done.9 = f32[64,1024]{1,0:T(8,128)S(1)} collective-permute-done((f32[64,1024]{1,0:T(8,128)S(1)}, f32[64,1024]{1,0:T(8,128)S(1)}, u32[]{:S(2)}, u32[]{:S(2)}) %collective-permute-start.9) | collective-permute-done | bytes 262176 | tf_op jit(solution)/shard_map/ppermute | solution.py:71
  81.7 0.7 reshape.213
  82.4 3.3 %all-to-all-start.2 = ((f32[8,1,256]{2,1,0:T(1,128)}), f32[8,1,256]{2,1,0:T(1,128)S(1)}, u32[]{:S(2)}, u32[]{:S(2)}) async-start(f32[8,1,256]{2,1,0:T(1,128)} %reshape.213), calls=%async_computation.2 | async-start | bytes 16384 | tf_op jit(solution)/shard_map/all_to_all | solution.py:39
  85.8 5.5 %all-to-all-done.2 = f32[8,1,256]{2,1,0:T(1,128)S(1)} async-done(((f32[8,1,256]{2,1,0:T(1,128)}), f32[8,1,256]{2,1,0:T(1,128)S(1)}, u32[]{:S(2)}, u32[]{:S(2)}) %all-to-all-start.2) | async-done | bytes 8224 | tf_op jit(solution)/shard_map/all_to_all | solution.py:39
  91.3 0.5 broadcast.140
  91.8 0.7 reduce.2
  92.6 0.6 multiply_add_fusion
  93.2 3.1 %fusion.7 = f32[64,2048]{1,0:T(8,128)S(1)} fusion(bf16[1024,2048]{1,0:T(8,128)(2,1)} %param.19, f32[64,1024]{1,0:T(8,128)S(1)} %get-tuple-element.16, f32[64,1024]{1,0:T(8,128)S(1)} %get-tuple-element.15, f32[64]{0:T(128)S(1)} %get-tuple-element.28, f32[64]{0:T(128)S(1)} %get-tuple-element.27, f32[64]{0:T(128)S(1)} %get-tuple-element.25, ...), kind=kOutput, calls=%fused_computation.28 | convolution fusion | flops 269025280 | bytes 5243904 | tf_op jit(solution)/shard_map/dot_general | solution.py:211
  96.3 0.3 reshape.185
  96.9 1.4 %collective-permute-done.10 = f32[4,4,2,2048]{3,2,1,0:T(2,128)S(1)} collective-permute-done((f32[4,4,2,2048]{3,2,1,0:T(2,128)S(1)}, f32[4,4,2,2048]{3,2,1,0:T(2,128)S(1)}, u32[]{:S(2)}, u32[]{:S(2)}) %collective-permute-start.10) | collective-permute-done | bytes 262176 | tf_op jit(solution)/shard_map/ppermute | solution.py:215
  98.3 0.8 bitcast_add_fusion
  99.1 3.5 %all-to-all-start.3 = ((f32[16,2,2048]{2,1,0:T(2,128)}), f32[16,2,2048]{2,1,0:T(2,128)S(1)}, u32[]{:S(2)}, u32[]{:S(2)}) async-start(f32[16,2,2048]{2,1,0:T(2,128)} %bitcast.26), calls=%async_computation.3 | async-start | bytes 524288 | tf_op jit(solution)/shard_map/all_to_all | solution.py:39
  102.7 11.1 %all-to-all-done.3 = f32[16,2,2048]{2,1,0:T(2,128)S(1)} async-done(((f32[16,2,2048]{2,1,0:T(2,128)}), f32[16,2,2048]{2,1,0:T(2,128)S(1)}, u32[]{:S(2)}, u32[]{:S(2)}) %all-to-all-start.3) | async-done | bytes 262176 | tf_op jit(solution)/shard_map/all_to_all | solution.py:39
  114.2 0.7 broadcast_in_dim.111
  114.9 2.6 %all-to-all-start.4 = ((bf16[32,2,1024]{2,1,0:T(2,128)(2,1)}), bf16[32,2,1024]{2,1,0:T(2,128)(2,1)S(1)}, u32[]{:S(2)}, u32[]{:S(2)}) async-start(bf16[32,2,1024]{2,1,0:T(2,128)(2,1)} %bitcast.33), calls=%async_computation.4 | async-start | bytes 262144 | tf_op jit(solution)/shard_map/all_to_all | solution.py:39
  118.2 7.7 %all-to-all-done.4 = bf16[32,2,1024]{2,1,0:T(2,128)(2,1)S(1)} async-done(((bf16[32,2,1024]{2,1,0:T(2,128)(2,1)}), bf16[32,2,1024]{2,1,0:T(2,128)(2,1)S(1)}, u32[]{:S(2)}, u32[]{:S(2)}) %all-to-all-start.4) | async-done | bytes 131104 | tf_op jit(solution)/shard_map/all_to_all | solution.py:39
  125.9 4.8 %fusion.37 = f32[2048,1024]{1,0:T(8,128)} fusion(bf16[64,1024]{1,0:T(8,128)(2,1)S(1)} %reshape.190, bf16[64,2048]{1,0:T(8,128)(2,1)S(1)} %gather_fusion.1, pred[64]{0:T(512)(128)(4,1)S(1)} %get-tuple-element.17), kind=kOutput, calls=%fused_computation.101 | convolution fusion | flops 268566528 | bytes 8781888 | tf_op jit(solution)/shard_map/dot_general | solution.py:24
  130.7 4.8 %fusion.15 = f32[2048,1024]{1,0:T(8,128)} fusion(bf16[64,1024]{1,0:T(8,128)(2,1)S(1)} %reshape.190, bf16[64,2048]{1,0:T(8,128)(2,1)S(1)} %gather_fusion, pred[64]{0:T(512)(128)(4,1)S(1)} %get-tuple-element.17), kind=kOutput, calls=%fused_computation.37 | convolution fusion | flops 268566528 | bytes 8781888 | tf_op jit(solution)/shard_map/dot_general | solution.py:24
  (55 shorter events, 3.0 us)
Async XLA Ops:
  0.6 18.0 %copy-start = (f32[2048]{0:T(1024)S(1)}, f32[2048]{0:T(1024)}, u32[]{:S(2)}) copy-start(f32[2048]{0:T(1024)} %param.18) | copy-start | bytes 24580
  3.6 14.1 %collective-permute-start.1 = (bf16[2,16,2048]{2,1,0:T(8,128)(2,1)S(1)}, bf16[2,16,2048]{2,1,0:T(8,128)(2,1)S(1)}, u32[]{:S(2)}, u32[]{:S(2)}) collective-permute-start(bf16[2,16,2048]{2,1,0:T(8,128)(2,1)S(1)} %get-tuple-element.24), channel_id=1, source_target_pairs={{0,2},{1,3},{2,0},{3,1},{4,6},{5,7},{6,4},{7,5},{8,10},{9,11},{10,... | collective-permute-start | bytes 393224 | tf_op jit(solution)/shard_map/ppermute | solution.py:45
  7.7 10.0 %collective-permute-start = (bf16[2,16,2048]{2,1,0:T(8,128)(2,1)S(1)}, bf16[2,16,2048]{2,1,0:T(8,128)(2,1)S(1)}, u32[]{:S(2)}, u32[]{:S(2)}) collective-permute-start(bf16[2,16,2048]{2,1,0:T(8,128)(2,1)S(1)} %get-tuple-element.24), channel_id=1, source_target_pairs={{0,1},{1,2},{2,3},{3,0},{4,5},{5,6},{6,7},{7,4},{8,9},{9,10},{10,1... | collective-permute-start | bytes 393224 | tf_op jit(solution)/shard_map/ppermute | solution.py:45
  9.3 9.2 %collective-permute-start.2 = (bf16[2,16,2048]{2,1,0:T(8,128)(2,1)S(1)}, bf16[2,16,2048]{2,1,0:T(8,128)(2,1)S(1)}, u32[]{:S(2)}, u32[]{:S(2)}) collective-permute-start(bf16[2,16,2048]{2,1,0:T(8,128)(2,1)S(1)} %get-tuple-element.24), channel_id=1, source_target_pairs={{0,3},{1,0},{2,1},{3,2},{4,7},{5,4},{6,5},{7,6},{8,11},{9,8},{10,9... | collective-permute-start | bytes 393224 | tf_op jit(solution)/shard_map/ppermute | solution.py:45
  18.5 2.0 %collective-permute-start.3 = (bf16[4,2,16,2048]{3,2,1,0:T(8,128)(2,1)S(1)}, bf16[4,2,16,2048]{3,2,1,0:T(8,128)(2,1)S(1)}, u32[]{:S(2)}, u32[]{:S(2)}) collective-permute-start(bf16[4,2,16,2048]{3,2,1,0:T(8,128)(2,1)S(1)} %get-tuple-element.22), channel_id=1, source_target_pairs={{0,4},{4,0},{1,5},{5,1},{2,6},{6,2},{3,7},{7,3},{8,12},{12,8},{9,1... | collective-permute-start | bytes 1572872 | tf_op jit(solution)/shard_map/ppermute | solution.py:45
  22.2 3.5 %copy-start.1 = (bf16[2048,1024]{1,0:T(8,128)(2,1)S(1)}, bf16[2048,1024]{1,0:T(8,128)(2,1)}, u32[]{:S(2)}) copy-start(bf16[2048,1024]{1,0:T(8,128)(2,1)} %param.21) | copy-start | bytes 12582916
  25.7 15.5 %copy-start.2 = (f32[2048]{0:T(1024)S(1)}, f32[2048]{0:T(1024)}, u32[]{:S(2)}) copy-start(f32[2048]{0:T(1024)} %param.17) | copy-start | bytes 24580
  27.6 17.2 %all-to-all-start = ((f32[32,2,1152]{2,1,0:T(2,128)}), f32[32,2,1152]{2,1,0:T(2,128)S(1)}, u32[]{:S(2)}, u32[]{:S(2)}) async-start(f32[32,2,1152]{2,1,0:T(2,128)} %pad_maximum_fusion.1), calls=%async_computation | async-start | bytes 589824 | tf_op jit(solution)/shard_map/all_to_all | solution.py:39
  33.9 3.7 %collective-permute-start.4 = (f32[64]{0:T(128)S(1)}, f32[64]{0:T(128)S(1)}, u32[]{:S(2)}, u32[]{:S(2)}) collective-permute-start(f32[64]{0:T(128)S(1)} %fusion), channel_id=1, source_target_pairs={{0,8},{4,20},{8,0},{12,28},{16,24},{20,4},{24,16},{28,12},{1,9},{5... | collective-permute-start | bytes 776 | tf_op jit(solution)/shard_map/ppermute | solution.py:71
  37.6 3.6 %collective-permute-start.5 = (f32[64]{0:T(128)S(1)}, f32[64]{0:T(128)S(1)}, u32[]{:S(2)}, u32[]{:S(2)}) collective-permute-start(f32[64]{0:T(128)S(1)} %add.144), channel_id=1, source_target_pairs={{0,16},{4,12},{8,24},{12,4},{16,0},{20,28},{24,8},{28,20},{1,17},{... | collective-permute-start | bytes 776 | tf_op jit(solution)/shard_map/ppermute | solution.py:71
  44.8 22.2 %copy-start.3 = (s32[4,256]{1,0:T(4,128)S(1)}, s32[4,256]{1,0:T(4,128)}, u32[]{:S(2)}) copy-start(s32[4,256]{1,0:T(4,128)} %param.14) | copy-start | bytes 12292
  46.2 16.0 %all-to-all-start.1 = ((bf16[32,2,2048]{2,1,0:T(2,128)(2,1)}), bf16[32,2,2048]{2,1,0:T(2,128)(2,1)S(1)}, u32[]{:S(2)}, u32[]{:S(2)}) async-start(bf16[32,2,2048]{2,1,0:T(2,128)(2,1)} %bitcast.16), calls=%async_computation.1 | async-start | bytes 524288 | tf_op jit(solution)/shard_map/all_to_all | solution.py:39
  52.0 15.0 %collective-permute-start.6 = (f32[64,1024]{1,0:T(8,128)S(1)}, f32[64,1024]{1,0:T(8,128)S(1)}, u32[]{:S(2)}, u32[]{:S(2)}) collective-permute-start(f32[64,1024]{1,0:T(8,128)S(1)} %fusion.3), channel_id=1, source_target_pairs={{0,8},{4,20},{8,0},{12,28},{16,24},{20,4},{24,16},{28,12},{1,9},{5... | collective-permute-start | bytes 786440 | tf_op jit(solution)/shard_map/ppermute | solution.py:71
  65.9 9.1 %collective-permute-start.8 = (f32[64,1024]{1,0:T(8,128)S(1)}, f32[64,1024]{1,0:T(8,128)S(1)}, u32[]{:S(2)}, u32[]{:S(2)}) collective-permute-start(f32[64,1024]{1,0:T(8,128)S(1)} %fusion.40), channel_id=1, source_target_pairs={{0,8},{4,20},{8,0},{12,28},{16,24},{20,4},{24,16},{28,12},{1,9},{5... | collective-permute-start | bytes 786440 | tf_op jit(solution)/shard_map/ppermute | solution.py:71
  67.0 9.2 %collective-permute-start.7 = (f32[64,1024]{1,0:T(8,128)S(1)}, f32[64,1024]{1,0:T(8,128)S(1)}, u32[]{:S(2)}, u32[]{:S(2)}) collective-permute-start(f32[64,1024]{1,0:T(8,128)S(1)} %add.148), channel_id=1, source_target_pairs={{0,16},{4,12},{8,24},{12,4},{16,0},{20,28},{24,8},{28,20},{1,17},{... | collective-permute-start | bytes 786440 | tf_op jit(solution)/shard_map/ppermute | solution.py:71
  75.0 6.4 %collective-permute-start.9 = (f32[64,1024]{1,0:T(8,128)S(1)}, f32[64,1024]{1,0:T(8,128)S(1)}, u32[]{:S(2)}, u32[]{:S(2)}) collective-permute-start(f32[64,1024]{1,0:T(8,128)S(1)} %add.151), channel_id=1, source_target_pairs={{0,16},{4,12},{8,24},{12,4},{16,0},{20,28},{24,8},{28,20},{1,17},{... | collective-permute-start | bytes 786440 | tf_op jit(solution)/shard_map/ppermute | solution.py:71
  82.4 8.9 %all-to-all-start.2 = ((f32[8,1,256]{2,1,0:T(1,128)}), f32[8,1,256]{2,1,0:T(1,128)S(1)}, u32[]{:S(2)}, u32[]{:S(2)}) async-start(f32[8,1,256]{2,1,0:T(1,128)} %reshape.213), calls=%async_computation.2 | async-start | bytes 16384 | tf_op jit(solution)/shard_map/all_to_all | solution.py:39
  96.7 1.6 %collective-permute-start.10 = (f32[4,4,2,2048]{3,2,1,0:T(2,128)S(1)}, f32[4,4,2,2048]{3,2,1,0:T(2,128)S(1)}, u32[]{:S(2)}, u32[]{:S(2)}) collective-permute-start(f32[4,4,2,2048]{3,2,1,0:T(2,128)S(1)} %dynamic-slice_bitcast_fusion), channel_id=1, source_target_pairs={{0,4},{4,0},{1,5},{5,1},{2,6},{6,2},{3,7},{7,3},{8,12},{12,8},{9,1... | collective-permute-start | bytes 786440 | tf_op jit(solution)/shard_map/ppermute | solution.py:215
  99.1 14.7 %all-to-all-start.3 = ((f32[16,2,2048]{2,1,0:T(2,128)}), f32[16,2,2048]{2,1,0:T(2,128)S(1)}, u32[]{:S(2)}, u32[]{:S(2)}) async-start(f32[16,2,2048]{2,1,0:T(2,128)} %bitcast.26), calls=%async_computation.3 | async-start | bytes 524288 | tf_op jit(solution)/shard_map/all_to_all | solution.py:39
  114.9 11.0 %all-to-all-start.4 = ((bf16[32,2,1024]{2,1,0:T(2,128)(2,1)}), bf16[32,2,1024]{2,1,0:T(2,128)(2,1)S(1)}, u32[]{:S(2)}, u32[]{:S(2)}) async-start(bf16[32,2,1024]{2,1,0:T(2,128)(2,1)} %bitcast.33), calls=%async_computation.4 | async-start | bytes 262144 | tf_op jit(solution)/shard_map/all_to_all | solution.py:39

commit v13 on v11

--- a/solution.py
+++ b/solution.py
@@ -167,9 +167,15 @@
 
     send2 = jnp.broadcast_to(
         draft_norm.reshape(per_dev, count_sec, 1, width).transpose(1, 2, 0, 3),
-        (count_sec, groups, per_dev, width),
-    ).reshape(n_dev, per_dev, width)
-    draft_norm_all = exchange(send2, ALL).reshape(total_rows, width)
+        (count_sec, count_dp, per_dev, width),
+    ).reshape(count_sec * count_dp, per_dev, width)
+    by_mp = shifted(exchange(send2, ("section", "dp")), "mp")
+    by_mp = jnp.take(by_mp, (my_mp - jnp.arange(count_mp, dtype=jnp.int32)) % count_mp, axis=0)
+    draft_norm_all = (
+        by_mp.reshape(count_mp, count_sec, count_dp, per_dev, width)
+        .transpose(1, 0, 2, 3, 4)
+        .reshape(total_rows, width)
+    )
 
     draft_logit = section_sum(contract_last(draft_norm_all, head))
     column_zero = (my_mp * count_dp + my_dp) * vocab_tile

time: 134 us -> 138 us (1.030)
    all_to_all x5, waiting for transfers between devices: 34.2 us -> 37.4 us  [exchange(): return lax.all_to_all(send, axes, split_axis=0, concat_axis=0, tiled=True)]
    ppermute x6, waiting for transfers between devices: 14.9 us -> 12.9 us  [section_sum(): x = x + lax.ppermute(x, ('section', 'mp'), pairs)]
    ppermute x4 -> x5, waiting for transfers between devices: 7.17 us -> 7.05 us  [shifted(): lax.ppermute(x, axis, [(i, (i + k) % count) for i in range(count)])]
    ppermute x4 -> x5, starting transfers between devices: 8.02 us -> 8.03 us  [shifted(): lax.ppermute(x, axis, [(i, (i + k) % count) for i in range(count)])]
  transfers between devices with their start and end apart: 16 -> 17, of which waited for: 12 -> 12; matrix products, arithmetic and copies ran while one was open for 8% -> 9% of each run, Pallas kernels for 0% -> 0%
where the time goes in v13:
time: 138 us
  waiting for transfers between devices  58.8 us (43%)
  starting transfers between devices  35.4 us (26%)
  matrix products  24 us (17%)
  local copies, waits for them, and re-layouts  8.95 us (6%)
  other arithmetic  6.94 us (5%)
  between operations  3.46 us (3%)
    all_to_all x5, waiting for transfers between devices, exchange(): return lax.all_to_all(send, axes, split_axis=0, concat_axis=0, tiled=True)  37.4 us
    all_to_all x5, starting transfers between devices, exchange(): return lax.all_to_all(send, axes, split_axis=0, concat_axis=0, tiled=True)  19.8 us
    ppermute x6, waiting for transfers between devices, section_sum(): x = x + lax.ppermute(x, ('section', 'mp'), pairs)  12.9 us
    dot_general x2, matrix products, contract_first(): lax.dot_general(operand, weights, (((0,), (0,)), ((), ())), preferred_ele...  9.52 us
    ppermute x5, starting transfers between devices, shifted(): lax.ppermute(x, axis, [(i, (i + k) % count) for i in range(count)])  8.03 us
    ppermute x6, starting transfers between devices, section_sum(): x = x + lax.ppermute(x, ('section', 'mp'), pairs)  7.46 us
    dot_general x2, matrix products, contract_last(): lax.dot_general(operand, weights, (((1,), (1,)), ((), ())), preferred_ele...  7.18 us
    ppermute x5, waiting for transfers between devices, shifted(): lax.ppermute(x, axis, [(i, (i + k) % count) for i in range(count)])  7.05 us
  transfers between devices with their start and end apart: 17, of which 12 were waited for; matrix products, arithmetic and copies ran while one was open for 9% of the time, Pallas kernels for 0%

profile of v13, /device:TPU:0, one launch (start us, length us, event | category | flops | bytes accessed | tf_op | source)
XLA Modules:
  0.0 137.5 jit_solution(5068044080119962097)
XLA Ops:
  0.7 1.2 dynamic_slice.15
  2.6 1.0 constant_dynamic-slice_fusion
  3.6 4.1 %collective-permute-start.1 = (bf16[2,16,2048]{2,1,0:T(8,128)(2,1)S(1)}, bf16[2,16,2048]{2,1,0:T(8,128)(2,1)S(1)}, u32[]{:S(2)}, u32[]{:S(2)}) collective-permute-start(bf16[2,16,2048]{2,1,0:T(8,128)(2,1)S(1)} %get-tuple-element.20), channel_id=1, source_target_pairs={{0,2},{1,3},{2,0},{3,1},{4,6},{5,7},{6,4},{7,5},{8,10},{9,11},{10,... | collective-permute-start | bytes 393224 | tf_op jit(solution)/shard_map/ppermute | solution.py:45
  7.7 1.6 %collective-permute-start = (bf16[2,16,2048]{2,1,0:T(8,128)(2,1)S(1)}, bf16[2,16,2048]{2,1,0:T(8,128)(2,1)S(1)}, u32[]{:S(2)}, u32[]{:S(2)}) collective-permute-start(bf16[2,16,2048]{2,1,0:T(8,128)(2,1)S(1)} %get-tuple-element.20), channel_id=1, source_target_pairs={{0,1},{1,2},{2,3},{3,0},{4,5},{5,6},{6,7},{7,4},{8,9},{9,10},{10,1... | collective-permute-start | bytes 393224 | tf_op jit(solution)/shard_map/ppermute | solution.py:45
  9.3 2.2 %collective-permute-start.2 = (bf16[2,16,2048]{2,1,0:T(8,128)(2,1)S(1)}, bf16[2,16,2048]{2,1,0:T(8,128)(2,1)S(1)}, u32[]{:S(2)}, u32[]{:S(2)}) collective-permute-start(bf16[2,16,2048]{2,1,0:T(8,128)(2,1)S(1)} %get-tuple-element.20), channel_id=1, source_target_pairs={{0,3},{1,0},{2,1},{3,2},{4,7},{5,4},{6,5},{7,6},{8,11},{9,8},{10,9... | collective-permute-start | bytes 393224 | tf_op jit(solution)/shard_map/ppermute | solution.py:45
  11.5 0.8 select_reduce_fusion.5
  12.3 5.4 %collective-permute-done.1 = bf16[2,16,2048]{2,1,0:T(8,128)(2,1)S(1)} collective-permute-done((bf16[2,16,2048]{2,1,0:T(8,128)(2,1)S(1)}, bf16[2,16,2048]{2,1,0:T(8,128)(2,1)S(1)}, u32[]{:S(2)}, u32[]{:S(2)}) %collective-permute-start.1) | collective-permute-done | bytes 131104 | tf_op jit(solution)/shard_map/ppermute | solution.py:45
  17.7 0.6 collective-permute-done.2
  18.6 0.8 select_reduce_fusion.4
  19.4 1.0 collective-permute-done.3
  20.6 0.7 gather_fusion.1
  21.4 0.7 gather_fusion.2
  22.1 3.2 %fusion.17 = f32[64,1024]{1,0:T(8,128)S(1)} fusion(bf16[2048,1024]{1,0:T(8,128)(2,1)} %param.20, bf16[64,2048]{1,0:T(8,128)(2,1)S(1)} %gather_fusion.2, pred[64]{0:T(512)(128)(4,1)S(1)} %get-tuple-element.13), kind=kOutput, calls=%fused_computation.42 | convolution fusion | flops 268566528 | bytes 4718656 | tf_op jit(solution)/shard_map/dot_general | solution.py:138
  25.6 0.9 convolution_add_fusion
  26.6 0.8 pad_maximum_fusion.1
  27.5 6.1 %all-to-all-start = ((f32[32,2,1152]{2,1,0:T(2,128)}), f32[32,2,1152]{2,1,0:T(2,128)S(1)}, u32[]{:S(2)}, u32[]{:S(2)}) async-start(f32[32,2,1152]{2,1,0:T(2,128)} %pad_maximum_fusion.1), calls=%async_computation | async-start | bytes 589824 | tf_op jit(solution)/shard_map/all_to_all | solution.py:39
  33.9 1.8 %collective-permute-start.4 = (f32[64]{0:T(128)S(1)}, f32[64]{0:T(128)S(1)}, u32[]{:S(2)}, u32[]{:S(2)}) collective-permute-start(f32[64]{0:T(128)S(1)} %fusion), channel_id=1, source_target_pairs={{0,8},{4,20},{8,0},{12,28},{16,24},{20,4},{24,16},{28,12},{1,9},{5... | collective-permute-start | bytes 776 | tf_op jit(solution)/shard_map/ppermute | solution.py:71
  35.7 1.8 %collective-permute-done.4 = f32[64]{0:T(128)S(1)} collective-permute-done((f32[64]{0:T(128)S(1)}, f32[64]{0:T(128)S(1)}, u32[]{:S(2)}, u32[]{:S(2)}) %collective-permute-start.4) | collective-permute-done | bytes 288 | tf_op jit(solution)/shard_map/ppermute | solution.py:71
  37.5 1.7 %collective-permute-start.5 = (f32[64]{0:T(128)S(1)}, f32[64]{0:T(128)S(1)}, u32[]{:S(2)}, u32[]{:S(2)}) collective-permute-start(f32[64]{0:T(128)S(1)} %add.173), channel_id=1, source_target_pairs={{0,16},{4,12},{8,24},{12,4},{16,0},{20,28},{24,8},{28,20},{1,17},{... | collective-permute-start | bytes 776 | tf_op jit(solution)/shard_map/ppermute | solution.py:71
  39.3 5.0 %all-to-all-done = f32[32,2,1152]{2,1,0:T(2,128)S(1)} async-done(((f32[32,2,1152]{2,1,0:T(2,128)}), f32[32,2,1152]{2,1,0:T(2,128)S(1)}, u32[]{:S(2)}, u32[]{:S(2)}) %all-to-all-start) | async-done | bytes 294944 | tf_op jit(solution)/shard_map/all_to_all | solution.py:39
  44.8 0.7 broadcast_in_dim.116
  45.6 3.9 %all-to-all-start.1 = ((bf16[16,2,2048]{2,1,0:T(2,128)(2,1)}), bf16[16,2,2048]{2,1,0:T(2,128)(2,1)S(1)}, u32[]{:S(2)}, u32[]{:S(2)}) async-start(bf16[16,2,2048]{2,1,0:T(2,128)(2,1)} %bitcast.16), calls=%async_computation.1 | async-start | bytes 262144 | tf_op jit(solution)/shard_map/all_to_all | solution.py:39
  49.5 8.3 %all-to-all-done.1 = bf16[16,2,2048]{2,1,0:T(2,128)(2,1)S(1)} async-done(((bf16[16,2,2048]{2,1,0:T(2,128)(2,1)}), bf16[16,2,2048]{2,1,0:T(2,128)(2,1)S(1)}, u32[]{:S(2)}, u32[]{:S(2)}) %all-to-all-start.1) | async-done | bytes 131104 | tf_op jit(solution)/shard_map/all_to_all | solution.py:39
  57.9 3.6 %fusion.3 = f32[64,1024]{1,0:T(8,128)S(1)} fusion(bf16[1024,2048]{1,0:T(8,128)(2,1)} %param.19, f32[2048]{0:T(1024)S(1)} %copy-done.2, f32[64]{0:T(128)S(1)} %add_rsqrt_fusion.1, bf16[64,2048]{1,0:T(8,128)(2,1)S(1)} %gather_fusion.1, pred[64]{0:T(512)(128)(4,1)S(1)} %get-tuple-element.13), kind=kOutput, calls=%fused_computation.13 | convolution fusion | flops 269090816 | bytes 4727104 | tf_op jit(solution)/shard_map/dot_general | solution.py:18
  61.5 0.4 collective-permute-start.6
  62.2 1.1 gather_fusion
  63.9 3.6 %fusion.44 = f32[64,1024]{1,0:T(8,128)S(1)} fusion(bf16[64,2048]{1,0:T(8,128)(2,1)S(1)} %reshape.239, bf16[1024,2048]{1,0:T(8,128)(2,1)} %param.19), kind=kOutput, calls=%fused_computation.121 | convolution fusion | flops 268435456 | bytes 4718592 | tf_op jit(solution)/shard_map/dot_general | solution.py:18
  67.5 1.8 %collective-permute-start.9 = (f32[64,1024]{1,0:T(8,128)S(1)}, f32[64,1024]{1,0:T(8,128)S(1)}, u32[]{:S(2)}, u32[]{:S(2)}) collective-permute-start(f32[64,1024]{1,0:T(8,128)S(1)} %fusion.44), channel_id=1, source_target_pairs={{0,8},{4,20},{8,0},{12,28},{16,24},{20,4},{24,16},{28,12},{1,9},{5... | collective-permute-start | bytes 786440 | tf_op jit(solution)/shard_map/ppermute | solution.py:71
  69.3 0.6 collective-permute-start.7
  69.9 6.0 %collective-permute-done.9 = f32[64,1024]{1,0:T(8,128)S(1)} collective-permute-done((f32[64,1024]{1,0:T(8,128)S(1)}, f32[64,1024]{1,0:T(8,128)S(1)}, u32[]{:S(2)}, u32[]{:S(2)}) %collective-permute-start.9) | collective-permute-done | bytes 262176 | tf_op jit(solution)/shard_map/ppermute | solution.py:71
  75.9 1.2 collective-permute-start.10
  77.3 5.1 %collective-permute-done.10 = f32[64,1024]{1,0:T(8,128)S(1)} collective-permute-done((f32[64,1024]{1,0:T(8,128)S(1)}, f32[64,1024]{1,0:T(8,128)S(1)}, u32[]{:S(2)}, u32[]{:S(2)}) %collective-permute-start.10) | collective-permute-done | bytes 262176 | tf_op jit(solution)/shard_map/ppermute | solution.py:71
  82.6 0.7 reshape.277
  83.3 3.3 %all-to-all-start.2 = ((f32[8,1,256]{2,1,0:T(1,128)}), f32[8,1,256]{2,1,0:T(1,128)S(1)}, u32[]{:S(2)}, u32[]{:S(2)}) async-start(f32[8,1,256]{2,1,0:T(1,128)} %reshape.277), calls=%async_computation.2 | async-start | bytes 16384 | tf_op jit(solution)/shard_map/all_to_all | solution.py:39
  86.7 5.5 %all-to-all-done.2 = f32[8,1,256]{2,1,0:T(1,128)S(1)} async-done(((f32[8,1,256]{2,1,0:T(1,128)}), f32[8,1,256]{2,1,0:T(1,128)S(1)}, u32[]{:S(2)}, u32[]{:S(2)}) %all-to-all-start.2) | async-done | bytes 8224 | tf_op jit(solution)/shard_map/all_to_all | solution.py:39
  92.2 0.5 broadcast.243
  92.7 0.7 reduce.2
  93.5 0.6 multiply_add_fusion
  94.1 3.1 %fusion.8 = f32[64,2048]{1,0:T(8,128)S(1)} fusion(bf16[1024,2048]{1,0:T(8,128)(2,1)} %param.19, f32[64,1024]{1,0:T(8,128)S(1)} %get-tuple-element.12, f32[64,1024]{1,0:T(8,128)S(1)} %get-tuple-element.11, f32[64]{0:T(128)S(1)} %get-tuple-element.24, f32[64]{0:T(128)S(1)} %get-tuple-element.23, f32[64]{0:T(128)S(1)} %get-tuple-element.21, ...), kind=kOutput, calls=%fused_computation.32 | convolution fusion | flops 269025280 | bytes 5243904 | tf_op jit(solution)/shard_map/dot_general | solution.py:215
  97.8 1.4 %collective-permute-done.11 = f32[4,4,2,2048]{3,2,1,0:T(2,128)S(1)} collective-permute-done((f32[4,4,2,2048]{3,2,1,0:T(2,128)S(1)}, f32[4,4,2,2048]{3,2,1,0:T(2,128)S(1)}, u32[]{:S(2)}, u32[]{:S(2)}) %collective-permute-start.11) | collective-permute-done | bytes 262176 | tf_op jit(solution)/shard_map/ppermute | solution.py:219
  99.2 0.8 bitcast_add_fusion
  100.0 3.7 %all-to-all-start.3 = ((f32[16,2,2048]{2,1,0:T(2,128)}), f32[16,2,2048]{2,1,0:T(2,128)S(1)}, u32[]{:S(2)}, u32[]{:S(2)}) async-start(f32[16,2,2048]{2,1,0:T(2,128)} %bitcast.31), calls=%async_computation.3 | async-start | bytes 524288 | tf_op jit(solution)/shard_map/all_to_all | solution.py:39
  103.8 11.0 %all-to-all-done.3 = f32[16,2,2048]{2,1,0:T(2,128)S(1)} async-done(((f32[16,2,2048]{2,1,0:T(2,128)}), f32[16,2,2048]{2,1,0:T(2,128)S(1)}, u32[]{:S(2)}, u32[]{:S(2)}) %all-to-all-start.3) | async-done | bytes 262176 | tf_op jit(solution)/shard_map/all_to_all | solution.py:39
  115.1 0.7 broadcast_in_dim.123
  115.8 2.8 %all-to-all-start.4 = ((bf16[32,2,1024]{2,1,0:T(2,128)(2,1)}), bf16[32,2,1024]{2,1,0:T(2,128)(2,1)S(1)}, u32[]{:S(2)}, u32[]{:S(2)}) async-start(bf16[32,2,1024]{2,1,0:T(2,128)(2,1)} %bitcast.38), calls=%async_computation.4 | async-start | bytes 262144 | tf_op jit(solution)/shard_map/all_to_all | solution.py:39
  119.2 7.6 %all-to-all-done.4 = bf16[32,2,1024]{2,1,0:T(2,128)(2,1)S(1)} async-done(((bf16[32,2,1024]{2,1,0:T(2,128)(2,1)}), bf16[32,2,1024]{2,1,0:T(2,128)(2,1)S(1)}, u32[]{:S(2)}, u32[]{:S(2)}) %all-to-all-start.4) | async-done | bytes 131104 | tf_op jit(solution)/shard_map/all_to_all | solution.py:39
  126.8 4.8 %fusion.41 = f32[2048,1024]{1,0:T(8,128)} fusion(bf16[64,1024]{1,0:T(8,128)(2,1)S(1)} %reshape.246, bf16[64,2048]{1,0:T(8,128)(2,1)S(1)} %gather_fusion.1, pred[64]{0:T(512)(128)(4,1)S(1)} %get-tuple-element.13), kind=kOutput, calls=%fused_computation.118 | convolution fusion | flops 268566528 | bytes 8781888 | tf_op jit(solution)/shard_map/dot_general | solution.py:24
  131.6 4.8 %fusion.16 = f32[2048,1024]{1,0:T(8,128)} fusion(bf16[64,1024]{1,0:T(8,128)(2,1)S(1)} %reshape.246, bf16[64,2048]{1,0:T(8,128)(2,1)S(1)} %gather_fusion.2, pred[64]{0:T(512)(128)(4,1)S(1)} %get-tuple-element.13), kind=kOutput, calls=%fused_computation.41 | convolution fusion | flops 268566528 | bytes 8781888 | tf_op jit(solution)/shard_map/dot_general | solution.py:24
  (64 shorter events, 4.2 us)
Async XLA Ops:
  0.6 17.9 %copy-start = (f32[2048]{0:T(1024)S(1)}, f32[2048]{0:T(1024)}, u32[]{:S(2)}) copy-start(f32[2048]{0:T(1024)} %param.18) | copy-start | bytes 24580
  3.6 14.1 %collective-permute-start.1 = (bf16[2,16,2048]{2,1,0:T(8,128)(2,1)S(1)}, bf16[2,16,2048]{2,1,0:T(8,128)(2,1)S(1)}, u32[]{:S(2)}, u32[]{:S(2)}) collective-permute-start(bf16[2,16,2048]{2,1,0:T(8,128)(2,1)S(1)} %get-tuple-element.20), channel_id=1, source_target_pairs={{0,2},{1,3},{2,0},{3,1},{4,6},{5,7},{6,4},{7,5},{8,10},{9,11},{10,... | collective-permute-start | bytes 393224 | tf_op jit(solution)/shard_map/ppermute | solution.py:45
  7.7 10.0 %collective-permute-start = (bf16[2,16,2048]{2,1,0:T(8,128)(2,1)S(1)}, bf16[2,16,2048]{2,1,0:T(8,128)(2,1)S(1)}, u32[]{:S(2)}, u32[]{:S(2)}) collective-permute-start(bf16[2,16,2048]{2,1,0:T(8,128)(2,1)S(1)} %get-tuple-element.20), channel_id=1, source_target_pairs={{0,1},{1,2},{2,3},{3,0},{4,5},{5,6},{6,7},{7,4},{8,9},{9,10},{10,1... | collective-permute-start | bytes 393224 | tf_op jit(solution)/shard_map/ppermute | solution.py:45
  9.3 9.1 %collective-permute-start.2 = (bf16[2,16,2048]{2,1,0:T(8,128)(2,1)S(1)}, bf16[2,16,2048]{2,1,0:T(8,128)(2,1)S(1)}, u32[]{:S(2)}, u32[]{:S(2)}) collective-permute-start(bf16[2,16,2048]{2,1,0:T(8,128)(2,1)S(1)} %get-tuple-element.20), channel_id=1, source_target_pairs={{0,3},{1,0},{2,1},{3,2},{4,7},{5,4},{6,5},{7,6},{8,11},{9,8},{10,9... | collective-permute-start | bytes 393224 | tf_op jit(solution)/shard_map/ppermute | solution.py:45
  18.4 2.0 %collective-permute-start.3 = (bf16[4,2,16,2048]{3,2,1,0:T(8,128)(2,1)S(1)}, bf16[4,2,16,2048]{3,2,1,0:T(8,128)(2,1)S(1)}, u32[]{:S(2)}, u32[]{:S(2)}) collective-permute-start(bf16[4,2,16,2048]{3,2,1,0:T(8,128)(2,1)S(1)} %get-tuple-element.18), channel_id=1, source_target_pairs={{0,4},{4,0},{1,5},{5,1},{2,6},{6,2},{3,7},{7,3},{8,12},{12,8},{9,1... | collective-permute-start | bytes 1572872 | tf_op jit(solution)/shard_map/ppermute | solution.py:45
  22.1 3.5 %copy-start.1 = (bf16[2048,1024]{1,0:T(8,128)(2,1)S(1)}, bf16[2048,1024]{1,0:T(8,128)(2,1)}, u32[]{:S(2)}) copy-start(bf16[2048,1024]{1,0:T(8,128)(2,1)} %param.21) | copy-start | bytes 12582916
  25.6 32.3 %copy-start.2 = (f32[2048]{0:T(1024)S(1)}, f32[2048]{0:T(1024)}, u32[]{:S(2)}) copy-start(f32[2048]{0:T(1024)} %param.17) | copy-start | bytes 24580
  27.5 16.8 %all-to-all-start = ((f32[32,2,1152]{2,1,0:T(2,128)}), f32[32,2,1152]{2,1,0:T(2,128)S(1)}, u32[]{:S(2)}, u32[]{:S(2)}) async-start(f32[32,2,1152]{2,1,0:T(2,128)} %pad_maximum_fusion.1), calls=%async_computation | async-start | bytes 589824 | tf_op jit(solution)/shard_map/all_to_all | solution.py:39
  33.9 3.7 %collective-permute-start.4 = (f32[64]{0:T(128)S(1)}, f32[64]{0:T(128)S(1)}, u32[]{:S(2)}, u32[]{:S(2)}) collective-permute-start(f32[64]{0:T(128)S(1)} %fusion), channel_id=1, source_target_pairs={{0,8},{4,20},{8,0},{12,28},{16,24},{20,4},{24,16},{28,12},{1,9},{5... | collective-permute-start | bytes 776 | tf_op jit(solution)/shard_map/ppermute | solution.py:71
  37.5 12.0 %collective-permute-start.5 = (f32[64]{0:T(128)S(1)}, f32[64]{0:T(128)S(1)}, u32[]{:S(2)}, u32[]{:S(2)}) collective-permute-start(f32[64]{0:T(128)S(1)} %add.173), channel_id=1, source_target_pairs={{0,16},{4,12},{8,24},{12,4},{16,0},{20,28},{24,8},{28,20},{1,17},{... | collective-permute-start | bytes 776 | tf_op jit(solution)/shard_map/ppermute | solution.py:71
  45.6 12.3 %all-to-all-start.1 = ((bf16[16,2,2048]{2,1,0:T(2,128)(2,1)}), bf16[16,2,2048]{2,1,0:T(2,128)(2,1)S(1)}, u32[]{:S(2)}, u32[]{:S(2)}) async-start(bf16[16,2,2048]{2,1,0:T(2,128)(2,1)} %bitcast.16), calls=%async_computation.1 | async-start | bytes 262144 | tf_op jit(solution)/shard_map/all_to_all | solution.py:39
  57.9 4.0 %collective-permute-start.8 = (bf16[16,2,2048]{2,1,0:T(2,128)(2,1)S(1)}, bf16[16,2,2048]{2,1,0:T(2,128)(2,1)S(1)}, u32[]{:S(2)}, u32[]{:S(2)}) collective-permute-start(bf16[16,2,2048]{2,1,0:T(2,128)(2,1)S(1)} %all-to-all-done.1), channel_id=1, source_target_pairs={{0,4},{4,0},{1,5},{5,1},{2,6},{6,2},{3,7},{7,3},{8,12},{12,8},{9,1... | collective-permute-start | bytes 393224 | tf_op jit(solution)/shard_map/ppermute | solution.py:45
  61.5 7.8 %copy-start.3 = (s32[4,256]{1,0:T(4,128)S(1)}, s32[4,256]{1,0:T(4,128)}, u32[]{:S(2)}) copy-start(s32[4,256]{1,0:T(4,128)} %param.14) | copy-start | bytes 12292
  61.5 7.8 %collective-permute-start.6 = (f32[64,1024]{1,0:T(8,128)S(1)}, f32[64,1024]{1,0:T(8,128)S(1)}, u32[]{:S(2)}, u32[]{:S(2)}) collective-permute-start(f32[64,1024]{1,0:T(8,128)S(1)} %fusion.3), channel_id=1, source_target_pairs={{0,8},{4,20},{8,0},{12,28},{16,24},{20,4},{24,16},{28,12},{1,9},{5... | collective-permute-start | bytes 786440 | tf_op jit(solution)/shard_map/ppermute | solution.py:71
  67.5 8.4 %collective-permute-start.9 = (f32[64,1024]{1,0:T(8,128)S(1)}, f32[64,1024]{1,0:T(8,128)S(1)}, u32[]{:S(2)}, u32[]{:S(2)}) collective-permute-start(f32[64,1024]{1,0:T(8,128)S(1)} %fusion.44), channel_id=1, source_target_pairs={{0,8},{4,20},{8,0},{12,28},{16,24},{20,4},{24,16},{28,12},{1,9},{5... | collective-permute-start | bytes 786440 | tf_op jit(solution)/shard_map/ppermute | solution.py:71
  69.3 8.0 %collective-permute-start.7 = (f32[64,1024]{1,0:T(8,128)S(1)}, f32[64,1024]{1,0:T(8,128)S(1)}, u32[]{:S(2)}, u32[]{:S(2)}) collective-permute-start(f32[64,1024]{1,0:T(8,128)S(1)} %add.177), channel_id=1, source_target_pairs={{0,16},{4,12},{8,24},{12,4},{16,0},{20,28},{24,8},{28,20},{1,17},{... | collective-permute-start | bytes 786440 | tf_op jit(solution)/shard_map/ppermute | solution.py:71
  75.9 6.4 %collective-permute-start.10 = (f32[64,1024]{1,0:T(8,128)S(1)}, f32[64,1024]{1,0:T(8,128)S(1)}, u32[]{:S(2)}, u32[]{:S(2)}) collective-permute-start(f32[64,1024]{1,0:T(8,128)S(1)} %add.187), channel_id=1, source_target_pairs={{0,16},{4,12},{8,24},{12,4},{16,0},{20,28},{24,8},{28,20},{1,17},{... | collective-permute-start | bytes 786440 | tf_op jit(solution)/shard_map/ppermute | solution.py:71
  83.3 8.9 %all-to-all-start.2 = ((f32[8,1,256]{2,1,0:T(1,128)}), f32[8,1,256]{2,1,0:T(1,128)S(1)}, u32[]{:S(2)}, u32[]{:S(2)}) async-start(f32[8,1,256]{2,1,0:T(1,128)} %reshape.277), calls=%async_computation.2 | async-start | bytes 16384 | tf_op jit(solution)/shard_map/all_to_all | solution.py:39
  97.6 1.6 %collective-permute-start.11 = (f32[4,4,2,2048]{3,2,1,0:T(2,128)S(1)}, f32[4,4,2,2048]{3,2,1,0:T(2,128)S(1)}, u32[]{:S(2)}, u32[]{:S(2)}) collective-permute-start(f32[4,4,2,2048]{3,2,1,0:T(2,128)S(1)} %dynamic-slice_bitcast_fusion), channel_id=1, source_target_pairs={{0,4},{4,0},{1,5},{5,1},{2,6},{6,2},{3,7},{7,3},{8,12},{12,8},{9,1... | collective-permute-start | bytes 786440 | tf_op jit(solution)/shard_map/ppermute | solution.py:219
  100.0 14.7 %all-to-all-start.3 = ((f32[16,2,2048]{2,1,0:T(2,128)}), f32[16,2,2048]{2,1,0:T(2,128)S(1)}, u32[]{:S(2)}, u32[]{:S(2)}) async-start(f32[16,2,2048]{2,1,0:T(2,128)} %bitcast.31), calls=%async_computation.3 | async-start | bytes 524288 | tf_op jit(solution)/shard_map/all_to_all | solution.py:39
  115.8 11.0 %all-to-all-start.4 = ((bf16[32,2,1024]{2,1,0:T(2,128)(2,1)}), bf16[32,2,1024]{2,1,0:T(2,128)(2,1)S(1)}, u32[]{:S(2)}, u32[]{:S(2)}) async-start(bf16[32,2,1024]{2,1,0:T(2,128)(2,1)} %bitcast.38), calls=%async_computation.4 | async-start | bytes 262144 | tf_op jit(solution)/shard_map/all_to_all | solution.py:39

commit v14 on v8

--- a/solution.py
+++ b/solution.py
@@ -60,10 +60,15 @@
             ]
         )
         return jnp.sum(jnp.take(parts, (mine - jnp.arange(count)) % count, axis=0), axis=0)
-    step = 1
-    while step < count:
-        x = x + lax.ppermute(x, "section", [(i, i ^ step) for i in range(count)])
-        step *= 2
+    count_mp = lax.axis_size("mp")
+    steps = [1 << b for b in range(count.bit_length() - 1)]
+    for level in range(len(steps)):
+        pairs = []
+        for i in range(count):
+            for m in range(count_mp):
+                step = steps[level] if m % 2 == 0 else steps[len(steps) - 1 - level]
+                pairs.append((i * count_mp + m, (i ^ step) * count_mp + m))
+        x = x + lax.ppermute(x, ("section", "mp"), pairs)
     return x
 
 
@@ -159,6 +164,7 @@
     target_norm = (feature_all.astype(jnp.float32) * target_scale[:, None] * target_gain).astype(
         jnp.bfloat16
     )
+    target_logit = section_sum(contract_last(target_norm, head))
     draft_square = jnp.sum(hidden * hidden, axis=1)
     draft_scale = lax.rsqrt(draft_square / D + eps_norm)
     draft_norm = (hidden * draft_scale[:, None] * gain_full).astype(jnp.bfloat16)
@@ -169,7 +175,6 @@
     ).reshape(n_dev, per_dev, width)
     draft_norm_all = exchange(send2, ALL).reshape(total_rows, width)
 
-    target_logit = section_sum(contract_last(target_norm, head))
     draft_logit = section_sum(contract_last(draft_norm_all, head))
     column_zero = (my_mp * count_dp + my_dp) * vocab_tile
     is_label = (

time: 135 us -> 134 us (level)
  no operation moved by 1% of the time
where the time goes in v14:
time: 134 us
  waiting for transfers between devices  50.2 us (37%)
  starting transfers between devices  25 us (19%)
  matrix products  23.9 us (18%)
  blocking collectives  16.9 us (13%)
  local copies, waits for them, and re-layouts  8.62 us (6%)
  other arithmetic  5.63 us (4%)
  between operations  3.41 us (3%)
    all_to_all x4, waiting for transfers between devices, exchange(): return lax.all_to_all(send, axes, split_axis=0, concat_axis=0, tiled=True)  29.2 us
    all_to_all x1, blocking collectives, exchange(): return lax.all_to_all(send, axes, split_axis=0, concat_axis=0, tiled=True)  16.9 us
    ppermute x4, waiting for transfers between devices, section_sum(): x = x + lax.ppermute(x, ('section', 'mp'), pairs)  13.1 us
    all_to_all x4, starting transfers between devices, exchange(): return lax.all_to_all(send, axes, split_axis=0, concat_axis=0, tiled=True)  12.7 us
    dot_general x2, matrix products, contract_first(): lax.dot_general(operand, weights, (((0,), (0,)), ((), ())), preferred_ele...  9.51 us
    ppermute x4, starting transfers between devices, shifted(): lax.ppermute(x, axis, [(i, (i + k) % count) for i in range(count)])  8.02 us
    dot_general x2, matrix products, contract_last(): lax.dot_general(operand, weights, (((1,), (1,)), ((), ())), preferred_ele...  7.17 us
    ppermute x4, waiting for transfers between devices, shifted(): lax.ppermute(x, axis, [(i, (i + k) % count) for i in range(count)])  6.49 us
  transfers between devices with their start and end apart: 13, of which 10 were waited for; matrix products, arithmetic and copies ran while one was open for 7% of the time, Pallas kernels for 0%

profile of v14, /device:TPU:0, one launch (start us, length us, event | category | flops | bytes accessed | tf_op | source)
XLA Modules:
  0.0 133.7 jit_solution(201324893599830085)
XLA Ops:
  0.6 1.2 dynamic_slice.15
  2.5 1.0 constant_dynamic-slice_fusion
  3.6 4.1 %collective-permute-start.1 = (bf16[2,16,2048]{2,1,0:T(8,128)(2,1)S(1)}, bf16[2,16,2048]{2,1,0:T(8,128)(2,1)S(1)}, u32[]{:S(2)}, u32[]{:S(2)}) collective-permute-start(bf16[2,16,2048]{2,1,0:T(8,128)(2,1)S(1)} %get-tuple-element.20), channel_id=1, source_target_pairs={{0,2},{1,3},{2,0},{3,1},{4,6},{5,7},{6,4},{7,5},{8,10},{9,11},{10,... | collective-permute-start | bytes 393224 | tf_op jit(solution)/shard_map/ppermute | solution.py:45
  7.7 1.6 %collective-permute-start = (bf16[2,16,2048]{2,1,0:T(8,128)(2,1)S(1)}, bf16[2,16,2048]{2,1,0:T(8,128)(2,1)S(1)}, u32[]{:S(2)}, u32[]{:S(2)}) collective-permute-start(bf16[2,16,2048]{2,1,0:T(8,128)(2,1)S(1)} %get-tuple-element.20), channel_id=1, source_target_pairs={{0,1},{1,2},{2,3},{3,0},{4,5},{5,6},{6,7},{7,4},{8,9},{9,10},{10,1... | collective-permute-start | bytes 393224 | tf_op jit(solution)/shard_map/ppermute | solution.py:45
  9.3 2.2 %collective-permute-start.2 = (bf16[2,16,2048]{2,1,0:T(8,128)(2,1)S(1)}, bf16[2,16,2048]{2,1,0:T(8,128)(2,1)S(1)}, u32[]{:S(2)}, u32[]{:S(2)}) collective-permute-start(bf16[2,16,2048]{2,1,0:T(8,128)(2,1)S(1)} %get-tuple-element.20), channel_id=1, source_target_pairs={{0,3},{1,0},{2,1},{3,2},{4,7},{5,4},{6,5},{7,6},{8,11},{9,8},{10,9... | collective-permute-start | bytes 393224 | tf_op jit(solution)/shard_map/ppermute | solution.py:45
  11.5 0.8 dynamic_slice.18
  12.3 5.4 %collective-permute-done.1 = bf16[2,16,2048]{2,1,0:T(8,128)(2,1)S(1)} collective-permute-done((bf16[2,16,2048]{2,1,0:T(8,128)(2,1)S(1)}, bf16[2,16,2048]{2,1,0:T(8,128)(2,1)S(1)}, u32[]{:S(2)}, u32[]{:S(2)}) %collective-permute-start.1) | collective-permute-done | bytes 131104 | tf_op jit(solution)/shard_map/ppermute | solution.py:45
  17.7 0.7 collective-permute-done.2
  18.6 0.8 select_reduce_fusion.5
  19.4 0.8 select_reduce_fusion.4
  20.2 0.3 collective-permute-done.3
  20.7 0.7 gather_fusion.1
  21.5 0.7 gather_fusion
  22.2 0.2 fusion
  22.6 3.2 %fusion.16 = f32[64,1024]{1,0:T(8,128)S(1)} fusion(bf16[2048,1024]{1,0:T(8,128)(2,1)} %param.20, bf16[64,2048]{1,0:T(8,128)(2,1)S(1)} %gather_fusion.1, pred[64]{0:T(512)(128)(4,1)S(1)} %get-tuple-element.13), kind=kOutput, calls=%fused_computation.38 | convolution fusion | flops 268566528 | bytes 4718656 | tf_op jit(solution)/shard_map/dot_general | solution.py:138
  25.8 0.2 copy-done
  26.0 0.9 convolution_add_fusion
  27.2 16.9 %all_to_all.25 = f32[32,2,1280]{2,1,0:T(2,128)S(1)} all-to-all(f32[32,2,1280]{2,1,0:T(2,128)S(1)} %pad_maximum_fusion.1), channel_id=1, replica_groups=mesh['section'=4,'mp'=2,'dp'=4] {'section','mp','dp'}, dimensions={0} | all-to-all | bytes 655360 | tf_op jit(solution)/shard_map/all_to_all | solution.py:39
  44.8 0.9 broadcast_in_dim.105
  45.7 3.2 %all-to-all-start.1 = ((bf16[32,2,2048]{2,1,0:T(2,128)(2,1)}), bf16[32,2,2048]{2,1,0:T(2,128)(2,1)S(1)}, u32[]{:S(2)}, u32[]{:S(2)}) async-start(bf16[32,2,2048]{2,1,0:T(2,128)(2,1)} %bitcast.15), calls=%async_computation.1 | async-start | bytes 524288 | tf_op jit(solution)/shard_map/all_to_all | solution.py:39
  49.0 3.6 %fusion.3 = f32[64,1024]{1,0:T(8,128)S(1)} fusion(bf16[1024,2048]{1,0:T(8,128)(2,1)} %param.19, f32[2048]{0:T(1024)S(1)} %copy-done.1, f32[64]{0:T(128)S(1)} %add_rsqrt_fusion.1, bf16[64,2048]{1,0:T(8,128)(2,1)S(1)} %gather_fusion, pred[64]{0:T(512)(128)(4,1)S(1)} %get-tuple-element.13), kind=kOutput, calls=%fused_computation.11 | convolution fusion | flops 269090816 | bytes 4727104 | tf_op jit(solution)/shard_map/dot_general | solution.py:18
  52.5 1.8 %collective-permute-start.4 = (f32[64,1024]{1,0:T(8,128)S(1)}, f32[64,1024]{1,0:T(8,128)S(1)}, u32[]{:S(2)}, u32[]{:S(2)}) collective-permute-start(f32[64,1024]{1,0:T(8,128)S(1)} %fusion.3), channel_id=1, source_target_pairs={{0,8},{4,20},{8,0},{12,28},{16,24},{20,4},{24,16},{28,12},{1,9},{5... | collective-permute-start | bytes 786440 | tf_op jit(solution)/shard_map/ppermute | solution.py:71
  54.4 4.9 %all-to-all-done.1 = bf16[32,2,2048]{2,1,0:T(2,128)(2,1)S(1)} async-done(((bf16[32,2,2048]{2,1,0:T(2,128)(2,1)}), bf16[32,2,2048]{2,1,0:T(2,128)(2,1)S(1)}, u32[]{:S(2)}, u32[]{:S(2)}) %all-to-all-start.1) | async-done | bytes 262176 | tf_op jit(solution)/shard_map/all_to_all | solution.py:39
  59.4 3.6 %fusion.41 = f32[64,1024]{1,0:T(8,128)S(1)} fusion(bf16[64,2048]{1,0:T(8,128)(2,1)S(1)} %reshape.191, bf16[1024,2048]{1,0:T(8,128)(2,1)} %param.19), kind=kOutput, calls=%fused_computation.108 | convolution fusion | flops 268435456 | bytes 4718592 | tf_op jit(solution)/shard_map/dot_general | solution.py:18
  62.9 1.0 collective-permute-start.6
  64.0 0.6 collective-permute-start.5
  64.5 7.6 %collective-permute-done.6 = f32[64,1024]{1,0:T(8,128)S(1)} collective-permute-done((f32[64,1024]{1,0:T(8,128)S(1)}, f32[64,1024]{1,0:T(8,128)S(1)}, u32[]{:S(2)}, u32[]{:S(2)}) %collective-permute-start.6) | collective-permute-done | bytes 262176 | tf_op jit(solution)/shard_map/ppermute | solution.py:71
  72.2 0.8 collective-permute-start.7
  72.9 0.2 select_reduce_fusion.1
  73.1 5.5 %collective-permute-done.7 = f32[64,1024]{1,0:T(8,128)S(1)} collective-permute-done((f32[64,1024]{1,0:T(8,128)S(1)}, f32[64,1024]{1,0:T(8,128)S(1)}, u32[]{:S(2)}, u32[]{:S(2)}) %collective-permute-start.7) | collective-permute-done | bytes 262176 | tf_op jit(solution)/shard_map/ppermute | solution.py:71
  78.6 0.2 exponential_reduce_fusion.1
  78.9 0.7 reshape.221
  79.5 3.3 %all-to-all-start.2 = ((f32[8,1,256]{2,1,0:T(1,128)}), f32[8,1,256]{2,1,0:T(1,128)S(1)}, u32[]{:S(2)}, u32[]{:S(2)}) async-start(f32[8,1,256]{2,1,0:T(1,128)} %reshape.221), calls=%async_computation.2 | async-start | bytes 16384 | tf_op jit(solution)/shard_map/all_to_all | solution.py:39
  82.9 5.5 %all-to-all-done.2 = f32[8,1,256]{2,1,0:T(1,128)S(1)} async-done(((f32[8,1,256]{2,1,0:T(1,128)}), f32[8,1,256]{2,1,0:T(1,128)S(1)}, u32[]{:S(2)}, u32[]{:S(2)}) %all-to-all-start.2) | async-done | bytes 8224 | tf_op jit(solution)/shard_map/all_to_all | solution.py:39
  88.4 0.5 broadcast.155
  88.9 0.7 reduce.3
  89.7 0.6 multiply_add_fusion
  90.3 3.1 %fusion.7 = f32[64,2048]{1,0:T(8,128)S(1)} fusion(bf16[1024,2048]{1,0:T(8,128)(2,1)} %param.19, f32[64,1024]{1,0:T(8,128)S(1)} %get-tuple-element.12, f32[64,1024]{1,0:T(8,128)S(1)} %get-tuple-element.11, f32[64]{0:T(128)S(1)} %get-tuple-element.26, f32[64]{0:T(128)S(1)} %get-tuple-element.25, f32[64]{0:T(128)S(1)} %get-tuple-element.23, ...), kind=kOutput, calls=%fused_computation.28 | convolution fusion | flops 269025280 | bytes 5243904 | tf_op jit(solution)/shard_map/dot_general | solution.py:213
  93.5 0.3 reshape.193
  94.0 1.4 %collective-permute-done.8 = f32[4,4,2,2048]{3,2,1,0:T(2,128)S(1)} collective-permute-done((f32[4,4,2,2048]{3,2,1,0:T(2,128)S(1)}, f32[4,4,2,2048]{3,2,1,0:T(2,128)S(1)}, u32[]{:S(2)}, u32[]{:S(2)}) %collective-permute-start.8) | collective-permute-done | bytes 262176 | tf_op jit(solution)/shard_map/ppermute | solution.py:217
  95.4 0.8 bitcast_add_fusion
  96.3 3.5 %all-to-all-start.3 = ((f32[16,2,2048]{2,1,0:T(2,128)}), f32[16,2,2048]{2,1,0:T(2,128)S(1)}, u32[]{:S(2)}, u32[]{:S(2)}) async-start(f32[16,2,2048]{2,1,0:T(2,128)} %bitcast.25), calls=%async_computation.3 | async-start | bytes 524288 | tf_op jit(solution)/shard_map/all_to_all | solution.py:39
  99.8 11.1 %all-to-all-done.3 = f32[16,2,2048]{2,1,0:T(2,128)S(1)} async-done(((f32[16,2,2048]{2,1,0:T(2,128)}), f32[16,2,2048]{2,1,0:T(2,128)S(1)}, u32[]{:S(2)}, u32[]{:S(2)}) %all-to-all-start.3) | async-done | bytes 262176 | tf_op jit(solution)/shard_map/all_to_all | solution.py:39
  111.3 0.7 broadcast_in_dim.111
  112.1 2.6 %all-to-all-start.4 = ((bf16[32,2,1024]{2,1,0:T(2,128)(2,1)}), bf16[32,2,1024]{2,1,0:T(2,128)(2,1)S(1)}, u32[]{:S(2)}, u32[]{:S(2)}) async-start(bf16[32,2,1024]{2,1,0:T(2,128)(2,1)} %bitcast.32), calls=%async_computation.4 | async-start | bytes 262144 | tf_op jit(solution)/shard_map/all_to_all | solution.py:39
  115.3 7.7 %all-to-all-done.4 = bf16[32,2,1024]{2,1,0:T(2,128)(2,1)S(1)} async-done(((bf16[32,2,1024]{2,1,0:T(2,128)(2,1)}), bf16[32,2,1024]{2,1,0:T(2,128)(2,1)S(1)}, u32[]{:S(2)}, u32[]{:S(2)}) %all-to-all-start.4) | async-done | bytes 131104 | tf_op jit(solution)/shard_map/all_to_all | solution.py:39
  123.1 4.8 %fusion.37 = f32[2048,1024]{1,0:T(8,128)} fusion(bf16[64,1024]{1,0:T(8,128)(2,1)S(1)} %reshape.198, bf16[64,2048]{1,0:T(8,128)(2,1)S(1)} %gather_fusion, pred[64]{0:T(512)(128)(4,1)S(1)} %get-tuple-element.13), kind=kOutput, calls=%fused_computation.104 | convolution fusion | flops 268566528 | bytes 8781888 | tf_op jit(solution)/shard_map/dot_general | solution.py:24
  127.8 4.8 %fusion.15 = f32[2048,1024]{1,0:T(8,128)} fusion(bf16[64,1024]{1,0:T(8,128)(2,1)S(1)} %reshape.198, bf16[64,2048]{1,0:T(8,128)(2,1)S(1)} %gather_fusion.1, pred[64]{0:T(512)(128)(4,1)S(1)} %get-tuple-element.13), kind=kOutput, calls=%fused_computation.37 | convolution fusion | flops 268566528 | bytes 8781888 | tf_op jit(solution)/shard_map/dot_general | solution.py:24
  (52 shorter events, 2.4 us)
Async XLA Ops:
  3.6 14.1 %collective-permute-start.1 = (bf16[2,16,2048]{2,1,0:T(8,128)(2,1)S(1)}, bf16[2,16,2048]{2,1,0:T(8,128)(2,1)S(1)}, u32[]{:S(2)}, u32[]{:S(2)}) collective-permute-start(bf16[2,16,2048]{2,1,0:T(8,128)(2,1)S(1)} %get-tuple-element.20), channel_id=1, source_target_pairs={{0,2},{1,3},{2,0},{3,1},{4,6},{5,7},{6,4},{7,5},{8,10},{9,11},{10,... | collective-permute-start | bytes 393224 | tf_op jit(solution)/shard_map/ppermute | solution.py:45
  7.7 10.0 %collective-permute-start = (bf16[2,16,2048]{2,1,0:T(8,128)(2,1)S(1)}, bf16[2,16,2048]{2,1,0:T(8,128)(2,1)S(1)}, u32[]{:S(2)}, u32[]{:S(2)}) collective-permute-start(bf16[2,16,2048]{2,1,0:T(8,128)(2,1)S(1)} %get-tuple-element.20), channel_id=1, source_target_pairs={{0,1},{1,2},{2,3},{3,0},{4,5},{5,6},{6,7},{7,4},{8,9},{9,10},{10,1... | collective-permute-start | bytes 393224 | tf_op jit(solution)/shard_map/ppermute | solution.py:45
  9.3 9.2 %collective-permute-start.2 = (bf16[2,16,2048]{2,1,0:T(8,128)(2,1)S(1)}, bf16[2,16,2048]{2,1,0:T(8,128)(2,1)S(1)}, u32[]{:S(2)}, u32[]{:S(2)}) collective-permute-start(bf16[2,16,2048]{2,1,0:T(8,128)(2,1)S(1)} %get-tuple-element.20), channel_id=1, source_target_pairs={{0,3},{1,0},{2,1},{3,2},{4,7},{5,4},{6,5},{7,6},{8,11},{9,8},{10,9... | collective-permute-start | bytes 393224 | tf_op jit(solution)/shard_map/ppermute | solution.py:45
  18.5 2.0 %collective-permute-start.3 = (bf16[4,2,16,2048]{3,2,1,0:T(8,128)(2,1)S(1)}, bf16[4,2,16,2048]{3,2,1,0:T(8,128)(2,1)S(1)}, u32[]{:S(2)}, u32[]{:S(2)}) collective-permute-start(bf16[4,2,16,2048]{3,2,1,0:T(8,128)(2,1)S(1)} %get-tuple-element.18), channel_id=1, source_target_pairs={{0,4},{4,0},{1,5},{5,1},{2,6},{6,2},{3,7},{7,3},{8,12},{12,8},{9,1... | collective-permute-start | bytes 1572872 | tf_op jit(solution)/shard_map/ppermute | solution.py:45
  22.6 3.5 %copy-start = (bf16[2048,1024]{1,0:T(8,128)(2,1)S(1)}, bf16[2048,1024]{1,0:T(8,128)(2,1)}, u32[]{:S(2)}) copy-start(bf16[2048,1024]{1,0:T(8,128)(2,1)} %param.21) | copy-start | bytes 12582916
  26.0 22.9 %copy-start.1 = (f32[2048]{0:T(1024)S(1)}, f32[2048]{0:T(1024)}, u32[]{:S(2)}) copy-start(f32[2048]{0:T(1024)} %param.17) | copy-start | bytes 24580
  45.7 13.5 %all-to-all-start.1 = ((bf16[32,2,2048]{2,1,0:T(2,128)(2,1)}), bf16[32,2,2048]{2,1,0:T(2,128)(2,1)S(1)}, u32[]{:S(2)}, u32[]{:S(2)}) async-start(bf16[32,2,2048]{2,1,0:T(2,128)(2,1)} %bitcast.15), calls=%async_computation.1 | async-start | bytes 524288 | tf_op jit(solution)/shard_map/all_to_all | solution.py:39
  48.9 14.9 %copy-start.2 = (s32[4,256]{1,0:T(4,128)S(1)}, s32[4,256]{1,0:T(4,128)}, u32[]{:S(2)}) copy-start(s32[4,256]{1,0:T(4,128)} %param.14) | copy-start | bytes 12292
  52.5 11.4 %collective-permute-start.4 = (f32[64,1024]{1,0:T(8,128)S(1)}, f32[64,1024]{1,0:T(8,128)S(1)}, u32[]{:S(2)}, u32[]{:S(2)}) collective-permute-start(f32[64,1024]{1,0:T(8,128)S(1)} %fusion.3), channel_id=1, source_target_pairs={{0,8},{4,20},{8,0},{12,28},{16,24},{20,4},{24,16},{28,12},{1,9},{5... | collective-permute-start | bytes 786440 | tf_op jit(solution)/shard_map/ppermute | solution.py:71
  62.9 9.2 %collective-permute-start.6 = (f32[64,1024]{1,0:T(8,128)S(1)}, f32[64,1024]{1,0:T(8,128)S(1)}, u32[]{:S(2)}, u32[]{:S(2)}) collective-permute-start(f32[64,1024]{1,0:T(8,128)S(1)} %fusion.41), channel_id=1, source_target_pairs={{0,8},{4,20},{8,0},{12,28},{16,24},{20,4},{24,16},{28,12},{1,9},{5... | collective-permute-start | bytes 786440 | tf_op jit(solution)/shard_map/ppermute | solution.py:71
  64.0 9.2 %collective-permute-start.5 = (f32[64,1024]{1,0:T(8,128)S(1)}, f32[64,1024]{1,0:T(8,128)S(1)}, u32[]{:S(2)}, u32[]{:S(2)}) collective-permute-start(f32[64,1024]{1,0:T(8,128)S(1)} %add.146), channel_id=1, source_target_pairs={{0,16},{4,12},{8,24},{12,4},{16,0},{20,28},{24,8},{28,20},{1,17},{... | collective-permute-start | bytes 786440 | tf_op jit(solution)/shard_map/ppermute | solution.py:71
  72.2 6.4 %collective-permute-start.7 = (f32[64,1024]{1,0:T(8,128)S(1)}, f32[64,1024]{1,0:T(8,128)S(1)}, u32[]{:S(2)}, u32[]{:S(2)}) collective-permute-start(f32[64,1024]{1,0:T(8,128)S(1)} %add.149), channel_id=1, source_target_pairs={{0,16},{4,12},{8,24},{12,4},{16,0},{20,28},{24,8},{28,20},{1,17},{... | collective-permute-start | bytes 786440 | tf_op jit(solution)/shard_map/ppermute | solution.py:71
  79.5 8.9 %all-to-all-start.2 = ((f32[8,1,256]{2,1,0:T(1,128)}), f32[8,1,256]{2,1,0:T(1,128)S(1)}, u32[]{:S(2)}, u32[]{:S(2)}) async-start(f32[8,1,256]{2,1,0:T(1,128)} %reshape.221), calls=%async_computation.2 | async-start | bytes 16384 | tf_op jit(solution)/shard_map/all_to_all | solution.py:39
  93.8 1.6 %collective-permute-start.8 = (f32[4,4,2,2048]{3,2,1,0:T(2,128)S(1)}, f32[4,4,2,2048]{3,2,1,0:T(2,128)S(1)}, u32[]{:S(2)}, u32[]{:S(2)}) collective-permute-start(f32[4,4,2,2048]{3,2,1,0:T(2,128)S(1)} %dynamic-slice_bitcast_fusion), channel_id=1, source_target_pairs={{0,4},{4,0},{1,5},{5,1},{2,6},{6,2},{3,7},{7,3},{8,12},{12,8},{9,1... | collective-permute-start | bytes 786440 | tf_op jit(solution)/shard_map/ppermute | solution.py:217
  96.3 14.7 %all-to-all-start.3 = ((f32[16,2,2048]{2,1,0:T(2,128)}), f32[16,2,2048]{2,1,0:T(2,128)S(1)}, u32[]{:S(2)}, u32[]{:S(2)}) async-start(f32[16,2,2048]{2,1,0:T(2,128)} %bitcast.25), calls=%async_computation.3 | async-start | bytes 524288 | tf_op jit(solution)/shard_map/all_to_all | solution.py:39
  112.1 11.0 %all-to-all-start.4 = ((bf16[32,2,1024]{2,1,0:T(2,128)(2,1)}), bf16[32,2,1024]{2,1,0:T(2,128)(2,1)S(1)}, u32[]{:S(2)}, u32[]{:S(2)}) async-start(bf16[32,2,1024]{2,1,0:T(2,128)(2,1)} %bitcast.32), calls=%async_computation.4 | async-start | bytes 262144 | tf_op jit(solution)/shard_map/all_to_all | solution.py:39
